TPU v7x, 32 devices: a whole 2x2x4 slice. The times are simulated.
32 devices in a mesh: seq: 2 (over x), mp: 4 (over z), dp: 4 (over y, core).
Axes of the slice: x: 2, y: 2, z: 4, core: 2. Of those that a mesh axis runs over, the one named last changes fastest.
Arguments:
- features: bfloat16 [4, 2048, 768], P('dp', 'seq'), may hold values from -6 to 6
- conv_weight: bfloat16 [5, 768, 768], P(None, 'mp'), may hold values from -0.09375 to 0.09375
- keep: int32 [4], P('dp'), may hold values 0 or 1
- tiles: int32 [4, 2, 2, 2], P('dp'), may hold values from 0 to 63, as said below
- counts: int32 [4, 2], P('dp'), may hold values from 0 to 2, as said below
- targets: float32 [4, 2, 2, 1024], P('dp', 'seq'), may hold values from -6 to 6
Outputs:
- conv_grad: float32 [5, 768, 768], P(None, 'mp', ('seq', 'dp'))
Inputs may be any that keep to these rules, and one draw needn't show every extreme that they name: `tiles`: entries are block numbers of 32 positions in a sequence. For every sequence and owner, listing the 2 row blocks and then the 2 column blocks, exactly 2 of these 4 entries lie in the positions of each index of seq. Each owner's live slots are its first counts slots; in every sequence some owner has all 2 slots live.
All inputs are finite; a program needn't handle non-finite values. No bound on the sum of `keep` on one device may be relied on, other than what follows from the above.
Results may differ from a plain program's by a relative error of at most 0.0015.
Values may be sent and summed in bfloat16 or wider, within the bound.
No kernel may reach another device: no remote copies, remote signals or barrier semaphores. Data moves between devices by JAX's collectives and lax.ppermute only.
A program may use at most 64 MiB of HBM per device.

v0:
```python
import math

import jax
import jax.numpy as jnp
from jax import lax
from jax.sharding import PartitionSpec as P

TB = 32
PER = 2


def extended(cells, sides, width):
    for axis, dim in sides:
        count = lax.axis_size(axis)
        ends = count - 1
        head = lax.slice_in_dim(cells, 0, width, axis=dim)
        tail = lax.slice_in_dim(cells, cells.shape[dim] - width, cells.shape[dim], axis=dim)
        cells = jnp.concatenate(
            [
                lax.ppermute(tail, axis, [(i, (i + 1) % count) for i in range(ends)]),
                cells,
                lax.ppermute(head, axis, [((i + 1) % count, i) for i in range(ends)]),
            ],
            axis=dim,
        )
    return cells


def take_rows(source_array, index_array):
    return jax.vmap(lambda table, picked: table[picked])(source_array, index_array)


def conv_apply(padded, weight, length):
    total = jnp.einsum(
        "mbi,oi->mbo", padded[:, 0:length], weight[0], preferred_element_type=jnp.float32
    )
    for offset in range(1, weight.shape[0]):
        total = total + jnp.einsum(
            "mbi,oi->mbo",
            padded[:, offset : offset + length],
            weight[offset],
            preferred_element_type=jnp.float32,
        )
    return total


def weight_term(padded, dconv, length, taps):
    return jnp.stack(
        [
            jnp.einsum(
                "mbi,mbo->oi",
                padded[:, offset : offset + length],
                dconv,
                preferred_element_type=jnp.float32,
            )
            for offset in range(taps)
        ]
    )


def per_device(features, conv_weight, keep, tiles, counts, targets):
    members, length, width = features.shape
    taps = conv_weight.shape[0]
    narrow = conv_weight.shape[1]
    seq_count = lax.axis_size("seq")
    my_index = lax.axis_index("seq")
    my_part = lax.axis_index("mp")
    x_float = features.astype(jnp.float32)
    activations = jax.nn.gelu(x_float).astype(jnp.bfloat16)
    padded = extended(activations, (("seq", 1),), 2)
    scaling = 1.25 * keep.astype(jnp.float32)
    conv_out = conv_apply(padded, conv_weight, length)
    x_local = lax.dynamic_slice_in_dim(x_float, my_part * narrow, narrow, 2)
    mixed_out = (x_local + scaling[:, None, None] * conv_out).astype(jnp.bfloat16)
    capacity = tiles.shape[2]
    n_sides = 2 * capacity
    per_block = length // TB
    sides = jnp.concatenate([tiles[..., 0], tiles[..., 1]], axis=-1)
    side_source = sides // per_block
    side_local = sides % per_block
    own_sides = lax.dynamic_index_in_dim(sides, my_index, 1, keepdims=False)
    own_source = own_sides // per_block
    before = jnp.arange(n_sides)[None, :] < jnp.arange(n_sides)[:, None]
    same_source = own_source[:, :, None] == own_source[:, None, :]
    rank_within = jnp.sum(jnp.logical_and(same_source, before[None]), axis=-1)
    slot_index = own_source * PER + rank_within
    held_here = side_source == my_index
    held_order = jnp.cumsum(held_here.astype(jnp.int32), axis=-1) - 1
    picks = jnp.stack(
        [
            jnp.sum(
                jnp.where(jnp.logical_and(held_here, held_order == position), side_local, 0),
                axis=-1,
            )
            for position in range(PER)
        ],
        axis=-1,
    )
    blocks = mixed_out.reshape(members, per_block, TB, narrow)
    whole = lax.all_gather(blocks, "seq", axis=1, tiled=True)
    side_rows = take_rows(whole, own_sides)
    row_side = side_rows[:, :capacity]
    col_side = side_rows[:, capacity:]
    partial_tiles = jnp.einsum(
        "mcid,mcjd->mcij", row_side, col_side, preferred_element_type=jnp.float32
    )
    predicted = lax.psum(partial_tiles, "mp") / math.sqrt(width)
    target_tiles = targets[:, 0].reshape(members, capacity, TB, TB)
    own_count = lax.dynamic_index_in_dim(counts, my_index, 1, keepdims=False)
    live_mask = (jnp.arange(capacity)[None, :] < own_count[:, None]).astype(jnp.float32)
    n_live = jnp.sum(counts, axis=-1).astype(jnp.float32)
    dpredicted = (
        2.0
        / math.sqrt(width)
        * live_mask[:, :, None, None]
        * (predicted - target_tiles)
        / n_live[:, None, None, None]
    )
    row_float = row_side.astype(jnp.float32)
    col_float = col_side.astype(jnp.float32)
    drow = jnp.einsum("mcij,mcjd->mcid", dpredicted, col_float, precision=lax.Precision.HIGHEST)
    dcol = jnp.einsum("mcij,mcid->mcjd", dpredicted, row_float, precision=lax.Precision.HIGHEST)
    dside = jnp.concatenate([drow, dcol], axis=1).astype(jnp.bfloat16)
    inverse = jnp.argsort(slot_index, axis=-1)
    outgoing_grads = take_rows(dside, inverse).reshape(members, seq_count, PER, TB, narrow)
    returned = lax.all_to_all(outgoing_grads, "seq", split_axis=1, concat_axis=1, tiled=True)
    selector = (
        picks.reshape(members, seq_count * PER)[:, :, None] == jnp.arange(per_block)[None, None, :]
    ).astype(jnp.bfloat16)
    dmixed = jnp.einsum(
        "mkn,mktd->mntd",
        selector,
        returned.reshape(members, seq_count * PER, TB, narrow),
        preferred_element_type=jnp.float32,
    ).reshape(members, length, narrow)
    dconv = (scaling[:, None, None] * dmixed).astype(jnp.bfloat16)
    weight_local = weight_term(padded, dconv, length, taps)
    return lax.psum_scatter(weight_local, ("seq", "dp"), scatter_dimension=2, tiled=True)


def solution(mesh):
    placed = (
        P("dp", "seq", None),
        P(None, "mp", None),
        P("dp"),
        P("dp", None, None, None),
        P("dp", None),
        P("dp", "seq", None, None),
    )
    return jax.shard_map(
        per_device,
        mesh=mesh,
        in_specs=placed,
        out_specs=P(None, "mp", ("seq", "dp")),
        check_vma=False,
    )
```

profile of v0, /device:TPU:0, one launch (start us, length us, event | category | flops | bytes accessed | tf_op | source)
XLA Modules:
  0.0 164.4 jit_solution(2295944380300024966)
XLA Ops:
  6.5 1.7 %copy.48 = bf16[1,1024,768]{1,2,0:T(8,128)(2,1)S(1)} copy(bf16[1,1024,768]{2,1,0:T(8,128)(2,1)} %param.6) | data formatting | bytes 3145728 | tf_op args[0]
  8.3 1.1 fusion.7
  9.3 0.1 fusion.79
  9.5 5.5 %collective-permute-start = (bf16[1,2,768]{1,2,0:T(8,128)(2,1)S(1)}, bf16[1,2,768]{1,2,0:T(8,128)(2,1)}, u32[]{:S(2)}, u32[]{:S(2)}) collective-permute-start(bf16[1,2,768]{1,2,0:T(8,128)(2,1)S(1)} %get-tuple-element.16), channel_id=1, source_target_pairs={{0,16},{1,17},{2,18},{3,19},{4,20},{5,21},{6,22},{7,23},{8,24},{9,... | collective-permute-start | bytes 9224 | tf_op jit(solution)/shard_map/ppermute | solution.py:20
  15.0 1.3 collective-permute-start.1
  16.3 0.2 slice_reduce_fusion.1
  16.5 0.6 fusion.77
  17.2 0.6 copy-done.4
  17.7 0.6 fusion.68
  18.3 0.5 compare_select_fusion.1
  18.8 1.3 constant_dynamic-slice_fusion.1
  20.1 0.7 reduce_window_sum.11
  20.9 0.7 pad_bitcast_fusion.1
  21.6 0.9 convert_reduce_fusion
  22.6 0.6 sort.17
  23.3 0.8 fusion.59
  24.1 2.3 %fusion.16 = f32[1024,192]{0,1:T(8,128)} fusion(bf16[1,1024,768]{1,2,0:T(8,128)(2,1)S(1)} %fusion.7, bf16[5,192,768]{2,1,0:T(8,128)(2,1)} %param.7), kind=kOutput, calls=%fused_computation.25 | convolution fusion | flops 301989888 | bytes 2654208 | tf_op jit(solution)/shard_map/mbi,oi->mbo/dot_general | solution.py:38
  26.4 0.7 fusion.64
  27.1 1.2 compare_select_fusion.2
  28.3 1.3 reduce_sum.40
  29.6 2.1 %convert_element_type.74 = f32[1,1024,768]{1,2,0:T(8,128)} convert(bf16[1,1024,768]{1,2,0:T(8,128)(2,1)S(1)} %copy.48) | non-fusion elementwise | flops 786432 | bytes 4718592 | tf_op jit(solution)/shard_map/convert_element_type | solution.py:68
  33.1 1.9 %fusion.41 = f32[1024,192]{0,1:T(8,128)S(1)} fusion(bf16[1,2,768]{1,2,0:T(8,128)(2,1)} %collective-permute-done.1, bf16[1,1024,768]{1,2,0:T(8,128)(2,1)S(1)} %fusion.7, bf16[5,192,768]{2,1,0:T(8,128)(2,1)} %param.7), kind=kOutput, calls=%fused_computation.53 | convolution fusion | flops 305135616 | bytes 2850816 | tf_op jit(solution)/shard_map/mbi,oi->mbo/dot_general | solution.py:38
  35.0 1.7 %fusion.38 = f32[1024,192]{0,1:T(8,128)S(1)} fusion(bf16[1,1024,768]{1,2,0:T(8,128)(2,1)S(1)} %fusion.7, bf16[1,2,768]{1,2,0:T(8,128)(2,1)} %collective-permute-done, bf16[5,192,768]{2,1,0:T(8,128)(2,1)S(1)} %copy-done.1), kind=kOutput, calls=%fused_computation.52 | convolution fusion | flops 305135616 | bytes 2657280 | tf_op jit(solution)/shard_map/mbi,oi->mbo/dot_general | solution.py:38
  36.8 1.7 %fusion.18 = f32[1024,192]{0,1:T(8,128)S(1)} fusion(f32[1024,192]{0,1:T(8,128)S(1)} %copy-done, f32[1024,192]{0,1:T(8,128)S(1)} %fusion.38, bf16[5,192,768]{2,1,0:T(8,128)(2,1)S(1)} %copy-done.1, bf16[1,2,768]{1,2,0:T(8,128)(2,1)} %collective-permute-done, bf16[1,1024,768]{1,2,0:T(8,128)(2,1)S(1)} %fusion.7), kind=kOutput, calls=%fused_computation.30 | convolution fusion | flops 305528832 | bytes 4230144 | tf_op jit(solution)/shard_map/mbi,oi->mbo/dot_general | solution.py:34
  38.5 2.1 %fusion.34 = bf16[1,1024,192]{1,2,0:T(8,128)(2,1)S(1)} fusion(f32[1024,192]{0,1:T(8,128)S(1)} %fusion.41, f32[1024,192]{0,1:T(8,128)S(1)} %fusion.18, f32[1,1024,768]{1,2,0:T(8,128)} %convert_element_type.74, s32[]{:T(128)S(6)} %select_n.115, f32[]{:T(128)} %bitcast, bf16[5,192,768]{2,1,0:T(8,128)(2,1)S(1)} %copy-done.1, ...), kind=kOutput, calls=%fused_computation.46 | convolution fusion | flops 306118656 | bytes 4623368 | tf_op jit(solution)/shard_map/mbi,oi->mbo/dot_general | solution.py:38
  40.6 0.2 copy.49
  40.8 15.3 %all_gather.3 = bf16[1,64,32,192]{3,2,0,1:T(8,128)(2,1)S(1)} all-gather(bf16[1,32,32,192]{3,2,0,1:T(8,128)(2,1)S(1)} %bitcast.138), channel_id=1, replica_groups=mesh['seq'=2,'mp'=4,'dp'=4] {'seq'}, dimensions={1}, use_global_device_ids=true | all-gather | bytes 1179648 | tf_op jit(solution)/shard_map/all_gather | solution.py:100
  56.2 0.6 gather_fusion
  56.7 0.1 convolution_bitcast_fusion.4
  56.8 19.3 %psum.7 = f32[1,2,32,32]{3,2,1,0:T(8,128)S(1)} all-reduce(f32[1,2,32,32]{3,2,1,0:T(8,128)S(1)} %convolution_bitcast_fusion.4), channel_id=1, replica_groups=mesh['seq'=2,'mp'=4,'dp'=4] {'mp'}, use_global_device_ids=true, to_apply=%region_3.4 | all-reduce | flops 2048 | bytes 16384 | tf_op jit(solution)/shard_map/psum | solution.py:107
  76.1 0.3 fusion.36
  76.4 0.2 fusion.35
  76.7 1.2 gather_fusion.1
  77.9 3.3 %all-to-all-start = ((bf16[1,2,2,32,192]{4,3,2,0,1:T(8,128)(2,1)}), bf16[1,2,2,32,192]{4,3,2,0,1:T(8,128)(2,1)S(1)}, u32[]{:S(2)}, u32[]{:S(2)}) async-start(bf16[1,2,2,32,192]{4,3,2,0,1:T(8,128)(2,1)} %bitcast.37), calls=%async_computation | async-start | bytes 131072 | tf_op jit(solution)/shard_map/all_to_all | solution.py:126
  81.2 0.2 reduce-scatter.4.cloned.1.call-start
  81.6 3.7 %all-to-all-done = bf16[1,2,2,32,192]{4,3,2,0,1:T(8,128)(2,1)S(1)} async-done(((bf16[1,2,2,32,192]{4,3,2,0,1:T(8,128)(2,1)}), bf16[1,2,2,32,192]{4,3,2,0,1:T(8,128)(2,1)S(1)}, u32[]{:S(2)}, u32[]{:S(2)}) %all-to-all-start) | async-done | bytes 49184 | tf_op jit(solution)/shard_map/all_to_all | solution.py:126
  85.3 0.4 fusion.22
  85.7 0.3 copy.60
  86.0 2.9 %fusion.33 = f32[5,192,768]{2,1,0:T(8,128)} fusion(bf16[1024,192]{1,0:T(8,128)(2,1)S(1)} %bitcast.139, bf16[1,2,768]{1,2,0:T(8,128)(2,1)} %collective-permute-done, bf16[1,1024,768]{1,2,0:T(8,128)(2,1)S(1)} %fusion.7), kind=kOutput, calls=%fused_computation.45 | convolution fusion | flops 305135616 | bytes 2558976 | tf_op jit(solution)/shard_map/mbi,mbo->oi/dot_general | solution.py:50
  88.9 3.0 %fusion.32 = f32[5,192,768]{2,1,0:T(8,128)} fusion(f32[5,192,768]{2,1,0:T(8,128)} %fusion.33, bf16[1024,192]{1,0:T(8,128)(2,1)S(1)} %bitcast.140, bf16[1,1024,768]{1,2,0:T(8,128)(2,1)S(1)} %fusion.7, bf16[1,2,768]{1,2,0:T(8,128)(2,1)} %collective-permute-done), kind=kOutput, calls=%fused_computation.43 | convolution fusion | flops 305135616 | bytes 2752512 | tf_op jit(solution)/shard_map/mbi,mbo->oi/dot_general | solution.py:50
  91.9 1.5 fusion.27
  93.4 3.0 %fusion.31 = f32[5,192,768]{2,1,0:T(8,128)} fusion(f32[5,192,768]{2,1,0:T(8,128)} %fusion.27, bf16[1024,192]{1,0:T(8,128)(2,1)S(1)} %bitcast.142, bf16[1,1024,768]{1,2,0:T(8,128)(2,1)S(1)} %fusion.7, bf16[1,2,768]{1,2,0:T(8,128)(2,1)} %collective-permute-done.1), kind=kOutput, calls=%fused_computation.41 | convolution fusion | flops 305135616 | bytes 2752512 | tf_op jit(solution)/shard_map/mbi,mbo->oi/dot_general | solution.py:50
  96.4 3.0 %fusion.30 = f32[5,192,768]{2,1,0:T(8,128)} fusion(f32[5,192,768]{2,1,0:T(8,128)} %fusion.31, bf16[1024,192]{1,0:T(8,128)(2,1)S(1)} %bitcast.143, bf16[1,2,768]{1,2,0:T(8,128)(2,1)} %collective-permute-done.1, bf16[1,1024,768]{1,2,0:T(8,128)(2,1)S(1)} %fusion.7), kind=kOutput, calls=%fused_computation.39 | convolution fusion | flops 305135616 | bytes 2752512 | tf_op jit(solution)/shard_map/mbi,mbo->oi/dot_general | solution.py:50
  99.4 6.0 %copy.63 = f32[5,192,768]{1,0,2:T(8,128)} copy(f32[5,192,768]{2,1,0:T(8,128)} %fusion.30) | data formatting | bytes 5898240
  105.4 6.1 %reshape.980 = f32[768,960]{1,0:T(8,128)} reshape(f32[768,5,192]{2,1,0:T(8,128)} %bitcast.136) | data formatting | bytes 5898240
  111.6 43.7 %reduce-scatter.4.cloned.1.call-done = f32[96,960]{1,0:T(8,128)} async-done(((f32[768,960]{1,0:T(8,128)}), f32[96,960]{1,0:T(8,128)}) %reduce-scatter.4.cloned.1.call-update) | async-done | bytes 368656
  155.3 1.2 reshape.981
  156.5 1.1 copy.64
  (37 shorter events, 0.6 us)
Async XLA Ops:
  8.3 8.0 %copy-start.3 = (s32[1,2,2,2]{3,2,1,0:T(2,128)S(1)}, s32[1,2,2,2]{3,2,1,0:T(2,128)}, u32[]{:S(2)}) copy-start(s32[1,2,2,2]{3,2,1,0:T(2,128)} %param.9) | copy-start | bytes 100
  9.5 25.5 %collective-permute-start = (bf16[1,2,768]{1,2,0:T(8,128)(2,1)S(1)}, bf16[1,2,768]{1,2,0:T(8,128)(2,1)}, u32[]{:S(2)}, u32[]{:S(2)}) collective-permute-start(bf16[1,2,768]{1,2,0:T(8,128)(2,1)S(1)} %get-tuple-element.16), channel_id=1, source_target_pairs={{0,16},{1,17},{2,18},{3,19},{4,20},{5,21},{6,22},{7,23},{8,24},{9,... | collective-permute-start | bytes 9224 | tf_op jit(solution)/shard_map/ppermute | solution.py:20
  15.0 18.1 %collective-permute-start.1 = (bf16[1,2,768]{1,2,0:T(8,128)(2,1)S(1)}, bf16[1,2,768]{1,2,0:T(8,128)(2,1)}, u32[]{:S(2)}, u32[]{:S(2)}) collective-permute-start(bf16[1,2,768]{1,2,0:T(8,128)(2,1)S(1)} %get-tuple-element.17), channel_id=1, source_target_pairs={{16,0},{17,1},{18,2},{19,3},{20,4},{21,5},{22,6},{23,7},{24,8},{25... | collective-permute-start | bytes 9224 | tf_op jit(solution)/shard_map/ppermute | solution.py:22
  17.1 0.6 copy-start.4
  22.6 3.8 %copy-start.5 = (s32[1,2,4]{2,1,0:T(2,128)S(1)}, s32[1,2,4]{2,1,0:T(2,128)}, u32[]{:S(2)}) copy-start(s32[1,2,4]{2,1,0:T(2,128)} %copy-done.4) | copy-start | bytes 100
  23.3 3.2 %copy-start.6 = (s32[1,2,4]{2,1,0:T(2,128)S(1)}, s32[1,2,4]{2,1,0:T(2,128)}, u32[]{:S(2)}) copy-start(s32[1,2,4]{2,1,0:T(2,128)} %reduce_window_sum.11) | copy-start | bytes 100
  23.3 3.2 %copy-start.7 = (pred[1,2,4]{2,1,0:T(4,128)(4,1)S(1)}, pred[1,2,4]{2,1,0:T(4,128)(4,1)}, u32[]{:S(2)}) copy-start(pred[1,2,4]{2,1,0:T(4,128)(4,1)} %get-tuple-element.12) | copy-start | bytes 28
  29.6 3.4 %copy-start.2 = (f32[1,1,2,1024]{3,2,1,0:T(2,128)S(1)}, f32[1,1,2,1024]{3,2,1,0:T(2,128)}, u32[]{:S(2)}) copy-start(f32[1,1,2,1024]{3,2,1,0:T(2,128)} %param.11) | copy-start | bytes 24580
  33.1 1.9 %copy-start.1 = (bf16[5,192,768]{2,1,0:T(8,128)(2,1)S(1)}, bf16[5,192,768]{2,1,0:T(8,128)(2,1)}, u32[]{:S(2)}) copy-start(bf16[5,192,768]{2,1,0:T(8,128)(2,1)} %param.7) | copy-start | bytes 4423684
  35.0 1.8 %copy-start = (f32[1024,192]{0,1:T(8,128)S(1)}, f32[1024,192]{0,1:T(8,128)}, u32[]{:S(2)}) copy-start(f32[1024,192]{0,1:T(8,128)} %fusion.16) | copy-start | bytes 2359300
  40.6 35.5 %copy-start.10 = (f32[2]{0:T(128)S(1)}, f32[2]{0:T(128)}, u32[]{:S(2)}) copy-start(f32[2]{0:T(128)} %compare_select_fusion.2) | copy-start | bytes 28
  40.6 40.8 %copy-start.8 = (s32[2]{0:T(128)S(1)}, s32[2]{0:T(128)}, u32[]{:S(2)}) copy-start(s32[2]{0:T(128)} %get-tuple-element.7) | copy-start | bytes 28
  40.6 40.8 %copy-start.9 = (s32[2]{0:T(128)S(1)}, s32[2]{0:T(128)}, u32[]{:S(2)}) copy-start(s32[2]{0:T(128)} %get-tuple-element.8) | copy-start | bytes 28
  77.9 7.4 %all-to-all-start = ((bf16[1,2,2,32,192]{4,3,2,0,1:T(8,128)(2,1)}), bf16[1,2,2,32,192]{4,3,2,0,1:T(8,128)(2,1)S(1)}, u32[]{:S(2)}, u32[]{:S(2)}) async-start(bf16[1,2,2,32,192]{4,3,2,0,1:T(8,128)(2,1)} %bitcast.37), calls=%async_computation | async-start | bytes 131072 | tf_op jit(solution)/shard_map/all_to_all | solution.py:126
  81.2 74.1 %reduce-scatter.4.cloned.1.call-start = ((), (), s32[]{:S(2)}) async-start(), calls=%async_computation.2 | async-start | bytes 3538944
Sparse Core Ops, SparseCore 0:
  111.7 43.5 reduce-scatter.3
where the time goes:
time: 165 us; the launch traced here: 164 us
  waiting for transfers between devices  47.4 us (29%)
  blocking collectives  34.6 us (21%)
  matrix products  24.3 us (15%)
  local copies, waits for them, and re-layouts  21.7 us (13%)
  between operations  15 us (9%)
  other arithmetic  11.2 us (7%)
  starting transfers between devices  10.3 us (6%)
    unnamed x2, waiting for transfers between devices  43.7 us
    psum x1, blocking collectives, per_device(): predicted = lax.psum(partial_tiles, 'mp') / math.sqrt(width)  19.3 us
    unnamed x27, local copies, waits for them, and re-layouts  16.7 us
    all_gather x1, blocking collectives, per_device(): whole = lax.all_gather(blocks, 'seq', axis=1, tiled=True)  15.3 us
    dot_general x5, matrix products, weight_term(): jnp.einsum('mbi,mbo->oi', padded[:, offset:offset + length], dconv, prefe...  13.4 us
    dot_general x4, matrix products, conv_apply(): jnp.einsum('mbi,oi->mbo', padded[:, offset:offset + length], weight[offse...  8.08 us
    ppermute x1, starting transfers between devices, extended(): lax.ppermute(tail, axis, [(i, (i + 1) % count) for i in range(ends)])  5.51 us
    all_to_all x1, waiting for transfers between devices, per_device(): lax.all_to_all(outgoing_grads, 'seq', split_axis=1, concat_axis=1, tiled=...  3.66 us
  transfers between devices with their start and end apart: 4, of which 2 were waited for; matrix products, arithmetic and copies ran while one was open for 10% of the time, Pallas kernels for 0%

commit v1 on v0

--- a/solution.py
+++ b/solution.py
@@ -58,7 +58,7 @@
     )
 
 
-def per_device(features, conv_weight, keep, tiles, counts, targets):
+def dense_path(features, conv_weight, keep, tiles, counts, targets):
     members, length, width = features.shape
     taps = conv_weight.shape[0]
     narrow = conv_weight.shape[1]
@@ -138,6 +138,123 @@
     return lax.psum_scatter(weight_local, ("seq", "dp"), scatter_dimension=2, tiled=True)
 
 
+def axis_sum(value, axis):
+    count = lax.axis_size(axis)
+    total = value
+    for shift in range(1, count):
+        total = total + lax.ppermute(value, axis, [(i, (i + shift) % count) for i in range(count)])
+    return total
+
+
+def sparse_path(features, conv_weight, keep, tiles, counts, targets):
+    _, length, width = features.shape
+    taps, narrow, _ = conv_weight.shape
+    halo = taps // 2
+    span = TB + 2 * halo
+    owners, capacity = tiles.shape[1], tiles.shape[2]
+    n_sides = 2 * capacity
+    per_block = length // TB
+    seq_count = lax.axis_size("seq")
+    groups = lax.axis_size("dp")
+    peers = seq_count * groups
+    held = owners * PER
+    cols = width // peers
+    my_index = lax.axis_index("seq")
+    my_part = lax.axis_index("mp")
+
+    tiles_all = lax.all_gather(tiles[0], "dp")
+    counts_all = lax.all_gather(counts[0], "dp")
+    keep_all = lax.all_gather(keep[0], "dp")
+    targets_all = lax.all_gather(targets[0, 0], ("seq", "dp"))
+
+    sides = jnp.concatenate([tiles_all[..., 0], tiles_all[..., 1]], axis=-1)
+    source = sides // per_block
+    local = sides % per_block
+    before = jnp.arange(n_sides)[None, :] < jnp.arange(n_sides)[:, None]
+    same_source = source[..., :, None] == source[..., None, :]
+    rank = jnp.sum(jnp.logical_and(same_source, before), axis=-1)
+    slot = (source * groups + jnp.arange(groups)[:, None, None]) * held + jnp.arange(owners)[None, :, None] * PER + rank
+
+    mine = lax.dynamic_index_in_dim(jnp.stack([source, local, rank], 0), lax.axis_index("dp"), 1, keepdims=False)
+    held_here = mine[0] == my_index
+    picks = jnp.stack(
+        [jnp.sum(jnp.where(jnp.logical_and(held_here, mine[2] == r), mine[1], 0), axis=-1) for r in range(PER)],
+        axis=-1,
+    ).reshape(held)
+
+    padded = extended(features[0], (("seq", 0),), halo)
+    rows = picks[:, None] * TB + jnp.arange(span)[None, :]
+    windows = jnp.take(padded, rows, axis=0)
+    x_float = windows.astype(jnp.float32)
+    act = jax.nn.gelu(x_float).astype(jnp.bfloat16)
+    conv_out = jnp.einsum("hti,oi->hto", act[:, 0:TB], conv_weight[0], preferred_element_type=jnp.float32)
+    for offset in range(1, taps):
+        conv_out = conv_out + jnp.einsum(
+            "hti,oi->hto", act[:, offset : offset + TB], conv_weight[offset], preferred_element_type=jnp.float32
+        )
+    scaling = 1.25 * keep_all.astype(jnp.float32)
+    my_scale = lax.dynamic_index_in_dim(scaling, lax.axis_index("dp"), 0, keepdims=False)
+    x_part = lax.dynamic_slice_in_dim(x_float[:, halo : halo + TB], my_part * narrow, narrow, 2)
+    mixed = (x_part + my_scale * conv_out).astype(jnp.bfloat16)
+
+    act_cut = act.reshape(held, span, peers, cols).transpose(2, 0, 1, 3).reshape(peers, -1)
+    mixed_rep = jnp.broadcast_to(mixed.reshape(1, -1), (peers, held * TB * narrow))
+    outgoing = jnp.concatenate([mixed_rep, act_cut], axis=1)
+    incoming = lax.all_to_all(outgoing, ("seq", "dp"), 0, 0, tiled=True)
+    mixed_in = incoming[:, : held * TB * narrow].reshape(peers * held, TB, narrow)
+    act_in = incoming[:, held * TB * narrow :].reshape(peers * held, span, cols)
+
+    side_rows = jnp.take(mixed_in, slot, axis=0)
+    row_side = side_rows[:, :, :capacity]
+    col_side = side_rows[:, :, capacity:]
+    partial_tiles = jnp.einsum("qocid,qocjd->qocij", row_side, col_side, preferred_element_type=jnp.float32)
+    predicted = axis_sum(partial_tiles, "mp") / math.sqrt(width)
+    target_tiles = targets_all.reshape(seq_count, groups, capacity, TB, TB).transpose(1, 0, 2, 3, 4)
+    live_mask = (jnp.arange(capacity)[None, None, :] < counts_all[:, :, None]).astype(jnp.float32)
+    n_live = jnp.sum(counts_all, axis=-1).astype(jnp.float32)
+    dpredicted = (
+        2.0
+        / math.sqrt(width)
+        * live_mask[..., None, None]
+        * (predicted - target_tiles)
+        / n_live[:, None, None, None, None]
+    )
+    row_float = row_side.astype(jnp.float32)
+    col_float = col_side.astype(jnp.float32)
+    drow = jnp.einsum("qocij,qocjd->qocid", dpredicted, col_float, precision=lax.Precision.HIGHEST)
+    dcol = jnp.einsum("qocij,qocid->qocjd", dpredicted, row_float, precision=lax.Precision.HIGHEST)
+    grads = jnp.concatenate([drow, dcol], axis=2).astype(jnp.bfloat16).astype(jnp.float32)
+    grads = grads.reshape(groups, owners * n_sides, TB, narrow)
+    flat_sides = sides.reshape(groups, owners * n_sides)
+    same_block = flat_sides[:, :, None] == flat_sides[:, None, :]
+    total = jnp.sum(jnp.where(same_block[..., None, None], grads[:, None], 0.0), axis=2)
+    earlier = jnp.arange(owners * n_sides)[None, :] < jnp.arange(owners * n_sides)[:, None]
+    first = jnp.logical_not(jnp.any(jnp.logical_and(same_block, earlier[None]), axis=-1))
+    dconv = (scaling[:, None, None, None] * total).astype(jnp.bfloat16)
+    dconv = jnp.where(first[..., None, None], dconv, jnp.zeros_like(dconv))
+    act_sides = jnp.take(act_in, slot.reshape(groups, owners * n_sides), axis=0)
+    return jnp.stack(
+        [
+            jnp.einsum(
+                "qato,qati->oi",
+                dconv,
+                act_sides[:, :, offset : offset + TB],
+                preferred_element_type=jnp.float32,
+            )
+            for offset in range(taps)
+        ]
+    )
+
+
+def per_device(features, conv_weight, keep, tiles, counts, targets):
+    members, length, _ = features.shape
+    owners, capacity = tiles.shape[1], tiles.shape[2]
+    fits = members == 1 and targets.shape[1] == 1 and 2 * owners * capacity * TB <= length
+    if fits:
+        return sparse_path(features, conv_weight, keep, tiles, counts, targets)
+    return dense_path(features, conv_weight, keep, tiles, counts, targets)
+
+
 def solution(mesh):
     placed = (
         P("dp", "seq", None),

time: 165 us -> 101 us (0.61)
  matrix products: 24.3 us -> 5.12 us
  waiting for transfers between devices: 47.4 us -> 29.5 us
  between operations: 15 us -> 1.09 us
  blocking collectives: 34.6 us -> 24.9 us
  other arithmetic: 11.2 us -> 5.48 us
  starting transfers between devices: 10.3 us -> 14.3 us
    unnamed x2 -> x0, waiting for transfers between devices: 43.7 us -> none
    ppermute x0 -> x3, waiting for transfers between devices: none -> 19.9 us  [axis_sum(): lax.ppermute(value, axis, [(i, (i + shift) % count) for i in range(count)])]
    psum x1 -> x0, blocking collectives: 19.3 us -> none  [per_device(): predicted = lax.psum(partial_tiles, 'mp') / math.sqrt(width)]
    dot_general x14 -> x13, matrix products: 24.3 us -> 5.12 us  [the longest x5 2.25 us: sparse_path(): jnp.einsum('qato,qati->oi', dconv, act_sides[:, :, offset:offset + TB], p...]
    unnamed x27 -> x11, local copies, waits for them, and re-layouts: 16.7 us -> 5.09 us
    concatenate x0 -> x3, local copies, waits for them, and re-layouts: none -> 7.68 us  [the longest x1 7.59 us: extended(): jnp.concatenate([lax.ppermute(tail, axis, [(i, (i + 1) % count) for i in...]
    all_to_all x1, waiting for transfers between devices: 3.66 us -> 9.56 us  [sparse_path(): incoming = lax.all_to_all(outgoing, ('seq', 'dp'), 0, 0, tiled=True)]
    unnamed x0 -> x1, blocking collectives: none -> 5.44 us
  transfers between devices with their start and end apart: 4 -> 6, of which waited for: 2 -> 3; matrix products, arithmetic and copies ran while one was open for 10% -> 7% of each run, Pallas kernels for 0% -> 0%
where the time goes in v1:
time: 101 us
  waiting for transfers between devices  29.5 us (29%)
  blocking collectives  24.9 us (25%)
  local copies, waits for them, and re-layouts  20.1 us (20%)
  starting transfers between devices  14.3 us (14%)
  other arithmetic  5.48 us (5%)
  matrix products  5.12 us (5%)
  between operations  1.09 us (1%)
    ppermute x3, waiting for transfers between devices, axis_sum(): lax.ppermute(value, axis, [(i, (i + shift) % count) for i in range(count)])  19.9 us
    all_to_all x1, waiting for transfers between devices, sparse_path(): incoming = lax.all_to_all(outgoing, ('seq', 'dp'), 0, 0, tiled=True)  9.56 us
    all_gather x1, blocking collectives, sparse_path(): targets_all = lax.all_gather(targets[0, 0], ('seq', 'dp'))  8.58 us
    concatenate x1, local copies, waits for them, and re-layouts, extended(): jnp.concatenate([lax.ppermute(tail, axis, [(i, (i + 1) % count) for i in...  7.59 us
    all_gather x1, blocking collectives, sparse_path(): tiles_all = lax.all_gather(tiles[0], 'dp')  5.72 us
    unnamed x1, blocking collectives  5.44 us
    all_gather x1, blocking collectives, sparse_path(): counts_all = lax.all_gather(counts[0], 'dp')  5.16 us
    unnamed x11, local copies, waits for them, and re-layouts  5.09 us
  transfers between devices with their start and end apart: 6, of which 3 were waited for; matrix products, arithmetic and copies ran while one was open for 7% of the time, Pallas kernels for 0%

profile of v1, /device:TPU:0, one launch (start us, length us, event | category | flops | bytes accessed | tf_op | source)
XLA Modules:
  0.0 100.5 jit_solution(111944570009031558)
XLA Ops:
  0.0 0.7 slice_bitcast_fusion
  0.7 1.3 %collective-permute-start.1 = (bf16[2,768]{1,0:T(2,128)(2,1)S(1)}, bf16[2,768]{1,0:T(2,128)(2,1)S(1)}, u32[]{:S(2)}, u32[]{:S(2)}) collective-permute-start(bf16[2,768]{1,0:T(2,128)(2,1)S(1)} %get-tuple-element.9), channel_id=1, source_target_pairs={{16,0},{17,1},{18,2},{19,3},{20,4},{21,5},{22,6},{23,7},{24,8},{25... | collective-permute-start | bytes 9224 | tf_op jit(solution)/shard_map/ppermute | solution.py:22
  2.0 4.8 %collective-permute-start = (bf16[2,768]{1,0:T(2,128)(2,1)S(1)}, bf16[2,768]{1,0:T(2,128)(2,1)S(1)}, u32[]{:S(2)}, u32[]{:S(2)}) collective-permute-start(bf16[2,768]{1,0:T(2,128)(2,1)S(1)} %get-tuple-element.10), channel_id=1, source_target_pairs={{0,16},{1,17},{2,18},{3,19},{4,20},{5,21},{6,22},{7,23},{8,24},{9,... | collective-permute-start | bytes 9224 | tf_op jit(solution)/shard_map/ppermute | solution.py:20
  6.9 0.8 copy.103
  7.7 5.7 %all_gather.12 = s32[4,2,2,2]{2,1,0,3:T(2,128)S(1)} all-gather(s32[1,2,2,2]{2,1,0,3:T(2,128)S(1)} %copy.103), channel_id=1, replica_groups=mesh['seq'=2,'mp'=4,'dp'=4] {'dp'}, dimensions={0}, use_global_device_ids=true | all-gather | bytes 160 | tf_op jit(solution)/shard_map/all_gather | solution.py:165
  13.9 0.3 convert_reduce_fusion
  15.6 1.2 %dynamic-slice = u32[1]{0:T(128)} dynamic-slice(u32[32]{0:T(128)} %constant.129, u32[]{:T(128)S(6)} %add.353), dynamic_slice_sizes={1} | dynamic-slice | bytes 12
  16.9 0.8 dynamic-update-slice
  17.7 5.4 %all-reduce = s32[4]{0:T(128)S(1)} all-reduce(s32[4]{0:T(128)S(1)} %dynamic-update-slice), channel_id=1, replica_groups=mesh['seq'=2,'mp'=4,'dp'=4] {'dp'}, use_global_device_ids=true, to_apply=%add | all-reduce | flops 4 | bytes 32
  23.5 0.2 and_reduce_fusion
  23.8 8.6 %all-gather = f32[8,1,2,1024]{3,2,1,0:T(2,128)S(1)} all-gather(f32[1,1,2,1024]{3,2,1,0:T(2,128)} %param.11), channel_id=2, replica_groups=mesh['seq'=2,'mp'=4,'dp'=4] {'seq','dp'}, dimensions={0}, use_global_device_ids=true | all-gather | bytes 73728 | tf_op jit(solution)/shard_map/all_gather | solution.py:168
  32.3 5.2 %all-gather.1 = s32[4,1,2]{2,1,0:T(1,128)S(1)} all-gather(s32[1,1,2]{2,1,0:T(1,128)} %bitcast.120), channel_id=1, replica_groups=mesh['seq'=2,'mp'=4,'dp'=4] {'dp'}, dimensions={0}, use_global_device_ids=true | all-gather | bytes 40 | tf_op jit(solution)/shard_map/all_gather | solution.py:166
  37.5 0.6 dynamic_slice.13
  38.7 7.6 %concatenate.114 = bf16[1028,768]{1,0:T(8,128)(2,1)S(1)} concatenate(bf16[2,768]{1,0:T(2,128)(2,1)S(1)} %collective-permute-done, bf16[1024,768]{1,0:T(8,128)(2,1)} %bitcast.112, bf16[2,768]{1,0:T(2,128)(2,1)S(1)} %collective-permute-done.1), dimensions={0} | concatenate | bytes 3158016 | tf_op jit(solution)/shard_map/concatenate | solution.py:18
  46.3 0.9 gather_fusion
  47.3 0.3 gather.15
  47.6 0.3 fusion.22
  48.0 0.3 fusion.23
  48.3 0.4 reshape.802
  48.7 0.2 fusion.28
  49.0 0.2 convolution_add_fusion.3
  49.2 0.2 convolution_add_fusion.2
  49.5 0.2 convolution_add_fusion.1
  49.8 0.9 fusion.2
  50.9 0.5 broadcast.609
  51.5 1.1 %reduce.3 = bf16[8,38400]{1,0:T(8,128)(2,1)S(1)} reduce(bf16[8,1,38400]{2,0,1:T(8,128)(2,1)S(1)} %maximum_bitcast_fusion, bf16[]{:T(256)} %broadcast.609), dimensions={1}, to_apply=%copy.115.reduce_sub_computation | reduce | bytes 1228802 | tf_op jit(solution)/shard_map/all_to_all | solution.py:203
  52.6 1.0 reshape.856
  53.5 3.5 %all-to-all-start = ((bf16[8,2,19200]{2,1,0:T(2,128)(2,1)}), bf16[8,2,19200]{2,1,0:T(2,128)(2,1)S(1)}, u32[]{:S(2)}, u32[]{:S(2)}) async-start(bf16[8,2,19200]{2,1,0:T(2,128)(2,1)} %reshape.856), calls=%async_computation | async-start | bytes 1228800 | tf_op jit(solution)/shard_map/all_to_all | solution.py:203
  57.2 9.6 %all-to-all-done = bf16[8,2,19200]{2,1,0:T(2,128)(2,1)S(1)} async-done(((bf16[8,2,19200]{2,1,0:T(2,128)(2,1)}), bf16[8,2,19200]{2,1,0:T(2,128)(2,1)S(1)}, u32[]{:S(2)}, u32[]{:S(2)}) %all-to-all-start) | async-done | bytes 614432 | tf_op jit(solution)/shard_map/all_to_all | solution.py:203
  66.8 0.5 reshape.857
  67.4 0.6 reshape.803
  68.1 0.6 gather_fusion.1
  68.8 0.2 fusion.49
  69.0 3.7 %collective-permute-start.4 = (f32[4,2,2,32,32]{4,3,2,1,0:T(8,128)S(1)}, f32[4,2,2,32,32]{4,3,2,1,0:T(8,128)S(1)}, u32[]{:S(2)}, u32[]{:S(2)}) collective-permute-start(f32[4,2,2,32,32]{4,3,2,1,0:T(8,128)S(1)} %fusion.49), channel_id=1, source_target_pairs={{0,12},{4,0},{8,4},{12,8},{1,13},{5,1},{9,5},{13,9},{2,14},{6,2},{... | collective-permute-start | bytes 196616 | tf_op jit(solution)/shard_map/ppermute | solution.py:145
  72.6 1.0 %collective-permute-start.2 = (f32[4,2,2,32,32]{4,3,2,1,0:T(8,128)S(1)}, f32[4,2,2,32,32]{4,3,2,1,0:T(8,128)S(1)}, u32[]{:S(2)}, u32[]{:S(2)}) collective-permute-start(f32[4,2,2,32,32]{4,3,2,1,0:T(8,128)S(1)} %fusion.49), channel_id=1, source_target_pairs={{0,4},{4,8},{8,12},{12,0},{1,5},{5,9},{9,13},{13,1},{2,6},{6,10},{... | collective-permute-start | bytes 196616 | tf_op jit(solution)/shard_map/ppermute | solution.py:145
  73.7 0.4 reshape.805
  74.1 0.6 gather_fusion.2
  74.8 4.6 %collective-permute-done.4 = f32[4,2,2,32,32]{4,3,2,1,0:T(8,128)S(1)} collective-permute-done((f32[4,2,2,32,32]{4,3,2,1,0:T(8,128)S(1)}, f32[4,2,2,32,32]{4,3,2,1,0:T(8,128)S(1)}, u32[]{:S(2)}, u32[]{:S(2)}) %collective-permute-start.4) | collective-permute-done | bytes 65568 | tf_op jit(solution)/shard_map/ppermute | solution.py:145
  79.4 15.3 %collective-permute-done.3 = f32[4,2,2,32,32]{4,3,2,1,0:T(8,128)S(1)} collective-permute-done((f32[4,2,2,32,32]{4,3,2,1,0:T(8,128)S(1)}, f32[4,2,2,32,32]{4,3,2,1,0:T(8,128)S(1)}, u32[]{:S(2)}, u32[]{:S(2)}) %collective-permute-start.3) | collective-permute-done | bytes 65568 | tf_op jit(solution)/shard_map/ppermute | solution.py:145
  94.9 0.4 convolution_convert_fusion
  95.3 0.3 convolution_convert_fusion.1
  95.9 1.4 %select_reduce_fusion = f32[4,8,32,192]{3,2,1,0:T(8,128)S(1)} fusion(f32[4,8,32,192]{3,2,1,0:T(8,128)S(1)} %convert.9, pred[4,8,8]{2,1,0:T(8,128)(4,1)S(1)} %get-tuple-element.18), kind=kLoop, calls=%fused_computation.3 | loop fusion | flops 2949120 | bytes 1573120 | tf_op jit(solution)/shard_map/reduce_sum | solution.py:230
  97.5 0.3 fusion.7
  97.8 0.3 fusion.6
  98.1 0.3 fusion.5
  98.4 0.3 fusion.4
  98.8 0.8 copy-done.1
  99.5 1.0 fusion.3
  (61 shorter events, 3.7 us)
Async XLA Ops:
  0.7 38.0 %collective-permute-start.1 = (bf16[2,768]{1,0:T(2,128)(2,1)S(1)}, bf16[2,768]{1,0:T(2,128)(2,1)S(1)}, u32[]{:S(2)}, u32[]{:S(2)}) collective-permute-start(bf16[2,768]{1,0:T(2,128)(2,1)S(1)} %get-tuple-element.9), channel_id=1, source_target_pairs={{16,0},{17,1},{18,2},{19,3},{20,4},{21,5},{22,6},{23,7},{24,8},{25... | collective-permute-start | bytes 9224 | tf_op jit(solution)/shard_map/ppermute | solution.py:22
  2.0 36.7 %collective-permute-start = (bf16[2,768]{1,0:T(2,128)(2,1)S(1)}, bf16[2,768]{1,0:T(2,128)(2,1)S(1)}, u32[]{:S(2)}, u32[]{:S(2)}) collective-permute-start(bf16[2,768]{1,0:T(2,128)(2,1)S(1)} %get-tuple-element.10), channel_id=1, source_target_pairs={{0,16},{1,17},{2,18},{3,19},{4,20},{5,21},{6,22},{7,23},{8,24},{9,... | collective-permute-start | bytes 9224 | tf_op jit(solution)/shard_map/ppermute | solution.py:20
  47.3 1.4 %copy-start = (bf16[5,192,768]{2,1,0:T(8,128)(2,1)S(1)}, bf16[5,192,768]{2,1,0:T(8,128)(2,1)}, u32[]{:S(2)}) copy-start(bf16[5,192,768]{2,1,0:T(8,128)(2,1)} %param.7) | copy-start | bytes 4423684
  53.5 13.3 %all-to-all-start = ((bf16[8,2,19200]{2,1,0:T(2,128)(2,1)}), bf16[8,2,19200]{2,1,0:T(2,128)(2,1)S(1)}, u32[]{:S(2)}, u32[]{:S(2)}) async-start(bf16[8,2,19200]{2,1,0:T(2,128)(2,1)} %reshape.856), calls=%async_computation | async-start | bytes 1228800 | tf_op jit(solution)/shard_map/all_to_all | solution.py:203
  69.0 10.4 %collective-permute-start.4 = (f32[4,2,2,32,32]{4,3,2,1,0:T(8,128)S(1)}, f32[4,2,2,32,32]{4,3,2,1,0:T(8,128)S(1)}, u32[]{:S(2)}, u32[]{:S(2)}) collective-permute-start(f32[4,2,2,32,32]{4,3,2,1,0:T(8,128)S(1)} %fusion.49), channel_id=1, source_target_pairs={{0,12},{4,0},{8,4},{12,8},{1,13},{5,1},{9,5},{13,9},{2,14},{6,2},{... | collective-permute-start | bytes 196616 | tf_op jit(solution)/shard_map/ppermute | solution.py:145
  72.6 22.1 %collective-permute-start.3 = (f32[4,2,2,32,32]{4,3,2,1,0:T(8,128)S(1)}, f32[4,2,2,32,32]{4,3,2,1,0:T(8,128)S(1)}, u32[]{:S(2)}, u32[]{:S(2)}) collective-permute-start(f32[4,2,2,32,32]{4,3,2,1,0:T(8,128)S(1)} %fusion.49), channel_id=1, source_target_pairs={{0,8},{4,12},{8,0},{12,4},{1,9},{5,13},{9,1},{13,5},{2,10},{6,14},... | collective-permute-start | bytes 196616 | tf_op jit(solution)/shard_map/ppermute | solution.py:145
  72.6 22.1 %collective-permute-start.2 = (f32[4,2,2,32,32]{4,3,2,1,0:T(8,128)S(1)}, f32[4,2,2,32,32]{4,3,2,1,0:T(8,128)S(1)}, u32[]{:S(2)}, u32[]{:S(2)}) collective-permute-start(f32[4,2,2,32,32]{4,3,2,1,0:T(8,128)S(1)} %fusion.49), channel_id=1, source_target_pairs={{0,4},{4,8},{8,12},{12,0},{1,5},{5,9},{9,13},{13,1},{2,6},{6,10},{... | collective-permute-start | bytes 196616 | tf_op jit(solution)/shard_map/ppermute | solution.py:145
  98.8 0.8 copy-start.1

commit v2 on v1

--- a/solution.py
+++ b/solution.py
@@ -162,10 +162,16 @@
     my_index = lax.axis_index("seq")
     my_part = lax.axis_index("mp")
 
-    tiles_all = lax.all_gather(tiles[0], "dp")
-    counts_all = lax.all_gather(counts[0], "dp")
-    keep_all = lax.all_gather(keep[0], "dp")
-    targets_all = lax.all_gather(targets[0, 0], ("seq", "dp"))
+    small = jnp.concatenate([tiles.reshape(-1), counts.reshape(-1), keep.reshape(-1)]).astype(jnp.float32)
+    bundle = jnp.concatenate([targets.reshape(-1), small])
+    gathered = lax.all_gather(bundle, ("seq", "dp")).reshape(seq_count, groups, -1)
+    n_targets = capacity * TB * TB
+    n_tiles = owners * capacity * 2
+    meta = gathered[0, :, n_targets:].astype(jnp.int32)
+    tiles_all = meta[:, :n_tiles].reshape(groups, owners, capacity, 2)
+    counts_all = meta[:, n_tiles : n_tiles + owners]
+    keep_all = meta[:, n_tiles + owners]
+    targets_all = gathered[:, :, :n_targets]
 
     sides = jnp.concatenate([tiles_all[..., 0], tiles_all[..., 1]], axis=-1)
     source = sides // per_block
@@ -182,9 +188,17 @@
         axis=-1,
     ).reshape(held)
 
-    padded = extended(features[0], (("seq", 0),), halo)
-    rows = picks[:, None] * TB + jnp.arange(span)[None, :]
-    windows = jnp.take(padded, rows, axis=0)
+    cells = features[0]
+    ends = seq_count - 1
+    head = lax.ppermute(cells[length - halo :], "seq", [(i, i + 1) for i in range(ends)])
+    tail = lax.ppermute(cells[:halo], "seq", [(i + 1, i) for i in range(ends)])
+    rows = picks[:, None] * TB - halo + jnp.arange(span)[None, :]
+    inside = jnp.take(cells, jnp.clip(rows, 0, length - 1), axis=0)
+    edge_rows = jnp.concatenate([head, tail], axis=0)
+    edge_index = jnp.where(rows < 0, rows + halo, rows - length + halo)
+    outside = jnp.take(edge_rows, jnp.clip(edge_index, 0, 2 * halo - 1), axis=0)
+    in_range = jnp.logical_and(rows >= 0, rows < length)
+    windows = jnp.where(in_range[..., None], inside, outside)
     x_float = windows.astype(jnp.float32)
     act = jax.nn.gelu(x_float).astype(jnp.bfloat16)
     conv_out = jnp.einsum("hti,oi->hto", act[:, 0:TB], conv_weight[0], preferred_element_type=jnp.float32)

time: 101 us -> 142 us (1.41)
  waiting for transfers between devices: 29.5 us -> 81.6 us
  blocking collectives: 24.9 us -> 0 us
  between operations: 1.09 us -> 15.2 us
  local copies, waits for them, and re-layouts: 20.1 us -> 18.4 us
    unnamed x0 -> x2, waiting for transfers between devices: none -> 51.9 us
    all_gather x3 -> x0, blocking collectives: 19.5 us -> none  [the longest x1 8.58 us: sparse_path(): targets_all = lax.all_gather(targets[0, 0], ('seq', 'dp'))]
    concatenate x1 -> x0, local copies, waits for them, and re-layouts: 7.59 us -> none  [extended(): jnp.concatenate([lax.ppermute(tail, axis, [(i, (i + 1) % count) for i in...]
    unnamed x1 -> x0, blocking collectives: 5.44 us -> none
    gather x3 -> x6, local copies, waits for them, and re-layouts: 1.29 us -> 4.31 us  [the longest x3 3.02 us: sparse_path(): inside = jnp.take(cells, jnp.clip(rows, 0, length - 1), axis=0)]
    reshape x0 -> x2, local copies, waits for them, and re-layouts: none -> 1.76 us  [the longest x1 0.99 us: sparse_path(): lax.all_gather(bundle, ('seq', 'dp')).reshape(seq_count, groups, -1)]
    unnamed x11 -> x14, local copies, waits for them, and re-layouts: 5.09 us -> 5.84 us
  transfers between devices with their start and end apart: 6 -> 7, of which waited for: 3 -> 4; matrix products, arithmetic and copies ran while one was open for 7% -> 4% of each run, Pallas kernels for 0% -> 0%
where the time goes in v2:
time: 142 us
  waiting for transfers between devices  81.6 us (57%)
  local copies, waits for them, and re-layouts  18.4 us (13%)
  between operations  15.2 us (11%)
  starting transfers between devices  14.5 us (10%)
  other arithmetic  6.7 us (5%)
  matrix products  5.11 us (4%)
    unnamed x2, waiting for transfers between devices  51.9 us
    ppermute x3, waiting for transfers between devices, axis_sum(): lax.ppermute(value, axis, [(i, (i + shift) % count) for i in range(count)])  20 us
    all_to_all x1, waiting for transfers between devices, sparse_path(): incoming = lax.all_to_all(outgoing, ('seq', 'dp'), 0, 0, tiled=True)  9.65 us
    unnamed x14, local copies, waits for them, and re-layouts  5.84 us
    ppermute x1, starting transfers between devices, sparse_path(): lax.ppermute(cells[length - halo:], 'seq', [(i, i + 1) for i in range(end...  4.83 us
    ppermute x3, starting transfers between devices, axis_sum(): lax.ppermute(value, axis, [(i, (i + shift) % count) for i in range(count)])  4.48 us
    all_to_all x1, starting transfers between devices, sparse_path(): incoming = lax.all_to_all(outgoing, ('seq', 'dp'), 0, 0, tiled=True)  3.92 us
    gather x3, local copies, waits for them, and re-layouts, sparse_path(): inside = jnp.take(cells, jnp.clip(rows, 0, length - 1), axis=0)  3.02 us
  transfers between devices with their start and end apart: 7, of which 4 were waited for; matrix products, arithmetic and copies ran while one was open for 4% of the time, Pallas kernels for 0%

profile of v2, /device:TPU:0, one launch (start us, length us, event | category | flops | bytes accessed | tf_op | source)
XLA Modules:
  0.0 141.5 jit_solution(4417940106494104526)
XLA Ops:
  6.5 0.7 slice_bitcast_fusion.1
  7.3 4.8 %collective-permute-start = (bf16[2,768]{1,0:T(2,128)(2,1)S(1)}, bf16[2,768]{1,0:T(2,128)(2,1)S(1)}, u32[]{:S(2)}, u32[]{:S(2)}) collective-permute-start(bf16[2,768]{1,0:T(2,128)(2,1)S(1)} %get-tuple-element.11), channel_id=1, source_target_pairs={{0,16},{1,17},{2,18},{3,19},{4,20},{5,21},{6,22},{7,23},{8,24},{9,... | collective-permute-start | bytes 9224 | tf_op jit(solution)/shard_map/ppermute | solution.py:193
  12.1 1.3 collective-permute-start.1
  14.1 0.8 reshape.924
  14.8 0.7 copy.140
  15.5 1.2 dynamic-slice.1
  17.4 0.7 add_convert_fusion
  18.3 0.6 copy-done
  19.2 51.9 %all-reduce.3.cloned.1.call-done = f32[16472]{0:T(1024)} async-done(((f32[16472]{0:T(1024)}), f32[16472]{0:T(1024)}) %all-reduce.3.cloned.1.call-update) | async-done | bytes 65904
  71.1 1.0 reshape.926
  73.1 0.3 convert_reduce_fusion
  74.4 2.6 %gather_fusion = bf16[144,768]{1,0:T(8,128)(2,1)S(1)} fusion(bf16[1024,768]{1,0:T(8,128)(2,1)} %bitcast.114, s32[1024]{0:T(1024)S(1)} %pad_clamp_fusion.3), kind=kCustom, calls=%fused_computation | custom fusion | bytes 442944 | tf_op jit(solution)/shard_map/jit(_take)/gather | solution.py:196
  77.1 0.3 gather.22
  77.5 0.9 gather_fusion.1
  78.5 0.3 gather.23
  78.9 0.5 constant_dynamic-slice_fusion
  80.4 0.4 fusion.23
  80.8 0.4 reshape.928
  81.2 0.4 fusion.22
  81.6 0.9 copy-done.2
  82.6 0.2 fusion.29
  82.8 0.2 convolution_add_fusion.3
  83.1 0.2 convolution_add_fusion.2
  83.4 0.2 convolution_add_fusion.1
  83.6 0.9 fusion.2
  84.8 0.5 broadcast.811
  85.3 1.1 reduce.4
  86.4 1.0 reshape.990
  87.4 3.9 %all-to-all-start = ((bf16[8,2,19200]{2,1,0:T(2,128)(2,1)}), bf16[8,2,19200]{2,1,0:T(2,128)(2,1)S(1)}, u32[]{:S(2)}, u32[]{:S(2)}) async-start(bf16[8,2,19200]{2,1,0:T(2,128)(2,1)} %reshape.990), calls=%async_computation | async-start | bytes 1228800 | tf_op jit(solution)/shard_map/all_to_all | solution.py:217
  91.4 9.7 %all-to-all-done = bf16[8,2,19200]{2,1,0:T(2,128)(2,1)S(1)} async-done(((bf16[8,2,19200]{2,1,0:T(2,128)(2,1)}), bf16[8,2,19200]{2,1,0:T(2,128)(2,1)S(1)}, u32[]{:S(2)}, u32[]{:S(2)}) %all-to-all-start) | async-done | bytes 614432 | tf_op jit(solution)/shard_map/all_to_all | solution.py:217
  101.1 0.5 reshape.991
  101.7 0.6 reshape.929
  102.4 0.6 gather_fusion.2
  103.3 3.4 %collective-permute-start.4 = (f32[4,2,2,32,32]{4,3,2,1,0:T(8,128)S(1)}, f32[4,2,2,32,32]{4,3,2,1,0:T(8,128)S(1)}, u32[]{:S(2)}, u32[]{:S(2)}) collective-permute-start(f32[4,2,2,32,32]{4,3,2,1,0:T(8,128)S(1)} %fusion.50), channel_id=1, source_target_pairs={{0,12},{4,0},{8,4},{12,8},{1,13},{5,1},{9,5},{13,9},{2,14},{6,2},{... | collective-permute-start | bytes 196616 | tf_op jit(solution)/shard_map/ppermute | solution.py:145
  106.7 1.1 collective-permute-start.2
  107.8 0.4 reshape.931
  108.2 0.6 gather_fusion.3
  108.9 4.5 %collective-permute-done.4 = f32[4,2,2,32,32]{4,3,2,1,0:T(8,128)S(1)} collective-permute-done((f32[4,2,2,32,32]{4,3,2,1,0:T(8,128)S(1)}, f32[4,2,2,32,32]{4,3,2,1,0:T(8,128)S(1)}, u32[]{:S(2)}, u32[]{:S(2)}) %collective-permute-start.4) | collective-permute-done | bytes 65568 | tf_op jit(solution)/shard_map/ppermute | solution.py:145
  113.5 15.5 %collective-permute-done.3 = f32[4,2,2,32,32]{4,3,2,1,0:T(8,128)S(1)} collective-permute-done((f32[4,2,2,32,32]{4,3,2,1,0:T(8,128)S(1)}, f32[4,2,2,32,32]{4,3,2,1,0:T(8,128)S(1)}, u32[]{:S(2)}, u32[]{:S(2)}) %collective-permute-start.3) | collective-permute-done | bytes 65568 | tf_op jit(solution)/shard_map/ppermute | solution.py:145
  129.1 0.4 convolution_convert_fusion
  129.5 0.3 convolution_convert_fusion.1
  130.1 1.4 select_reduce_fusion
  131.7 0.3 fusion.7
  132.0 0.3 fusion.6
  132.3 0.3 fusion.5
  132.6 0.3 fusion.4
  133.0 0.8 copy-done.3
  133.7 1.0 fusion.3
  (78 shorter events, 4.9 us)
Async XLA Ops:
  6.5 64.6 %all-reduce.3.cloned.1.call-start = ((), (), s32[]{:S(2)}) async-start(), calls=%async_computation.1 | async-start | bytes 139264
  7.3 11.9 %collective-permute-start = (bf16[2,768]{1,0:T(2,128)(2,1)S(1)}, bf16[2,768]{1,0:T(2,128)(2,1)S(1)}, u32[]{:S(2)}, u32[]{:S(2)}) collective-permute-start(bf16[2,768]{1,0:T(2,128)(2,1)S(1)} %get-tuple-element.11), channel_id=1, source_target_pairs={{0,16},{1,17},{2,18},{3,19},{4,20},{5,21},{6,22},{7,23},{8,24},{9,... | collective-permute-start | bytes 9224 | tf_op jit(solution)/shard_map/ppermute | solution.py:193
  12.1 7.1 %collective-permute-start.1 = (bf16[2,768]{1,0:T(2,128)(2,1)S(1)}, bf16[2,768]{1,0:T(2,128)(2,1)S(1)}, u32[]{:S(2)}, u32[]{:S(2)}) collective-permute-start(bf16[2,768]{1,0:T(2,128)(2,1)S(1)} %get-tuple-element.12), channel_id=1, source_target_pairs={{16,0},{17,1},{18,2},{19,3},{20,4},{21,5},{22,6},{23,7},{24,8},{25... | collective-permute-start | bytes 9224 | tf_op jit(solution)/shard_map/ppermute | solution.py:194
  18.3 0.6 copy-start
  72.1 4.9 %copy-start.1 = (f32[2,4,2059]{2,1,0:T(4,128)}, f32[2,4,2059]{2,1,0:T(4,128)S(1)}, u32[]{:S(2)}) copy-start(f32[2,4,2059]{2,1,0:T(4,128)S(1)} %reshape.926) | copy-start | bytes 197668
  77.5 1.3 slice-start
  81.2 1.4 copy-start.2
  87.4 13.7 %all-to-all-start = ((bf16[8,2,19200]{2,1,0:T(2,128)(2,1)}), bf16[8,2,19200]{2,1,0:T(2,128)(2,1)S(1)}, u32[]{:S(2)}, u32[]{:S(2)}) async-start(bf16[8,2,19200]{2,1,0:T(2,128)(2,1)} %reshape.990), calls=%async_computation | async-start | bytes 1228800 | tf_op jit(solution)/shard_map/all_to_all | solution.py:217
  103.3 10.2 %collective-permute-start.4 = (f32[4,2,2,32,32]{4,3,2,1,0:T(8,128)S(1)}, f32[4,2,2,32,32]{4,3,2,1,0:T(8,128)S(1)}, u32[]{:S(2)}, u32[]{:S(2)}) collective-permute-start(f32[4,2,2,32,32]{4,3,2,1,0:T(8,128)S(1)} %fusion.50), channel_id=1, source_target_pairs={{0,12},{4,0},{8,4},{12,8},{1,13},{5,1},{9,5},{13,9},{2,14},{6,2},{... | collective-permute-start | bytes 196616 | tf_op jit(solution)/shard_map/ppermute | solution.py:145
  106.7 22.3 %collective-permute-start.3 = (f32[4,2,2,32,32]{4,3,2,1,0:T(8,128)S(1)}, f32[4,2,2,32,32]{4,3,2,1,0:T(8,128)S(1)}, u32[]{:S(2)}, u32[]{:S(2)}) collective-permute-start(f32[4,2,2,32,32]{4,3,2,1,0:T(8,128)S(1)} %fusion.50), channel_id=1, source_target_pairs={{0,8},{4,12},{8,0},{12,4},{1,9},{5,13},{9,1},{13,5},{2,10},{6,14},... | collective-permute-start | bytes 196616 | tf_op jit(solution)/shard_map/ppermute | solution.py:145
  106.7 22.3 %collective-permute-start.2 = (f32[4,2,2,32,32]{4,3,2,1,0:T(8,128)S(1)}, f32[4,2,2,32,32]{4,3,2,1,0:T(8,128)S(1)}, u32[]{:S(2)}, u32[]{:S(2)}) collective-permute-start(f32[4,2,2,32,32]{4,3,2,1,0:T(8,128)S(1)} %fusion.50), channel_id=1, source_target_pairs={{0,4},{4,8},{8,12},{12,0},{1,5},{5,9},{9,13},{13,1},{2,6},{6,10},{... | collective-permute-start | bytes 196616 | tf_op jit(solution)/shard_map/ppermute | solution.py:145
  132.9 0.8 copy-start.3
Sparse Core Ops, SparseCore 0:
  19.1 51.9 all-reduce.2

commit v3 on v2

--- a/solution.py
+++ b/solution.py
@@ -164,7 +164,10 @@
 
     small = jnp.concatenate([tiles.reshape(-1), counts.reshape(-1), keep.reshape(-1)]).astype(jnp.float32)
     bundle = jnp.concatenate([targets.reshape(-1), small])
-    gathered = lax.all_gather(bundle, ("seq", "dp")).reshape(seq_count, groups, -1)
+    lanes = 128
+    padding = -bundle.shape[0] % lanes
+    bundle = jnp.pad(bundle, (0, padding)).reshape(-1, lanes)
+    gathered = lax.all_gather(bundle, ("seq", "dp"), tiled=True).reshape(seq_count, groups, -1)
     n_targets = capacity * TB * TB
     n_tiles = owners * capacity * 2
     meta = gathered[0, :, n_targets:].astype(jnp.int32)

time: 142 us -> 82.9 us (0.58)
  waiting for transfers between devices: 81.6 us -> 29.5 us
  between operations: 15.2 us -> 1.14 us
  blocking collectives: 0 us -> 10.3 us
  local copies, waits for them, and re-layouts: 18.4 us -> 15.5 us
    unnamed x2 -> x0, waiting for transfers between devices: 51.9 us -> none
    all_gather x0 -> x1, blocking collectives: none -> 10.3 us  [sparse_path(): lax.all_gather(bundle, ('seq', 'dp'), tiled=True)]
    unnamed x14 -> x8, local copies, waits for them, and re-layouts: 5.84 us -> 3.96 us
  transfers between devices with their start and end apart: 7 -> 6, of which waited for: 4 -> 3; matrix products, arithmetic and copies ran while one was open for 4% -> 13% of each run, Pallas kernels for 0% -> 0%
where the time goes in v3:
time: 82.9 us; the launch traced here: 82.5 us
  waiting for transfers between devices  29.5 us (36%)
  local copies, waits for them, and re-layouts  15.5 us (19%)
  starting transfers between devices  14.3 us (17%)
  blocking collectives  10.3 us (12%)
  other arithmetic  6.55 us (8%)
  matrix products  5.11 us (6%)
  between operations  1.14 us (1%)
    ppermute x3, waiting for transfers between devices, axis_sum(): lax.ppermute(value, axis, [(i, (i + shift) % count) for i in range(count)])  20 us
    all_gather x1, blocking collectives, sparse_path(): lax.all_gather(bundle, ('seq', 'dp'), tiled=True)  10.3 us
    all_to_all x1, waiting for transfers between devices, sparse_path(): incoming = lax.all_to_all(outgoing, ('seq', 'dp'), 0, 0, tiled=True)  9.56 us
    ppermute x1, starting transfers between devices, sparse_path(): lax.ppermute(cells[length - halo:], 'seq', [(i, i + 1) for i in range(end...  4.83 us
    ppermute x3, starting transfers between devices, axis_sum(): lax.ppermute(value, axis, [(i, (i + shift) % count) for i in range(count)])  4.66 us
    unnamed x8, local copies, waits for them, and re-layouts  3.96 us
    all_to_all x1, starting transfers between devices, sparse_path(): incoming = lax.all_to_all(outgoing, ('seq', 'dp'), 0, 0, tiled=True)  3.54 us
    gather x3, local copies, waits for them, and re-layouts, sparse_path(): inside = jnp.take(cells, jnp.clip(rows, 0, length - 1), axis=0)  3.02 us
  transfers between devices with their start and end apart: 6, of which 3 were waited for; matrix products, arithmetic and copies ran while one was open for 13% of the time, Pallas kernels for 0%

profile of v3, /device:TPU:0, one launch (start us, length us, event | category | flops | bytes accessed | tf_op | source)
XLA Modules:
  0.0 82.5 jit_solution(13249803319621283043)
XLA Ops:
  0.0 0.7 slice_bitcast_fusion.1
  0.7 4.8 %collective-permute-start = (bf16[2,768]{1,0:T(2,128)(2,1)S(1)}, bf16[2,768]{1,0:T(2,128)(2,1)S(1)}, u32[]{:S(2)}, u32[]{:S(2)}) collective-permute-start(bf16[2,768]{1,0:T(2,128)(2,1)S(1)} %get-tuple-element.11), channel_id=1, source_target_pairs={{0,16},{1,17},{2,18},{3,19},{4,20},{5,21},{6,22},{7,23},{8,24},{9,... | collective-permute-start | bytes 9224 | tf_op jit(solution)/shard_map/ppermute | solution.py:196
  5.6 1.3 %collective-permute-start.1 = (bf16[2,768]{1,0:T(2,128)(2,1)S(1)}, bf16[2,768]{1,0:T(2,128)(2,1)S(1)}, u32[]{:S(2)}, u32[]{:S(2)}) collective-permute-start(bf16[2,768]{1,0:T(2,128)(2,1)S(1)} %get-tuple-element.12), channel_id=1, source_target_pairs={{16,0},{17,1},{18,2},{19,3},{20,4},{21,5},{22,6},{23,7},{24,8},{25... | collective-permute-start | bytes 9224 | tf_op jit(solution)/shard_map/ppermute | solution.py:197
  7.6 0.8 reshape.927
  8.3 0.7 copy.161
  9.0 0.7 add_convert_fusion
  9.8 10.3 %all-gather = f32[8,17,128]{2,1,0:T(8,128)S(1)} all-gather(f32[1,17,128]{2,1,0:T(8,128)S(1)} %fusion.57), channel_id=1, replica_groups=mesh['seq'=2,'mp'=4,'dp'=4] {'seq','dp'}, dimensions={0}, use_global_device_ids=true | all-gather | bytes 78336 | tf_op jit(solution)/shard_map/all_gather | solution.py:170
  20.3 0.2 fusion.80
  21.1 0.3 convert_reduce_fusion
  22.8 0.2 and_reduce_fusion
  23.1 2.6 %gather_fusion = bf16[144,768]{1,0:T(8,128)(2,1)S(1)} fusion(bf16[1024,768]{1,0:T(8,128)(2,1)} %bitcast.115, s32[1024]{0:T(1024)S(1)} %pad_clamp_fusion.3), kind=kCustom, calls=%fused_computation | custom fusion | bytes 442944 | tf_op jit(solution)/shard_map/jit(_take)/gather | solution.py:199
  25.8 0.3 gather.22
  26.2 0.5 constant_dynamic-slice_fusion
  27.3 0.9 %gather_fusion.1 = bf16[144,768]{1,0:T(8,128)(2,1)S(1)} fusion(bf16[4,768]{1,0:T(4,128)(2,1)S(1)} %pad_maximum_fusion.1, s32[1024]{0:T(1024)S(1)} %pad_clamp_fusion.2), kind=kCustom, calls=%fused_computation.1 | custom fusion | bytes 442944 | tf_op jit(solution)/shard_map/jit(_take)/gather | solution.py:202
  28.2 0.3 gather.23
  28.6 0.4 fusion.23
  29.0 0.4 reshape.932
  29.4 0.4 fusion.22
  29.8 0.9 %copy-done = bf16[5,192,768]{2,1,0:T(8,128)(2,1)S(1)} copy-done((bf16[5,192,768]{2,1,0:T(8,128)(2,1)S(1)}, bf16[5,192,768]{2,1,0:T(8,128)(2,1)}, u32[]{:S(2)}) %copy-start) | copy-done | bytes 1474584
  30.8 0.2 fusion.29
  31.0 0.2 convolution_add_fusion.3
  31.3 0.2 convolution_add_fusion.2
  31.5 0.2 convolution_add_fusion.1
  31.8 0.9 %fusion.2 = bf16[4,32,192]{2,1,0:T(8,128)(2,1)S(1)} fusion(f32[4,32,192]{2,1,0:T(8,128)S(1)} %convolution_add_fusion.1, bf16[5,192,768]{2,1,0:T(8,128)(2,1)S(1)} %copy-done, bf16[4,36,768]{2,1,0:T(8,128)(2,1)S(1)} %get-tuple-element.7, f32[4,32,768]{2,1,0:T(8,128)S(1)} %slice.155, s32[]{:T(128)S(6)} %select_n.207, f32[]{:T(128)} %bitcast.14), kind=kOutput, calls=%fused_computation.17 | convolution fusion | flops 37847040 | bytes 802824 | tf_op jit(solution)/shard_map/hti,oi->hto/dot_general | solution.py:209
  33.0 0.5 broadcast.818
  33.5 1.1 %reduce.4 = bf16[8,38400]{1,0:T(8,128)(2,1)S(1)} reduce(bf16[8,1,38400]{2,0,1:T(8,128)(2,1)S(1)} %maximum_bitcast_fusion, bf16[]{:T(256)} %broadcast.818), dimensions={1}, to_apply=%copy.116.reduce_sub_computation | reduce | bytes 1228802 | tf_op jit(solution)/shard_map/all_to_all | solution.py:220
  34.6 1.0 %reshape.991 = bf16[8,2,19200]{2,1,0:T(2,128)(2,1)} reshape(bf16[8,38400]{1,0:T(8,128)(2,1)S(1)} %reduce.4) | data formatting | bytes 1228800
  35.5 3.5 %all-to-all-start = ((bf16[8,2,19200]{2,1,0:T(2,128)(2,1)}), bf16[8,2,19200]{2,1,0:T(2,128)(2,1)S(1)}, u32[]{:S(2)}, u32[]{:S(2)}) async-start(bf16[8,2,19200]{2,1,0:T(2,128)(2,1)} %reshape.991), calls=%async_computation | async-start | bytes 1228800 | tf_op jit(solution)/shard_map/all_to_all | solution.py:220
  39.2 9.6 %all-to-all-done = bf16[8,2,19200]{2,1,0:T(2,128)(2,1)S(1)} async-done(((bf16[8,2,19200]{2,1,0:T(2,128)(2,1)}), bf16[8,2,19200]{2,1,0:T(2,128)(2,1)S(1)}, u32[]{:S(2)}, u32[]{:S(2)}) %all-to-all-start) | async-done | bytes 614432 | tf_op jit(solution)/shard_map/all_to_all | solution.py:220
  48.8 0.5 reshape.992
  49.5 0.6 reshape.933
  50.1 0.6 gather_fusion.2
  50.8 0.2 fusion.50
  51.0 3.7 %collective-permute-start.4 = (f32[4,2,2,32,32]{4,3,2,1,0:T(8,128)S(1)}, f32[4,2,2,32,32]{4,3,2,1,0:T(8,128)S(1)}, u32[]{:S(2)}, u32[]{:S(2)}) collective-permute-start(f32[4,2,2,32,32]{4,3,2,1,0:T(8,128)S(1)} %fusion.50), channel_id=1, source_target_pairs={{0,12},{4,0},{8,4},{12,8},{1,13},{5,1},{9,5},{13,9},{2,14},{6,2},{... | collective-permute-start | bytes 196616 | tf_op jit(solution)/shard_map/ppermute | solution.py:145
  54.7 1.0 %collective-permute-start.2 = (f32[4,2,2,32,32]{4,3,2,1,0:T(8,128)S(1)}, f32[4,2,2,32,32]{4,3,2,1,0:T(8,128)S(1)}, u32[]{:S(2)}, u32[]{:S(2)}) collective-permute-start(f32[4,2,2,32,32]{4,3,2,1,0:T(8,128)S(1)} %fusion.50), channel_id=1, source_target_pairs={{0,4},{4,8},{8,12},{12,0},{1,5},{5,9},{9,13},{13,1},{2,6},{6,10},{... | collective-permute-start | bytes 196616 | tf_op jit(solution)/shard_map/ppermute | solution.py:145
  55.7 0.4 reshape.935
  56.1 0.6 gather_fusion.3
  56.8 4.6 %collective-permute-done.4 = f32[4,2,2,32,32]{4,3,2,1,0:T(8,128)S(1)} collective-permute-done((f32[4,2,2,32,32]{4,3,2,1,0:T(8,128)S(1)}, f32[4,2,2,32,32]{4,3,2,1,0:T(8,128)S(1)}, u32[]{:S(2)}, u32[]{:S(2)}) %collective-permute-start.4) | collective-permute-done | bytes 65568 | tf_op jit(solution)/shard_map/ppermute | solution.py:145
  61.4 15.3 %collective-permute-done.3 = f32[4,2,2,32,32]{4,3,2,1,0:T(8,128)S(1)} collective-permute-done((f32[4,2,2,32,32]{4,3,2,1,0:T(8,128)S(1)}, f32[4,2,2,32,32]{4,3,2,1,0:T(8,128)S(1)}, u32[]{:S(2)}, u32[]{:S(2)}) %collective-permute-start.3) | collective-permute-done | bytes 65568 | tf_op jit(solution)/shard_map/ppermute | solution.py:145
  76.9 0.4 convolution_convert_fusion
  77.3 0.3 convolution_convert_fusion.1
  77.9 1.4 %select_reduce_fusion = f32[4,8,32,192]{3,2,1,0:T(8,128)S(1)} fusion(f32[4,8,32,192]{3,2,1,0:T(8,128)S(1)} %convert.9, pred[4,8,8]{2,1,0:T(8,128)(4,1)S(1)} %get-tuple-element.18), kind=kLoop, calls=%fused_computation.4 | loop fusion | flops 2949120 | bytes 1573120 | tf_op jit(solution)/shard_map/reduce_sum | solution.py:247
  79.5 0.3 fusion.7
  79.8 0.3 fusion.6
  80.1 0.3 fusion.5
  80.4 0.3 fusion.4
  80.8 0.8 copy-done.1
  81.5 1.0 %fusion.3 = f32[5,192,96]{2,1,0:T(8,128)} fusion(f32[5,192,96]{2,1,0:T(8,128)} %copy-done.1, bf16[4,8,32,192]{3,2,1,0:T(8,128)(2,1)S(1)} %fusion.14, bf16[4,8,36,96]{3,2,0,1:T(8,128)(2,1)S(1)} %copy_select_fusion), kind=kOutput, calls=%fused_computation.19 | convolution fusion | flops 37748736 | bytes 884736 | tf_op jit(solution)/shard_map/qato,qati->oi/dot_general | solution.py:255
  (69 shorter events, 4.1 us)
Async XLA Ops:
  0.7 26.5 %collective-permute-start = (bf16[2,768]{1,0:T(2,128)(2,1)S(1)}, bf16[2,768]{1,0:T(2,128)(2,1)S(1)}, u32[]{:S(2)}, u32[]{:S(2)}) collective-permute-start(bf16[2,768]{1,0:T(2,128)(2,1)S(1)} %get-tuple-element.11), channel_id=1, source_target_pairs={{0,16},{1,17},{2,18},{3,19},{4,20},{5,21},{6,22},{7,23},{8,24},{9,... | collective-permute-start | bytes 9224 | tf_op jit(solution)/shard_map/ppermute | solution.py:196
  5.6 21.7 %collective-permute-start.1 = (bf16[2,768]{1,0:T(2,128)(2,1)S(1)}, bf16[2,768]{1,0:T(2,128)(2,1)S(1)}, u32[]{:S(2)}, u32[]{:S(2)}) collective-permute-start(bf16[2,768]{1,0:T(2,128)(2,1)S(1)} %get-tuple-element.12), channel_id=1, source_target_pairs={{16,0},{17,1},{18,2},{19,3},{20,4},{21,5},{22,6},{23,7},{24,8},{25... | collective-permute-start | bytes 9224 | tf_op jit(solution)/shard_map/ppermute | solution.py:197
  29.4 1.4 %copy-start = (bf16[5,192,768]{2,1,0:T(8,128)(2,1)S(1)}, bf16[5,192,768]{2,1,0:T(8,128)(2,1)}, u32[]{:S(2)}) copy-start(bf16[5,192,768]{2,1,0:T(8,128)(2,1)} %param.7) | copy-start | bytes 4423684
  35.5 13.3 %all-to-all-start = ((bf16[8,2,19200]{2,1,0:T(2,128)(2,1)}), bf16[8,2,19200]{2,1,0:T(2,128)(2,1)S(1)}, u32[]{:S(2)}, u32[]{:S(2)}) async-start(bf16[8,2,19200]{2,1,0:T(2,128)(2,1)} %reshape.991), calls=%async_computation | async-start | bytes 1228800 | tf_op jit(solution)/shard_map/all_to_all | solution.py:220
  51.0 10.4 %collective-permute-start.4 = (f32[4,2,2,32,32]{4,3,2,1,0:T(8,128)S(1)}, f32[4,2,2,32,32]{4,3,2,1,0:T(8,128)S(1)}, u32[]{:S(2)}, u32[]{:S(2)}) collective-permute-start(f32[4,2,2,32,32]{4,3,2,1,0:T(8,128)S(1)} %fusion.50), channel_id=1, source_target_pairs={{0,12},{4,0},{8,4},{12,8},{1,13},{5,1},{9,5},{13,9},{2,14},{6,2},{... | collective-permute-start | bytes 196616 | tf_op jit(solution)/shard_map/ppermute | solution.py:145
  54.6 22.1 %collective-permute-start.3 = (f32[4,2,2,32,32]{4,3,2,1,0:T(8,128)S(1)}, f32[4,2,2,32,32]{4,3,2,1,0:T(8,128)S(1)}, u32[]{:S(2)}, u32[]{:S(2)}) collective-permute-start(f32[4,2,2,32,32]{4,3,2,1,0:T(8,128)S(1)} %fusion.50), channel_id=1, source_target_pairs={{0,8},{4,12},{8,0},{12,4},{1,9},{5,13},{9,1},{13,5},{2,10},{6,14},... | collective-permute-start | bytes 196616 | tf_op jit(solution)/shard_map/ppermute | solution.py:145
  54.7 22.1 %collective-permute-start.2 = (f32[4,2,2,32,32]{4,3,2,1,0:T(8,128)S(1)}, f32[4,2,2,32,32]{4,3,2,1,0:T(8,128)S(1)}, u32[]{:S(2)}, u32[]{:S(2)}) collective-permute-start(f32[4,2,2,32,32]{4,3,2,1,0:T(8,128)S(1)} %fusion.50), channel_id=1, source_target_pairs={{0,4},{4,8},{8,12},{12,0},{1,5},{5,9},{9,13},{13,1},{2,6},{6,10},{... | collective-permute-start | bytes 196616 | tf_op jit(solution)/shard_map/ppermute | solution.py:145
  80.8 0.8 copy-start.1

commit v4 on v3

--- a/solution.py
+++ b/solution.py
@@ -184,10 +184,16 @@
     rank = jnp.sum(jnp.logical_and(same_source, before), axis=-1)
     slot = (source * groups + jnp.arange(groups)[:, None, None]) * held + jnp.arange(owners)[None, :, None] * PER + rank
 
-    mine = lax.dynamic_index_in_dim(jnp.stack([source, local, rank], 0), lax.axis_index("dp"), 1, keepdims=False)
-    held_here = mine[0] == my_index
+    own_sides = jnp.concatenate([tiles[0, ..., 0], tiles[0, ..., 1]], axis=-1)
+    own_source = own_sides // per_block
+    own_same = own_source[:, :, None] == own_source[:, None, :]
+    own_rank = jnp.sum(jnp.logical_and(own_same, before), axis=-1)
+    held_here = own_source == my_index
     picks = jnp.stack(
-        [jnp.sum(jnp.where(jnp.logical_and(held_here, mine[2] == r), mine[1], 0), axis=-1) for r in range(PER)],
+        [
+            jnp.sum(jnp.where(jnp.logical_and(held_here, own_rank == r), own_sides % per_block, 0), axis=-1)
+            for r in range(PER)
+        ],
         axis=-1,
     ).reshape(held)
 
@@ -210,7 +216,7 @@
             "hti,oi->hto", act[:, offset : offset + TB], conv_weight[offset], preferred_element_type=jnp.float32
         )
     scaling = 1.25 * keep_all.astype(jnp.float32)
-    my_scale = lax.dynamic_index_in_dim(scaling, lax.axis_index("dp"), 0, keepdims=False)
+    my_scale = 1.25 * keep[0].astype(jnp.float32)
     x_part = lax.dynamic_slice_in_dim(x_float[:, halo : halo + TB], my_part * narrow, narrow, 2)
     mixed = (x_part + my_scale * conv_out).astype(jnp.bfloat16)
 
@@ -225,7 +231,9 @@
     row_side = side_rows[:, :, :capacity]
     col_side = side_rows[:, :, capacity:]
     partial_tiles = jnp.einsum("qocid,qocjd->qocij", row_side, col_side, preferred_element_type=jnp.float32)
-    predicted = axis_sum(partial_tiles, "mp") / math.sqrt(width)
+    lanes_shape = partial_tiles.shape
+    summed = axis_sum(partial_tiles.reshape(-1, 128), "mp").reshape(lanes_shape)
+    predicted = summed / math.sqrt(width)
     target_tiles = targets_all.reshape(seq_count, groups, capacity, TB, TB).transpose(1, 0, 2, 3, 4)
     live_mask = (jnp.arange(capacity)[None, None, :] < counts_all[:, :, None]).astype(jnp.float32)
     n_live = jnp.sum(counts_all, axis=-1).astype(jnp.float32)

time: 82.9 us -> 67.1 us (0.81)
  waiting for transfers between devices: 29.5 us -> 13.5 us
    ppermute x3, waiting for transfers between devices: 20 us -> 4.1 us  [axis_sum(): lax.ppermute(value, axis, [(i, (i + shift) % count) for i in range(count)])]
    slice x0 -> x1, local copies, waits for them, and re-layouts: none -> 0.97 us  [sparse_path(): own_sides = jnp.concatenate([tiles[0, ..., 0], tiles[0, ..., 1]], axis=-1)]
  transfers between devices with their start and end apart: 6 -> 6, of which waited for: 3 -> 3; matrix products, arithmetic and copies ran while one was open for 13% -> 16% of each run, Pallas kernels for 0% -> 0%
where the time goes in v4:
time: 67.1 us; the launch traced here: 66.6 us
  local copies, waits for them, and re-layouts  16 us (24%)
  starting transfers between devices  14.3 us (21%)
  waiting for transfers between devices  13.5 us (20%)
  blocking collectives  10.3 us (15%)
  other arithmetic  6.65 us (10%)
  matrix products  4.62 us (7%)
  between operations  1.14 us (2%)
    all_gather x1, blocking collectives, sparse_path(): lax.all_gather(bundle, ('seq', 'dp'), tiled=True)  10.3 us
    all_to_all x1, waiting for transfers between devices, sparse_path(): incoming = lax.all_to_all(outgoing, ('seq', 'dp'), 0, 0, tiled=True)  9.39 us
    ppermute x1, starting transfers between devices, sparse_path(): lax.ppermute(cells[length - halo:], 'seq', [(i, i + 1) for i in range(end...  4.83 us
    ppermute x3, starting transfers between devices, axis_sum(): lax.ppermute(value, axis, [(i, (i + shift) % count) for i in range(count)])  4.67 us
    ppermute x3, waiting for transfers between devices, axis_sum(): lax.ppermute(value, axis, [(i, (i + shift) % count) for i in range(count)])  4.1 us
    unnamed x8, local copies, waits for them, and re-layouts  3.96 us
    all_to_all x1, starting transfers between devices, sparse_path(): incoming = lax.all_to_all(outgoing, ('seq', 'dp'), 0, 0, tiled=True)  3.54 us
    gather x3, local copies, waits for them, and re-layouts, sparse_path(): inside = jnp.take(cells, jnp.clip(rows, 0, length - 1), axis=0)  3.02 us
  transfers between devices with their start and end apart: 6, of which 3 were waited for; matrix products, arithmetic and copies ran while one was open for 16% of the time, Pallas kernels for 0%

profile of v4, /device:TPU:0, one launch (start us, length us, event | category | flops | bytes accessed | tf_op | source)
XLA Modules:
  0.0 66.6 jit_solution(12548127950016695544)
XLA Ops:
  0.0 0.7 %slice_bitcast_fusion.1 = (bf16[2,768]{1,0:T(2,128)(2,1)S(1)}, bf16[2,768]{1,0:T(2,128)(2,1)S(1)}) fusion(bf16[1,1024,768]{2,1,0:T(8,128)(2,1)} %param.6), kind=kLoop, calls=%fused_computation.132 | loop fusion | bytes 12288 | tf_op jit(solution)/shard_map/slice | solution.py:202
  0.7 4.8 %collective-permute-start = (bf16[2,768]{1,0:T(2,128)(2,1)S(1)}, bf16[2,768]{1,0:T(2,128)(2,1)S(1)}, u32[]{:S(2)}, u32[]{:S(2)}) collective-permute-start(bf16[2,768]{1,0:T(2,128)(2,1)S(1)} %get-tuple-element.13), channel_id=1, source_target_pairs={{0,16},{1,17},{2,18},{3,19},{4,20},{5,21},{6,22},{7,23},{8,24},{9,... | collective-permute-start | bytes 9224 | tf_op jit(solution)/shard_map/ppermute | solution.py:202
  5.6 1.3 %collective-permute-start.1 = (bf16[2,768]{1,0:T(2,128)(2,1)S(1)}, bf16[2,768]{1,0:T(2,128)(2,1)S(1)}, u32[]{:S(2)}, u32[]{:S(2)}) collective-permute-start(bf16[2,768]{1,0:T(2,128)(2,1)S(1)} %get-tuple-element.14), channel_id=1, source_target_pairs={{16,0},{17,1},{18,2},{19,3},{20,4},{21,5},{22,6},{23,7},{24,8},{25... | collective-permute-start | bytes 9224 | tf_op jit(solution)/shard_map/ppermute | solution.py:203
  6.9 0.8 %reshape.846 = s32[8]{0:T(128)S(1)} reshape(s32[1,2,2,2]{3,2,1,0:T(2,128)} %param.9) | data formatting | bytes 64 | tf_op jit(solution)/shard_map/reshape | solution.py:165
  7.7 1.0 %slice_reduce_fusion.1 = (s32[2,2]{1,0:T(2,128)S(1)}, s32[2,2]{1,0:T(2,128)S(1)}) fusion(s32[1,2,2,2]{3,2,1,0:T(2,128)} %param.9), kind=kLoop, calls=%fused_computation.156 | loop fusion | bytes 64 | tf_op jit(solution)/shard_map/slice | solution.py:187
  8.7 0.2 convert_reduce_fusion.1
  10.1 0.7 %copy.153 = f32[1,8,2,128]{3,1,2,0:T(8,128)S(1)} copy(f32[1,8,2,128]{3,2,1,0:T(2,128)} %bitcast.124) | data formatting | bytes 16384
  10.8 0.7 %add_convert_fusion = f32[11]{0:T(128)S(1)} fusion(s32[1]{0:T(128)S(6)} %copy.159, s32[2]{0:T(128)} %bitcast.127, s32[8]{0:T(128)S(1)} %reshape.846), kind=kLoop, calls=%fused_computation.177 | loop fusion | flops 33 | bytes 88 | tf_op jit(solution)/shard_map/convert_element_type | solution.py:165
  11.6 10.3 %all-gather = f32[8,17,128]{2,1,0:T(8,128)S(1)} all-gather(f32[1,17,128]{2,1,0:T(8,128)S(1)} %fusion.57), channel_id=1, replica_groups=mesh['seq'=2,'mp'=4,'dp'=4] {'seq','dp'}, dimensions={0}, use_global_device_ids=true | all-gather | bytes 78336 | tf_op jit(solution)/shard_map/all_gather | solution.py:170
  22.7 0.3 convert_reduce_fusion
  23.6 0.2 and_reduce_fusion
  24.2 2.6 %gather_fusion = bf16[144,768]{1,0:T(8,128)(2,1)S(1)} fusion(bf16[1024,768]{1,0:T(8,128)(2,1)} %bitcast.112, s32[1024]{0:T(1024)S(1)} %pad_clamp_fusion.3), kind=kCustom, calls=%fused_computation | custom fusion | bytes 442944 | tf_op jit(solution)/shard_map/jit(_take)/gather | solution.py:205
  26.9 0.3 gather.22
  27.6 0.9 %gather_fusion.1 = bf16[144,768]{1,0:T(8,128)(2,1)S(1)} fusion(bf16[4,768]{1,0:T(4,128)(2,1)S(1)} %pad_maximum_fusion.1, s32[1024]{0:T(1024)S(1)} %pad_clamp_fusion.2), kind=kCustom, calls=%fused_computation.1 | custom fusion | bytes 442944 | tf_op jit(solution)/shard_map/jit(_take)/gather | solution.py:208
  28.5 0.3 gather.23
  28.9 0.4 fusion.23
  29.3 0.4 reshape.851
  29.7 0.4 fusion.22
  30.1 0.9 %copy-done = bf16[5,192,768]{2,1,0:T(8,128)(2,1)S(1)} copy-done((bf16[5,192,768]{2,1,0:T(8,128)(2,1)S(1)}, bf16[5,192,768]{2,1,0:T(8,128)(2,1)}, u32[]{:S(2)}) %copy-start) | copy-done | bytes 1474584
  31.1 0.2 fusion.29
  31.3 0.2 convolution_add_fusion.3
  31.6 0.2 convolution_add_fusion.2
  31.8 0.2 convolution_add_fusion.1
  32.1 0.3 fusion.2
  32.6 0.5 broadcast.807
  33.1 1.1 %reduce.6 = bf16[8,38400]{1,0:T(8,128)(2,1)S(1)} reduce(bf16[8,1,38400]{2,0,1:T(8,128)(2,1)S(1)} %maximum_bitcast_fusion, bf16[]{:T(256)} %broadcast.807), dimensions={1}, to_apply=%copy.105.reduce_sub_computation | reduce | bytes 1228802 | tf_op jit(solution)/shard_map/all_to_all | solution.py:226
  34.2 1.0 %reshape.913 = bf16[8,2,19200]{2,1,0:T(2,128)(2,1)} reshape(bf16[8,38400]{1,0:T(8,128)(2,1)S(1)} %reduce.6) | data formatting | bytes 1228800
  35.2 3.5 %all-to-all-start = ((bf16[8,2,19200]{2,1,0:T(2,128)(2,1)}), bf16[8,2,19200]{2,1,0:T(2,128)(2,1)S(1)}, u32[]{:S(2)}, u32[]{:S(2)}) async-start(bf16[8,2,19200]{2,1,0:T(2,128)(2,1)} %reshape.913), calls=%async_computation | async-start | bytes 1228800 | tf_op jit(solution)/shard_map/all_to_all | solution.py:226
  39.1 9.4 %all-to-all-done = bf16[8,2,19200]{2,1,0:T(2,128)(2,1)S(1)} async-done(((bf16[8,2,19200]{2,1,0:T(2,128)(2,1)}), bf16[8,2,19200]{2,1,0:T(2,128)(2,1)S(1)}, u32[]{:S(2)}, u32[]{:S(2)}) %all-to-all-start) | async-done | bytes 614432 | tf_op jit(solution)/shard_map/all_to_all | solution.py:226
  48.5 0.5 reshape.914
  49.1 0.6 reshape.852
  49.7 0.6 gather_fusion.2
  50.4 0.2 fusion.50
  50.8 3.6 %collective-permute-start.4 = (f32[128,128]{1,0:T(8,128)S(1)}, f32[128,128]{1,0:T(8,128)S(1)}, u32[]{:S(2)}, u32[]{:S(2)}) collective-permute-start(f32[128,128]{1,0:T(8,128)S(1)} %reshape.853), channel_id=1, source_target_pairs={{0,12},{4,0},{8,4},{12,8},{1,13},{5,1},{9,5},{13,9},{2,14},{6,2},{... | collective-permute-start | bytes 196616 | tf_op jit(solution)/shard_map/ppermute | solution.py:145
  54.4 1.0 %collective-permute-start.2 = (f32[128,128]{1,0:T(8,128)S(1)}, f32[128,128]{1,0:T(8,128)S(1)}, u32[]{:S(2)}, u32[]{:S(2)}) collective-permute-start(f32[128,128]{1,0:T(8,128)S(1)} %reshape.853), channel_id=1, source_target_pairs={{0,4},{4,8},{8,12},{12,0},{1,5},{5,9},{9,13},{13,1},{2,6},{6,10},{... | collective-permute-start | bytes 196616 | tf_op jit(solution)/shard_map/ppermute | solution.py:145
  55.4 0.4 reshape.855
  55.9 0.6 gather_fusion.3
  56.6 0.4 collective-permute-done.4
  57.0 3.7 %collective-permute-done.3 = f32[128,128]{1,0:T(8,128)S(1)} collective-permute-done((f32[128,128]{1,0:T(8,128)S(1)}, f32[128,128]{1,0:T(8,128)S(1)}, u32[]{:S(2)}, u32[]{:S(2)}) %collective-permute-start.3) | collective-permute-done | bytes 65568 | tf_op jit(solution)/shard_map/ppermute | solution.py:145
  60.8 0.5 convolution_convert_fusion
  61.4 0.4 convolution_convert_fusion.1
  62.0 1.4 %select_reduce_fusion = f32[4,8,32,192]{3,2,1,0:T(8,128)S(1)} fusion(f32[4,8,32,192]{3,2,1,0:T(8,128)S(1)} %convert.9, pred[4,8,8]{2,1,0:T(8,128)(4,1)S(1)} %get-tuple-element.18), kind=kLoop, calls=%fused_computation.4 | loop fusion | flops 2949120 | bytes 1573120 | tf_op jit(solution)/shard_map/reduce_sum | solution.py:255
  63.6 0.3 fusion.7
  63.9 0.3 fusion.6
  64.2 0.3 fusion.5
  64.5 0.3 fusion.4
  64.9 0.8 %copy-done.1 = f32[5,192,96]{2,1,0:T(8,128)} copy-done((f32[5,192,96]{2,1,0:T(8,128)}, f32[5,192,96]{2,1,0:T(8,128)S(1)}, u32[]{:S(2)}) %copy-start.1) | copy-done | bytes 368664
  65.6 1.0 %fusion.3 = f32[5,192,96]{2,1,0:T(8,128)} fusion(f32[5,192,96]{2,1,0:T(8,128)} %copy-done.1, bf16[4,8,32,192]{3,2,1,0:T(8,128)(2,1)S(1)} %fusion.14, bf16[4,8,36,96]{3,2,0,1:T(8,128)(2,1)S(1)} %copy_select_fusion), kind=kOutput, calls=%fused_computation.19 | convolution fusion | flops 37748736 | bytes 884736 | tf_op jit(solution)/shard_map/qato,qati->oi/dot_general | solution.py:263
  (69 shorter events, 4.3 us)
Async XLA Ops:
  0.7 26.8 %collective-permute-start = (bf16[2,768]{1,0:T(2,128)(2,1)S(1)}, bf16[2,768]{1,0:T(2,128)(2,1)S(1)}, u32[]{:S(2)}, u32[]{:S(2)}) collective-permute-start(bf16[2,768]{1,0:T(2,128)(2,1)S(1)} %get-tuple-element.13), channel_id=1, source_target_pairs={{0,16},{1,17},{2,18},{3,19},{4,20},{5,21},{6,22},{7,23},{8,24},{9,... | collective-permute-start | bytes 9224 | tf_op jit(solution)/shard_map/ppermute | solution.py:202
  5.6 22.0 %collective-permute-start.1 = (bf16[2,768]{1,0:T(2,128)(2,1)S(1)}, bf16[2,768]{1,0:T(2,128)(2,1)S(1)}, u32[]{:S(2)}, u32[]{:S(2)}) collective-permute-start(bf16[2,768]{1,0:T(2,128)(2,1)S(1)} %get-tuple-element.14), channel_id=1, source_target_pairs={{16,0},{17,1},{18,2},{19,3},{20,4},{21,5},{22,6},{23,7},{24,8},{25... | collective-permute-start | bytes 9224 | tf_op jit(solution)/shard_map/ppermute | solution.py:203
  29.7 1.4 %copy-start = (bf16[5,192,768]{2,1,0:T(8,128)(2,1)S(1)}, bf16[5,192,768]{2,1,0:T(8,128)(2,1)}, u32[]{:S(2)}) copy-start(bf16[5,192,768]{2,1,0:T(8,128)(2,1)} %param.7) | copy-start | bytes 4423684
  35.2 13.3 %all-to-all-start = ((bf16[8,2,19200]{2,1,0:T(2,128)(2,1)}), bf16[8,2,19200]{2,1,0:T(2,128)(2,1)S(1)}, u32[]{:S(2)}, u32[]{:S(2)}) async-start(bf16[8,2,19200]{2,1,0:T(2,128)(2,1)} %reshape.913), calls=%async_computation | async-start | bytes 1228800 | tf_op jit(solution)/shard_map/all_to_all | solution.py:226
  50.8 6.2 %collective-permute-start.4 = (f32[128,128]{1,0:T(8,128)S(1)}, f32[128,128]{1,0:T(8,128)S(1)}, u32[]{:S(2)}, u32[]{:S(2)}) collective-permute-start(f32[128,128]{1,0:T(8,128)S(1)} %reshape.853), channel_id=1, source_target_pairs={{0,12},{4,0},{8,4},{12,8},{1,13},{5,1},{9,5},{13,9},{2,14},{6,2},{... | collective-permute-start | bytes 196616 | tf_op jit(solution)/shard_map/ppermute | solution.py:145
  54.4 6.3 %collective-permute-start.3 = (f32[128,128]{1,0:T(8,128)S(1)}, f32[128,128]{1,0:T(8,128)S(1)}, u32[]{:S(2)}, u32[]{:S(2)}) collective-permute-start(f32[128,128]{1,0:T(8,128)S(1)} %reshape.853), channel_id=1, source_target_pairs={{0,8},{4,12},{8,0},{12,4},{1,9},{5,13},{9,1},{13,5},{2,10},{6,14},... | collective-permute-start | bytes 196616 | tf_op jit(solution)/shard_map/ppermute | solution.py:145
  54.4 6.3 %collective-permute-start.2 = (f32[128,128]{1,0:T(8,128)S(1)}, f32[128,128]{1,0:T(8,128)S(1)}, u32[]{:S(2)}, u32[]{:S(2)}) collective-permute-start(f32[128,128]{1,0:T(8,128)S(1)} %reshape.853), channel_id=1, source_target_pairs={{0,4},{4,8},{8,12},{12,0},{1,5},{5,9},{9,13},{13,1},{2,6},{6,10},{... | collective-permute-start | bytes 196616 | tf_op jit(solution)/shard_map/ppermute | solution.py:145
  64.9 0.8 %copy-start.1 = (f32[5,192,96]{2,1,0:T(8,128)}, f32[5,192,96]{2,1,0:T(8,128)S(1)}, u32[]{:S(2)}) copy-start(f32[5,192,96]{2,1,0:T(8,128)S(1)} %fusion.4) | copy-start | bytes 1105924

commit v5 on v4

--- a/solution.py
+++ b/solution.py
@@ -162,28 +162,7 @@
     my_index = lax.axis_index("seq")
     my_part = lax.axis_index("mp")
 
-    small = jnp.concatenate([tiles.reshape(-1), counts.reshape(-1), keep.reshape(-1)]).astype(jnp.float32)
-    bundle = jnp.concatenate([targets.reshape(-1), small])
-    lanes = 128
-    padding = -bundle.shape[0] % lanes
-    bundle = jnp.pad(bundle, (0, padding)).reshape(-1, lanes)
-    gathered = lax.all_gather(bundle, ("seq", "dp"), tiled=True).reshape(seq_count, groups, -1)
-    n_targets = capacity * TB * TB
-    n_tiles = owners * capacity * 2
-    meta = gathered[0, :, n_targets:].astype(jnp.int32)
-    tiles_all = meta[:, :n_tiles].reshape(groups, owners, capacity, 2)
-    counts_all = meta[:, n_tiles : n_tiles + owners]
-    keep_all = meta[:, n_tiles + owners]
-    targets_all = gathered[:, :, :n_targets]
-
-    sides = jnp.concatenate([tiles_all[..., 0], tiles_all[..., 1]], axis=-1)
-    source = sides // per_block
-    local = sides % per_block
     before = jnp.arange(n_sides)[None, :] < jnp.arange(n_sides)[:, None]
-    same_source = source[..., :, None] == source[..., None, :]
-    rank = jnp.sum(jnp.logical_and(same_source, before), axis=-1)
-    slot = (source * groups + jnp.arange(groups)[:, None, None]) * held + jnp.arange(owners)[None, :, None] * PER + rank
-
     own_sides = jnp.concatenate([tiles[0, ..., 0], tiles[0, ..., 1]], axis=-1)
     own_source = own_sides // per_block
     own_same = own_source[:, :, None] == own_source[:, None, :]
@@ -201,13 +180,18 @@
     ends = seq_count - 1
     head = lax.ppermute(cells[length - halo :], "seq", [(i, i + 1) for i in range(ends)])
     tail = lax.ppermute(cells[:halo], "seq", [(i + 1, i) for i in range(ends)])
-    rows = picks[:, None] * TB - halo + jnp.arange(span)[None, :]
-    inside = jnp.take(cells, jnp.clip(rows, 0, length - 1), axis=0)
-    edge_rows = jnp.concatenate([head, tail], axis=0)
-    edge_index = jnp.where(rows < 0, rows + halo, rows - length + halo)
-    outside = jnp.take(edge_rows, jnp.clip(edge_index, 0, 2 * halo - 1), axis=0)
-    in_range = jnp.logical_and(rows >= 0, rows < length)
-    windows = jnp.where(in_range[..., None], inside, outside)
+    starts = picks * TB
+    last = per_block - 1
+
+    def window(block, start):
+        before = lax.dynamic_slice_in_dim(cells, jnp.maximum(start - halo, 0), halo, 0)
+        middle = lax.dynamic_slice_in_dim(cells, start, TB, 0)
+        after = lax.dynamic_slice_in_dim(cells, jnp.minimum(start + TB, length - halo), halo, 0)
+        before = jnp.where(block == 0, head, before)
+        after = jnp.where(block == last, tail, after)
+        return jnp.concatenate([before, middle, after], axis=0)
+
+    windows = jnp.stack([window(picks[h], starts[h]) for h in range(held)])
     x_float = windows.astype(jnp.float32)
     act = jax.nn.gelu(x_float).astype(jnp.bfloat16)
     conv_out = jnp.einsum("hti,oi->hto", act[:, 0:TB], conv_weight[0], preferred_element_type=jnp.float32)
@@ -215,17 +199,43 @@
         conv_out = conv_out + jnp.einsum(
             "hti,oi->hto", act[:, offset : offset + TB], conv_weight[offset], preferred_element_type=jnp.float32
         )
-    scaling = 1.25 * keep_all.astype(jnp.float32)
     my_scale = 1.25 * keep[0].astype(jnp.float32)
     x_part = lax.dynamic_slice_in_dim(x_float[:, halo : halo + TB], my_part * narrow, narrow, 2)
     mixed = (x_part + my_scale * conv_out).astype(jnp.bfloat16)
 
     act_cut = act.reshape(held, span, peers, cols).transpose(2, 0, 1, 3).reshape(peers, -1)
     mixed_rep = jnp.broadcast_to(mixed.reshape(1, -1), (peers, held * TB * narrow))
-    outgoing = jnp.concatenate([mixed_rep, act_cut], axis=1)
+    wide = targets.reshape(-1)
+    pieces = []
+    for _ in range(3):
+        piece = lax.reduce_precision(wide, exponent_bits=8, mantissa_bits=7)
+        pieces.append(piece)
+        wide = wide - piece
+    small = jnp.concatenate([tiles.reshape(-1), counts.reshape(-1), keep.reshape(-1)]).astype(jnp.float32)
+    meta = jnp.concatenate(pieces + [small]).astype(jnp.bfloat16)
+    meta_rep = jnp.broadcast_to(meta[None], (peers, meta.shape[0]))
+    outgoing = jnp.concatenate([mixed_rep, act_cut, meta_rep], axis=1)
     incoming = lax.all_to_all(outgoing, ("seq", "dp"), 0, 0, tiled=True)
-    mixed_in = incoming[:, : held * TB * narrow].reshape(peers * held, TB, narrow)
-    act_in = incoming[:, held * TB * narrow :].reshape(peers * held, span, cols)
+    n_mixed = held * TB * narrow
+    n_act = held * span * cols
+    mixed_in = incoming[:, :n_mixed].reshape(peers * held, TB, narrow)
+    act_in = incoming[:, n_mixed : n_mixed + n_act].reshape(peers * held, span, cols)
+    meta_in = incoming[:, n_mixed + n_act :].astype(jnp.float32).reshape(seq_count, groups, -1)
+    n_targets = capacity * TB * TB
+    n_tiles = owners * capacity * 2
+    targets_all = meta_in[:, :, :n_targets] + meta_in[:, :, n_targets : 2 * n_targets]
+    targets_all = targets_all + meta_in[:, :, 2 * n_targets : 3 * n_targets]
+    ints = meta_in[0, :, 3 * n_targets :].astype(jnp.int32)
+    tiles_all = ints[:, :n_tiles].reshape(groups, owners, capacity, 2)
+    counts_all = ints[:, n_tiles : n_tiles + owners]
+    keep_all = ints[:, n_tiles + owners]
+
+    sides = jnp.concatenate([tiles_all[..., 0], tiles_all[..., 1]], axis=-1)
+    source = sides // per_block
+    local = sides % per_block
+    same_source = source[..., :, None] == source[..., None, :]
+    rank = jnp.sum(jnp.logical_and(same_source, before), axis=-1)
+    slot = (source * groups + jnp.arange(groups)[:, None, None]) * held + jnp.arange(owners)[None, :, None] * PER + rank
 
     side_rows = jnp.take(mixed_in, slot, axis=0)
     row_side = side_rows[:, :, :capacity]
@@ -255,6 +265,7 @@
     total = jnp.sum(jnp.where(same_block[..., None, None], grads[:, None], 0.0), axis=2)
     earlier = jnp.arange(owners * n_sides)[None, :] < jnp.arange(owners * n_sides)[:, None]
     first = jnp.logical_not(jnp.any(jnp.logical_and(same_block, earlier[None]), axis=-1))
+    scaling = 1.25 * keep_all.astype(jnp.float32)
     dconv = (scaling[:, None, None, None] * total).astype(jnp.bfloat16)
     dconv = jnp.where(first[..., None, None], dconv, jnp.zeros_like(dconv))
     act_sides = jnp.take(act_in, slot.reshape(groups, owners * n_sides), axis=0)
@@ -274,7 +285,9 @@
 def per_device(features, conv_weight, keep, tiles, counts, targets):
     members, length, _ = features.shape
     owners, capacity = tiles.shape[1], tiles.shape[2]
+    blocks = lax.axis_size("seq") * length // TB
     fits = members == 1 and targets.shape[1] == 1 and 2 * owners * capacity * TB <= length
+    fits = fits and blocks <= 256 and capacity <= 256
     if fits:
         return sparse_path(features, conv_weight, keep, tiles, counts, targets)
     return dense_path(features, conv_weight, keep, tiles, counts, targets)

time: 67.1 us -> 80.8 us (1.20)
  between operations: 1.14 us -> 18.4 us
  blocking collectives: 10.3 us -> 0 us
  waiting for transfers between devices: 13.5 us -> 19.6 us
  starting transfers between devices: 14.3 us -> 16.6 us
  local copies, waits for them, and re-layouts: 16 us -> 13.8 us
    all_gather x1 -> x0, blocking collectives: 10.3 us -> none  [sparse_path(): lax.all_gather(bundle, ('seq', 'dp'), tiled=True)]
    all_to_all x1, waiting for transfers between devices: 9.39 us -> 18.4 us  [sparse_path(): incoming = lax.all_to_all(outgoing, ('seq', 'dp'), 0, 0, tiled=True)]
    gather x6 -> x0, local copies, waits for them, and re-layouts: 4.31 us -> none  [the longest x3 3.02 us: sparse_path(): inside = jnp.take(cells, jnp.clip(rows, 0, length - 1), axis=0)]
    unnamed x8 -> x5, local copies, waits for them, and re-layouts: 3.96 us -> 0.86 us
    ppermute x3, waiting for transfers between devices: 4.1 us -> 1.18 us  [axis_sum(): lax.ppermute(value, axis, [(i, (i + shift) % count) for i in range(count)])]
    concatenate x1 -> x14, local copies, waits for them, and re-layouts: 0.01 us -> 1.94 us  [the longest x12 1.17 us: window(): return jnp.concatenate([before, middle, after], axis=0)]
    all_to_all x1, local copies, waits for them, and re-layouts: 0.51 us -> 2.22 us  [sparse_path(): incoming = lax.all_to_all(outgoing, ('seq', 'dp'), 0, 0, tiled=True)]
    another operation x0 -> x5, other arithmetic: none -> 1.55 us
  transfers between devices with their start and end apart: 6 -> 6, of which waited for: 3 -> 2; matrix products, arithmetic and copies ran while one was open for 16% -> 11% of each run, Pallas kernels for 0% -> 0%
where the time goes in v5:
time: 80.8 us; the launch traced here: 80.1 us
  waiting for transfers between devices  19.6 us (24%)
  between operations  18.4 us (23%)
  starting transfers between devices  16.6 us (21%)
  local copies, waits for them, and re-layouts  13.8 us (17%)
  other arithmetic  7.11 us (9%)
  matrix products  4.63 us (6%)
    all_to_all x1, waiting for transfers between devices, sparse_path(): incoming = lax.all_to_all(outgoing, ('seq', 'dp'), 0, 0, tiled=True)  18.4 us
    ppermute x3, starting transfers between devices, axis_sum(): lax.ppermute(value, axis, [(i, (i + shift) % count) for i in range(count)])  5.55 us
    all_to_all x1, starting transfers between devices, sparse_path(): incoming = lax.all_to_all(outgoing, ('seq', 'dp'), 0, 0, tiled=True)  4.87 us
    ppermute x1, starting transfers between devices, sparse_path(): lax.ppermute(cells[length - halo:], 'seq', [(i, i + 1) for i in range(end...  4.83 us
    dot_general x5, matrix products, sparse_path(): jnp.einsum('qato,qati->oi', dconv, act_sides[:, :, offset:offset + TB], p...  2.25 us
    all_to_all x1, local copies, waits for them, and re-layouts, sparse_path(): incoming = lax.all_to_all(outgoing, ('seq', 'dp'), 0, 0, tiled=True)  2.22 us
  transfers between devices with their start and end apart: 6, of which 2 were waited for; matrix products, arithmetic and copies ran while one was open for 11% of the time, Pallas kernels for 0%

profile of v5, /device:TPU:0, one launch (start us, length us, event | category | flops | bytes accessed | tf_op | source)
XLA Modules:
  0.0 80.1 jit_solution(8349133966660874054)
XLA Ops:
  0.0 0.7 slice_bitcast_fusion.1
  0.7 4.8 %collective-permute-start = (bf16[2,768]{1,0:T(2,128)(2,1)S(1)}, bf16[2,768]{1,0:T(2,128)(2,1)S(1)}, u32[]{:S(2)}, u32[]{:S(2)}) collective-permute-start(bf16[2,768]{1,0:T(2,128)(2,1)S(1)} %get-tuple-element.27), channel_id=1, source_target_pairs={{0,16},{1,17},{2,18},{3,19},{4,20},{5,21},{6,22},{7,23},{8,24},{9,... | collective-permute-start | bytes 9224 | tf_op jit(solution)/shard_map/ppermute | solution.py:181
  5.6 1.3 %collective-permute-start.1 = (bf16[2,768]{1,0:T(2,128)(2,1)S(1)}, bf16[2,768]{1,0:T(2,128)(2,1)S(1)}, u32[]{:S(2)}, u32[]{:S(2)}) collective-permute-start(bf16[2,768]{1,0:T(2,128)(2,1)S(1)} %get-tuple-element.28), channel_id=1, source_target_pairs={{16,0},{17,1},{18,2},{19,3},{20,4},{21,5},{22,6},{23,7},{24,8},{25... | collective-permute-start | bytes 9224 | tf_op jit(solution)/shard_map/ppermute | solution.py:182
  6.9 1.0 %slice_reduce_fusion.1 = (s32[2,2]{1,0:T(2,128)S(1)}, s32[2,2]{1,0:T(2,128)S(1)}) fusion(s32[1,2,2,2]{3,2,1,0:T(2,128)} %param.9), kind=kLoop, calls=%fused_computation.180 | loop fusion | bytes 64 | tf_op jit(solution)/shard_map/slice | solution.py:166
  8.0 0.2 convert_reduce_fusion.1
  8.2 0.2 fusion.81
  8.5 0.7 fusion.88
  14.1 0.7 fusion.89
  14.7 0.8 concatenate.179
  16.8 0.7 reduce-precision_convert_fusion.1
  20.0 0.7 fusion.83
  20.7 1.0 %constant_dynamic-slice_fusion.10 = (bf16[1,32,768]{2,1,0:T(8,128)(2,1)S(1)}, bf16[1,32,768]{2,1,0:T(8,128)(2,1)S(1)}, bf16[1,32,768]{2,1,0:T(8,128)(2,1)S(1)}, bf16[1,32,768]{2,1,0:T(8,128)(2,1)S(1)}) fusion(bf16[1,1024,768]{2,1,0:T(8,128)(2,1)} %param.6, s32[]{:T(128)S(6)} %select_n.200, s32[]{:T(128)S(6)} %select_n.212, s32[]{:T(128)S(6)} %select_n.206, ...), kind=kLoop, calls=%fused_computation.141 | loop fusion | bytes 393232 | tf_op jit(solution)/shard_map/dynamic_slice | solution.py:188
  31.5 1.0 %broadcast_select_fusion.8 = (bf16[2,768]{1,0:T(2,128)(2,1)S(1)}, bf16[2,768]{1,0:T(2,128)(2,1)S(1)}, bf16[2,768]{1,0:T(2,128)(2,1)S(1)}, bf16[2,768]{1,0:T(2,12...) fusion(bf16[2,768]{1,0:T(2,128)(2,1)S(1)} %collective-permute-d, ...), kind=kLoop, calls=%fused_computation.122 | loop fusion | flops 12288 | bytes 55336 | tf_op jit(solution)/shard_map/jit(_where)/select_n | solution.py:190
  32.7 0.2 fusion.22
  33.7 0.2 fusion.28
  33.9 0.2 convolution_add_fusion.3
  34.2 0.2 convolution_add_fusion.2
  34.4 0.2 convolution_add_fusion.1
  34.7 0.3 fusion.2
  35.1 0.3 fusion.23
  35.5 0.4 reshape.773
  35.9 0.2 maximum_bitcast_fusion
  36.1 2.2 %copy.89 = bf16[8,1,44555]{2,1,0:T(2,128)(2,1)} copy(bf16[8,1,44555]{2,0,1:T(8,128)(2,1)S(1)} %maximum_bitcast_fusion) | data formatting | bytes 1425760 | tf_op jit(solution)/shard_map/all_to_all | solution.py:218
  38.3 4.9 %all-to-all-start = ((bf16[8,1,44555]{2,1,0:T(2,128)(2,1)}), bf16[8,1,44555]{2,1,0:T(2,128)(2,1)S(1)}, u32[]{:S(2)}, u32[]{:S(2)}) async-start(bf16[8,1,44555]{2,1,0:T(2,128)(2,1)} %copy.89), calls=%async_computation | async-start | bytes 2859008 | tf_op jit(solution)/shard_map/all_to_all | solution.py:218
  43.3 18.4 %all-to-all-done = bf16[8,1,44555]{2,1,0:T(2,128)(2,1)S(1)} async-done(((bf16[8,1,44555]{2,1,0:T(2,128)(2,1)}), bf16[8,1,44555]{2,1,0:T(2,128)(2,1)S(1)}, u32[]{:S(2)}, u32[]{:S(2)}) %all-to-all-start) | async-done | bytes 712912 | tf_op jit(solution)/shard_map/all_to_all | solution.py:218
  62.3 0.3 convert_reduce_fusion
  63.4 0.6 reshape.778
  64.0 0.6 gather_fusion
  64.8 0.2 fusion.49
  65.1 1.6 %collective-permute-start.2 = (f32[128,128]{1,0:T(8,128)S(1)}, f32[128,128]{1,0:T(8,128)S(1)}, u32[]{:S(2)}, u32[]{:S(2)}) collective-permute-start(f32[128,128]{1,0:T(8,128)S(1)} %reshape.779), channel_id=1, source_target_pairs={{0,4},{4,8},{8,12},{12,0},{1,5},{5,9},{9,13},{13,1},{2,6},{6,10},{... | collective-permute-start | bytes 196616 | tf_op jit(solution)/shard_map/ppermute | solution.py:145
  66.7 2.6 %collective-permute-start.3 = (f32[128,128]{1,0:T(8,128)S(1)}, f32[128,128]{1,0:T(8,128)S(1)}, u32[]{:S(2)}, u32[]{:S(2)}) collective-permute-start(f32[128,128]{1,0:T(8,128)S(1)} %reshape.779), channel_id=1, source_target_pairs={{0,8},{4,12},{8,0},{12,4},{1,9},{5,13},{9,1},{13,5},{2,10},{6,14},... | collective-permute-start | bytes 196616 | tf_op jit(solution)/shard_map/ppermute | solution.py:145
  69.3 1.3 %collective-permute-start.4 = (f32[128,128]{1,0:T(8,128)S(1)}, f32[128,128]{1,0:T(8,128)S(1)}, u32[]{:S(2)}, u32[]{:S(2)}) collective-permute-start(f32[128,128]{1,0:T(8,128)S(1)} %reshape.779), channel_id=1, source_target_pairs={{0,12},{4,0},{8,4},{12,8},{1,13},{5,1},{9,5},{13,9},{2,14},{6,2},{... | collective-permute-start | bytes 196616 | tf_op jit(solution)/shard_map/ppermute | solution.py:145
  70.7 0.2 fusion.87
  71.1 0.4 reshape.781
  71.8 0.2 and_reduce_fusion
  72.0 0.6 gather_fusion.1
  72.8 0.2 multiply_reduce_fusion
  73.0 1.2 %collective-permute-done.3 = f32[128,128]{1,0:T(8,128)S(1)} collective-permute-done((f32[128,128]{1,0:T(8,128)S(1)}, f32[128,128]{1,0:T(8,128)S(1)}, u32[]{:S(2)}, u32[]{:S(2)}) %collective-permute-start.3) | collective-permute-done | bytes 65568 | tf_op jit(solution)/shard_map/ppermute | solution.py:145
  74.3 0.4 convolution_convert_fusion.1
  74.7 0.5 convolution_convert_fusion
  75.4 1.4 %select_reduce_fusion = f32[4,8,32,192]{3,2,1,0:T(8,128)S(1)} fusion(f32[4,8,32,192]{3,2,1,0:T(8,128)S(1)} %convert.26, pred[4,8,8]{2,1,0:T(8,128)(4,1)S(1)} %get-tuple-element.35), kind=kLoop, calls=%fused_computation.2 | loop fusion | flops 2949120 | bytes 1573120 | tf_op jit(solution)/shard_map/reduce_sum | solution.py:265
  76.8 0.2 fusion.14
  77.0 0.3 fusion.7
  77.3 0.3 fusion.6
  77.7 0.3 fusion.5
  78.0 0.3 fusion.4
  78.3 0.8 copy-done.1
  79.1 1.0 %fusion.3 = f32[5,192,96]{2,1,0:T(8,128)} fusion(f32[5,192,96]{2,1,0:T(8,128)} %copy-done.1, bf16[4,8,32,192]{3,2,1,0:T(8,128)(2,1)S(1)} %fusion.14, bf16[4,8,36,96]{3,2,0,1:T(8,128)(2,1)S(1)} %copy_select_fusion), kind=kOutput, calls=%fused_computation.13 | convolution fusion | flops 37748736 | bytes 884736 | tf_op jit(solution)/shard_map/qato,qati->oi/dot_general | solution.py:274
  (76 shorter events, 4.6 us)
Async XLA Ops:
  0.7 30.8 %collective-permute-start = (bf16[2,768]{1,0:T(2,128)(2,1)S(1)}, bf16[2,768]{1,0:T(2,128)(2,1)S(1)}, u32[]{:S(2)}, u32[]{:S(2)}) collective-permute-start(bf16[2,768]{1,0:T(2,128)(2,1)S(1)} %get-tuple-element.27), channel_id=1, source_target_pairs={{0,16},{1,17},{2,18},{3,19},{4,20},{5,21},{6,22},{7,23},{8,24},{9,... | collective-permute-start | bytes 9224 | tf_op jit(solution)/shard_map/ppermute | solution.py:181
  5.6 26.0 %collective-permute-start.1 = (bf16[2,768]{1,0:T(2,128)(2,1)S(1)}, bf16[2,768]{1,0:T(2,128)(2,1)S(1)}, u32[]{:S(2)}, u32[]{:S(2)}) collective-permute-start(bf16[2,768]{1,0:T(2,128)(2,1)S(1)} %get-tuple-element.28), channel_id=1, source_target_pairs={{16,0},{17,1},{18,2},{19,3},{20,4},{21,5},{22,6},{23,7},{24,8},{25... | collective-permute-start | bytes 9224 | tf_op jit(solution)/shard_map/ppermute | solution.py:182
  31.2 2.4 %copy-start = (bf16[5,192,768]{2,1,0:T(8,128)(2,1)S(1)}, bf16[5,192,768]{2,1,0:T(8,128)(2,1)}, u32[]{:S(2)}) copy-start(bf16[5,192,768]{2,1,0:T(8,128)(2,1)} %param.7) | copy-start | bytes 4423684
  38.3 23.4 %all-to-all-start = ((bf16[8,1,44555]{2,1,0:T(2,128)(2,1)}), bf16[8,1,44555]{2,1,0:T(2,128)(2,1)S(1)}, u32[]{:S(2)}, u32[]{:S(2)}) async-start(bf16[8,1,44555]{2,1,0:T(2,128)(2,1)} %copy.89), calls=%async_computation | async-start | bytes 2859008 | tf_op jit(solution)/shard_map/all_to_all | solution.py:218
  65.1 7.9 %collective-permute-start.2 = (f32[128,128]{1,0:T(8,128)S(1)}, f32[128,128]{1,0:T(8,128)S(1)}, u32[]{:S(2)}, u32[]{:S(2)}) collective-permute-start(f32[128,128]{1,0:T(8,128)S(1)} %reshape.779), channel_id=1, source_target_pairs={{0,4},{4,8},{8,12},{12,0},{1,5},{5,9},{9,13},{13,1},{2,6},{6,10},{... | collective-permute-start | bytes 196616 | tf_op jit(solution)/shard_map/ppermute | solution.py:145
  66.7 7.4 %collective-permute-start.3 = (f32[128,128]{1,0:T(8,128)S(1)}, f32[128,128]{1,0:T(8,128)S(1)}, u32[]{:S(2)}, u32[]{:S(2)}) collective-permute-start(f32[128,128]{1,0:T(8,128)S(1)} %reshape.779), channel_id=1, source_target_pairs={{0,8},{4,12},{8,0},{12,4},{1,9},{5,13},{9,1},{13,5},{2,10},{6,14},... | collective-permute-start | bytes 196616 | tf_op jit(solution)/shard_map/ppermute | solution.py:145
  69.3 4.8 %collective-permute-start.4 = (f32[128,128]{1,0:T(8,128)S(1)}, f32[128,128]{1,0:T(8,128)S(1)}, u32[]{:S(2)}, u32[]{:S(2)}) collective-permute-start(f32[128,128]{1,0:T(8,128)S(1)} %reshape.779), channel_id=1, source_target_pairs={{0,12},{4,0},{8,4},{12,8},{1,13},{5,1},{9,5},{13,9},{2,14},{6,2},{... | collective-permute-start | bytes 196616 | tf_op jit(solution)/shard_map/ppermute | solution.py:145
  78.3 0.8 copy-start.1

commit v6 on v5

--- a/solution.py
+++ b/solution.py
@@ -178,8 +178,15 @@
 
     cells = features[0]
     ends = seq_count - 1
-    head = lax.ppermute(cells[length - halo :], "seq", [(i, i + 1) for i in range(ends)])
-    tail = lax.ppermute(cells[:halo], "seq", [(i + 1, i) for i in range(ends)])
+    if seq_count == 2:
+        swapped = lax.ppermute(
+            jnp.concatenate([cells[length - halo :], cells[:halo]]), "seq", [(0, 1), (1, 0)]
+        )
+        head = jnp.where(my_index == 0, jnp.zeros_like(swapped[:halo]), swapped[:halo])
+        tail = jnp.where(my_index == ends, jnp.zeros_like(swapped[halo:]), swapped[halo:])
+    else:
+        head = lax.ppermute(cells[length - halo :], "seq", [(i, i + 1) for i in range(ends)])
+        tail = lax.ppermute(cells[:halo], "seq", [(i + 1, i) for i in range(ends)])
     starts = picks * TB
     last = per_block - 1
 
@@ -215,6 +222,7 @@
     meta = jnp.concatenate(pieces + [small]).astype(jnp.bfloat16)
     meta_rep = jnp.broadcast_to(meta[None], (peers, meta.shape[0]))
     outgoing = jnp.concatenate([mixed_rep, act_cut, meta_rep], axis=1)
+    outgoing = jnp.pad(outgoing, ((0, 0), (0, -outgoing.shape[1] % 128)))
     incoming = lax.all_to_all(outgoing, ("seq", "dp"), 0, 0, tiled=True)
     n_mixed = held * TB * narrow
     n_act = held * span * cols

time: 80.8 us -> 74.3 us (0.920)
  waiting for transfers between devices: 19.6 us -> 13.9 us
  starting transfers between devices: 16.6 us -> 11.2 us
  local copies, waits for them, and re-layouts: 13.8 us -> 16.4 us
  other arithmetic: 7.11 us -> 8.95 us
    all_to_all x1, waiting for transfers between devices: 18.4 us -> 10.7 us  [sparse_path(): incoming = lax.all_to_all(outgoing, ('seq', 'dp'), 0, 0, tiled=True)]
    unnamed x5 -> x7, local copies, waits for them, and re-layouts: 0.86 us -> 5.21 us
    ppermute x2 -> x1, starting transfers between devices: 6.13 us -> 3 us  [sparse_path(): lax.ppermute(jnp.concatenate([cells[length - halo:], cells[:halo]]), 'seq...]
    ppermute x3, waiting for transfers between devices: 1.18 us -> 3.24 us  [axis_sum(): lax.ppermute(value, axis, [(i, (i + shift) % count) for i in range(count)])]
    all_to_all x1 -> x2, local copies, waits for them, and re-layouts: 2.22 us -> 0.56 us  [sparse_path(): incoming = lax.all_to_all(outgoing, ('seq', 'dp'), 0, 0, tiled=True)]
    all_to_all x1, starting transfers between devices: 4.87 us -> 3.54 us  [sparse_path(): incoming = lax.all_to_all(outgoing, ('seq', 'dp'), 0, 0, tiled=True)]
    all_to_all x1, other arithmetic: 0.2 us -> 1.18 us  [sparse_path(): incoming = lax.all_to_all(outgoing, ('seq', 'dp'), 0, 0, tiled=True)]
    ppermute x3, starting transfers between devices: 5.55 us -> 4.67 us  [axis_sum(): lax.ppermute(value, axis, [(i, (i + shift) % count) for i in range(count)])]
  transfers between devices with their start and end apart: 6 -> 5, of which waited for: 2 -> 2; matrix products, arithmetic and copies ran while one was open for 11% -> 12% of each run, Pallas kernels for 0% -> 0%
where the time goes in v6:
time: 74.3 us; the launch traced here: 73.5 us
  between operations  18.4 us (25%)
  local copies, waits for them, and re-layouts  16.4 us (22%)
  waiting for transfers between devices  13.9 us (19%)
  starting transfers between devices  11.2 us (15%)
  other arithmetic  8.95 us (12%)
  matrix products  4.63 us (6%)
    all_to_all x1, waiting for transfers between devices, sparse_path(): incoming = lax.all_to_all(outgoing, ('seq', 'dp'), 0, 0, tiled=True)  10.7 us
    unnamed x7, local copies, waits for them, and re-layouts  5.21 us
    ppermute x3, starting transfers between devices, axis_sum(): lax.ppermute(value, axis, [(i, (i + shift) % count) for i in range(count)])  4.67 us
    all_to_all x1, starting transfers between devices, sparse_path(): incoming = lax.all_to_all(outgoing, ('seq', 'dp'), 0, 0, tiled=True)  3.54 us
    ppermute x3, waiting for transfers between devices, axis_sum(): lax.ppermute(value, axis, [(i, (i + shift) % count) for i in range(count)])  3.24 us
    ppermute x1, starting transfers between devices, sparse_path(): lax.ppermute(jnp.concatenate([cells[length - halo:], cells[:halo]]), 'seq...  3 us
    dot_general x5, matrix products, sparse_path(): jnp.einsum('qato,qati->oi', dconv, act_sides[:, :, offset:offset + TB], p...  2.25 us
  transfers between devices with their start and end apart: 5, of which 2 were waited for; matrix products, arithmetic and copies ran while one was open for 12% of the time, Pallas kernels for 0%

profile of v6, /device:TPU:0, one launch (start us, length us, event | category | flops | bytes accessed | tf_op | source)
XLA Modules:
  0.0 73.5 jit_solution(4261742004174727275)
XLA Ops:
  0.0 0.7 slice_bitcast_fusion.1
  0.7 3.0 %collective-permute-start = (bf16[4,768]{1,0:T(4,128)(2,1)S(1)}, bf16[4,768]{1,0:T(4,128)(2,1)S(1)}, u32[]{:S(2)}, u32[]{:S(2)}) collective-permute-start(bf16[4,768]{1,0:T(4,128)(2,1)S(1)} %pad_maximum_fusion.4), channel_id=1, source_target_pairs={{0,16},{16,0},{1,17},{17,1},{2,18},{18,2},{3,19},{19,3},{4,20},{20... | collective-permute-start | bytes 18440 | tf_op jit(solution)/shard_map/ppermute | solution.py:182
  3.8 0.8 %concatenate.183 = s32[8]{0:T(128)S(1)} reshape(s32[1,2,2,2]{3,2,1,0:T(2,128)} %param.9) | data formatting | bytes 64 | tf_op jit(solution)/shard_map/concatenate | solution.py:221
  4.5 1.0 %slice_reduce_fusion.1 = (s32[2,2]{1,0:T(2,128)S(1)}, s32[2,2]{1,0:T(2,128)S(1)}) fusion(s32[1,2,2,2]{3,2,1,0:T(2,128)} %param.9), kind=kLoop, calls=%fused_computation.184 | loop fusion | bytes 64 | tf_op jit(solution)/shard_map/slice | solution.py:166
  5.6 0.2 convert_reduce_fusion.1
  6.2 0.7 fusion.88
  12.3 0.7 reduce-precision_convert_fusion.1
  15.5 0.7 %fusion.83 = bf16[11]{0:T(256)(128)(2,1)S(1)} fusion(s32[1]{0:T(128)S(6)} %copy.157, s32[2]{0:T(128)} %bitcast.183, s32[8]{0:T(128)S(1)} %concatenate.183), kind=kLoop, calls=%fused_computation.200 | loop fusion | flops 44 | bytes 66 | tf_op jit(solution)/shard_map/convert.7
  16.2 1.0 %constant_dynamic-slice_fusion.10 = (bf16[1,32,768]{2,1,0:T(8,128)(2,1)S(1)}, bf16[1,32,768]{2,1,0:T(8,128)(2,1)S(1)}, bf16[1,32,768]{2,1,0:T(8,128)(2,1)S(1)}, bf16[1,32,768]{2,1,0:T(8,128)(2,1)S(1)}) fusion(bf16[1,1024,768]{2,1,0:T(8,128)(2,1)} %param.6, s32[]{:T(128)S(6)} %select_n.214, s32[]{:T(128)S(6)} %select_n.228, s32[]{:T(128)S(6)} %select_n.222, ...), kind=kLoop, calls=%fused_computation.145 | loop fusion | bytes 393232 | tf_op jit(solution)/shard_map/dynamic_slice | solution.py:195
  17.2 0.7 fusion.89
  28.3 0.9 %broadcast_select_fusion.10 = (bf16[2,768]{1,0:T(2,128)(2,1)S(1)}, bf16[2,768]{1,0:T(2,128)(2,1)S(1)}, bf16[2,768]{1,0:T(2,128)(2,1)S(1)}, bf16[2,768]{1,0:T(2,128)(2,1)S(1)}, bf16[2,768]{1,0:T(2,128)(2,1)S(1)}) fusion(pred[]{:T(512)} %bitcast.2, bf16[1,1024,768]{2,1,0:T(8,128)(2,1)} %param.6, s32[]{:T(128)S(6)} %max.12, ...), kind=kLoop, calls=%fused_computation.126 | loop fusion | flops 10752 | bytes 36891 | tf_op jit(solution)/shard_map/jit(_where)/select_n | solution.py:197
  29.7 0.8 %broadcast_select_fusion.8 = (bf16[2,768]{1,0:T(2,128)(2,1)S(1)}, bf16[2,768]{1,0:T(2,128)(2,1)S(1)}, bf16[2,768]{1,0:T(2,128)(2,1)S(1)}) fusion(pred[]{:T(512)} %bitcast.8, bf16[1,1024,768]{2,1,0:T(8,128)(2,1)} %param.6, s32[]{:T(128)S(6)} %select_n.218, bf16[4,768]{1,0:T(4,128)(2,1)S(1)} %collective-permute-done, pred[]{:T(512)S(6)} %eq.126, s32[]{:T(128)S(6)} %max.13, ...), kind=kLoop, calls=%fused_computation.124 | loop fusion | flops 7680 | bytes 24593 | tf_op jit(solution)/shard_map/jit(_where)/select_n | solution.py:198
  31.1 0.3 fusion.23
  31.5 0.4 reshape.773
  31.8 0.4 copy-done
  32.2 0.2 fusion.28
  32.5 0.2 convolution_add_fusion.3
  32.7 0.2 convolution_add_fusion.2
  33.0 0.2 convolution_add_fusion.1
  33.3 0.3 fusion.2
  33.7 0.2 maximum_maximum_fusion
  34.0 0.5 broadcast.561
  34.5 1.2 %reduce.6 = bf16[8,44672]{1,0:T(8,128)(2,1)S(1)} reduce(bf16[8,1,44672]{2,0,1:T(8,128)(2,1)S(1)} %pad_bitcast_fusion, bf16[]{:T(256)} %broadcast.561), dimensions={1}, to_apply=%copy.104.reduce_sub_computation | reduce | bytes 1429506 | tf_op jit(solution)/shard_map/all_to_all | solution.py:226
  35.6 1.4 %reshape.819 = bf16[8,2,22336]{2,1,0:T(2,128)(2,1)} reshape(bf16[8,44672]{1,0:T(8,128)(2,1)S(1)} %reduce.6) | data formatting | bytes 1429504
  37.0 3.5 %all-to-all-start = ((bf16[8,2,22336]{2,1,0:T(2,128)(2,1)}), bf16[8,2,22336]{2,1,0:T(2,128)(2,1)S(1)}, u32[]{:S(2)}, u32[]{:S(2)}) async-start(bf16[8,2,22336]{2,1,0:T(2,128)(2,1)} %reshape.819), calls=%async_computation | async-start | bytes 1433600 | tf_op jit(solution)/shard_map/all_to_all | solution.py:226
  40.8 10.7 %all-to-all-done = bf16[8,2,22336]{2,1,0:T(2,128)(2,1)S(1)} async-done(((bf16[8,2,22336]{2,1,0:T(2,128)(2,1)}), bf16[8,2,22336]{2,1,0:T(2,128)(2,1)S(1)}, u32[]{:S(2)}, u32[]{:S(2)}) %all-to-all-start) | async-done | bytes 714784 | tf_op jit(solution)/shard_map/all_to_all | solution.py:226
  51.4 2.6 %reshape.820 = bf16[8,1,44672]{2,1,0:T(2,128)(2,1)S(1)} reshape(bf16[8,2,22336]{2,1,0:T(2,128)(2,1)S(1)} %all-to-all-done) | data formatting | bytes 1429504
  54.2 0.2 fusion.87
  55.0 0.3 convert_reduce_fusion
  55.9 0.6 reshape.778
  56.6 0.6 gather_fusion
  57.3 0.2 fusion.49
  57.6 3.7 %collective-permute-start.3 = (f32[128,128]{1,0:T(8,128)S(1)}, f32[128,128]{1,0:T(8,128)S(1)}, u32[]{:S(2)}, u32[]{:S(2)}) collective-permute-start(f32[128,128]{1,0:T(8,128)S(1)} %reshape.779), channel_id=1, source_target_pairs={{0,12},{4,0},{8,4},{12,8},{1,13},{5,1},{9,5},{13,9},{2,14},{6,2},{... | collective-permute-start | bytes 196616 | tf_op jit(solution)/shard_map/ppermute | solution.py:145
  61.3 1.0 %collective-permute-start.1 = (f32[128,128]{1,0:T(8,128)S(1)}, f32[128,128]{1,0:T(8,128)S(1)}, u32[]{:S(2)}, u32[]{:S(2)}) collective-permute-start(f32[128,128]{1,0:T(8,128)S(1)} %reshape.779), channel_id=1, source_target_pairs={{0,4},{4,8},{8,12},{12,0},{1,5},{5,9},{9,13},{13,1},{2,6},{6,10},{... | collective-permute-start | bytes 196616 | tf_op jit(solution)/shard_map/ppermute | solution.py:145
  62.6 0.2 and_reduce_fusion
  63.0 0.4 reshape.781
  63.4 0.6 gather_fusion.1
  64.1 0.2 multiply_reduce_fusion
  64.3 3.2 %collective-permute-done.2 = f32[128,128]{1,0:T(8,128)S(1)} collective-permute-done((f32[128,128]{1,0:T(8,128)S(1)}, f32[128,128]{1,0:T(8,128)S(1)}, u32[]{:S(2)}, u32[]{:S(2)}) %collective-permute-start.2) | collective-permute-done | bytes 65568 | tf_op jit(solution)/shard_map/ppermute | solution.py:145
  67.7 0.5 convolution_convert_fusion
  68.2 0.4 convolution_convert_fusion.1
  68.8 1.4 %select_reduce_fusion = f32[4,8,32,192]{3,2,1,0:T(8,128)S(1)} fusion(f32[4,8,32,192]{3,2,1,0:T(8,128)S(1)} %convert.26, pred[4,8,8]{2,1,0:T(8,128)(4,1)S(1)} %get-tuple-element.31), kind=kLoop, calls=%fused_computation.2 | loop fusion | flops 2949120 | bytes 1573120 | tf_op jit(solution)/shard_map/reduce_sum | solution.py:273
  70.4 0.3 fusion.7
  70.7 0.3 fusion.6
  71.1 0.3 fusion.5
  71.4 0.3 fusion.4
  71.7 0.8 %copy-done.1 = f32[5,192,96]{2,1,0:T(8,128)} copy-done((f32[5,192,96]{2,1,0:T(8,128)}, f32[5,192,96]{2,1,0:T(8,128)S(1)}, u32[]{:S(2)}) %copy-start.1) | copy-done | bytes 368664
  72.5 1.0 %fusion.3 = f32[5,192,96]{2,1,0:T(8,128)} fusion(f32[5,192,96]{2,1,0:T(8,128)} %copy-done.1, bf16[4,8,32,192]{3,2,1,0:T(8,128)(2,1)S(1)} %fusion.14, bf16[4,8,36,96]{3,2,0,1:T(8,128)(2,1)S(1)} %copy_select_fusion), kind=kOutput, calls=%fused_computation.13 | convolution fusion | flops 37748736 | bytes 884736 | tf_op jit(solution)/shard_map/qato,qati->oi/dot_general | solution.py:282
  (79 shorter events, 5.1 us)
Async XLA Ops:
  0.7 27.6 %collective-permute-start = (bf16[4,768]{1,0:T(4,128)(2,1)S(1)}, bf16[4,768]{1,0:T(4,128)(2,1)S(1)}, u32[]{:S(2)}, u32[]{:S(2)}) collective-permute-start(bf16[4,768]{1,0:T(4,128)(2,1)S(1)} %pad_maximum_fusion.4), channel_id=1, source_target_pairs={{0,16},{16,0},{1,17},{17,1},{2,18},{18,2},{3,19},{19,3},{4,20},{20... | collective-permute-start | bytes 18440 | tf_op jit(solution)/shard_map/ppermute | solution.py:182
  30.8 1.4 %copy-start = (bf16[5,192,768]{2,1,0:T(8,128)(2,1)S(1)}, bf16[5,192,768]{2,1,0:T(8,128)(2,1)}, u32[]{:S(2)}) copy-start(bf16[5,192,768]{2,1,0:T(8,128)(2,1)} %param.7) | copy-start | bytes 4423684
  37.0 14.4 %all-to-all-start = ((bf16[8,2,22336]{2,1,0:T(2,128)(2,1)}), bf16[8,2,22336]{2,1,0:T(2,128)(2,1)S(1)}, u32[]{:S(2)}, u32[]{:S(2)}) async-start(bf16[8,2,22336]{2,1,0:T(2,128)(2,1)} %reshape.819), calls=%async_computation | async-start | bytes 1433600 | tf_op jit(solution)/shard_map/all_to_all | solution.py:226
  57.6 6.7 %collective-permute-start.3 = (f32[128,128]{1,0:T(8,128)S(1)}, f32[128,128]{1,0:T(8,128)S(1)}, u32[]{:S(2)}, u32[]{:S(2)}) collective-permute-start(f32[128,128]{1,0:T(8,128)S(1)} %reshape.779), channel_id=1, source_target_pairs={{0,12},{4,0},{8,4},{12,8},{1,13},{5,1},{9,5},{13,9},{2,14},{6,2},{... | collective-permute-start | bytes 196616 | tf_op jit(solution)/shard_map/ppermute | solution.py:145
  61.3 6.3 %collective-permute-start.2 = (f32[128,128]{1,0:T(8,128)S(1)}, f32[128,128]{1,0:T(8,128)S(1)}, u32[]{:S(2)}, u32[]{:S(2)}) collective-permute-start(f32[128,128]{1,0:T(8,128)S(1)} %reshape.779), channel_id=1, source_target_pairs={{0,8},{4,12},{8,0},{12,4},{1,9},{5,13},{9,1},{13,5},{2,10},{6,14},... | collective-permute-start | bytes 196616 | tf_op jit(solution)/shard_map/ppermute | solution.py:145
  61.3 6.3 %collective-permute-start.1 = (f32[128,128]{1,0:T(8,128)S(1)}, f32[128,128]{1,0:T(8,128)S(1)}, u32[]{:S(2)}, u32[]{:S(2)}) collective-permute-start(f32[128,128]{1,0:T(8,128)S(1)} %reshape.779), channel_id=1, source_target_pairs={{0,4},{4,8},{8,12},{12,0},{1,5},{5,9},{9,13},{13,1},{2,6},{6,10},{... | collective-permute-start | bytes 196616 | tf_op jit(solution)/shard_map/ppermute | solution.py:145
  71.7 0.8 %copy-start.1 = (f32[5,192,96]{2,1,0:T(8,128)}, f32[5,192,96]{2,1,0:T(8,128)S(1)}, u32[]{:S(2)}) copy-start(f32[5,192,96]{2,1,0:T(8,128)S(1)} %fusion.4) | copy-start | bytes 1105924

commit v7 on v6

--- a/solution.py
+++ b/solution.py
@@ -187,18 +187,13 @@
     else:
         head = lax.ppermute(cells[length - halo :], "seq", [(i, i + 1) for i in range(ends)])
         tail = lax.ppermute(cells[:halo], "seq", [(i + 1, i) for i in range(ends)])
-    starts = picks * TB
-    last = per_block - 1
-
-    def window(block, start):
-        before = lax.dynamic_slice_in_dim(cells, jnp.maximum(start - halo, 0), halo, 0)
-        middle = lax.dynamic_slice_in_dim(cells, start, TB, 0)
-        after = lax.dynamic_slice_in_dim(cells, jnp.minimum(start + TB, length - halo), halo, 0)
-        before = jnp.where(block == 0, head, before)
-        after = jnp.where(block == last, tail, after)
-        return jnp.concatenate([before, middle, after], axis=0)
-
-    windows = jnp.stack([window(picks[h], starts[h]) for h in range(held)])
+    rows = picks[:, None] * TB - halo + jnp.arange(span)[None, :]
+    inside = jnp.take(cells, jnp.clip(rows, 0, length - 1), axis=0)
+    edge_rows = jnp.concatenate([head, tail], axis=0)
+    edge_index = jnp.where(rows < 0, rows + halo, rows - length + halo)
+    outside = jnp.take(edge_rows, jnp.clip(edge_index, 0, 2 * halo - 1), axis=0)
+    in_range = jnp.logical_and(rows >= 0, rows < length)
+    windows = jnp.where(in_range[..., None], inside, outside)
     x_float = windows.astype(jnp.float32)
     act = jax.nn.gelu(x_float).astype(jnp.bfloat16)
     conv_out = jnp.einsum("hti,oi->hto", act[:, 0:TB], conv_weight[0], preferred_element_type=jnp.float32)

time: 74.3 us -> 57 us (0.77)
  between operations: 18.4 us -> 1.14 us
  local copies, waits for them, and re-layouts: 16.4 us -> 17.9 us
  other arithmetic: 8.95 us -> 7.61 us
    gather x0 -> x6, local copies, waits for them, and re-layouts: none -> 4.31 us  [the longest x3 3.02 us: sparse_path(): inside = jnp.take(cells, jnp.clip(rows, 0, length - 1), axis=0)]
    select_n x2, other arithmetic: 1.68 us -> 0.09 us  [the longest x1 0.08 us: sparse_path(): inside = jnp.take(cells, jnp.clip(rows, 0, length - 1), axis=0)]
    slice x2 -> x0, local copies, waits for them, and re-layouts: 1.33 us -> none  [sparse_path(): windows = jnp.stack([window(picks[h], starts[h]) for h in range(held)])]
    concatenate x12 -> x0, local copies, waits for them, and re-layouts: 1.17 us -> none  [window(): return jnp.concatenate([before, middle, after], axis=0)]
    dynamic_slice x1 -> x0, local copies, waits for them, and re-layouts: 0.96 us -> none  [window(): middle = lax.dynamic_slice_in_dim(cells, start, TB, 0)]
    another operation x5 -> x2, other arithmetic: 1.55 us -> 1.44 us
  transfers between devices with their start and end apart: 5 -> 5, of which waited for: 2 -> 2; matrix products, arithmetic and copies ran while one was open for 12% -> 16% of each run, Pallas kernels for 0% -> 0%
where the time goes in v7:
time: 57 us; the launch traced here: 56.5 us
  local copies, waits for them, and re-layouts  17.9 us (31%)
  waiting for transfers between devices  14 us (25%)
  starting transfers between devices  11.2 us (20%)
  other arithmetic  7.61 us (13%)
  matrix products  4.61 us (8%)
  between operations  1.14 us (2%)
    all_to_all x1, waiting for transfers between devices, sparse_path(): incoming = lax.all_to_all(outgoing, ('seq', 'dp'), 0, 0, tiled=True)  10.7 us
    unnamed x7, local copies, waits for them, and re-layouts  5.8 us
    ppermute x3, starting transfers between devices, axis_sum(): lax.ppermute(value, axis, [(i, (i + shift) % count) for i in range(count)])  4.68 us
    all_to_all x1, starting transfers between devices, sparse_path(): incoming = lax.all_to_all(outgoing, ('seq', 'dp'), 0, 0, tiled=True)  3.54 us
    ppermute x3, waiting for transfers between devices, axis_sum(): lax.ppermute(value, axis, [(i, (i + shift) % count) for i in range(count)])  3.35 us
    gather x3, local copies, waits for them, and re-layouts, sparse_path(): inside = jnp.take(cells, jnp.clip(rows, 0, length - 1), axis=0)  3.02 us
    ppermute x1, starting transfers between devices, sparse_path(): lax.ppermute(jnp.concatenate([cells[length - halo:], cells[:halo]]), 'seq...  3 us
    dot_general x5, matrix products, sparse_path(): jnp.einsum('qato,qati->oi', dconv, act_sides[:, :, offset:offset + TB], p...  2.22 us
  transfers between devices with their start and end apart: 5, of which 2 were waited for; matrix products, arithmetic and copies ran while one was open for 16% of the time, Pallas kernels for 0%

profile of v7, /device:TPU:0, one launch (start us, length us, event | category | flops | bytes accessed | tf_op | source)
XLA Modules:
  0.0 56.5 jit_solution(14279959236402407145)
XLA Ops:
  0.0 0.7 %slice_bitcast_fusion.1 = (bf16[2,768]{1,0:T(2,128)(2,1)S(1)}, bf16[2,768]{1,0:T(2,128)(2,1)S(1)}) fusion(bf16[1,1024,768]{2,1,0:T(8,128)(2,1)} %param.6), kind=kLoop, calls=%fused_computation.144 | loop fusion | bytes 12288 | tf_op jit(solution)/shard_map/slice | solution.py:183
  0.7 3.0 %collective-permute-start = (bf16[4,768]{1,0:T(4,128)(2,1)S(1)}, bf16[4,768]{1,0:T(4,128)(2,1)S(1)}, u32[]{:S(2)}, u32[]{:S(2)}) collective-permute-start(bf16[4,768]{1,0:T(4,128)(2,1)S(1)} %pad_maximum_fusion.4), channel_id=1, source_target_pairs={{0,16},{16,0},{1,17},{17,1},{2,18},{18,2},{3,19},{19,3},{4,20},{20... | collective-permute-start | bytes 18440 | tf_op jit(solution)/shard_map/ppermute | solution.py:182
  3.8 0.8 %concatenate.118 = s32[8]{0:T(128)S(1)} reshape(s32[1,2,2,2]{3,2,1,0:T(2,128)} %param.9) | data formatting | bytes 64 | tf_op jit(solution)/shard_map/concatenate | solution.py:216
  4.5 1.0 %slice_reduce_fusion.1 = (s32[2,2]{1,0:T(2,128)S(1)}, s32[2,2]{1,0:T(2,128)S(1)}) fusion(s32[1,2,2,2]{3,2,1,0:T(2,128)} %param.9), kind=kLoop, calls=%fused_computation.170 | loop fusion | bytes 64 | tf_op jit(solution)/shard_map/slice | solution.py:166
  5.6 0.2 convert_reduce_fusion.1
  7.1 0.7 %reduce-precision_convert_fusion.1 = (bf16[2048]{0:T(1024)(128)(2,1)S(1)}, bf16[2048]{0:T(1024)(128)(2,1)S(1)}, bf16[2048]{0:T(1024)(128)(2,1)S(1)}) fusion(f32[1,8,2,128]{3,2,1,0:T(2,128)} %bitcast.126), kind=kLoop, calls=%fused_computation.104 | loop fusion | flops 16384 | bytes 20480 | tf_op jit(solution)/shard_map/convert.4
  7.9 0.7 %fusion.82 = bf16[11]{0:T(256)(128)(2,1)S(1)} fusion(s32[1]{0:T(128)S(6)} %copy.163, s32[2]{0:T(128)} %bitcast.129, s32[8]{0:T(128)S(1)} %concatenate.118), kind=kLoop, calls=%fused_computation.190 | loop fusion | flops 44 | bytes 66 | tf_op jit(solution)/shard_map/convert.7
  8.6 2.6 %gather_fusion = bf16[144,768]{1,0:T(8,128)(2,1)S(1)} fusion(bf16[1024,768]{1,0:T(8,128)(2,1)} %bitcast.117, s32[1024]{0:T(1024)S(1)} %pad_clamp_fusion.3), kind=kCustom, calls=%fused_computation | custom fusion | bytes 442944 | tf_op jit(solution)/shard_map/jit(_take)/gather | solution.py:191
  11.3 0.3 gather.22
  11.7 0.9 %gather_fusion.1 = bf16[144,768]{1,0:T(8,128)(2,1)S(1)} fusion(bf16[4,768]{1,0:T(4,128)(2,1)S(1)} %pad_maximum_fusion.5, s32[1024]{0:T(1024)S(1)} %pad_clamp_fusion.2), kind=kCustom, calls=%fused_computation.1 | custom fusion | bytes 442944 | tf_op jit(solution)/shard_map/jit(_take)/gather | solution.py:194
  12.7 0.3 gather.23
  13.0 0.4 fusion.23
  13.5 0.4 reshape.879
  13.9 0.4 fusion.22
  14.3 0.9 %copy-done = bf16[5,192,768]{2,1,0:T(8,128)(2,1)S(1)} copy-done((bf16[5,192,768]{2,1,0:T(8,128)(2,1)S(1)}, bf16[5,192,768]{2,1,0:T(8,128)(2,1)}, u32[]{:S(2)}) %copy-start) | copy-done | bytes 1474584
  15.2 0.2 fusion.29
  15.5 0.2 convolution_add_fusion.3
  15.7 0.2 convolution_add_fusion.2
  16.0 0.2 convolution_add_fusion.1
  16.2 0.3 fusion.2
  16.7 0.2 maximum_maximum_fusion
  16.9 0.5 broadcast.809
  17.4 1.2 %reduce.6 = bf16[8,44672]{1,0:T(8,128)(2,1)S(1)} reduce(bf16[8,1,44672]{2,0,1:T(8,128)(2,1)S(1)} %pad_bitcast_fusion, bf16[]{:T(256)} %broadcast.809), dimensions={1}, to_apply=%copy.102.reduce_sub_computation | reduce | bytes 1429506 | tf_op jit(solution)/shard_map/all_to_all | solution.py:221
  18.6 1.4 %reshape.945 = bf16[8,2,22336]{2,1,0:T(2,128)(2,1)} reshape(bf16[8,44672]{1,0:T(8,128)(2,1)S(1)} %reduce.6) | data formatting | bytes 1429504
  20.0 3.5 %all-to-all-start = ((bf16[8,2,22336]{2,1,0:T(2,128)(2,1)}), bf16[8,2,22336]{2,1,0:T(2,128)(2,1)S(1)}, u32[]{:S(2)}, u32[]{:S(2)}) async-start(bf16[8,2,22336]{2,1,0:T(2,128)(2,1)} %reshape.945), calls=%async_computation | async-start | bytes 1433600 | tf_op jit(solution)/shard_map/all_to_all | solution.py:221
  23.7 10.7 %all-to-all-done = bf16[8,2,22336]{2,1,0:T(2,128)(2,1)S(1)} async-done(((bf16[8,2,22336]{2,1,0:T(2,128)(2,1)}), bf16[8,2,22336]{2,1,0:T(2,128)(2,1)S(1)}, u32[]{:S(2)}, u32[]{:S(2)}) %all-to-all-start) | async-done | bytes 714784 | tf_op jit(solution)/shard_map/all_to_all | solution.py:221
  34.4 2.6 %reshape.946 = bf16[8,1,44672]{2,1,0:T(2,128)(2,1)S(1)} reshape(bf16[8,2,22336]{2,1,0:T(2,128)(2,1)S(1)} %all-to-all-done) | data formatting | bytes 1429504
  37.2 0.2 fusion.86
  37.9 0.3 convert_reduce_fusion
  39.0 0.6 %reshape.884 = bf16[32,32,192]{2,1,0:T(8,128)(2,1)S(1)} reshape(bf16[8,24576]{1,0:T(8,128)(2,1)S(1)} %slice.172) | data formatting | bytes 786432 | tf_op jit(solution)/shard_map/reshape | solution.py:224
  39.6 0.6 %gather_fusion.2 = bf16[32,32,192]{2,1,0:T(8,128)(2,1)S(1)} fusion(bf16[32,32,192]{2,1,0:T(8,128)(2,1)S(1)} %reshape.884, s32[1024]{0:T(1024)S(1)} %get-tuple-element.34), kind=kCustom, calls=%fused_computation.2 | custom fusion | bytes 786560 | tf_op jit(solution)/shard_map/jit(_take)/gather | solution.py:243
  40.3 0.2 fusion.50
  40.7 3.7 %collective-permute-start.3 = (f32[128,128]{1,0:T(8,128)S(1)}, f32[128,128]{1,0:T(8,128)S(1)}, u32[]{:S(2)}, u32[]{:S(2)}) collective-permute-start(f32[128,128]{1,0:T(8,128)S(1)} %reshape.885), channel_id=1, source_target_pairs={{0,12},{4,0},{8,4},{12,8},{1,13},{5,1},{9,5},{13,9},{2,14},{6,2},{... | collective-permute-start | bytes 196616 | tf_op jit(solution)/shard_map/ppermute | solution.py:145
  44.3 1.0 %collective-permute-start.1 = (f32[128,128]{1,0:T(8,128)S(1)}, f32[128,128]{1,0:T(8,128)S(1)}, u32[]{:S(2)}, u32[]{:S(2)}) collective-permute-start(f32[128,128]{1,0:T(8,128)S(1)} %reshape.885), channel_id=1, source_target_pairs={{0,4},{4,8},{8,12},{12,0},{1,5},{5,9},{9,13},{13,1},{2,6},{6,10},{... | collective-permute-start | bytes 196616 | tf_op jit(solution)/shard_map/ppermute | solution.py:145
  45.6 0.2 and_reduce_fusion
  45.9 0.4 reshape.887
  46.3 0.6 %gather_fusion.3 = bf16[32,36,96]{2,1,0:T(8,128)(2,1)S(1)} fusion(bf16[32,36,96]{2,1,0:T(8,128)(2,1)S(1)} %reshape.887, s32[1024]{0:T(1024)S(1)} %get-tuple-element.33), kind=kCustom, calls=%fused_computation.3 | custom fusion | bytes 442496 | tf_op jit(solution)/shard_map/jit(_take)/gather | solution.py:274
  47.1 0.2 multiply_reduce_fusion
  47.3 3.3 %collective-permute-done.2 = f32[128,128]{1,0:T(8,128)S(1)} collective-permute-done((f32[128,128]{1,0:T(8,128)S(1)}, f32[128,128]{1,0:T(8,128)S(1)}, u32[]{:S(2)}, u32[]{:S(2)}) %collective-permute-start.2) | collective-permute-done | bytes 65568 | tf_op jit(solution)/shard_map/ppermute | solution.py:145
  50.8 0.5 convolution_convert_fusion
  51.3 0.4 convolution_convert_fusion.1
  51.9 1.4 %select_reduce_fusion = f32[4,8,32,192]{3,2,1,0:T(8,128)S(1)} fusion(f32[4,8,32,192]{3,2,1,0:T(8,128)S(1)} %convert.26, pred[4,8,8]{2,1,0:T(8,128)(4,1)S(1)} %get-tuple-element.23), kind=kLoop, calls=%fused_computation.4 | loop fusion | flops 2949120 | bytes 1573120 | tf_op jit(solution)/shard_map/reduce_sum | solution.py:268
  53.5 0.3 fusion.7
  53.8 0.3 fusion.6
  54.1 0.3 fusion.5
  54.5 0.3 fusion.4
  54.8 0.8 %copy-done.1 = f32[5,192,96]{2,1,0:T(8,128)} copy-done((f32[5,192,96]{2,1,0:T(8,128)}, f32[5,192,96]{2,1,0:T(8,128)S(1)}, u32[]{:S(2)}) %copy-start.1) | copy-done | bytes 368664
  55.6 1.0 %fusion.3 = f32[5,192,96]{2,1,0:T(8,128)} fusion(f32[5,192,96]{2,1,0:T(8,128)} %copy-done.1, bf16[4,8,32,192]{3,2,1,0:T(8,128)(2,1)S(1)} %fusion.14, bf16[4,8,36,96]{3,2,0,1:T(8,128)(2,1)S(1)} %copy_select_fusion), kind=kOutput, calls=%fused_computation.19 | convolution fusion | flops 37748736 | bytes 884736 | tf_op jit(solution)/shard_map/qato,qati->oi/dot_general | solution.py:277
  (70 shorter events, 4.0 us)
Async XLA Ops:
  0.7 10.9 %collective-permute-start = (bf16[4,768]{1,0:T(4,128)(2,1)S(1)}, bf16[4,768]{1,0:T(4,128)(2,1)S(1)}, u32[]{:S(2)}, u32[]{:S(2)}) collective-permute-start(bf16[4,768]{1,0:T(4,128)(2,1)S(1)} %pad_maximum_fusion.4), channel_id=1, source_target_pairs={{0,16},{16,0},{1,17},{17,1},{2,18},{18,2},{3,19},{19,3},{4,20},{20... | collective-permute-start | bytes 18440 | tf_op jit(solution)/shard_map/ppermute | solution.py:182
  13.8 1.4 %copy-start = (bf16[5,192,768]{2,1,0:T(8,128)(2,1)S(1)}, bf16[5,192,768]{2,1,0:T(8,128)(2,1)}, u32[]{:S(2)}) copy-start(bf16[5,192,768]{2,1,0:T(8,128)(2,1)} %param.7) | copy-start | bytes 4423684
  20.0 14.4 %all-to-all-start = ((bf16[8,2,22336]{2,1,0:T(2,128)(2,1)}), bf16[8,2,22336]{2,1,0:T(2,128)(2,1)S(1)}, u32[]{:S(2)}, u32[]{:S(2)}) async-start(bf16[8,2,22336]{2,1,0:T(2,128)(2,1)} %reshape.945), calls=%async_computation | async-start | bytes 1433600 | tf_op jit(solution)/shard_map/all_to_all | solution.py:221
  40.7 6.6 %collective-permute-start.3 = (f32[128,128]{1,0:T(8,128)S(1)}, f32[128,128]{1,0:T(8,128)S(1)}, u32[]{:S(2)}, u32[]{:S(2)}) collective-permute-start(f32[128,128]{1,0:T(8,128)S(1)} %reshape.885), channel_id=1, source_target_pairs={{0,12},{4,0},{8,4},{12,8},{1,13},{5,1},{9,5},{13,9},{2,14},{6,2},{... | collective-permute-start | bytes 196616 | tf_op jit(solution)/shard_map/ppermute | solution.py:145
  44.3 6.3 %collective-permute-start.2 = (f32[128,128]{1,0:T(8,128)S(1)}, f32[128,128]{1,0:T(8,128)S(1)}, u32[]{:S(2)}, u32[]{:S(2)}) collective-permute-start(f32[128,128]{1,0:T(8,128)S(1)} %reshape.885), channel_id=1, source_target_pairs={{0,8},{4,12},{8,0},{12,4},{1,9},{5,13},{9,1},{13,5},{2,10},{6,14},... | collective-permute-start | bytes 196616 | tf_op jit(solution)/shard_map/ppermute | solution.py:145
  44.3 6.3 %collective-permute-start.1 = (f32[128,128]{1,0:T(8,128)S(1)}, f32[128,128]{1,0:T(8,128)S(1)}, u32[]{:S(2)}, u32[]{:S(2)}) collective-permute-start(f32[128,128]{1,0:T(8,128)S(1)} %reshape.885), channel_id=1, source_target_pairs={{0,4},{4,8},{8,12},{12,0},{1,5},{5,9},{9,13},{13,1},{2,6},{6,10},{... | collective-permute-start | bytes 196616 | tf_op jit(solution)/shard_map/ppermute | solution.py:145
  54.8 0.8 %copy-start.1 = (f32[5,192,96]{2,1,0:T(8,128)}, f32[5,192,96]{2,1,0:T(8,128)S(1)}, u32[]{:S(2)}) copy-start(f32[5,192,96]{2,1,0:T(8,128)S(1)} %fusion.4) | copy-start | bytes 1105924

commit v8 on v7

--- a/solution.py
+++ b/solution.py
@@ -205,8 +205,13 @@
     x_part = lax.dynamic_slice_in_dim(x_float[:, halo : halo + TB], my_part * narrow, narrow, 2)
     mixed = (x_part + my_scale * conv_out).astype(jnp.bfloat16)
 
-    act_cut = act.reshape(held, span, peers, cols).transpose(2, 0, 1, 3).reshape(peers, -1)
-    mixed_rep = jnp.broadcast_to(mixed.reshape(1, -1), (peers, held * TB * narrow))
+    def lanes(part):
+        flat = part.reshape(part.shape[0], -1)
+        flat = jnp.pad(flat, ((0, 0), (0, -flat.shape[1] % 128)))
+        return flat.reshape(flat.shape[0], -1, 128)
+
+    act_cut = lanes(act.reshape(held, span, peers, cols).transpose(2, 0, 1, 3))
+    mixed_part = lanes(mixed.reshape(1, -1))
     wide = targets.reshape(-1)
     pieces = []
     for _ in range(3):
@@ -214,16 +219,25 @@
         pieces.append(piece)
         wide = wide - piece
     small = jnp.concatenate([tiles.reshape(-1), counts.reshape(-1), keep.reshape(-1)]).astype(jnp.float32)
-    meta = jnp.concatenate(pieces + [small]).astype(jnp.bfloat16)
-    meta_rep = jnp.broadcast_to(meta[None], (peers, meta.shape[0]))
-    outgoing = jnp.concatenate([mixed_rep, act_cut, meta_rep], axis=1)
-    outgoing = jnp.pad(outgoing, ((0, 0), (0, -outgoing.shape[1] % 128)))
+    meta_part = lanes(jnp.concatenate(pieces + [small]).astype(jnp.bfloat16).reshape(1, -1))
+    rows_mixed, rows_act, rows_meta = mixed_part.shape[1], act_cut.shape[1], meta_part.shape[1]
+    outgoing = jnp.concatenate(
+        [
+            jnp.broadcast_to(mixed_part, (peers, rows_mixed, 128)),
+            act_cut,
+            jnp.broadcast_to(meta_part, (peers, rows_meta, 128)),
+        ],
+        axis=1,
+    )
+    outgoing = jnp.pad(outgoing, ((0, 0), (0, -outgoing.shape[1] % 16), (0, 0)))
     incoming = lax.all_to_all(outgoing, ("seq", "dp"), 0, 0, tiled=True)
     n_mixed = held * TB * narrow
     n_act = held * span * cols
-    mixed_in = incoming[:, :n_mixed].reshape(peers * held, TB, narrow)
-    act_in = incoming[:, n_mixed : n_mixed + n_act].reshape(peers * held, span, cols)
-    meta_in = incoming[:, n_mixed + n_act :].astype(jnp.float32).reshape(seq_count, groups, -1)
+    mixed_in = incoming[:, :rows_mixed].reshape(peers, -1)[:, :n_mixed].reshape(peers * held, TB, narrow)
+    act_in = incoming[:, rows_mixed : rows_mixed + rows_act].reshape(peers, -1)[:, :n_act]
+    act_in = act_in.reshape(peers * held, span, cols)
+    meta_in = incoming[:, rows_mixed + rows_act : rows_mixed + rows_act + rows_meta].reshape(peers, -1)
+    meta_in = meta_in.astype(jnp.float32).reshape(seq_count, groups, -1)
     n_targets = capacity * TB * TB
     n_tiles = owners * capacity * 2
     targets_all = meta_in[:, :, :n_targets] + meta_in[:, :, n_targets : 2 * n_targets]

time: 57 us -> 51.5 us (0.904)
  local copies, waits for them, and re-layouts: 17.9 us -> 12.8 us
    unnamed x7 -> x4, local copies, waits for them, and re-layouts: 5.8 us -> 1.24 us
    concatenate x2, other arithmetic: 0.21 us -> 1.67 us  [the longest x1 0.94 us: sparse_path(): jnp.concatenate([jnp.broadcast_to(mixed_part, (peers, rows_mixed, 128)),...]
    all_to_all x1 -> x0, other arithmetic: 1.18 us -> none  [sparse_path(): incoming = lax.all_to_all(outgoing, ('seq', 'dp'), 0, 0, tiled=True)]
    reshape x4 -> x1, local copies, waits for them, and re-layouts: 1.44 us -> 0.48 us  [lanes(): return flat.reshape(flat.shape[0], -1, 128)]
    another operation x0 -> x2, local copies, waits for them, and re-layouts: none -> 0.8 us  [the longest x1 0.46 us: sparse_path(): act_in = act_in.reshape(peers * held, span, cols)]
    another operation x2 -> x1, other arithmetic: 1.44 us -> 0.71 us
  transfers between devices with their start and end apart: 5 -> 5, of which waited for: 2 -> 2; matrix products, arithmetic and copies ran while one was open for 16% -> 18% of each run, Pallas kernels for 0% -> 0%
where the time goes in v8:
time: 51.5 us; the launch traced here: 51 us
  waiting for transfers between devices  14 us (27%)
  local copies, waits for them, and re-layouts  12.8 us (25%)
  starting transfers between devices  11.2 us (22%)
  other arithmetic  7.26 us (14%)
  matrix products  4.6 us (9%)
  between operations  1.13 us (2%)
    all_to_all x1, waiting for transfers between devices, sparse_path(): incoming = lax.all_to_all(outgoing, ('seq', 'dp'), 0, 0, tiled=True)  10.7 us
    ppermute x3, starting transfers between devices, axis_sum(): lax.ppermute(value, axis, [(i, (i + shift) % count) for i in range(count)])  4.66 us
    all_to_all x1, starting transfers between devices, sparse_path(): incoming = lax.all_to_all(outgoing, ('seq', 'dp'), 0, 0, tiled=True)  3.54 us
    ppermute x3, waiting for transfers between devices, axis_sum(): lax.ppermute(value, axis, [(i, (i + shift) % count) for i in range(count)])  3.28 us
    gather x3, local copies, waits for them, and re-layouts, sparse_path(): inside = jnp.take(cells, jnp.clip(rows, 0, length - 1), axis=0)  3.02 us
    ppermute x1, starting transfers between devices, sparse_path(): lax.ppermute(jnp.concatenate([cells[length - halo:], cells[:halo]]), 'seq...  3 us
    dot_general x5, matrix products, sparse_path(): jnp.einsum('qato,qati->oi', dconv, act_sides[:, :, offset:offset + TB], p...  2.22 us
    reduce_sum x1, other arithmetic, sparse_path(): jnp.sum(jnp.where(same_block[..., None, None], grads[:, None], 0.0), axis=2)  1.4 us
  transfers between devices with their start and end apart: 5, of which 2 were waited for; matrix products, arithmetic and copies ran while one was open for 18% of the time, Pallas kernels for 0%

profile of v8, /device:TPU:0, one launch (start us, length us, event | category | flops | bytes accessed | tf_op | source)
XLA Modules:
  0.0 51.0 jit_solution(5744250994693468645)
XLA Ops:
  0.0 0.7 %slice_bitcast_fusion.1 = (bf16[2,768]{1,0:T(2,128)(2,1)S(1)}, bf16[2,768]{1,0:T(2,128)(2,1)S(1)}) fusion(bf16[1,1024,768]{2,1,0:T(8,128)(2,1)} %param.6), kind=kLoop, calls=%fused_computation.149 | loop fusion | bytes 12288 | tf_op jit(solution)/shard_map/slice | solution.py:183
  0.7 3.0 %collective-permute-start = (bf16[4,768]{1,0:T(4,128)(2,1)S(1)}, bf16[4,768]{1,0:T(4,128)(2,1)S(1)}, u32[]{:S(2)}, u32[]{:S(2)}) collective-permute-start(bf16[4,768]{1,0:T(4,128)(2,1)S(1)} %pad_maximum_fusion.1), channel_id=1, source_target_pairs={{0,16},{16,0},{1,17},{17,1},{2,18},{18,2},{3,19},{19,3},{4,20},{20... | collective-permute-start | bytes 18440 | tf_op jit(solution)/shard_map/ppermute | solution.py:182
  3.8 0.8 %concatenate.136 = s32[8]{0:T(128)S(1)} reshape(s32[1,2,2,2]{3,2,1,0:T(2,128)} %param.9) | data formatting | bytes 64 | tf_op jit(solution)/shard_map/concatenate | solution.py:221
  4.5 1.0 %slice_reduce_fusion.1 = (s32[2,2]{1,0:T(2,128)S(1)}, s32[2,2]{1,0:T(2,128)S(1)}) fusion(s32[1,2,2,2]{3,2,1,0:T(2,128)} %param.9), kind=kLoop, calls=%fused_computation.175 | loop fusion | bytes 64 | tf_op jit(solution)/shard_map/slice | solution.py:166
  5.6 0.2 convert_reduce_fusion.1
  5.8 0.2 fusion.85
  7.2 0.7 %reduce-precision_convert_fusion.1 = (bf16[2048]{0:T(1024)(128)(2,1)S(1)}, bf16[2048]{0:T(1024)(128)(2,1)S(1)}, bf16[2048]{0:T(1024)(128)(2,1)S(1)}) fusion(f32[1,8,2,128]{3,2,1,0:T(2,128)} %bitcast.122), kind=kLoop, calls=%fused_computation.109 | loop fusion | flops 16384 | bytes 20480 | tf_op jit(solution)/shard_map/convert.11
  7.9 0.7 %fusion.89 = bf16[1,11]{1,0:T(2,128)(2,1)S(1)} fusion(s32[1]{0:T(128)S(6)} %copy.119, s32[2]{0:T(128)} %bitcast.125, s32[8]{0:T(128)S(1)} %concatenate.136), kind=kLoop, calls=%fused_computation.196 | loop fusion | flops 44 | bytes 66 | tf_op jit(solution)/shard_map/concatenate | solution.py:222
  8.7 2.6 %gather_fusion = bf16[144,768]{1,0:T(8,128)(2,1)S(1)} fusion(bf16[1024,768]{1,0:T(8,128)(2,1)} %bitcast.112, s32[1024]{0:T(1024)S(1)} %pad_clamp_fusion.3), kind=kCustom, calls=%fused_computation | custom fusion | bytes 442944 | tf_op jit(solution)/shard_map/jit(_take)/gather | solution.py:191
  11.4 0.3 gather.22
  11.8 0.9 %gather_fusion.1 = bf16[144,768]{1,0:T(8,128)(2,1)S(1)} fusion(bf16[4,768]{1,0:T(4,128)(2,1)S(1)} %pad_maximum_fusion.2, s32[1024]{0:T(1024)S(1)} %pad_clamp_fusion.2), kind=kCustom, calls=%fused_computation.1 | custom fusion | bytes 442944 | tf_op jit(solution)/shard_map/jit(_take)/gather | solution.py:194
  12.8 0.3 gather.23
  13.1 0.4 fusion.28
  13.6 0.5 reshape.925
  14.1 0.4 fusion.27
  14.5 0.5 copy-done
  15.0 0.2 fusion.34
  15.2 0.2 convolution_add_fusion.3
  15.5 0.2 convolution_add_fusion.2
  15.7 0.2 convolution_add_fusion.1
  16.0 0.3 fusion.5
  16.2 0.1 broadcast_in_dim.128
  16.5 0.9 %fusion.12 = bf16[8,352,128]{2,1,0:T(8,128)(2,1)} fusion(bf16[8,49,128]{2,1,0:T(8,128)(2,1)S(1)} %broadcast_in_dim.135, bf16[8,108,128]{2,1,0:T(8,128)(2,1)S(1)} %reshape.925, bf16[8,192,128]{2,1,0:T(8,128)(2,1)S(1)} %broadcast_in_dim.129), kind=kLoop, calls=%fused_computation.35 | loop fusion | flops 3604480 | bytes 1435648 | tf_op jit(solution)/shard_map/concatenate | solution.py:224
  17.4 3.5 %all-to-all-start = ((bf16[8,352,128]{2,1,0:T(8,128)(2,1)}), bf16[8,352,128]{2,1,0:T(8,128)(2,1)S(1)}, u32[]{:S(2)}, u32[]{:S(2)}) async-start(bf16[8,352,128]{2,1,0:T(8,128)(2,1)} %fusion.12), calls=%async_computation | async-start | bytes 1441792 | tf_op jit(solution)/shard_map/all_to_all | solution.py:233
  21.1 10.7 %all-to-all-done = bf16[8,352,128]{2,1,0:T(8,128)(2,1)S(1)} async-done(((bf16[8,352,128]{2,1,0:T(8,128)(2,1)}), bf16[8,352,128]{2,1,0:T(8,128)(2,1)S(1)}, u32[]{:S(2)}, u32[]{:S(2)}) %all-to-all-start) | async-done | bytes 720928 | tf_op jit(solution)/shard_map/all_to_all | solution.py:233
  32.0 0.2 fusion.93
  32.7 0.3 convert_reduce_fusion
  33.8 0.3 reshape_reshape.6
  34.1 0.6 %gather_fusion.2 = bf16[32,32,192]{2,1,0:T(8,128)(2,1)S(1)} fusion(bf16[32,32,192]{2,1,0:T(8,128)(2,1)S(1)} %reshape_reshape.6, s32[1024]{0:T(1024)S(1)} %get-tuple-element.34), kind=kCustom, calls=%fused_computation.2 | custom fusion | bytes 786560 | tf_op jit(solution)/shard_map/jit(_take)/gather | solution.py:257
  34.8 0.2 fusion.55
  35.2 3.7 %collective-permute-start.3 = (f32[128,128]{1,0:T(8,128)S(1)}, f32[128,128]{1,0:T(8,128)S(1)}, u32[]{:S(2)}, u32[]{:S(2)}) collective-permute-start(f32[128,128]{1,0:T(8,128)S(1)} %reshape.928), channel_id=1, source_target_pairs={{0,12},{4,0},{8,4},{12,8},{1,13},{5,1},{9,5},{13,9},{2,14},{6,2},{... | collective-permute-start | bytes 196616 | tf_op jit(solution)/shard_map/ppermute | solution.py:145
  38.8 1.0 %collective-permute-start.1 = (f32[128,128]{1,0:T(8,128)S(1)}, f32[128,128]{1,0:T(8,128)S(1)}, u32[]{:S(2)}, u32[]{:S(2)}) collective-permute-start(f32[128,128]{1,0:T(8,128)S(1)} %reshape.928), channel_id=1, source_target_pairs={{0,4},{4,8},{8,12},{12,0},{1,5},{5,9},{9,13},{13,1},{2,6},{6,10},{... | collective-permute-start | bytes 196616 | tf_op jit(solution)/shard_map/ppermute | solution.py:145
  39.9 0.5 reshape_reshape.7
  40.5 0.2 and_reduce_fusion
  40.8 0.1 reshape.929
  40.9 0.6 %gather_fusion.3 = bf16[32,36,96]{2,1,0:T(8,128)(2,1)S(1)} fusion(bf16[32,36,96]{2,1,0:T(8,128)(2,1)S(1)} %reshape_reshape.7, s32[1024]{0:T(1024)S(1)} %get-tuple-element.33), kind=kCustom, calls=%fused_computation.3 | custom fusion | bytes 442496 | tf_op jit(solution)/shard_map/jit(_take)/gather | solution.py:288
  41.6 0.2 multiply_reduce_fusion
  41.8 3.3 %collective-permute-done.2 = f32[128,128]{1,0:T(8,128)S(1)} collective-permute-done((f32[128,128]{1,0:T(8,128)S(1)}, f32[128,128]{1,0:T(8,128)S(1)}, u32[]{:S(2)}, u32[]{:S(2)}) %collective-permute-start.2) | collective-permute-done | bytes 65568 | tf_op jit(solution)/shard_map/ppermute | solution.py:145
  45.3 0.5 convolution_convert_fusion
  45.8 0.4 convolution_convert_fusion.1
  46.4 1.4 %select_reduce_fusion = f32[4,8,32,192]{3,2,1,0:T(8,128)S(1)} fusion(f32[4,8,32,192]{3,2,1,0:T(8,128)S(1)} %convert.30, pred[4,8,8]{2,1,0:T(8,128)(4,1)S(1)} %get-tuple-element.23), kind=kLoop, calls=%fused_computation.4 | loop fusion | flops 2949120 | bytes 1573120 | tf_op jit(solution)/shard_map/reduce_sum | solution.py:282
  47.8 0.2 fusion.19
  48.0 0.3 fusion.10
  48.3 0.3 fusion.9
  48.6 0.3 fusion.8
  48.9 0.3 fusion.7
  49.3 0.8 %copy-done.1 = f32[5,192,96]{2,1,0:T(8,128)} copy-done((f32[5,192,96]{2,1,0:T(8,128)}, f32[5,192,96]{2,1,0:T(8,128)S(1)}, u32[]{:S(2)}) %copy-start.1) | copy-done | bytes 368664
  50.0 1.0 %fusion.6 = f32[5,192,96]{2,1,0:T(8,128)} fusion(f32[5,192,96]{2,1,0:T(8,128)} %copy-done.1, bf16[4,8,32,192]{3,2,1,0:T(8,128)(2,1)S(1)} %fusion.19, bf16[4,8,36,96]{3,2,0,1:T(8,128)(2,1)S(1)} %copy_select_fusion), kind=kOutput, calls=%fused_computation.23 | convolution fusion | flops 37748736 | bytes 884736 | tf_op jit(solution)/shard_map/qato,qati->oi/dot_general | solution.py:291
  (68 shorter events, 3.4 us)
Async XLA Ops:
  0.7 11.0 %collective-permute-start = (bf16[4,768]{1,0:T(4,128)(2,1)S(1)}, bf16[4,768]{1,0:T(4,128)(2,1)S(1)}, u32[]{:S(2)}, u32[]{:S(2)}) collective-permute-start(bf16[4,768]{1,0:T(4,128)(2,1)S(1)} %pad_maximum_fusion.1), channel_id=1, source_target_pairs={{0,16},{16,0},{1,17},{17,1},{2,18},{18,2},{3,19},{19,3},{4,20},{20... | collective-permute-start | bytes 18440 | tf_op jit(solution)/shard_map/ppermute | solution.py:182
  13.6 1.4 %copy-start = (bf16[5,192,768]{2,1,0:T(8,128)(2,1)S(1)}, bf16[5,192,768]{2,1,0:T(8,128)(2,1)}, u32[]{:S(2)}) copy-start(bf16[5,192,768]{2,1,0:T(8,128)(2,1)} %param.7) | copy-start | bytes 4423684
  17.4 14.4 %all-to-all-start = ((bf16[8,352,128]{2,1,0:T(8,128)(2,1)}), bf16[8,352,128]{2,1,0:T(8,128)(2,1)S(1)}, u32[]{:S(2)}, u32[]{:S(2)}) async-start(bf16[8,352,128]{2,1,0:T(8,128)(2,1)} %fusion.12), calls=%async_computation | async-start | bytes 1441792 | tf_op jit(solution)/shard_map/all_to_all | solution.py:233
  35.2 6.6 %collective-permute-start.3 = (f32[128,128]{1,0:T(8,128)S(1)}, f32[128,128]{1,0:T(8,128)S(1)}, u32[]{:S(2)}, u32[]{:S(2)}) collective-permute-start(f32[128,128]{1,0:T(8,128)S(1)} %reshape.928), channel_id=1, source_target_pairs={{0,12},{4,0},{8,4},{12,8},{1,13},{5,1},{9,5},{13,9},{2,14},{6,2},{... | collective-permute-start | bytes 196616 | tf_op jit(solution)/shard_map/ppermute | solution.py:145
  38.8 6.3 %collective-permute-start.2 = (f32[128,128]{1,0:T(8,128)S(1)}, f32[128,128]{1,0:T(8,128)S(1)}, u32[]{:S(2)}, u32[]{:S(2)}) collective-permute-start(f32[128,128]{1,0:T(8,128)S(1)} %reshape.928), channel_id=1, source_target_pairs={{0,8},{4,12},{8,0},{12,4},{1,9},{5,13},{9,1},{13,5},{2,10},{6,14},... | collective-permute-start | bytes 196616 | tf_op jit(solution)/shard_map/ppermute | solution.py:145
  38.8 6.3 %collective-permute-start.1 = (f32[128,128]{1,0:T(8,128)S(1)}, f32[128,128]{1,0:T(8,128)S(1)}, u32[]{:S(2)}, u32[]{:S(2)}) collective-permute-start(f32[128,128]{1,0:T(8,128)S(1)} %reshape.928), channel_id=1, source_target_pairs={{0,4},{4,8},{8,12},{12,0},{1,5},{5,9},{9,13},{13,1},{2,6},{6,10},{... | collective-permute-start | bytes 196616 | tf_op jit(solution)/shard_map/ppermute | solution.py:145
  49.3 0.8 %copy-start.1 = (f32[5,192,96]{2,1,0:T(8,128)}, f32[5,192,96]{2,1,0:T(8,128)S(1)}, u32[]{:S(2)}) copy-start(f32[5,192,96]{2,1,0:T(8,128)S(1)} %fusion.7) | copy-start | bytes 1105924

commit v9 on v8

--- a/solution.py
+++ b/solution.py
@@ -188,12 +188,17 @@
         head = lax.ppermute(cells[length - halo :], "seq", [(i, i + 1) for i in range(ends)])
         tail = lax.ppermute(cells[:halo], "seq", [(i + 1, i) for i in range(ends)])
     rows = picks[:, None] * TB - halo + jnp.arange(span)[None, :]
-    inside = jnp.take(cells, jnp.clip(rows, 0, length - 1), axis=0)
+    flat_rows = rows.reshape(-1)
+    pick_inside = (flat_rows[:, None] == jnp.arange(length)[None, :]).astype(cells.dtype)
+    inside = jnp.dot(pick_inside, cells, preferred_element_type=jnp.float32)
     edge_rows = jnp.concatenate([head, tail], axis=0)
-    edge_index = jnp.where(rows < 0, rows + halo, rows - length + halo)
-    outside = jnp.take(edge_rows, jnp.clip(edge_index, 0, 2 * halo - 1), axis=0)
-    in_range = jnp.logical_and(rows >= 0, rows < length)
-    windows = jnp.where(in_range[..., None], inside, outside)
+    edge_index = jnp.where(flat_rows < 0, flat_rows + halo, flat_rows - length + halo)
+    in_range = jnp.logical_and(flat_rows >= 0, flat_rows < length)
+    pick_edge = jnp.logical_and(
+        edge_index[:, None] == jnp.arange(2 * halo)[None, :], jnp.logical_not(in_range)[:, None]
+    ).astype(cells.dtype)
+    outside = jnp.dot(pick_edge, edge_rows, preferred_element_type=jnp.float32)
+    windows = (inside + outside).astype(cells.dtype).reshape(held, span, width)
     x_float = windows.astype(jnp.float32)
     act = jax.nn.gelu(x_float).astype(jnp.bfloat16)
     conv_out = jnp.einsum("hti,oi->hto", act[:, 0:TB], conv_weight[0], preferred_element_type=jnp.float32)
@@ -279,7 +284,9 @@
     grads = grads.reshape(groups, owners * n_sides, TB, narrow)
     flat_sides = sides.reshape(groups, owners * n_sides)
     same_block = flat_sides[:, :, None] == flat_sides[:, None, :]
-    total = jnp.sum(jnp.where(same_block[..., None, None], grads[:, None], 0.0), axis=2)
+    total = jnp.einsum(
+        "qab,qbtd->qatd", same_block.astype(jnp.float32), grads, precision=lax.Precision.HIGHEST
+    )
     earlier = jnp.arange(owners * n_sides)[None, :] < jnp.arange(owners * n_sides)[:, None]
     first = jnp.logical_not(jnp.any(jnp.logical_and(same_block, earlier[None]), axis=-1))
     scaling = 1.25 * keep_all.astype(jnp.float32)

time: 51.5 us -> 46.5 us (0.903)
  local copies, waits for them, and re-layouts: 12.8 us -> 8.98 us
  other arithmetic: 7.26 us -> 3.71 us
  matrix products: 4.6 us -> 7.18 us
    gather x6 -> x0, local copies, waits for them, and re-layouts: 4.31 us -> none  [the longest x3 3.02 us: sparse_path(): inside = jnp.take(cells, jnp.clip(rows, 0, length - 1), axis=0)]
    dot_general x0 -> x3, matrix products: none -> 2.56 us  [the longest x1 1.85 us: sparse_path(): inside = jnp.dot(pick_inside, cells, preferred_element_type=jnp.float32)]
    reduce_sum x1 -> x0, other arithmetic: 1.4 us -> none  [sparse_path(): jnp.sum(jnp.where(same_block[..., None, None], grads[:, None], 0.0), axis=2)]
    another operation x1, other arithmetic: 0.71 us -> 0.01 us
    concatenate x1, other arithmetic: 0.74 us -> 0.08 us  [sparse_path(): jnp.concatenate(pieces + [small]).astype(jnp.bfloat16).reshape(1, -1)]
    unnamed x4 -> x8, local copies, waits for them, and re-layouts: 1.24 us -> 1.35 us
  transfers between devices with their start and end apart: 5 -> 5, of which waited for: 2 -> 2; matrix products, arithmetic and copies ran while one was open for 18% -> 14% of each run, Pallas kernels for 0% -> 0%
where the time goes in v9:
time: 46.5 us; the launch traced here: 46.2 us
  waiting for transfers between devices  14 us (30%)
  starting transfers between devices  11.2 us (24%)
  local copies, waits for them, and re-layouts  8.98 us (19%)
  matrix products  7.18 us (15%)
  other arithmetic  3.71 us (8%)
  between operations  1.11 us (2%)
    all_to_all x1, waiting for transfers between devices, sparse_path(): incoming = lax.all_to_all(outgoing, ('seq', 'dp'), 0, 0, tiled=True)  10.7 us
    ppermute x3, starting transfers between devices, axis_sum(): lax.ppermute(value, axis, [(i, (i + shift) % count) for i in range(count)])  4.68 us
    all_to_all x1, starting transfers between devices, sparse_path(): incoming = lax.all_to_all(outgoing, ('seq', 'dp'), 0, 0, tiled=True)  3.54 us
    ppermute x3, waiting for transfers between devices, axis_sum(): lax.ppermute(value, axis, [(i, (i + shift) % count) for i in range(count)])  3.28 us
    ppermute x1, starting transfers between devices, sparse_path(): lax.ppermute(jnp.concatenate([cells[length - halo:], cells[:halo]]), 'seq...  3 us
    dot_general x5, matrix products, sparse_path(): jnp.einsum('qato,qati->oi', dconv, act_sides[:, :, offset:offset + TB], p...  2.25 us
    dot_general x1, matrix products, sparse_path(): inside = jnp.dot(pick_inside, cells, preferred_element_type=jnp.float32)  1.85 us
    unnamed x8, local copies, waits for them, and re-layouts  1.35 us
  transfers between devices with their start and end apart: 5, of which 2 were waited for; matrix products, arithmetic and copies ran while one was open for 14% of the time, Pallas kernels for 0%

profile of v9, /device:TPU:0, one launch (start us, length us, event | category | flops | bytes accessed | tf_op | source)
XLA Modules:
  0.0 46.2 jit_solution(17087928608264508839)
XLA Ops:
  0.0 0.8 %slice_bitcast_fusion.1 = (bf16[2,768]{1,0:T(2,128)(2,1)S(1)}, bf16[2,768]{1,0:T(2,128)(2,1)S(1)}) fusion(bf16[1,1024,768]{2,1,0:T(8,128)(2,1)} %param.6), kind=kLoop, calls=%fused_computation.153 | loop fusion | bytes 12288 | tf_op jit(solution)/shard_map/slice | solution.py:183
  0.8 3.0 %collective-permute-start = (bf16[4,768]{1,0:T(4,128)(2,1)S(1)}, bf16[4,768]{1,0:T(4,128)(2,1)S(1)}, u32[]{:S(2)}, u32[]{:S(2)}) collective-permute-start(bf16[4,768]{1,0:T(4,128)(2,1)S(1)} %pad_maximum_fusion.1), channel_id=1, source_target_pairs={{0,16},{16,0},{1,17},{17,1},{2,18},{18,2},{3,19},{19,3},{4,20},{20... | collective-permute-start | bytes 18440 | tf_op jit(solution)/shard_map/ppermute | solution.py:182
  3.8 0.8 %concatenate.136 = s32[8]{0:T(128)S(1)} reshape(s32[1,2,2,2]{3,2,1,0:T(2,128)} %param.9) | data formatting | bytes 64 | tf_op jit(solution)/shard_map/concatenate | solution.py:226
  4.6 1.0 %slice_reduce_fusion.1 = (s32[2,2]{1,0:T(2,128)S(1)}, s32[2,2]{1,0:T(2,128)S(1)}) fusion(s32[1,2,2,2]{3,2,1,0:T(2,128)} %param.9), kind=kLoop, calls=%fused_computation.174 | loop fusion | bytes 64 | tf_op jit(solution)/shard_map/slice | solution.py:166
  5.6 0.2 convert_reduce_fusion.1
  5.8 0.2 fusion.98
  6.4 1.8 %fusion = f32[144,768]{1,0:T(8,128)S(1)} fusion(bf16[1,1024,768]{2,1,0:T(8,128)(2,1)} %param.6, s32[144]{0:T(256)S(1)} %add.311), kind=kOutput, calls=%fused_computation.2 | convolution fusion | flops 226639872 | bytes 2015808 | tf_op jit(solution)/shard_map/dot_general | solution.py:193
  9.2 0.3 fusion.8
  9.5 0.3 reshape.818
  9.8 0.2 fusion.35
  10.0 0.2 fusion.48
  10.3 0.5 %reshape.812 = bf16[8,108,128]{2,1,0:T(8,128)(2,1)S(1)} reshape(bf16[8,4,36,96]{3,2,1,0:T(8,128)(2,1)S(1)} %copy.107) | data formatting | bytes 442368 | tf_op jit(solution)/shard_map/reshape | solution.py:216
  10.8 0.6 %copy-done.2 = bf16[5,192,768]{2,1,0:T(8,128)(2,1)S(1)} copy-done((bf16[5,192,768]{2,1,0:T(8,128)(2,1)S(1)}, bf16[5,192,768]{2,1,0:T(8,128)(2,1)}, u32[]{:S(2)}) %copy-start.2) | copy-done | bytes 1474584
  11.3 0.2 fusion.40
  11.6 0.2 convolution_add_fusion.4
  11.8 0.2 convolution_add_fusion.3
  12.1 0.2 convolution_add_fusion.2
  12.3 0.3 fusion.11
  12.6 0.1 broadcast_in_dim.35
  12.8 0.9 %fusion.18 = bf16[8,352,128]{2,1,0:T(8,128)(2,1)} fusion(bf16[8,49,128]{2,1,0:T(8,128)(2,1)S(1)} %broadcast_in_dim.38, bf16[8,108,128]{2,1,0:T(8,128)(2,1)S(1)} %reshape.812, bf16[8,192,128]{2,1,0:T(8,128)(2,1)S(1)} %broadcast_in_dim.36), kind=kLoop, calls=%fused_computation.36 | loop fusion | flops 3604480 | bytes 1435648 | tf_op jit(solution)/shard_map/concatenate | solution.py:229
  13.8 3.5 %all-to-all-start = ((bf16[8,352,128]{2,1,0:T(8,128)(2,1)}), bf16[8,352,128]{2,1,0:T(8,128)(2,1)S(1)}, u32[]{:S(2)}, u32[]{:S(2)}) async-start(bf16[8,352,128]{2,1,0:T(8,128)(2,1)} %fusion.18), calls=%async_computation | async-start | bytes 1441792 | tf_op jit(solution)/shard_map/all_to_all | solution.py:238
  17.5 10.7 %all-to-all-done = bf16[8,352,128]{2,1,0:T(8,128)(2,1)S(1)} async-done(((bf16[8,352,128]{2,1,0:T(8,128)(2,1)}), bf16[8,352,128]{2,1,0:T(8,128)(2,1)S(1)}, u32[]{:S(2)}, u32[]{:S(2)}) %all-to-all-start) | async-done | bytes 720928 | tf_op jit(solution)/shard_map/all_to_all | solution.py:238
  28.4 0.2 fusion.107
  29.1 0.3 convert_reduce_fusion
  30.1 0.4 reshape_reshape.6
  30.5 0.6 %gather_fusion = bf16[32,32,192]{2,1,0:T(8,128)(2,1)S(1)} fusion(bf16[32,32,192]{2,1,0:T(8,128)(2,1)S(1)} %reshape_reshape.6, s32[1024]{0:T(1024)S(1)} %get-tuple-element.25), kind=kCustom, calls=%fused_computation | custom fusion | bytes 786560 | tf_op jit(solution)/shard_map/jit(_take)/gather | solution.py:262
  31.1 0.1 broadcast_select_fusion
  31.2 0.2 fusion.63
  31.4 0.1 reshape.815
  31.6 3.7 %collective-permute-start.3 = (f32[128,128]{1,0:T(8,128)S(1)}, f32[128,128]{1,0:T(8,128)S(1)}, u32[]{:S(2)}, u32[]{:S(2)}) collective-permute-start(f32[128,128]{1,0:T(8,128)S(1)} %reshape.815), channel_id=1, source_target_pairs={{0,12},{4,0},{8,4},{12,8},{1,13},{5,1},{9,5},{13,9},{2,14},{6,2},{... | collective-permute-start | bytes 196616 | tf_op jit(solution)/shard_map/ppermute | solution.py:145
  35.2 1.0 %collective-permute-start.1 = (f32[128,128]{1,0:T(8,128)S(1)}, f32[128,128]{1,0:T(8,128)S(1)}, u32[]{:S(2)}, u32[]{:S(2)}) collective-permute-start(f32[128,128]{1,0:T(8,128)S(1)} %reshape.815), channel_id=1, source_target_pairs={{0,4},{4,8},{8,12},{12,0},{1,5},{5,9},{9,13},{13,1},{2,6},{6,10},{... | collective-permute-start | bytes 196616 | tf_op jit(solution)/shard_map/ppermute | solution.py:145
  36.3 0.5 reshape_reshape.7
  36.8 0.2 fusion.75
  37.2 0.1 reshape.816
  37.3 0.6 %gather_fusion.1 = bf16[32,36,96]{2,1,0:T(8,128)(2,1)S(1)} fusion(bf16[32,36,96]{2,1,0:T(8,128)(2,1)S(1)} %reshape_reshape.7, s32[1024]{0:T(1024)S(1)} %get-tuple-element.24), kind=kCustom, calls=%fused_computation.1 | custom fusion | bytes 442496 | tf_op jit(solution)/shard_map/jit(_take)/gather | solution.py:295
  37.9 0.1 copy_select_fusion
  38.0 0.2 multiply_reduce_fusion
  38.2 3.3 %collective-permute-done.2 = f32[128,128]{1,0:T(8,128)S(1)} collective-permute-done((f32[128,128]{1,0:T(8,128)S(1)}, f32[128,128]{1,0:T(8,128)S(1)}, u32[]{:S(2)}, u32[]{:S(2)}) %collective-permute-start.2) | collective-permute-done | bytes 65568 | tf_op jit(solution)/shard_map/ppermute | solution.py:145
  41.5 0.1 div.78
  41.7 0.5 %convolution_convert_fusion = bf16[4,2,2,32,192]{4,3,2,1,0:T(8,128)(2,1)S(1)} fusion(bf16[4,2,4,32,192]{4,3,2,1,0:T(8,128)(2,1)S(1)} %broadcast_select_fusion, f32[4,2,2,32,32]{4,3,2,1,0:T(8,128)S(1)} %div.78, f32[2,4,2,32,32]{4,3,2,1,0:T(8,128)S(1)} %reshape.816, f32[4]{0:T(128)S(1)} %convert_element_type.116, f32[4,2,2]{2,1,0:T(2,128)S(1)} %compare_select_fusion.6), kind=kOutput, calls=%fused_computation.12 | convolution fusion | flops 37896192 | bytes 987648 | tf_op jit(solution)/shard_map/qocij,qocid->qocjd/dot_general | solution.py:282
  42.2 0.4 convolution_convert_fusion.1
  42.7 0.4 fusion.6
  43.1 0.3 fusion.16
  43.5 0.3 fusion.15
  43.8 0.3 fusion.14
  44.1 0.3 fusion.13
  44.5 0.8 %copy-done.3 = f32[5,192,96]{2,1,0:T(8,128)} copy-done((f32[5,192,96]{2,1,0:T(8,128)}, f32[5,192,96]{2,1,0:T(8,128)S(1)}, u32[]{:S(2)}) %copy-start.3) | copy-done | bytes 368664
  45.2 1.0 %fusion.12 = f32[5,192,96]{2,1,0:T(8,128)} fusion(f32[5,192,96]{2,1,0:T(8,128)} %copy-done.3, bf16[4,8,32,192]{3,1,2,0:T(8,128)(2,1)S(1)} %fusion.6, bf16[4,8,36,96]{3,2,0,1:T(8,128)(2,1)S(1)} %copy_select_fusion), kind=kOutput, calls=%fused_computation.24 | convolution fusion | flops 37748736 | bytes 884736 | tf_op jit(solution)/shard_map/qato,qati->oi/dot_general | solution.py:298
  (66 shorter events, 2.8 us)
Async XLA Ops:
  0.0 8.9 %copy-start = (f32[1,1,2,1024]{3,2,1,0:T(2,128)S(1)}, f32[1,1,2,1024]{3,2,1,0:T(2,128)}, u32[]{:S(2)}) copy-start(f32[1,1,2,1024]{3,2,1,0:T(2,128)} %param.11) | copy-start | bytes 24580
  0.0 8.9 %copy-start.1 = (s32[1,2]{1,0:T(1,128)S(1)}, s32[1,2]{1,0:T(1,128)}, u32[]{:S(2)}) copy-start(s32[1,2]{1,0:T(1,128)} %param.10) | copy-start | bytes 28
  0.8 8.4 %collective-permute-start = (bf16[4,768]{1,0:T(4,128)(2,1)S(1)}, bf16[4,768]{1,0:T(4,128)(2,1)S(1)}, u32[]{:S(2)}, u32[]{:S(2)}) collective-permute-start(bf16[4,768]{1,0:T(4,128)(2,1)S(1)} %pad_maximum_fusion.1), channel_id=1, source_target_pairs={{0,16},{16,0},{1,17},{17,1},{2,18},{18,2},{3,19},{19,3},{4,20},{20... | collective-permute-start | bytes 18440 | tf_op jit(solution)/shard_map/ppermute | solution.py:182
  10.0 1.4 %copy-start.2 = (bf16[5,192,768]{2,1,0:T(8,128)(2,1)S(1)}, bf16[5,192,768]{2,1,0:T(8,128)(2,1)}, u32[]{:S(2)}) copy-start(bf16[5,192,768]{2,1,0:T(8,128)(2,1)} %param.7) | copy-start | bytes 4423684
  13.8 14.4 %all-to-all-start = ((bf16[8,352,128]{2,1,0:T(8,128)(2,1)}), bf16[8,352,128]{2,1,0:T(8,128)(2,1)S(1)}, u32[]{:S(2)}, u32[]{:S(2)}) async-start(bf16[8,352,128]{2,1,0:T(8,128)(2,1)} %fusion.18), calls=%async_computation | async-start | bytes 1441792 | tf_op jit(solution)/shard_map/all_to_all | solution.py:238
  31.6 6.7 %collective-permute-start.3 = (f32[128,128]{1,0:T(8,128)S(1)}, f32[128,128]{1,0:T(8,128)S(1)}, u32[]{:S(2)}, u32[]{:S(2)}) collective-permute-start(f32[128,128]{1,0:T(8,128)S(1)} %reshape.815), channel_id=1, source_target_pairs={{0,12},{4,0},{8,4},{12,8},{1,13},{5,1},{9,5},{13,9},{2,14},{6,2},{... | collective-permute-start | bytes 196616 | tf_op jit(solution)/shard_map/ppermute | solution.py:145
  35.2 6.3 %collective-permute-start.2 = (f32[128,128]{1,0:T(8,128)S(1)}, f32[128,128]{1,0:T(8,128)S(1)}, u32[]{:S(2)}, u32[]{:S(2)}) collective-permute-start(f32[128,128]{1,0:T(8,128)S(1)} %reshape.815), channel_id=1, source_target_pairs={{0,8},{4,12},{8,0},{12,4},{1,9},{5,13},{9,1},{13,5},{2,10},{6,14},... | collective-permute-start | bytes 196616 | tf_op jit(solution)/shard_map/ppermute | solution.py:145
  35.2 6.3 %collective-permute-start.1 = (f32[128,128]{1,0:T(8,128)S(1)}, f32[128,128]{1,0:T(8,128)S(1)}, u32[]{:S(2)}, u32[]{:S(2)}) collective-permute-start(f32[128,128]{1,0:T(8,128)S(1)} %reshape.815), channel_id=1, source_target_pairs={{0,4},{4,8},{8,12},{12,0},{1,5},{5,9},{9,13},{13,1},{2,6},{6,10},{... | collective-permute-start | bytes 196616 | tf_op jit(solution)/shard_map/ppermute | solution.py:145
  44.4 0.8 %copy-start.3 = (f32[5,192,96]{2,1,0:T(8,128)}, f32[5,192,96]{2,1,0:T(8,128)S(1)}, u32[]{:S(2)}) copy-start(f32[5,192,96]{2,1,0:T(8,128)S(1)} %fusion.13) | copy-start | bytes 1105924

commit v10 on v9

--- a/solution.py
+++ b/solution.py
@@ -187,27 +187,46 @@
     else:
         head = lax.ppermute(cells[length - halo :], "seq", [(i, i + 1) for i in range(ends)])
         tail = lax.ppermute(cells[:halo], "seq", [(i + 1, i) for i in range(ends)])
-    rows = picks[:, None] * TB - halo + jnp.arange(span)[None, :]
-    flat_rows = rows.reshape(-1)
-    pick_inside = (flat_rows[:, None] == jnp.arange(length)[None, :]).astype(cells.dtype)
-    inside = jnp.dot(pick_inside, cells, preferred_element_type=jnp.float32)
-    edge_rows = jnp.concatenate([head, tail], axis=0)
-    edge_index = jnp.where(flat_rows < 0, flat_rows + halo, flat_rows - length + halo)
-    in_range = jnp.logical_and(flat_rows >= 0, flat_rows < length)
-    pick_edge = jnp.logical_and(
-        edge_index[:, None] == jnp.arange(2 * halo)[None, :], jnp.logical_not(in_range)[:, None]
+    block_rows = (picks[:, None] * TB + jnp.arange(TB)[None, :]).reshape(-1)
+    pick_block = (block_rows[:, None] == jnp.arange(length)[None, :]).astype(cells.dtype)
+    block = jnp.dot(pick_block, cells, preferred_element_type=jnp.float32).reshape(held, TB, width)
+    edge_offsets = jnp.concatenate([jnp.arange(-halo, 0), jnp.arange(TB, TB + halo)])
+    edge_pos = (picks[:, None] * TB + edge_offsets[None, :]).reshape(-1)
+    in_range = jnp.logical_and(edge_pos >= 0, edge_pos < length)
+    pick_local = jnp.logical_and(edge_pos[:, None] == jnp.arange(length)[None, :], in_range[:, None])
+    local_edges = jnp.dot(pick_local.astype(cells.dtype), cells, preferred_element_type=jnp.float32)
+    halo_rows = jnp.concatenate([head, tail], axis=0)
+    halo_index = jnp.where(edge_pos < 0, edge_pos + halo, edge_pos - length + halo)
+    pick_halo = jnp.logical_and(
+        halo_index[:, None] == jnp.arange(2 * halo)[None, :], jnp.logical_not(in_range)[:, None]
     ).astype(cells.dtype)
-    outside = jnp.dot(pick_edge, edge_rows, preferred_element_type=jnp.float32)
-    windows = (inside + outside).astype(cells.dtype).reshape(held, span, width)
-    x_float = windows.astype(jnp.float32)
-    act = jax.nn.gelu(x_float).astype(jnp.bfloat16)
-    conv_out = jnp.einsum("hti,oi->hto", act[:, 0:TB], conv_weight[0], preferred_element_type=jnp.float32)
-    for offset in range(1, taps):
-        conv_out = conv_out + jnp.einsum(
-            "hti,oi->hto", act[:, offset : offset + TB], conv_weight[offset], preferred_element_type=jnp.float32
+    halo_edges = jnp.dot(pick_halo, halo_rows, preferred_element_type=jnp.float32)
+    edges = (local_edges + halo_edges).reshape(held, 2 * halo, width)
+
+    act_block = jax.nn.gelu(block).astype(jnp.bfloat16)
+    act_edges = jax.nn.gelu(edges).astype(jnp.bfloat16)
+
+    def conv_rows(source, count):
+        total = jnp.einsum(
+            "hti,oi->hto", source[:, 0:count], conv_weight[0], preferred_element_type=jnp.float32
         )
+        for offset in range(1, taps):
+            total = total + jnp.einsum(
+                "hti,oi->hto",
+                source[:, offset : offset + count],
+                conv_weight[offset],
+                preferred_element_type=jnp.float32,
+            )
+        return total
+
+    lower = jnp.concatenate([act_edges[:, :halo], act_block[:, : 2 * halo]], axis=1)
+    upper = jnp.concatenate([act_block[:, TB - 2 * halo :], act_edges[:, halo:]], axis=1)
+    conv_out = jnp.concatenate(
+        [conv_rows(lower, halo), conv_rows(act_block, TB - 2 * halo), conv_rows(upper, halo)], axis=1
+    )
+    act = jnp.concatenate([act_edges[:, :halo], act_block, act_edges[:, halo:]], axis=1)
     my_scale = 1.25 * keep[0].astype(jnp.float32)
-    x_part = lax.dynamic_slice_in_dim(x_float[:, halo : halo + TB], my_part * narrow, narrow, 2)
+    x_part = lax.dynamic_slice_in_dim(block, my_part * narrow, narrow, 2)
     mixed = (x_part + my_scale * conv_out).astype(jnp.bfloat16)
 
     def lanes(part):

time: 46.5 us -> 55.8 us (1.20)
  matrix products: 7.18 us -> 16.3 us
    dot_general x7 -> x18, matrix products: 3.36 us -> 12.4 us  [the longest x12 8.43 us: conv_rows(): jnp.einsum('hti,oi->hto', source[:, offset:offset + count], conv_weight[o...]
    unnamed x8 -> x10, local copies, waits for them, and re-layouts: 1.35 us -> 0.89 us
  transfers between devices with their start and end apart: 5 -> 5, of which waited for: 2 -> 2; matrix products, arithmetic and copies ran while one was open for 14% -> 17% of each run, Pallas kernels for 0% -> 0%
where the time goes in v10:
time: 55.8 us; the launch traced here: 55.3 us
  matrix products  16.3 us (29%)
  waiting for transfers between devices  13.9 us (25%)
  starting transfers between devices  11.2 us (20%)
  local copies, waits for them, and re-layouts  8.8 us (16%)
  other arithmetic  3.88 us (7%)
  between operations  1.27 us (2%)
    all_to_all x1, waiting for transfers between devices, sparse_path(): incoming = lax.all_to_all(outgoing, ('seq', 'dp'), 0, 0, tiled=True)  10.7 us
    dot_general x12, matrix products, conv_rows(): jnp.einsum('hti,oi->hto', source[:, offset:offset + count], conv_weight[o...  8.43 us
    ppermute x3, starting transfers between devices, axis_sum(): lax.ppermute(value, axis, [(i, (i + shift) % count) for i in range(count)])  4.67 us
    all_to_all x1, starting transfers between devices, sparse_path(): incoming = lax.all_to_all(outgoing, ('seq', 'dp'), 0, 0, tiled=True)  3.54 us
    ppermute x3, waiting for transfers between devices, axis_sum(): lax.ppermute(value, axis, [(i, (i + shift) % count) for i in range(count)])  3.18 us
    ppermute x1, starting transfers between devices, sparse_path(): lax.ppermute(jnp.concatenate([cells[length - halo:], cells[:halo]]), 'seq...  3 us
    dot_general x5, matrix products, sparse_path(): jnp.einsum('qato,qati->oi', dconv, act_sides[:, :, offset:offset + TB], p...  2.25 us
    dot_general x1, matrix products, sparse_path(): jnp.dot(pick_block, cells, preferred_element_type=jnp.float32)  1.88 us
  transfers between devices with their start and end apart: 5, of which 2 were waited for; matrix products, arithmetic and copies ran while one was open for 17% of the time, Pallas kernels for 0%

profile of v10, /device:TPU:0, one launch (start us, length us, event | category | flops | bytes accessed | tf_op | source)
XLA Modules:
  0.0 55.3 jit_solution(9219092057741963807)
XLA Ops:
  0.0 0.9 %slice_bitcast_fusion.1 = (bf16[2,768]{1,0:T(2,128)(2,1)S(1)}, bf16[2,768]{1,0:T(2,128)(2,1)S(1)}) fusion(bf16[1,1024,768]{2,1,0:T(8,128)(2,1)} %param.6), kind=kLoop, calls=%fused_computation.200 | loop fusion | bytes 12288 | tf_op jit(solution)/shard_map/slice | solution.py:183
  0.9 3.0 %collective-permute-start = (bf16[4,768]{1,0:T(4,128)(2,1)S(1)}, bf16[4,768]{1,0:T(4,128)(2,1)S(1)}, u32[]{:S(2)}, u32[]{:S(2)}) collective-permute-start(bf16[4,768]{1,0:T(4,128)(2,1)S(1)} %pad_maximum_fusion.4), channel_id=1, source_target_pairs={{0,16},{16,0},{1,17},{17,1},{2,18},{18,2},{3,19},{19,3},{4,20},{20... | collective-permute-start | bytes 18440 | tf_op jit(solution)/shard_map/ppermute | solution.py:182
  3.9 0.8 %concatenate.156 = s32[8]{0:T(128)S(1)} reshape(s32[1,2,2,2]{3,2,1,0:T(2,128)} %param.9) | data formatting | bytes 64 | tf_op jit(solution)/shard_map/concatenate | solution.py:245
  4.7 1.0 %slice_reduce_fusion.1 = (s32[2,2]{1,0:T(2,128)S(1)}, s32[2,2]{1,0:T(2,128)S(1)}) fusion(s32[1,2,2,2]{3,2,1,0:T(2,128)} %param.9), kind=kLoop, calls=%fused_computation.221 | loop fusion | bytes 64 | tf_op jit(solution)/shard_map/slice | solution.py:166
  5.7 0.2 convert_reduce_fusion.1
  6.6 1.9 %fusion.26 = (bf16[4,32,768]{2,1,0:T(8,128)(2,1)S(1)}, f32[4,32,768]{2,1,0:T(8,128)S(1)}) fusion(bf16[1,1024,768]{2,1,0:T(8,128)(2,1)} %param.6, s32[4,32]{1,0:T(4,128)S(1)} %iota_add_fusion), kind=kOutput, calls=%fused_computation.53 | convolution fusion | flops 202342400 | bytes 2163200 | tf_op jit(solution)/shard_map/dot_general | solution.py:192
  9.4 0.4 fusion.2
  9.9 0.2 fusion.41
  10.3 0.3 convolution_add_fusion.3
  10.6 0.2 convolution_add_fusion.2
  10.9 0.2 convolution_add_fusion.1
  11.1 0.2 convolution_add_fusion
  11.4 0.2 convolution_add_fusion.8
  11.6 0.2 convolution_add_fusion.7
  12.0 0.2 convolution_add_fusion.4
  12.3 1.1 %fusion.43 = f32[4,2,192]{2,0,1:T(4,128)S(1)} fusion(bf16[5,192,768]{2,1,0:T(8,128)(2,1)} %param.7, bf16[4,2,768]{2,1,0:T(2,128)(2,1)S(1)} %get-tuple-element.21), kind=kOutput, calls=%fused_computation.71 | convolution fusion | flops 2359296 | bytes 313344 | tf_op jit(solution)/shard_map/hti,oi->hto/dot_general | solution.py:210
  13.7 1.1 %convolution_add_fusion.12 = f32[4,2,192]{2,0,1:T(4,128)S(1)} fusion(f32[4,2,192]{2,0,1:T(4,128)S(1)} %fusion.43, bf16[5,192,768]{2,1,0:T(8,128)(2,1)} %param.7, bf16[4,2,768]{2,1,0:T(2,128)(2,1)S(1)} %pad_maximum_fusion.3), kind=kOutput, calls=%fused_computation.37 | convolution fusion | flops 2360832 | bytes 319488 | tf_op jit(solution)/shard_map/hti,oi->hto/dot_general | solution.py:214
  14.8 1.2 %convolution_add_fusion.11 = f32[4,2,192]{2,0,1:T(4,128)S(1)} fusion(f32[4,2,192]{2,0,1:T(4,128)S(1)} %convolution_add_fusion.12, bf16[5,192,768]{2,1,0:T(8,128)(2,1)} %param.7, bf16[4,2,768]{2,1,0:T(2,128)(2,1)S(1)} %get-tuple-element.18), kind=kOutput, calls=%fused_computation.36 | convolution fusion | flops 2360832 | bytes 319488 | tf_op jit(solution)/shard_map/hti,oi->hto/dot_general | solution.py:214
  16.0 1.2 %convolution_add_fusion.10 = f32[4,2,192]{2,0,1:T(4,128)S(1)} fusion(f32[4,2,192]{2,0,1:T(4,128)S(1)} %convolution_add_fusion.11, bf16[5,192,768]{2,1,0:T(8,128)(2,1)} %param.7, bf16[4,2,768]{2,1,0:T(2,128)(2,1)S(1)} %get-tuple-element.17), kind=kOutput, calls=%fused_computation.35 | convolution fusion | flops 2360832 | bytes 319488 | tf_op jit(solution)/shard_map/hti,oi->hto/dot_general | solution.py:214
  17.2 1.2 %convolution_add_fusion.9 = f32[4,2,192]{2,0,1:T(4,128)S(1)} fusion(f32[4,2,192]{2,0,1:T(4,128)S(1)} %convolution_add_fusion.10, bf16[5,192,768]{2,1,0:T(8,128)(2,1)} %param.7, bf16[4,2,768]{2,1,0:T(2,128)(2,1)S(1)} %get-tuple-element.13), kind=kOutput, calls=%fused_computation.34 | convolution fusion | flops 2360832 | bytes 319488 | tf_op jit(solution)/shard_map/hti,oi->hto/dot_general | solution.py:214
  18.4 1.1 %convolution_add_fusion.6 = f32[4,2,192]{2,0,1:T(4,128)S(1)} fusion(f32[4,2,192]{2,0,1:T(4,128)S(1)} %convolution_add_fusion.7, bf16[5,192,768]{2,1,0:T(8,128)(2,1)} %param.7, bf16[4,2,768]{2,1,0:T(2,128)(2,1)S(1)} %pad_maximum_fusion.2), kind=kOutput, calls=%fused_computation.31 | convolution fusion | flops 2360832 | bytes 319488 | tf_op jit(solution)/shard_map/hti,oi->hto/dot_general | solution.py:214
  19.6 1.2 %convolution_add_fusion.5 = f32[4,2,192]{2,0,1:T(4,128)S(1)} fusion(f32[4,2,192]{2,0,1:T(4,128)S(1)} %convolution_add_fusion.6, bf16[5,192,768]{2,1,0:T(8,128)(2,1)} %param.7, bf16[4,2,768]{2,1,0:T(2,128)(2,1)S(1)} %get-tuple-element.22), kind=kOutput, calls=%fused_computation.30 | convolution fusion | flops 2360832 | bytes 319488 | tf_op jit(solution)/shard_map/hti,oi->hto/dot_general | solution.py:214
  21.2 0.2 reshape.850
  21.5 0.5 reshape.851
  22.1 0.9 %fusion.15 = bf16[8,352,128]{2,1,0:T(8,128)(2,1)} fusion(bf16[8,49,128]{2,1,0:T(8,128)(2,1)S(1)} %broadcast_in_dim.38, bf16[8,108,128]{2,1,0:T(8,128)(2,1)S(1)} %reshape.851, bf16[8,192,128]{2,1,0:T(8,128)(2,1)S(1)} %broadcast_in_dim.36), kind=kLoop, calls=%fused_computation.39 | loop fusion | flops 3604480 | bytes 1435648 | tf_op jit(solution)/shard_map/concatenate | solution.py:248
  23.0 3.5 %all-to-all-start = ((bf16[8,352,128]{2,1,0:T(8,128)(2,1)}), bf16[8,352,128]{2,1,0:T(8,128)(2,1)S(1)}, u32[]{:S(2)}, u32[]{:S(2)}) async-start(bf16[8,352,128]{2,1,0:T(8,128)(2,1)} %fusion.15), calls=%async_computation | async-start | bytes 1441792 | tf_op jit(solution)/shard_map/all_to_all | solution.py:257
  26.7 10.7 %all-to-all-done = bf16[8,352,128]{2,1,0:T(8,128)(2,1)S(1)} async-done(((bf16[8,352,128]{2,1,0:T(8,128)(2,1)}), bf16[8,352,128]{2,1,0:T(8,128)(2,1)S(1)}, u32[]{:S(2)}, u32[]{:S(2)}) %all-to-all-start) | async-done | bytes 720928 | tf_op jit(solution)/shard_map/all_to_all | solution.py:257
  37.6 0.2 fusion.146
  38.3 0.3 convert_reduce_fusion
  39.3 0.3 reshape_reshape.6
  39.6 0.6 %gather_fusion = bf16[32,32,192]{2,1,0:T(8,128)(2,1)S(1)} fusion(bf16[32,32,192]{2,1,0:T(8,128)(2,1)S(1)} %reshape_reshape.6, s32[1024]{0:T(1024)S(1)} %pad_clamp_fusion.1), kind=kCustom, calls=%fused_computation | custom fusion | bytes 786560 | tf_op jit(solution)/shard_map/jit(_take)/gather | solution.py:281
  40.4 0.2 fusion.60
  40.7 3.7 %collective-permute-start.3 = (f32[128,128]{1,0:T(8,128)S(1)}, f32[128,128]{1,0:T(8,128)S(1)}, u32[]{:S(2)}, u32[]{:S(2)}) collective-permute-start(f32[128,128]{1,0:T(8,128)S(1)} %reshape.854), channel_id=1, source_target_pairs={{0,12},{4,0},{8,4},{12,8},{1,13},{5,1},{9,5},{13,9},{2,14},{6,2},{... | collective-permute-start | bytes 196616 | tf_op jit(solution)/shard_map/ppermute | solution.py:145
  44.3 1.0 %collective-permute-start.1 = (f32[128,128]{1,0:T(8,128)S(1)}, f32[128,128]{1,0:T(8,128)S(1)}, u32[]{:S(2)}, u32[]{:S(2)}) collective-permute-start(f32[128,128]{1,0:T(8,128)S(1)} %reshape.854), channel_id=1, source_target_pairs={{0,4},{4,8},{8,12},{12,0},{1,5},{5,9},{9,13},{13,1},{2,6},{6,10},{... | collective-permute-start | bytes 196616 | tf_op jit(solution)/shard_map/ppermute | solution.py:145
  45.4 0.5 reshape_reshape.7
  45.9 0.2 fusion.97
  46.5 0.6 %gather_fusion.1 = bf16[32,36,96]{2,1,0:T(8,128)(2,1)S(1)} fusion(bf16[32,36,96]{2,1,0:T(8,128)(2,1)S(1)} %reshape_reshape.7, s32[1024]{0:T(1024)S(1)} %pad_clamp_fusion), kind=kCustom, calls=%fused_computation.1 | custom fusion | bytes 442496 | tf_op jit(solution)/shard_map/jit(_take)/gather | solution.py:314
  47.3 0.2 multiply_reduce_fusion
  47.4 3.2 %collective-permute-done.2 = f32[128,128]{1,0:T(8,128)S(1)} collective-permute-done((f32[128,128]{1,0:T(8,128)S(1)}, f32[128,128]{1,0:T(8,128)S(1)}, u32[]{:S(2)}, u32[]{:S(2)}) %collective-permute-start.2) | collective-permute-done | bytes 65568 | tf_op jit(solution)/shard_map/ppermute | solution.py:145
  50.8 0.5 convolution_convert_fusion
  51.3 0.4 convolution_convert_fusion.1
  51.8 0.4 fusion.8
  52.2 0.3 fusion.13
  52.6 0.3 fusion.12
  52.9 0.3 fusion.11
  53.2 0.3 fusion.10
  53.6 0.8 %copy-done.4 = f32[5,192,96]{2,1,0:T(8,128)} copy-done((f32[5,192,96]{2,1,0:T(8,128)}, f32[5,192,96]{2,1,0:T(8,128)S(1)}, u32[]{:S(2)}) %copy-start.4) | copy-done | bytes 368664
  54.3 1.0 %fusion.9 = f32[5,192,96]{2,1,0:T(8,128)} fusion(f32[5,192,96]{2,1,0:T(8,128)} %copy-done.4, bf16[4,8,32,192]{3,1,2,0:T(8,128)(2,1)S(1)} %fusion.8, bf16[4,8,36,96]{3,2,0,1:T(8,128)(2,1)S(1)} %copy_select_fusion), kind=kOutput, calls=%fused_computation.20 | convolution fusion | flops 37748736 | bytes 884736 | tf_op jit(solution)/shard_map/qato,qati->oi/dot_general | solution.py:317
  (91 shorter events, 4.8 us)
Async XLA Ops:
  0.0 9.4 %copy-start = (bf16[1,1024,768]{2,1,0:T(8,128)(2,1)S(1)}, bf16[1,1024,768]{2,1,0:T(8,128)(2,1)}, u32[]{:S(2)}) copy-start(bf16[1,1024,768]{2,1,0:T(8,128)(2,1)} %param.6) | copy-start | bytes 4718596
  0.0 9.4 %copy-start.1 = (f32[1,1,2,1024]{3,2,1,0:T(2,128)S(1)}, f32[1,1,2,1024]{3,2,1,0:T(2,128)}, u32[]{:S(2)}) copy-start(f32[1,1,2,1024]{3,2,1,0:T(2,128)} %param.11) | copy-start | bytes 24580
  0.9 11.1 %collective-permute-start = (bf16[4,768]{1,0:T(4,128)(2,1)S(1)}, bf16[4,768]{1,0:T(4,128)(2,1)S(1)}, u32[]{:S(2)}, u32[]{:S(2)}) collective-permute-start(bf16[4,768]{1,0:T(4,128)(2,1)S(1)} %pad_maximum_fusion.4), channel_id=1, source_target_pairs={{0,16},{16,0},{1,17},{17,1},{2,18},{18,2},{3,19},{19,3},{4,20},{20... | collective-permute-start | bytes 18440 | tf_op jit(solution)/shard_map/ppermute | solution.py:182
  8.5 1.4 %copy-start.3 = (bf16[5,192,768]{2,1,0:T(8,128)(2,1)S(1)}, bf16[5,192,768]{2,1,0:T(8,128)(2,1)}, u32[]{:S(2)}) copy-start(bf16[5,192,768]{2,1,0:T(8,128)(2,1)} %param.7) | copy-start | bytes 4423684
  10.9 0.9 %copy-start.2 = (s32[1,2]{1,0:T(1,128)S(1)}, s32[1,2]{1,0:T(1,128)}, u32[]{:S(2)}) copy-start(s32[1,2]{1,0:T(1,128)} %param.10) | copy-start | bytes 28
  23.0 14.4 %all-to-all-start = ((bf16[8,352,128]{2,1,0:T(8,128)(2,1)}), bf16[8,352,128]{2,1,0:T(8,128)(2,1)S(1)}, u32[]{:S(2)}, u32[]{:S(2)}) async-start(bf16[8,352,128]{2,1,0:T(8,128)(2,1)} %fusion.15), calls=%async_computation | async-start | bytes 1441792 | tf_op jit(solution)/shard_map/all_to_all | solution.py:257
  40.7 6.8 %collective-permute-start.3 = (f32[128,128]{1,0:T(8,128)S(1)}, f32[128,128]{1,0:T(8,128)S(1)}, u32[]{:S(2)}, u32[]{:S(2)}) collective-permute-start(f32[128,128]{1,0:T(8,128)S(1)} %reshape.854), channel_id=1, source_target_pairs={{0,12},{4,0},{8,4},{12,8},{1,13},{5,1},{9,5},{13,9},{2,14},{6,2},{... | collective-permute-start | bytes 196616 | tf_op jit(solution)/shard_map/ppermute | solution.py:145
  44.3 6.3 %collective-permute-start.2 = (f32[128,128]{1,0:T(8,128)S(1)}, f32[128,128]{1,0:T(8,128)S(1)}, u32[]{:S(2)}, u32[]{:S(2)}) collective-permute-start(f32[128,128]{1,0:T(8,128)S(1)} %reshape.854), channel_id=1, source_target_pairs={{0,8},{4,12},{8,0},{12,4},{1,9},{5,13},{9,1},{13,5},{2,10},{6,14},... | collective-permute-start | bytes 196616 | tf_op jit(solution)/shard_map/ppermute | solution.py:145
  44.3 6.3 %collective-permute-start.1 = (f32[128,128]{1,0:T(8,128)S(1)}, f32[128,128]{1,0:T(8,128)S(1)}, u32[]{:S(2)}, u32[]{:S(2)}) collective-permute-start(f32[128,128]{1,0:T(8,128)S(1)} %reshape.854), channel_id=1, source_target_pairs={{0,4},{4,8},{8,12},{12,0},{1,5},{5,9},{9,13},{13,1},{2,6},{6,10},{... | collective-permute-start | bytes 196616 | tf_op jit(solution)/shard_map/ppermute | solution.py:145
  53.6 0.8 %copy-start.4 = (f32[5,192,96]{2,1,0:T(8,128)}, f32[5,192,96]{2,1,0:T(8,128)S(1)}, u32[]{:S(2)}) copy-start(f32[5,192,96]{2,1,0:T(8,128)S(1)} %fusion.10) | copy-start | bytes 1105924

commit v11 on v9

--- a/solution.py
+++ b/solution.py
@@ -178,27 +178,15 @@
 
     cells = features[0]
     ends = seq_count - 1
-    if seq_count == 2:
-        swapped = lax.ppermute(
-            jnp.concatenate([cells[length - halo :], cells[:halo]]), "seq", [(0, 1), (1, 0)]
-        )
-        head = jnp.where(my_index == 0, jnp.zeros_like(swapped[:halo]), swapped[:halo])
-        tail = jnp.where(my_index == ends, jnp.zeros_like(swapped[halo:]), swapped[halo:])
-    else:
-        head = lax.ppermute(cells[length - halo :], "seq", [(i, i + 1) for i in range(ends)])
-        tail = lax.ppermute(cells[:halo], "seq", [(i + 1, i) for i in range(ends)])
+    last = per_block - 1
     rows = picks[:, None] * TB - halo + jnp.arange(span)[None, :]
     flat_rows = rows.reshape(-1)
     pick_inside = (flat_rows[:, None] == jnp.arange(length)[None, :]).astype(cells.dtype)
     inside = jnp.dot(pick_inside, cells, preferred_element_type=jnp.float32)
-    edge_rows = jnp.concatenate([head, tail], axis=0)
-    edge_index = jnp.where(flat_rows < 0, flat_rows + halo, flat_rows - length + halo)
-    in_range = jnp.logical_and(flat_rows >= 0, flat_rows < length)
-    pick_edge = jnp.logical_and(
-        edge_index[:, None] == jnp.arange(2 * halo)[None, :], jnp.logical_not(in_range)[:, None]
-    ).astype(cells.dtype)
-    outside = jnp.dot(pick_edge, edge_rows, preferred_element_type=jnp.float32)
-    windows = (inside + outside).astype(cells.dtype).reshape(held, span, width)
+    windows = inside.astype(cells.dtype).reshape(held, span, width)
+    filler = jnp.zeros((TB, width), cells.dtype)
+    boundary = jnp.concatenate([cells[length - halo :], filler, cells[:halo]], axis=0)
+    windows = jnp.concatenate([windows, boundary[None]], axis=0)
     x_float = windows.astype(jnp.float32)
     act = jax.nn.gelu(x_float).astype(jnp.bfloat16)
     conv_out = jnp.einsum("hti,oi->hto", act[:, 0:TB], conv_weight[0], preferred_element_type=jnp.float32)
@@ -207,8 +195,27 @@
             "hti,oi->hto", act[:, offset : offset + TB], conv_weight[offset], preferred_element_type=jnp.float32
         )
     my_scale = 1.25 * keep[0].astype(jnp.float32)
-    x_part = lax.dynamic_slice_in_dim(x_float[:, halo : halo + TB], my_part * narrow, narrow, 2)
-    mixed = (x_part + my_scale * conv_out).astype(jnp.bfloat16)
+    x_part = lax.dynamic_slice_in_dim(x_float[:held, halo : halo + TB], my_part * narrow, narrow, 2)
+    raw = x_part + my_scale * conv_out[:held]
+    mixed = raw.astype(jnp.bfloat16)
+    edge_t = jnp.concatenate([jnp.arange(halo), jnp.arange(TB - halo, TB)])
+    edge_values = raw[:, edge_t]
+    corrections = conv_out[held, edge_t]
+    edge_act = act[held, jnp.concatenate([jnp.arange(halo), jnp.arange(span - halo, span)])]
+    act = act[:held]
+
+    def split3(values):
+        wide = values.reshape(-1)
+        pieces = []
+        for _ in range(3):
+            piece = lax.reduce_precision(wide, exponent_bits=8, mantissa_bits=7)
+            pieces.append(piece)
+            wide = wide - piece
+        return jnp.concatenate(pieces).astype(jnp.bfloat16)
+
+    def join3(flat, count):
+        flat = flat.astype(jnp.float32)
+        return flat[..., :count] + flat[..., count : 2 * count] + flat[..., 2 * count : 3 * count]
 
     def lanes(part):
         flat = part.reshape(part.shape[0], -1)
@@ -216,20 +223,23 @@
         return flat.reshape(flat.shape[0], -1, 128)
 
     act_cut = lanes(act.reshape(held, span, peers, cols).transpose(2, 0, 1, 3))
+    edge_cut = lanes(edge_act.reshape(2 * halo, peers, cols).transpose(1, 0, 2))
     mixed_part = lanes(mixed.reshape(1, -1))
-    wide = targets.reshape(-1)
-    pieces = []
-    for _ in range(3):
-        piece = lax.reduce_precision(wide, exponent_bits=8, mantissa_bits=7)
-        pieces.append(piece)
-        wide = wide - piece
-    small = jnp.concatenate([tiles.reshape(-1), counts.reshape(-1), keep.reshape(-1)]).astype(jnp.float32)
-    meta_part = lanes(jnp.concatenate(pieces + [small]).astype(jnp.bfloat16).reshape(1, -1))
-    rows_mixed, rows_act, rows_meta = mixed_part.shape[1], act_cut.shape[1], meta_part.shape[1]
+    small = jnp.concatenate(
+        [tiles.reshape(-1), counts.reshape(-1), keep.reshape(-1), picks.reshape(-1)]
+    ).astype(jnp.float32)
+    n_edge = held * 2 * halo * narrow
+    n_corr = 2 * halo * narrow
+    exact = jnp.concatenate([split3(targets), split3(edge_values), split3(corrections), small.astype(jnp.bfloat16)])
+    meta_part = lanes(exact.reshape(1, -1))
+    rows_mixed, rows_act, rows_edge, rows_meta = (
+        mixed_part.shape[1], act_cut.shape[1], edge_cut.shape[1], meta_part.shape[1]
+    )
     outgoing = jnp.concatenate(
         [
             jnp.broadcast_to(mixed_part, (peers, rows_mixed, 128)),
             act_cut,
+            edge_cut,
             jnp.broadcast_to(meta_part, (peers, rows_meta, 128)),
         ],
         axis=1,
@@ -238,19 +248,50 @@
     incoming = lax.all_to_all(outgoing, ("seq", "dp"), 0, 0, tiled=True)
     n_mixed = held * TB * narrow
     n_act = held * span * cols
-    mixed_in = incoming[:, :rows_mixed].reshape(peers, -1)[:, :n_mixed].reshape(peers * held, TB, narrow)
+    mixed_in = incoming[:, :rows_mixed].reshape(peers, -1)[:, :n_mixed].reshape(peers, held, TB, narrow)
     act_in = incoming[:, rows_mixed : rows_mixed + rows_act].reshape(peers, -1)[:, :n_act]
-    act_in = act_in.reshape(peers * held, span, cols)
-    meta_in = incoming[:, rows_mixed + rows_act : rows_mixed + rows_act + rows_meta].reshape(peers, -1)
-    meta_in = meta_in.astype(jnp.float32).reshape(seq_count, groups, -1)
+    act_in = act_in.reshape(seq_count, groups, held, span, cols)
+    cut = rows_mixed + rows_act
+    edge_in = incoming[:, cut : cut + rows_edge].reshape(peers, -1)[:, : 2 * halo * cols]
+    edge_in = edge_in.reshape(seq_count, groups, 2 * halo, cols)
+    cut = cut + rows_edge
+    meta_flat = incoming[:, cut : cut + rows_meta].reshape(peers, -1)
     n_targets = capacity * TB * TB
+    targets_all = join3(meta_flat[:, : 3 * n_targets], n_targets).reshape(seq_count, groups, -1)
+    cut = 3 * n_targets
+    edge_in_values = join3(meta_flat[:, cut : cut + 3 * n_edge], n_edge)
+    edge_in_values = edge_in_values.reshape(seq_count, groups, held, 2 * halo, narrow)
+    cut = cut + 3 * n_edge
+    corr_in = join3(meta_flat[:, cut : cut + 3 * n_corr], n_corr).reshape(seq_count, groups, 2 * halo, narrow)
+    cut = cut + 3 * n_corr
+    meta_in = meta_flat[:, cut:].astype(jnp.float32).reshape(seq_count, groups, -1)
     n_tiles = owners * capacity * 2
-    targets_all = meta_in[:, :, :n_targets] + meta_in[:, :, n_targets : 2 * n_targets]
-    targets_all = targets_all + meta_in[:, :, 2 * n_targets : 3 * n_targets]
-    ints = meta_in[0, :, 3 * n_targets :].astype(jnp.int32)
+    ints = meta_in[0].astype(jnp.int32)
     tiles_all = ints[:, :n_tiles].reshape(groups, owners, capacity, 2)
     counts_all = ints[:, n_tiles : n_tiles + owners]
     keep_all = ints[:, n_tiles + owners]
+    picks_all = meta_in[..., n_tiles + owners + 1 : n_tiles + owners + 1 + held].astype(jnp.int32)
+    seq_ids = jnp.arange(seq_count)[:, None, None]
+    first = jnp.logical_and(picks_all == 0, seq_ids > 0)
+    final = jnp.logical_and(picks_all == last, seq_ids < ends)
+    zeros_corr = jnp.zeros_like(corr_in[:1])
+    from_prev = jnp.concatenate([zeros_corr, corr_in[:-1]], axis=0)[:, :, None, :halo]
+    from_next = jnp.concatenate([corr_in[1:], zeros_corr], axis=0)[:, :, None, halo:]
+    scale_in = (1.25 * keep_all.astype(jnp.float32))[None, :, None, None, None]
+    fixed_lo = (edge_in_values[..., :halo, :] + scale_in * from_prev).astype(jnp.bfloat16)
+    fixed_hi = (edge_in_values[..., halo:, :] + scale_in * from_next).astype(jnp.bfloat16)
+    mixed_in = mixed_in.reshape(seq_count, groups, held, TB, narrow)
+    lo = jnp.where(first[..., None, None], fixed_lo, mixed_in[..., :halo, :])
+    hi = jnp.where(final[..., None, None], fixed_hi, mixed_in[..., TB - halo :, :])
+    mixed_in = jnp.concatenate([lo, mixed_in[..., halo : TB - halo, :], hi], axis=3)
+    mixed_in = mixed_in.reshape(peers * held, TB, narrow)
+    zeros_edge = jnp.zeros_like(edge_in[:1])
+    act_prev = jnp.concatenate([zeros_edge, edge_in[:-1]], axis=0)[:, :, None, :halo]
+    act_next = jnp.concatenate([edge_in[1:], zeros_edge], axis=0)[:, :, None, halo:]
+    act_lo = jnp.where(first[..., None, None], act_prev, act_in[..., :halo, :])
+    act_hi = jnp.where(final[..., None, None], act_next, act_in[..., span - halo :, :])
+    act_in = jnp.concatenate([act_lo, act_in[..., halo : span - halo, :], act_hi], axis=3)
+    act_in = act_in.reshape(peers * held, span, cols)
 
     sides = jnp.concatenate([tiles_all[..., 0], tiles_all[..., 1]], axis=-1)
     source = sides // per_block

time: 46.5 us -> 104 us (2.24); the launches traced: 46.2 us -> 102 us
  other arithmetic: 3.71 us -> 34.7 us
  local copies, waits for them, and re-layouts: 8.98 us -> 37.8 us
  waiting for transfers between devices: 14 us -> 11.2 us
  starting transfers between devices: 11.2 us -> 9.85 us
    slice x1 -> x16, local copies, waits for them, and re-layouts: 0.03 us -> 11.7 us  [the longest x2 3.39 us: sparse_path(): meta_flat = incoming[:, cut:cut + rows_meta].reshape(peers, -1)]
    convert_element_type x2 -> x8, other arithmetic: 0.03 us -> 7.24 us  [the longest x3 6.23 us: join3(): flat = flat.astype(jnp.float32)]
    add x1 -> x3, other arithmetic: 0.03 us -> 6.2 us  [join3(): flat[..., :count] + flat[..., count:2 * count]]
    ppermute x3, waiting for transfers between devices: 3.28 us -> 0.01 us  [axis_sum(): lax.ppermute(value, axis, [(i, (i + shift) % count) for i in range(count)])]
    ppermute x1 -> x0, starting transfers between devices: 3 us -> none  [sparse_path(): lax.ppermute(jnp.concatenate([cells[length - halo:], cells[:halo]]), 'seq...]
    concatenate x2 -> x4, other arithmetic: 0.09 us -> 2.41 us  [the longest x1 2.17 us: sparse_path(): jnp.concatenate([lo, mixed_in[..., halo:TB - halo, :], hi], axis=3)]
    select_n x2, other arithmetic: 0.02 us -> 2.24 us  [the longest x1 1.14 us: sparse_path(): lo = jnp.where(first[..., None, None], fixed_lo, mixed_in[..., :halo, :])]
    add x0 -> x3, local copies, waits for them, and re-layouts: none -> 2.22 us  [the longest x2 2.13 us: join3(): flat[..., :count] + flat[..., count:2 * count]]
  transfers between devices with their start and end apart: 5 -> 4, of which waited for: 2 -> 1; matrix products, arithmetic and copies ran while one was open for 14% -> 19% of each run, Pallas kernels for 0% -> 0%
where the time goes in v11:
time: 104 us; the launch traced here: 102 us
  local copies, waits for them, and re-layouts  37.8 us (36%)
  other arithmetic  34.7 us (33%)
  waiting for transfers between devices  11.2 us (11%)
  starting transfers between devices  9.85 us (9%)
  matrix products  7.64 us (7%)
  between operations  1.27 us (1%)
    all_to_all x1, waiting for transfers between devices, sparse_path(): incoming = lax.all_to_all(outgoing, ('seq', 'dp'), 0, 0, tiled=True)  11.2 us
    convert_element_type x3, other arithmetic, join3(): flat = flat.astype(jnp.float32)  6.23 us
    add x3, other arithmetic, join3(): flat[..., :count] + flat[..., count:2 * count]  6.2 us
    all_to_all x1, starting transfers between devices, sparse_path(): incoming = lax.all_to_all(outgoing, ('seq', 'dp'), 0, 0, tiled=True)  5.18 us
    ppermute x3, starting transfers between devices, axis_sum(): lax.ppermute(value, axis, [(i, (i + shift) % count) for i in range(count)])  4.67 us
    slice x2, local copies, waits for them, and re-layouts, sparse_path(): meta_flat = incoming[:, cut:cut + rows_meta].reshape(peers, -1)  3.39 us
    unnamed x45, local copies, waits for them, and re-layouts  3.22 us
    gather x1, local copies, waits for them, and re-layouts, sparse_path(): side_rows = jnp.take(mixed_in, slot, axis=0)  2.41 us
  transfers between devices with their start and end apart: 4, of which 1 were waited for; matrix products, arithmetic and copies ran while one was open for 19% of the time, Pallas kernels for 0%

profile of v11, /device:TPU:0, one launch (start us, length us, event | category | flops | bytes accessed | tf_op | source)
XLA Modules:
  0.0 102.4 jit_solution(18031658406441311343)
XLA Ops:
  0.0 0.8 reshape.866
  0.8 1.0 slice_reduce_fusion.1
  3.3 1.9 %fusion.8 = bf16[144,768]{1,0:T(8,128)(2,1)S(1)} fusion(bf16[1,1024,768]{2,1,0:T(8,128)(2,1)} %param.6, s32[144]{0:T(256)S(1)} %add.363), kind=kOutput, calls=%fused_computation.21 | convolution fusion | flops 226750464 | bytes 1794624 | tf_op jit(solution)/shard_map/dot_general | solution.py:185
  12.6 1.1 %fusion.18 = bf16[8,448,128]{2,1,0:T(8,128)(2,1)} fusion(bf16[8,139,128]{2,1,0:T(8,128)(2,1)S(1)} %broadcast_in_dim.134, bf16[8,3,128]{2,1,0:T(4,128)(2,1)S(1)} %reshape.862, bf16[8,108,128]{2,1,0:T(8,128)(2,1)S(1)} %reshape.860, bf16[8,192,128]{2,1,0:T(8,128)(2,1)S(1)} %broadcast_in_dim.132), kind=kLoop, calls=%fused_computation.41 | loop fusion | flops 5963776 | bytes 1822720 | tf_op jit(solution)/shard_map/concatenate | solution.py:238
  13.6 5.2 %all-to-all-start = ((bf16[8,448,128]{2,1,0:T(8,128)(2,1)}), bf16[8,448,128]{2,1,0:T(8,128)(2,1)S(1)}, u32[]{:S(2)}, u32[]{:S(2)}) async-start(bf16[8,448,128]{2,1,0:T(8,128)(2,1)} %fusion.18), calls=%async_computation | async-start | bytes 1835008 | tf_op jit(solution)/shard_map/all_to_all | solution.py:248
  20.7 11.2 %all-to-all-done = bf16[8,448,128]{2,1,0:T(8,128)(2,1)S(1)} async-done(((bf16[8,448,128]{2,1,0:T(8,128)(2,1)}), bf16[8,448,128]{2,1,0:T(8,128)(2,1)S(1)}, u32[]{:S(2)}, u32[]{:S(2)}) %all-to-all-start) | async-done | bytes 917536 | tf_op jit(solution)/shard_map/all_to_all | solution.py:248
  31.9 3.3 %copy.167 = bf16[8,139,128]{0,2,1:T(8,128)(2,1)} copy(bf16[8,139,128]{2,1,0:T(8,128)(2,1)S(1)} %slice.298) | data formatting | bytes 569344 | tf_op jit(solution)/shard_map/slice | solution.py:258
  35.3 0.8 slice_convert_fusion.4
  37.2 1.1 %fusion.109 = (s32[4,2]{0,1:T(2,128)}, s32[4]{0:T(128)}) fusion(s32[4,128]{0,1:T(8,128)S(1)} %slice_convert_fusion.3), kind=kLoop, calls=%fused_computation.238 | loop fusion | flops 4 | bytes 80 | tf_op jit(solution)/shard_map/slice | solution.py:271
  42.2 2.2 %slice_convert_fusion.2 = f32[8,2304]{0,1:T(8,128)} fusion(bf16[8,17792]{0,1:T(8,128)(2,1)} %bitcast.142), kind=kLoop, calls=%fused_computation.50 | loop fusion | flops 18432 | bytes 110592 | tf_op jit(solution)/shard_map/convert_element_type | solution.py:217
  44.4 1.8 %slice_convert_fusion.1 = f32[8,6144]{0,1:T(8,128)S(1)} fusion(bf16[8,17792]{0,1:T(8,128)(2,1)} %bitcast.143), kind=kLoop, calls=%fused_computation.11 | loop fusion | flops 49152 | bytes 294912 | tf_op jit(solution)/shard_map/convert_element_type | solution.py:217
  46.1 1.0 copy-done
  47.1 2.3 %slice_convert_fusion = f32[8,9216]{0,1:T(8,128)} fusion(bf16[8,17792]{0,1:T(8,128)(2,1)S(1)} %bitcast.144), kind=kLoop, calls=%fused_computation.5 | loop fusion | flops 73728 | bytes 442368 | tf_op jit(solution)/shard_map/convert_element_type | solution.py:217
  49.4 1.2 %reshape_reshape_reshape.3 = bf16[2,4,4,32,192]{4,3,2,1,0:T(8,128)(2,1)} reshape(bf16[8,192,128]{2,1,0:T(8,128)(2,1)S(1)} %slice-done) | data formatting | bytes 786432 | tf_op jit(solution)/shard_map/reshape;reshape;reshape | solution.py:283
  50.6 2.1 %slice.319 = bf16[2,4,4,28,192]{4,3,2,1,0:T(8,128)(2,1)} slice(bf16[2,4,4,32,192]{4,3,2,1,0:T(8,128)(2,1)} %reshape_reshape_reshape.3), slice={[0:2], [0:4], [0:4], [2:30], [0:192]} | slice | bytes 688128 | tf_op jit(solution)/shard_map/slice | solution.py:286
  53.7 1.3 %slice_add_fusion.4 = f32[8,768]{0,1:T(8,128)S(1)} fusion(f32[8,2304]{0,1:T(8,128)} %slice_convert_fusion.2), kind=kLoop, calls=%fused_computation.56 | loop fusion | flops 12288 | bytes 98304 | tf_op jit(solution)/shard_map/add | solution.py:218
  55.0 0.9 fusion.108
  55.8 1.2 %copy.174 = f32[1,4,4,192]{3,1,2,0:T(4,128)S(1)} copy(f32[1,4,4,192]{1,3,2,0:T(8,128)} %bitcast.148) | data formatting | bytes 24576 | tf_op jit(solution)/shard_map/slice | solution.py:278
  57.0 0.8 copy.177
  57.8 0.8 fusion.64
  58.6 3.8 %slice_add_fusion = f32[8,3072]{0,1:T(8,128)} fusion(f32[8,9216]{0,1:T(8,128)} %slice_convert_fusion), kind=kLoop, calls=%fused_computation.12 | loop fusion | flops 49152 | bytes 393216 | tf_op jit(solution)/shard_map/add | solution.py:218
  62.4 1.8 %copy.172 = f32[8,3072]{1,0:T(8,128)S(1)} copy(f32[8,3072]{0,1:T(8,128)} %slice_add_fusion) | data formatting | bytes 196608 | tf_op jit(solution)/shard_map/add | solution.py:218
  64.5 1.1 %broadcast_select_fusion.2 = (bf16[2,4,4,2,192]{4,3,2,1,0:T(2,128)(2,1)S(1)}, bf16[2,4,4,2,192]{4,3,2,1,0:T(2,128)(2,1)S(1)}) fusion(pred[2,4,4]{2,1,0:T(4,128)(4,1)S(1)} %get-tuple-element.29, f32[2,4,4,4,192]{4,3,2,1,0:T(4,128)S(1)} %reshape.872, bf16[2,4,4,32,192]{4,3,2,1,0:T(8,128)(2,1)} %reshape_reshape_reshape.3, f32[2,4,2,192]{3,2,1,0:T(2,128)S(1)} %copy.175, ...), kind=kLoop, calls=%fused_computation.105 | loop fusion | flops 73728 | bytes 221248 | tf_op jit(solution)/shard_map/jit(_where)/select_n | solution.py:284
  65.6 2.2 %pad_maximum_fusion = bf16[2,4,4,32,192]{4,3,2,1,0:T(8,128)(2,1)} fusion(bf16[2,4,4,2,192]{4,3,2,1,0:T(2,128)(2,1)S(1)} %get-tuple-element.20, bf16[2,4,4,28,192]{4,3,2,1,0:T(8,128)(2,1)} %slice.319, bf16[2,4,4,2,192]{4,3,2,1,0:T(2,128)(2,1)S(1)} %get-tuple-element.19), kind=kLoop, calls=%fused_computation.52 | loop fusion | flops 1179648 | bytes 786432 | tf_op jit(solution)/shard_map/concatenate | solution.py:286
  67.8 2.4 %gather_fusion.3 = bf16[32,32,192]{2,1,0:T(8,128)(2,1)} fusion(bf16[32,32,192]{2,1,0:T(8,128)(2,1)} %bitcast.145, s32[1024]{0:T(1024)S(1)} %copy-done.7), kind=kCustom, calls=%fused_computation.3 | custom fusion | bytes 786560 | tf_op jit(solution)/shard_map/jit(_take)/gather | solution.py:303
  70.2 1.2 %broadcast_select_fusion = bf16[4,2,4,32,192]{4,3,2,1,0:T(8,128)(2,1)S(1)} fusion(bf16[4,2,4,32,192]{4,3,2,1,0:T(8,128)(2,1)} %bitcast.146, pred[4,2,4]{2,1,0:T(4,128)(4,1)S(1)} %copy-done.11), kind=kLoop, calls=%fused_computation.55 | loop fusion | flops 196608 | bytes 786464 | tf_op jit(solution)/shard_map/jit(_take)/select_n | solution.py:303
  71.4 0.8 copy-done.3
  72.2 0.9 fusion.59
  73.2 1.1 %reshape.874 = f32[128,128]{1,0:T(8,128)S(1)} reshape(f32[4,2,2,32,32]{4,3,2,1,0:T(8,128)} %fusion.59) | data formatting | bytes 131072 | tf_op jit(solution)/shard_map/reshape | solution.py:308
  74.2 3.7 %collective-permute-start.2 = (f32[128,128]{1,0:T(8,128)S(1)}, f32[128,128]{1,0:T(8,128)S(1)}, u32[]{:S(2)}, u32[]{:S(2)}) collective-permute-start(f32[128,128]{1,0:T(8,128)S(1)} %reshape.874), channel_id=1, source_target_pairs={{0,12},{4,0},{8,4},{12,8},{1,13},{5,1},{9,5},{13,9},{2,14},{6,2},{... | collective-permute-start | bytes 196616 | tf_op jit(solution)/shard_map/ppermute | solution.py:145
  77.9 1.0 collective-permute-start
  79.8 1.2 %reshape_reshape.8 = bf16[2,4,4,36,96]{4,3,2,1,0:T(8,128)(2,1)} reshape(bf16[8,108,128]{2,1,0:T(8,128)(2,1)S(1)} %slice-done.1) | data formatting | bytes 442368 | tf_op jit(solution)/shard_map/reshape;reshape | solution.py:253
  81.0 1.1 %slice.332 = bf16[2,4,4,32,96]{4,3,2,1,0:T(8,128)(2,1)S(1)} slice(bf16[2,4,4,36,96]{4,3,2,1,0:T(8,128)(2,1)} %reshape_reshape.8), slice={[0:2], [0:4], [0:4], [2:34], [0:96]} | slice | bytes 393216 | tf_op jit(solution)/shard_map/slice | solution.py:293
  82.1 1.1 %convert_element_type.112 = f32[4]{0:T(128)} convert(s32[4]{0:T(128)} %get-tuple-element.26) | non-fusion elementwise | flops 4 | bytes 32 | tf_op jit(solution)/shard_map/convert_element_type | solution.py:312
  83.2 1.3 %copy.170 = s32[4,2]{1,0:T(4,128)} copy(s32[4,2]{0,1:T(2,128)} %get-tuple-element.25) | data formatting | bytes 64 | tf_op jit(solution)/shard_map/slice | solution.py:271
  84.5 1.3 %compare_select_fusion.5 = f32[4,2,2]{2,1,0:T(2,128)} fusion(s32[4,2]{1,0:T(4,128)} %copy.170), kind=kLoop, calls=%fused_computation.144 | loop fusion | flops 32 | bytes 96 | tf_op jit(solution)/shard_map/mul | solution.py:314
  85.8 1.3 %compare_select_fusion.6 = s32[4,8,1]{1,0,2:T(4,128)} fusion(s32[4,8,1]{1,0,2:T(4,128)} %reduce_sum.58, s32[4,8,1]{1,0,2:T(4,128)} %concatenate.204, s32[8]{0:T(128)} %add.405), kind=kLoop, calls=%fused_computation.151 | loop fusion | flops 736 | bytes 416 | tf_op jit(solution)/shard_map/jit(_take)/jit(_where)/select_n | solution.py:336
  87.1 1.3 %reshape.906 = s32[32]{0:T(128)} reshape(s32[4,8,1]{1,0,2:T(4,128)} %compare_select_fusion.6) | data formatting | bytes 256 | tf_op jit(solution)/shard_map/jit(_take)/jit(_where)/select_n | solution.py:336
  88.4 1.2 %compare_and_fusion.4 = pred[4,8]{1,0:T(4,128)(4,1)} fusion(s32[4,8]{1,0:T(4,128)} %reduce_sum.57, s32[4,8]{1,0:T(4,128)S(1)} %copy-done.6, s32[8]{0:T(128)} %add.405), kind=kLoop, calls=%fused_computation.203 | loop fusion | flops 832 | bytes 320 | tf_op jit(solution)/shard_map/jit(_take)/and | solution.py:336
  89.6 1.3 %copy.185 = pred[4,8]{0,1:T(8,128)(4,1)} copy(pred[4,8]{1,0:T(4,128)(4,1)} %compare_and_fusion.4) | data formatting | bytes 64 | tf_op jit(solution)/shard_map/jit(_take)/and | solution.py:336
  90.9 1.2 %pad_clamp_fusion = s32[1024]{0:T(1024)} fusion(s32[32]{0:T(128)} %reshape.906), kind=kLoop, calls=%fused_computation.162 | loop fusion | flops 1024 | bytes 4224 | tf_op jit(solution)/shard_map/jit(_take)/gather | solution.py:336
  92.1 1.1 %slice_add_fusion.2 = f32[8,2048]{0,1:T(8,128)} fusion(f32[8,6144]{0,1:T(8,128)S(1)} %slice_convert_fusion.1), kind=kLoop, calls=%fused_computation.36 | loop fusion | flops 32768 | bytes 262144 | tf_op jit(solution)/shard_map/add | solution.py:218
  93.2 1.1 %broadcast_select_fusion.4 = (bf16[2,4,4,2,96]{4,3,2,1,0:T(2,128)(2,1)S(1)}, bf16[2,4,4,2,96]{4,3,2,1,0:T(2,128)(2,1)S(1)}) fusion(pred[2,4,4]{2,1,0:T(4,128)(4,1)S(1)} %get-tuple-element.29, bf16[2,4,4,36,96]{4,3,2,1,0:T(8,128)(2,1)} %reshape_reshape.8, bf16[2,4,2,96]{3,2,1,0:T(2,128)(2,1)S(1)} %pad_slice_fusion.3, ...), kind=kLoop, calls=%fused_computation.111 | loop fusion | flops 12288 | bytes 55360 | tf_op jit(solution)/shard_map/jit(_where)/select_n | solution.py:291
  94.5 0.9 gather_fusion.4
  95.4 0.8 copy_select_fusion
  96.8 0.9 add_multiply_fusion
  100.7 0.8 copy-done.20
  101.5 1.0 fusion.11
  (155 shorter events, 20.9 us)
Async XLA Ops:
  3.3 3.1 %copy-start.5 = (f32[1,1,2,1024]{3,2,1,0:T(2,128)S(1)}, f32[1,1,2,1024]{3,2,1,0:T(2,128)}, u32[]{:S(2)}) copy-start(f32[1,1,2,1024]{3,2,1,0:T(2,128)} %param.11) | copy-start | bytes 24580
  5.2 2.1 %copy-start.18 = (bf16[5,192,768]{2,1,0:T(8,128)(2,1)S(1)}, bf16[5,192,768]{2,1,0:T(8,128)(2,1)}, u32[]{:S(2)}) copy-start(bf16[5,192,768]{2,1,0:T(8,128)(2,1)} %param.7) | copy-start | bytes 4423684
  9.6 1.7 %copy-start.17 = (s32[1,2]{1,0:T(1,128)S(1)}, s32[1,2]{1,0:T(1,128)}, u32[]{:S(2)}) copy-start(s32[1,2]{1,0:T(1,128)} %param.10) | copy-start | bytes 28
  13.6 18.2 %all-to-all-start = ((bf16[8,448,128]{2,1,0:T(8,128)(2,1)}), bf16[8,448,128]{2,1,0:T(8,128)(2,1)S(1)}, u32[]{:S(2)}, u32[]{:S(2)}) async-start(bf16[8,448,128]{2,1,0:T(8,128)(2,1)} %fusion.18), calls=%async_computation | async-start | bytes 1835008 | tf_op jit(solution)/shard_map/all_to_all | solution.py:248
  31.9 3.4 %copy-start.2 = (bf16[8,448,128]{2,1,0:T(8,128)(2,1)}, bf16[8,448,128]{2,1,0:T(8,128)(2,1)S(1)}, u32[]{:S(2)}) copy-start(bf16[8,448,128]{2,1,0:T(8,128)(2,1)S(1)} %all-to-all-done) | copy-start | bytes 2752516
  44.4 2.8 %copy-start = (bf16[8,139,128]{0,2,1:T(8,128)(2,1)S(1)}, bf16[8,139,128]{0,2,1:T(8,128)(2,1)}, u32[]{:S(2)}) copy-start(bf16[8,139,128]{0,2,1:T(8,128)(2,1)} %copy.167) | copy-start | bytes 854020
  47.1 2.3 %slice-start = ((bf16[8,448,128]{2,1,0:T(8,128)(2,1)}), bf16[8,192,128]{2,1,0:T(8,128)(2,1)S(1)}, s32[]{:S(2)}) async-start(bf16[8,448,128]{2,1,0:T(8,128)(2,1)} %copy-done.2), calls=%async_computation.1 | async-start | bytes 786432 | tf_op jit(solution)/shard_map/slice | solution.py:251
  62.4 2.0 %copy-start.8 = (f32[8,128]{1,0:T(8,128)S(1)}, f32[8,128]{1,0:T(8,128)}, u32[]{:S(2)}) copy-start(f32[8,128]{1,0:T(8,128)} %copy.171) | copy-start | bytes 12292
  62.4 2.0 %copy-start.15 = (pred[2]{0:T(512)(128)(4,1)S(1)}, pred[2]{0:T(512)(128)(4,1)}, u32[]{:S(2)}) copy-start(pred[2]{0:T(512)(128)(4,1)} %get-tuple-element.41) | copy-start | bytes 10
  62.4 2.0 %copy-start.16 = (pred[2]{0:T(512)(128)(4,1)S(1)}, pred[2]{0:T(512)(128)(4,1)}, u32[]{:S(2)}) copy-start(pred[2]{0:T(512)(128)(4,1)} %get-tuple-element.42) | copy-start | bytes 10
  62.4 5.4 %copy-start.7 = (s32[1024]{0:T(1024)S(1)}, s32[1024]{0:T(1024)}, u32[]{:S(2)}) copy-start(s32[1024]{0:T(1024)} %pad_clamp_fusion.1) | copy-start | bytes 12292
  64.2 6.0 %copy-start.11 = (pred[4,2,4]{2,1,0:T(4,128)(4,1)S(1)}, pred[4,2,4]{2,1,0:T(4,128)(4,1)}, u32[]{:S(2)}) copy-start(pred[4,2,4]{2,1,0:T(4,128)(4,1)} %compare_and_fusion.1) | copy-start | bytes 100
  64.5 3.3 %copy-start.9 = (pred[2,4,4]{2,1,0:T(4,128)(4,1)}, pred[2,4,4]{2,1,0:T(4,128)(4,1)S(1)}, u32[]{:S(2)}) copy-start(pred[2,4,4]{2,1,0:T(4,128)(4,1)S(1)} %get-tuple-element.30) | copy-start | bytes 100
  70.2 9.6 %slice-start.1 = ((bf16[8,448,128]{2,1,0:T(8,128)(2,1)}), bf16[8,108,128]{2,1,0:T(8,128)(2,1)S(1)}, s32[]{:S(2)}) async-start(bf16[8,448,128]{2,1,0:T(8,128)(2,1)} %copy-done.2), calls=%async_computation.2 | async-start | bytes 458752 | tf_op jit(solution)/shard_map/slice | solution.py:252
  71.4 0.8 copy-start.3
  72.2 16.1 %copy-start.6 = (s32[4,8]{1,0:T(4,128)S(1)}, s32[4,8]{1,0:T(4,128)}, u32[]{:S(2)}) copy-start(s32[4,8]{1,0:T(4,128)} %eq.91) | copy-start | bytes 388
  74.2 22.6 %collective-permute-start.2 = (f32[128,128]{1,0:T(8,128)S(1)}, f32[128,128]{1,0:T(8,128)S(1)}, u32[]{:S(2)}, u32[]{:S(2)}) collective-permute-start(f32[128,128]{1,0:T(8,128)S(1)} %reshape.874), channel_id=1, source_target_pairs={{0,12},{4,0},{8,4},{12,8},{1,13},{5,1},{9,5},{13,9},{2,14},{6,2},{... | collective-permute-start | bytes 196616 | tf_op jit(solution)/shard_map/ppermute | solution.py:145
  77.9 18.9 %collective-permute-start.1 = (f32[128,128]{1,0:T(8,128)S(1)}, f32[128,128]{1,0:T(8,128)}, u32[]{:S(2)}, u32[]{:S(2)}) collective-permute-start(f32[128,128]{1,0:T(8,128)S(1)} %reshape.874), channel_id=1, source_target_pairs={{0,8},{4,12},{8,0},{12,4},{1,9},{5,13},{9,1},{13,5},{2,10},{6,14},... | collective-permute-start | bytes 196616 | tf_op jit(solution)/shard_map/ppermute | solution.py:145
  77.9 19.0 %collective-permute-start = (f32[128,128]{1,0:T(8,128)S(1)}, f32[128,128]{1,0:T(8,128)}, u32[]{:S(2)}, u32[]{:S(2)}) collective-permute-start(f32[128,128]{1,0:T(8,128)S(1)} %reshape.874), channel_id=1, source_target_pairs={{0,4},{4,8},{8,12},{12,0},{1,5},{5,9},{9,13},{13,1},{2,6},{6,10},{... | collective-permute-start | bytes 196616 | tf_op jit(solution)/shard_map/ppermute | solution.py:145
  92.1 1.1 %copy-start.10 = (pred[2,4,4]{2,1,0:T(4,128)(4,1)S(1)}, pred[2,4,4]{2,1,0:T(4,128)(4,1)}, u32[]{:S(2)}) copy-start(pred[2,4,4]{2,1,0:T(4,128)(4,1)} %copy-done.9) | copy-start | bytes 100
  93.2 2.9 %copy-start.13 = (pred[8,8]{1,0:T(8,128)(4,1)S(1)}, pred[8,8]{1,0:T(8,128)(4,1)}, u32[]{:S(2)}) copy-start(pred[8,8]{1,0:T(8,128)(4,1)} %iota_compare_fusion.3) | copy-start | bytes 196
  93.2 3.2 %copy-start.1 = (f32[8,2048]{0,1:T(8,128)S(1)}, f32[8,2048]{0,1:T(8,128)}, u32[]{:S(2)}) copy-start(f32[8,2048]{0,1:T(8,128)} %slice_add_fusion.2) | copy-start | bytes 196612
  94.5 3.4 %copy-start.4 = (bf16[4,2,4,32,192]{4,3,2,1,0:T(8,128)(2,1)S(1)}, bf16[4,2,4,32,192]{4,3,2,1,0:T(8,128)(2,1)}, u32[]{:S(2)}) copy-start(bf16[4,2,4,32,192]{4,3,2,1,0:T(8,128)(2,1)} %copy-done.3) | copy-start | bytes 1179652
  94.5 3.4 %copy-start.12 = (f32[4,2,2]{2,1,0:T(2,128)S(1)}, f32[4,2,2]{2,1,0:T(2,128)}, u32[]{:S(2)}) copy-start(f32[4,2,2]{2,1,0:T(2,128)} %compare_select_fusion.5) | copy-start | bytes 196
  94.5 3.4 %copy-start.19 = (f32[4]{0:T(128)S(1)}, f32[4]{0:T(128)}, u32[]{:S(2)}) copy-start(f32[4]{0:T(128)} %convert_element_type.112) | copy-start | bytes 52
  97.9 1.0 %copy-start.14 = (f32[4]{0:T(128)S(1)}, f32[4]{0:T(128)}, u32[]{:S(2)}) copy-start(f32[4]{0:T(128)} %fusion.101) | copy-start | bytes 52
  100.7 0.8 copy-start.20

commit v12 on v8

--- a/solution.py
+++ b/solution.py
@@ -140,6 +140,12 @@
 
 def axis_sum(value, axis):
     count = lax.axis_size(axis)
+    if count & (count - 1) == 0:
+        step = 1
+        while step < count:
+            value = value + lax.ppermute(value, axis, [(i, i ^ step) for i in range(count)])
+            step *= 2
+        return value
     total = value
     for shift in range(1, count):
         total = total + lax.ppermute(value, axis, [(i, (i + shift) % count) for i in range(count)])
@@ -187,13 +193,20 @@
     else:
         head = lax.ppermute(cells[length - halo :], "seq", [(i, i + 1) for i in range(ends)])
         tail = lax.ppermute(cells[:halo], "seq", [(i + 1, i) for i in range(ends)])
-    rows = picks[:, None] * TB - halo + jnp.arange(span)[None, :]
-    inside = jnp.take(cells, jnp.clip(rows, 0, length - 1), axis=0)
-    edge_rows = jnp.concatenate([head, tail], axis=0)
-    edge_index = jnp.where(rows < 0, rows + halo, rows - length + halo)
-    outside = jnp.take(edge_rows, jnp.clip(edge_index, 0, 2 * halo - 1), axis=0)
-    in_range = jnp.logical_and(rows >= 0, rows < length)
-    windows = jnp.where(in_range[..., None], inside, outside)
+    last = per_block - 1
+    stacked = cells.reshape(per_block, TB, width)
+    block_ids = jnp.arange(per_block)[None, :]
+    choose = (picks[:, None] == block_ids).astype(cells.dtype)
+    choose_prev = (picks[:, None] - 1 == block_ids).astype(cells.dtype)
+    choose_next = (picks[:, None] + 1 == block_ids).astype(cells.dtype)
+    middle = jnp.einsum("hb,btd->htd", choose, stacked, preferred_element_type=jnp.float32)
+    prev_tail = jnp.einsum("hb,btd->htd", choose_prev, stacked[:, TB - halo :], preferred_element_type=jnp.float32)
+    next_head = jnp.einsum("hb,btd->htd", choose_next, stacked[:, :halo], preferred_element_type=jnp.float32)
+    at_start = (picks == 0)[:, None, None]
+    at_end = (picks == last)[:, None, None]
+    lower = jnp.where(at_start, head[None].astype(jnp.float32), prev_tail)
+    upper = jnp.where(at_end, tail[None].astype(jnp.float32), next_head)
+    windows = jnp.concatenate([lower, middle, upper], axis=1).astype(cells.dtype)
     x_float = windows.astype(jnp.float32)
     act = jax.nn.gelu(x_float).astype(jnp.bfloat16)
     conv_out = jnp.einsum("hti,oi->hto", act[:, 0:TB], conv_weight[0], preferred_element_type=jnp.float32)
@@ -279,7 +292,9 @@
     grads = grads.reshape(groups, owners * n_sides, TB, narrow)
     flat_sides = sides.reshape(groups, owners * n_sides)
     same_block = flat_sides[:, :, None] == flat_sides[:, None, :]
-    total = jnp.sum(jnp.where(same_block[..., None, None], grads[:, None], 0.0), axis=2)
+    total = jnp.einsum(
+        "qab,qbtd->qatd", same_block.astype(jnp.float32), grads, precision=lax.Precision.HIGHEST
+    )
     earlier = jnp.arange(owners * n_sides)[None, :] < jnp.arange(owners * n_sides)[:, None]
     first = jnp.logical_not(jnp.any(jnp.logical_and(same_block, earlier[None]), axis=-1))
     scaling = 1.25 * keep_all.astype(jnp.float32)

time: 51.5 us -> 48.2 us (0.936)
  other arithmetic: 7.26 us -> 4.03 us
  local copies, waits for them, and re-layouts: 12.8 us -> 10.5 us
  matrix products: 4.6 us -> 6.69 us
  waiting for transfers between devices: 14 us -> 14.6 us
    gather x6 -> x0, local copies, waits for them, and re-layouts: 4.31 us -> none  [the longest x3 3.02 us: sparse_path(): inside = jnp.take(cells, jnp.clip(rows, 0, length - 1), axis=0)]
    another operation x0 -> x2, local copies, waits for them, and re-layouts: none -> 2.49 us  [the longest x1 2.39 us: sparse_path(): stacked = cells.reshape(per_block, TB, width)]
    dot_general x0 -> x4, matrix products: none -> 2.06 us  [the longest x1 1.24 us: sparse_path(): jnp.einsum('hb,btd->htd', choose, stacked, preferred_element_type=jnp.flo...]
    reduce_sum x1 -> x0, other arithmetic: 1.4 us -> none  [sparse_path(): jnp.sum(jnp.where(same_block[..., None, None], grads[:, None], 0.0), axis=2)]
    concatenate x1, local copies, waits for them, and re-layouts: 0.76 us -> 0.08 us  [sparse_path(): jnp.concatenate([tiles.reshape(-1), counts.reshape(-1), keep.reshape(-1)])]
    concatenate x1, other arithmetic: 0.74 us -> 0.08 us  [sparse_path(): jnp.concatenate(pieces + [small]).astype(jnp.bfloat16).reshape(1, -1)]
    ppermute x3 -> x2, waiting for transfers between devices: 3.28 us -> 3.91 us  [axis_sum(): lax.ppermute(value, axis, [(i, i ^ step) for i in range(count)])]
    another operation x1 -> x3, other arithmetic: 0.71 us -> 0.12 us
  transfers between devices with their start and end apart: 5 -> 4, of which waited for: 2 -> 3; matrix products, arithmetic and copies ran while one was open for 18% -> 16% of each run, Pallas kernels for 0% -> 0%
where the time goes in v12:
time: 48.2 us; the launch traced here: 47.8 us
  waiting for transfers between devices  14.6 us (30%)
  starting transfers between devices  10.8 us (22%)
  local copies, waits for them, and re-layouts  10.5 us (22%)
  matrix products  6.69 us (14%)
  other arithmetic  4.03 us (8%)
  between operations  1.15 us (2%)
    all_to_all x1, waiting for transfers between devices, sparse_path(): incoming = lax.all_to_all(outgoing, ('seq', 'dp'), 0, 0, tiled=True)  10.7 us
    ppermute x2, starting transfers between devices, axis_sum(): lax.ppermute(value, axis, [(i, i ^ step) for i in range(count)])  4.29 us
    ppermute x2, waiting for transfers between devices, axis_sum(): lax.ppermute(value, axis, [(i, i ^ step) for i in range(count)])  3.91 us
    all_to_all x1, starting transfers between devices, sparse_path(): incoming = lax.all_to_all(outgoing, ('seq', 'dp'), 0, 0, tiled=True)  3.54 us
    ppermute x1, starting transfers between devices, sparse_path(): lax.ppermute(jnp.concatenate([cells[length - halo:], cells[:halo]]), 'seq...  3 us
    another operation x1, local copies, waits for them, and re-layouts, sparse_path(): stacked = cells.reshape(per_block, TB, width)  2.39 us
    dot_general x5, matrix products, sparse_path(): jnp.einsum('qato,qati->oi', dconv, act_sides[:, :, offset:offset + TB], p...  2.25 us
    dot_general x1, matrix products, sparse_path(): jnp.einsum('hb,btd->htd', choose, stacked, preferred_element_type=jnp.flo...  1.24 us
  transfers between devices with their start and end apart: 4, of which 3 were waited for; matrix products, arithmetic and copies ran while one was open for 16% of the time, Pallas kernels for 0%

profile of v12, /device:TPU:0, one launch (start us, length us, event | category | flops | bytes accessed | tf_op | source)
XLA Modules:
  0.0 47.8 jit_solution(3277025527511281571)
XLA Ops:
  0.0 0.7 %slice_bitcast_fusion.1 = (bf16[2,768]{1,0:T(2,128)(2,1)S(1)}, bf16[2,768]{1,0:T(2,128)(2,1)S(1)}) fusion(bf16[1,1024,768]{2,1,0:T(8,128)(2,1)} %param.6), kind=kLoop, calls=%fused_computation.152 | loop fusion | bytes 12288 | tf_op jit(solution)/shard_map/slice | solution.py:189
  0.7 3.0 %collective-permute-start = (bf16[4,768]{1,0:T(4,128)(2,1)S(1)}, bf16[4,768]{1,0:T(4,128)(2,1)S(1)}, u32[]{:S(2)}, u32[]{:S(2)}) collective-permute-start(bf16[4,768]{1,0:T(4,128)(2,1)S(1)} %pad_maximum_fusion.1), channel_id=1, source_target_pairs={{0,16},{16,0},{1,17},{17,1},{2,18},{18,2},{3,19},{19,3},{4,20},{20... | collective-permute-start | bytes 18440 | tf_op jit(solution)/shard_map/ppermute | solution.py:188
  3.8 1.0 %slice_reduce_fusion.1 = (s32[2,2]{1,0:T(2,128)S(1)}, s32[2,2]{1,0:T(2,128)S(1)}) fusion(s32[1,2,2,2]{3,2,1,0:T(2,128)} %param.9), kind=kLoop, calls=%fused_computation.175 | loop fusion | bytes 64 | tf_op jit(solution)/shard_map/slice | solution.py:172
  4.8 0.2 convert_reduce_fusion.1
  5.0 0.2 fusion.99
  5.4 2.4 %copy.153 = bf16[32,32,768]{2,0,1:T(8,128)(2,1)S(1)} copy(bf16[32,32,768]{2,1,0:T(8,128)(2,1)} %bitcast.121) | data formatting | bytes 3145728 | tf_op jit(solution)/shard_map/reshape;squeeze | solution.py:197
  7.8 1.2 %fusion.93 = bf16[4,32,768]{2,0,1:T(4,128)(2,1)S(1)} fusion(s32[4]{0:T(128)S(1)} %reshape.794, bf16[32,32,768]{2,1,0:T(8,128)(2,1)S(1)} %bitcast.122), kind=kOutput, calls=%fused_computation.178 | convolution fusion | flops 6291584 | bytes 1769488 | tf_op jit(solution)/shard_map/hb,btd->htd/dot_general | solution.py:202
  9.2 0.2 fusion.63
  9.4 0.2 fusion.65
  10.5 0.3 concatenate.145
  11.1 0.2 fusion.29
  11.6 0.3 copy-done.4
  11.9 0.2 fusion.35
  12.1 0.2 convolution_add_fusion.3
  12.4 0.2 convolution_add_fusion.2
  12.6 0.2 convolution_add_fusion.1
  12.9 0.3 fusion.7
  13.2 0.1 broadcast_in_dim.102
  13.3 0.3 fusion.30
  13.7 0.5 reshape.795
  14.3 0.9 %fusion.14 = bf16[8,352,128]{2,1,0:T(8,128)(2,1)} fusion(bf16[8,49,128]{2,1,0:T(8,128)(2,1)S(1)} %broadcast_in_dim.105, bf16[8,108,128]{2,1,0:T(8,128)(2,1)S(1)} %reshape.795, bf16[8,192,128]{2,1,0:T(8,128)(2,1)S(1)} %broadcast_in_dim.103), kind=kLoop, calls=%fused_computation.34 | loop fusion | flops 3604480 | bytes 1435648 | tf_op jit(solution)/shard_map/concatenate | solution.py:237
  15.2 3.5 %all-to-all-start = ((bf16[8,352,128]{2,1,0:T(8,128)(2,1)}), bf16[8,352,128]{2,1,0:T(8,128)(2,1)S(1)}, u32[]{:S(2)}, u32[]{:S(2)}) async-start(bf16[8,352,128]{2,1,0:T(8,128)(2,1)} %fusion.14), calls=%async_computation | async-start | bytes 1441792 | tf_op jit(solution)/shard_map/all_to_all | solution.py:246
  18.9 10.7 %all-to-all-done = bf16[8,352,128]{2,1,0:T(8,128)(2,1)S(1)} async-done(((bf16[8,352,128]{2,1,0:T(8,128)(2,1)}), bf16[8,352,128]{2,1,0:T(8,128)(2,1)S(1)}, u32[]{:S(2)}, u32[]{:S(2)}) %all-to-all-start) | async-done | bytes 720928 | tf_op jit(solution)/shard_map/all_to_all | solution.py:246
  30.1 0.3 convert_reduce_fusion
  30.9 0.2 fusion.110
  31.3 0.5 reshape_reshape.7
  32.2 0.3 reshape_reshape.6
  32.5 0.6 %gather_fusion = bf16[32,32,192]{2,1,0:T(8,128)(2,1)S(1)} fusion(bf16[32,32,192]{2,1,0:T(8,128)(2,1)S(1)} %reshape_reshape.6, s32[1024]{0:T(1024)S(1)} %pad_clamp_fusion.1), kind=kCustom, calls=%fused_computation | custom fusion | bytes 786560 | tf_op jit(solution)/shard_map/jit(_take)/gather | solution.py:270
  33.1 0.1 broadcast_select_fusion
  33.3 0.2 fusion.56
  33.6 1.6 %collective-permute-start.1 = (f32[128,128]{1,0:T(8,128)S(1)}, f32[128,128]{1,0:T(8,128)S(1)}, u32[]{:S(2)}, u32[]{:S(2)}) collective-permute-start(f32[128,128]{1,0:T(8,128)S(1)} %reshape.798), channel_id=1, source_target_pairs={{0,4},{4,0},{8,12},{12,8},{1,5},{5,1},{9,13},{13,9},{2,6},{6,2},{1... | collective-permute-start | bytes 196616 | tf_op jit(solution)/shard_map/ppermute | solution.py:146
  35.2 0.1 reshape.799
  35.4 0.6 %gather_fusion.1 = bf16[32,36,96]{2,1,0:T(8,128)(2,1)S(1)} fusion(bf16[32,36,96]{2,1,0:T(8,128)(2,1)S(1)} %reshape_reshape.7, s32[1024]{0:T(1024)S(1)} %pad_clamp_fusion), kind=kCustom, calls=%fused_computation.1 | custom fusion | bytes 442496 | tf_op jit(solution)/shard_map/jit(_take)/gather | solution.py:303
  36.2 0.2 fusion.70
  36.4 1.5 %collective-permute-done.1 = f32[128,128]{1,0:T(8,128)S(1)} collective-permute-done((f32[128,128]{1,0:T(8,128)S(1)}, f32[128,128]{1,0:T(8,128)S(1)}, u32[]{:S(2)}, u32[]{:S(2)}) %collective-permute-start.1) | collective-permute-done | bytes 65568 | tf_op jit(solution)/shard_map/ppermute | solution.py:146
  37.9 2.7 %collective-permute-start.2 = (f32[128,128]{1,0:T(8,128)S(1)}, f32[128,128]{1,0:T(8,128)S(1)}, u32[]{:S(2)}, u32[]{:S(2)}) collective-permute-start(f32[128,128]{1,0:T(8,128)S(1)} %add.287), channel_id=1, source_target_pairs={{0,8},{4,12},{8,0},{12,4},{1,9},{5,13},{9,1},{13,5},{2,10},{6,14},... | collective-permute-start | bytes 196616 | tf_op jit(solution)/shard_map/ppermute | solution.py:146
  40.6 0.2 multiply_reduce_fusion
  40.8 2.4 %collective-permute-done.2 = f32[128,128]{1,0:T(8,128)S(1)} collective-permute-done((f32[128,128]{1,0:T(8,128)S(1)}, f32[128,128]{1,0:T(8,128)S(1)}, u32[]{:S(2)}, u32[]{:S(2)}) %collective-permute-start.2) | collective-permute-done | bytes 65568 | tf_op jit(solution)/shard_map/ppermute | solution.py:146
  43.2 0.1 div.78
  43.3 0.4 convolution_convert_fusion.1
  43.7 0.5 %convolution_convert_fusion = bf16[4,2,2,32,192]{4,3,2,1,0:T(8,128)(2,1)S(1)} fusion(bf16[4,2,4,32,192]{4,3,2,1,0:T(8,128)(2,1)S(1)} %broadcast_select_fusion, f32[4,2,2,32,32]{4,3,2,1,0:T(8,128)S(1)} %div.78, f32[2,4,2,32,32]{4,3,2,1,0:T(8,128)S(1)} %reshape.799, f32[4]{0:T(128)S(1)} %convert_element_type.117, f32[4,2,2]{2,1,0:T(2,128)S(1)} %compare_select_fusion.6), kind=kOutput, calls=%fused_computation.9 | convolution fusion | flops 37896192 | bytes 987648 | tf_op jit(solution)/shard_map/qocij,qocid->qocjd/dot_general | solution.py:290
  44.3 0.4 fusion.4
  44.8 0.3 fusion.12
  45.1 0.3 fusion.11
  45.4 0.3 fusion.10
  45.8 0.3 fusion.9
  46.1 0.8 %copy-done.5 = f32[5,192,96]{2,1,0:T(8,128)} copy-done((f32[5,192,96]{2,1,0:T(8,128)}, f32[5,192,96]{2,1,0:T(8,128)S(1)}, u32[]{:S(2)}) %copy-start.5) | copy-done | bytes 368664
  46.9 1.0 %fusion.8 = f32[5,192,96]{2,1,0:T(8,128)} fusion(f32[5,192,96]{2,1,0:T(8,128)} %copy-done.5, bf16[4,8,32,192]{3,1,2,0:T(8,128)(2,1)S(1)} %fusion.4, bf16[4,8,36,96]{3,2,0,1:T(8,128)(2,1)S(1)} %copy_select_fusion), kind=kOutput, calls=%fused_computation.23 | convolution fusion | flops 37748736 | bytes 884736 | tf_op jit(solution)/shard_map/qato,qati->oi/dot_general | solution.py:306
  (76 shorter events, 3.3 us)
Async XLA Ops:
  0.7 10.1 %collective-permute-start = (bf16[4,768]{1,0:T(4,128)(2,1)S(1)}, bf16[4,768]{1,0:T(4,128)(2,1)S(1)}, u32[]{:S(2)}, u32[]{:S(2)}) collective-permute-start(bf16[4,768]{1,0:T(4,128)(2,1)S(1)} %pad_maximum_fusion.1), channel_id=1, source_target_pairs={{0,16},{16,0},{1,17},{17,1},{2,18},{18,2},{3,19},{19,3},{4,20},{20... | collective-permute-start | bytes 18440 | tf_op jit(solution)/shard_map/ppermute | solution.py:188
  5.4 2.4 %copy-start = (bf16[1,1024,768]{2,1,0:T(8,128)(2,1)S(1)}, bf16[1,1024,768]{2,1,0:T(8,128)(2,1)}, u32[]{:S(2)}) copy-start(bf16[1,1024,768]{2,1,0:T(8,128)(2,1)} %param.6) | copy-start | bytes 4718596
  7.8 1.3 %copy-start.1 = (s32[1,2,2,2]{3,2,1,0:T(2,128)S(1)}, s32[1,2,2,2]{3,2,1,0:T(2,128)}, u32[]{:S(2)}) copy-start(s32[1,2,2,2]{3,2,1,0:T(2,128)} %param.9) | copy-start | bytes 100
  7.8 2.4 %copy-start.2 = (f32[1,1,2,1024]{3,2,1,0:T(2,128)S(1)}, f32[1,1,2,1024]{3,2,1,0:T(2,128)}, u32[]{:S(2)}) copy-start(f32[1,1,2,1024]{3,2,1,0:T(2,128)} %param.11) | copy-start | bytes 24580
  7.8 2.5 %copy-start.3 = (s32[1,2]{1,0:T(1,128)S(1)}, s32[1,2]{1,0:T(1,128)}, u32[]{:S(2)}) copy-start(s32[1,2]{1,0:T(1,128)} %param.10) | copy-start | bytes 28
  10.5 1.4 %copy-start.4 = (bf16[5,192,768]{2,1,0:T(8,128)(2,1)S(1)}, bf16[5,192,768]{2,1,0:T(8,128)(2,1)}, u32[]{:S(2)}) copy-start(bf16[5,192,768]{2,1,0:T(8,128)(2,1)} %param.7) | copy-start | bytes 4423684
  15.2 14.4 %all-to-all-start = ((bf16[8,352,128]{2,1,0:T(8,128)(2,1)}), bf16[8,352,128]{2,1,0:T(8,128)(2,1)S(1)}, u32[]{:S(2)}, u32[]{:S(2)}) async-start(bf16[8,352,128]{2,1,0:T(8,128)(2,1)} %fusion.14), calls=%async_computation | async-start | bytes 1441792 | tf_op jit(solution)/shard_map/all_to_all | solution.py:246
  33.6 4.3 %collective-permute-start.1 = (f32[128,128]{1,0:T(8,128)S(1)}, f32[128,128]{1,0:T(8,128)S(1)}, u32[]{:S(2)}, u32[]{:S(2)}) collective-permute-start(f32[128,128]{1,0:T(8,128)S(1)} %reshape.798), channel_id=1, source_target_pairs={{0,4},{4,0},{8,12},{12,8},{1,5},{5,1},{9,13},{13,9},{2,6},{6,2},{1... | collective-permute-start | bytes 196616 | tf_op jit(solution)/shard_map/ppermute | solution.py:146
  37.9 5.2 %collective-permute-start.2 = (f32[128,128]{1,0:T(8,128)S(1)}, f32[128,128]{1,0:T(8,128)S(1)}, u32[]{:S(2)}, u32[]{:S(2)}) collective-permute-start(f32[128,128]{1,0:T(8,128)S(1)} %add.287), channel_id=1, source_target_pairs={{0,8},{4,12},{8,0},{12,4},{1,9},{5,13},{9,1},{13,5},{2,10},{6,14},... | collective-permute-start | bytes 196616 | tf_op jit(solution)/shard_map/ppermute | solution.py:146
  46.1 0.8 %copy-start.5 = (f32[5,192,96]{2,1,0:T(8,128)}, f32[5,192,96]{2,1,0:T(8,128)S(1)}, u32[]{:S(2)}) copy-start(f32[5,192,96]{2,1,0:T(8,128)S(1)} %fusion.9) | copy-start | bytes 1105924

commit v13 on v9

--- a/solution.py
+++ b/solution.py
@@ -140,6 +140,12 @@
 
 def axis_sum(value, axis):
     count = lax.axis_size(axis)
+    if count & (count - 1) == 0:
+        step = 1
+        while step < count:
+            value = value + lax.ppermute(value, axis, [(i, i ^ step) for i in range(count)])
+            step *= 2
+        return value
     total = value
     for shift in range(1, count):
         total = total + lax.ppermute(value, axis, [(i, (i + shift) % count) for i in range(count)])
@@ -293,17 +299,11 @@
     dconv = (scaling[:, None, None, None] * total).astype(jnp.bfloat16)
     dconv = jnp.where(first[..., None, None], dconv, jnp.zeros_like(dconv))
     act_sides = jnp.take(act_in, slot.reshape(groups, owners * n_sides), axis=0)
-    return jnp.stack(
-        [
-            jnp.einsum(
-                "qato,qati->oi",
-                dconv,
-                act_sides[:, :, offset : offset + TB],
-                preferred_element_type=jnp.float32,
-            )
-            for offset in range(taps)
-        ]
-    )
+    shifted = jnp.concatenate([act_sides[:, :, offset : offset + TB] for offset in range(taps)], axis=-1)
+    product = jnp.dot(
+        dconv.reshape(-1, narrow).T, shifted.reshape(-1, taps * cols), preferred_element_type=jnp.float32
+    )
+    return product.reshape(narrow, taps, cols).transpose(1, 0, 2)
 
 
 def per_device(features, conv_weight, keep, tiles, counts, targets):

time: 46.5 us -> 47.4 us (1.019)
  local copies, waits for them, and re-layouts: 8.98 us -> 11.4 us
  matrix products: 7.18 us -> 6.35 us
    concatenate x0 -> x1, local copies, waits for them, and re-layouts: none -> 2.38 us  [sparse_path(): jnp.concatenate([act_sides[:, :, offset:offset + TB] for offset in range(...]
    dot_general x5 -> x1, matrix products: 2.25 us -> 1.41 us  [sparse_path(): jnp.dot(dconv.reshape(-1, narrow).T, shifted.reshape(-1, taps * cols), pr...]
    unnamed x8 -> x6, local copies, waits for them, and re-layouts: 1.35 us -> 0.58 us
    dot_general x0 -> x1, local copies, waits for them, and re-layouts: none -> 0.53 us  [sparse_path(): jnp.dot(dconv.reshape(-1, narrow).T, shifted.reshape(-1, taps * cols), pr...]
    ppermute x3 -> x2, starting transfers between devices: 4.68 us -> 4.3 us  [axis_sum(): lax.ppermute(value, axis, [(i, i ^ step) for i in range(count)])]
    ppermute x3 -> x2, waiting for transfers between devices: 3.28 us -> 2.98 us  [axis_sum(): lax.ppermute(value, axis, [(i, i ^ step) for i in range(count)])]
  transfers between devices with their start and end apart: 5 -> 4, of which waited for: 2 -> 2; matrix products, arithmetic and copies ran while one was open for 14% -> 20% of each run, Pallas kernels for 0% -> 0%
where the time goes in v13:
time: 47.4 us; the launch traced here: 47.1 us
  waiting for transfers between devices  13.7 us (29%)
  local copies, waits for them, and re-layouts  11.4 us (24%)
  starting transfers between devices  10.8 us (23%)
  matrix products  6.35 us (13%)
  other arithmetic  3.72 us (8%)
  between operations  1.11 us (2%)
    all_to_all x1, waiting for transfers between devices, sparse_path(): incoming = lax.all_to_all(outgoing, ('seq', 'dp'), 0, 0, tiled=True)  10.7 us
    ppermute x2, starting transfers between devices, axis_sum(): lax.ppermute(value, axis, [(i, i ^ step) for i in range(count)])  4.3 us
    all_to_all x1, starting transfers between devices, sparse_path(): incoming = lax.all_to_all(outgoing, ('seq', 'dp'), 0, 0, tiled=True)  3.54 us
    ppermute x1, starting transfers between devices, sparse_path(): lax.ppermute(jnp.concatenate([cells[length - halo:], cells[:halo]]), 'seq...  3 us
    ppermute x2, waiting for transfers between devices, axis_sum(): lax.ppermute(value, axis, [(i, i ^ step) for i in range(count)])  2.98 us
    concatenate x1, local copies, waits for them, and re-layouts, sparse_path(): jnp.concatenate([act_sides[:, :, offset:offset + TB] for offset in range(...  2.38 us
    dot_general x1, matrix products, sparse_path(): inside = jnp.dot(pick_inside, cells, preferred_element_type=jnp.float32)  1.85 us
    dot_general x1, matrix products, sparse_path(): jnp.dot(dconv.reshape(-1, narrow).T, shifted.reshape(-1, taps * cols), pr...  1.41 us
  transfers between devices with their start and end apart: 4, of which 2 were waited for; matrix products, arithmetic and copies ran while one was open for 20% of the time, Pallas kernels for 0%

profile of v13, /device:TPU:0, one launch (start us, length us, event | category | flops | bytes accessed | tf_op | source)
XLA Modules:
  0.0 47.1 jit_solution(17863952061698850943)
XLA Ops:
  0.0 0.8 %slice_bitcast_fusion.1 = (bf16[2,768]{1,0:T(2,128)(2,1)S(1)}, bf16[2,768]{1,0:T(2,128)(2,1)S(1)}) fusion(bf16[1,1024,768]{2,1,0:T(8,128)(2,1)} %param.6), kind=kLoop, calls=%fused_computation.134 | loop fusion | bytes 12288 | tf_op jit(solution)/shard_map/slice | solution.py:189
  0.8 3.0 %collective-permute-start = (bf16[4,768]{1,0:T(4,128)(2,1)S(1)}, bf16[4,768]{1,0:T(4,128)(2,1)S(1)}, u32[]{:S(2)}, u32[]{:S(2)}) collective-permute-start(bf16[4,768]{1,0:T(4,128)(2,1)S(1)} %pad_maximum_fusion.1), channel_id=1, source_target_pairs={{0,16},{16,0},{1,17},{17,1},{2,18},{18,2},{3,19},{19,3},{4,20},{20... | collective-permute-start | bytes 18440 | tf_op jit(solution)/shard_map/ppermute | solution.py:188
  3.8 0.8 %concatenate.139 = s32[8]{0:T(128)S(1)} reshape(s32[1,2,2,2]{3,2,1,0:T(2,128)} %param.9) | data formatting | bytes 64 | tf_op jit(solution)/shard_map/concatenate | solution.py:232
  4.6 1.0 %slice_reduce_fusion.1 = (s32[2,2]{1,0:T(2,128)S(1)}, s32[2,2]{1,0:T(2,128)S(1)}) fusion(s32[1,2,2,2]{3,2,1,0:T(2,128)} %param.9), kind=kLoop, calls=%fused_computation.155 | loop fusion | bytes 64 | tf_op jit(solution)/shard_map/slice | solution.py:172
  5.6 0.2 convert_reduce_fusion.1
  5.8 0.2 fusion.83
  6.4 1.8 %fusion = f32[144,768]{1,0:T(8,128)S(1)} fusion(bf16[1,1024,768]{2,1,0:T(8,128)(2,1)} %param.6, s32[144]{0:T(256)S(1)} %add.308), kind=kOutput, calls=%fused_computation.2 | convolution fusion | flops 226639872 | bytes 2015808 | tf_op jit(solution)/shard_map/dot_general | solution.py:199
  9.2 0.3 fusion.8
  9.5 0.3 reshape.828
  9.8 0.2 fusion.30
  10.0 0.2 fusion.43
  10.3 0.5 %reshape.820 = bf16[8,108,128]{2,1,0:T(8,128)(2,1)S(1)} reshape(bf16[8,4,36,96]{3,2,1,0:T(8,128)(2,1)S(1)} %copy.86) | data formatting | bytes 442368 | tf_op jit(solution)/shard_map/reshape | solution.py:222
  10.8 0.6 %copy-done.2 = bf16[5,192,768]{2,1,0:T(8,128)(2,1)S(1)} copy-done((bf16[5,192,768]{2,1,0:T(8,128)(2,1)S(1)}, bf16[5,192,768]{2,1,0:T(8,128)(2,1)}, u32[]{:S(2)}) %copy-start.2) | copy-done | bytes 1474584
  11.3 0.2 fusion.35
  11.6 0.2 convolution_add_fusion.4
  11.8 0.2 convolution_add_fusion.3
  12.1 0.2 convolution_add_fusion.2
  12.3 0.3 fusion.11
  12.6 0.1 broadcast_in_dim.35
  12.8 0.9 %fusion.13 = bf16[8,352,128]{2,1,0:T(8,128)(2,1)} fusion(bf16[8,49,128]{2,1,0:T(8,128)(2,1)S(1)} %broadcast_in_dim.38, bf16[8,108,128]{2,1,0:T(8,128)(2,1)S(1)} %reshape.820, bf16[8,192,128]{2,1,0:T(8,128)(2,1)S(1)} %broadcast_in_dim.36), kind=kLoop, calls=%fused_computation.27 | loop fusion | flops 3604480 | bytes 1435648 | tf_op jit(solution)/shard_map/concatenate | solution.py:235
  13.8 3.5 %all-to-all-start = ((bf16[8,352,128]{2,1,0:T(8,128)(2,1)}), bf16[8,352,128]{2,1,0:T(8,128)(2,1)S(1)}, u32[]{:S(2)}, u32[]{:S(2)}) async-start(bf16[8,352,128]{2,1,0:T(8,128)(2,1)} %fusion.13), calls=%async_computation | async-start | bytes 1441792 | tf_op jit(solution)/shard_map/all_to_all | solution.py:244
  17.5 10.7 %all-to-all-done = bf16[8,352,128]{2,1,0:T(8,128)(2,1)S(1)} async-done(((bf16[8,352,128]{2,1,0:T(8,128)(2,1)}), bf16[8,352,128]{2,1,0:T(8,128)(2,1)S(1)}, u32[]{:S(2)}, u32[]{:S(2)}) %all-to-all-start) | async-done | bytes 720928 | tf_op jit(solution)/shard_map/all_to_all | solution.py:244
  28.4 0.2 fusion.93
  28.6 0.1 copy.89
  29.1 0.3 convert_reduce_fusion
  29.6 0.5 reshape_reshape.7
  30.7 0.4 reshape_reshape.6
  31.1 0.6 %gather_fusion = bf16[32,32,192]{2,1,0:T(8,128)(2,1)S(1)} fusion(bf16[32,32,192]{2,1,0:T(8,128)(2,1)S(1)} %reshape_reshape.6, s32[1024]{0:T(1024)S(1)} %pad_clamp_fusion.1), kind=kCustom, calls=%fused_computation | custom fusion | bytes 786560 | tf_op jit(solution)/shard_map/jit(_take)/gather | solution.py:268
  31.7 0.1 broadcast_select_fusion
  31.8 0.2 fusion.48
  32.0 0.1 reshape.823
  32.1 1.6 %collective-permute-start.1 = (f32[128,128]{1,0:T(8,128)S(1)}, f32[128,128]{1,0:T(8,128)S(1)}, u32[]{:S(2)}, u32[]{:S(2)}) collective-permute-start(f32[128,128]{1,0:T(8,128)S(1)} %reshape.823), channel_id=1, source_target_pairs={{0,4},{4,0},{8,12},{12,8},{1,5},{5,1},{9,13},{13,9},{2,6},{6,2},{1... | collective-permute-start | bytes 196616 | tf_op jit(solution)/shard_map/ppermute | solution.py:146
  33.8 0.6 %gather_fusion.1 = bf16[32,36,96]{2,1,0:T(8,128)(2,1)S(1)} fusion(bf16[32,36,96]{2,1,0:T(8,128)(2,1)S(1)} %reshape_reshape.7, s32[1024]{0:T(1024)S(1)} %pad_clamp_fusion), kind=kCustom, calls=%fused_computation.1 | custom fusion | bytes 442496 | tf_op jit(solution)/shard_map/jit(_take)/gather | solution.py:301
  34.4 0.1 broadcast_select_fusion.1
  34.5 0.3 fusion.91
  34.8 0.2 fusion.60
  35.0 0.1 reshape.824
  35.2 2.4 %concatenate.149 = bf16[4,8,32,480]{3,2,1,0:T(8,128)(2,1)S(1)} concatenate(bf16[4,8,32,96]{3,2,1,0:T(8,128)(2,1)S(1)} %get-tuple-element.17, bf16[4,8,32,96]{3,2,1,0:T(8,128)(2,1)S(1)} %get-tuple-element.16, bf16[4,8,32,96]{3,2,1,0:T(8,128)(2,1)S(1)} %get-tuple-element.15, bf16[4,8,32,96]{3,2,1,0:T(8,128)(2,1)S(1)} %get-tuple-element.14, bf16[4,8,32,96]{3,2,1,0:T(8,128)(2,1)S(1)} %get-tuple-element.13), dimensions={3} | concatenate | bytes 1966080 | tf_op jit(solution)/shard_map/concatenate | solution.py:302
  37.6 0.5 %copy.96 = bf16[480,1024]{1,0:T(8,128)(2,1)S(1)} copy(bf16[480,1024]{0,1:T(8,128)(2,1)S(1)} %bitcast.85) | data formatting | bytes 1966080 | tf_op jit(solution)/shard_map/dot_general | solution.py:303
  38.1 2.7 %collective-permute-start.2 = (f32[128,128]{1,0:T(8,128)S(1)}, f32[128,128]{1,0:T(8,128)S(1)}, u32[]{:S(2)}, u32[]{:S(2)}) collective-permute-start(f32[128,128]{1,0:T(8,128)S(1)} %add.337), channel_id=1, source_target_pairs={{0,8},{4,12},{8,0},{12,4},{1,9},{5,13},{9,1},{13,5},{2,10},{6,14},... | collective-permute-start | bytes 196616 | tf_op jit(solution)/shard_map/ppermute | solution.py:146
  40.8 0.2 multiply_reduce_fusion
  41.0 3.0 %collective-permute-done.2 = f32[128,128]{1,0:T(8,128)S(1)} collective-permute-done((f32[128,128]{1,0:T(8,128)S(1)}, f32[128,128]{1,0:T(8,128)S(1)}, u32[]{:S(2)}, u32[]{:S(2)}) %collective-permute-start.2) | collective-permute-done | bytes 65568 | tf_op jit(solution)/shard_map/ppermute | solution.py:146
  44.0 0.1 div.78
  44.1 0.5 %convolution_convert_fusion = bf16[4,2,2,32,192]{4,3,2,1,0:T(8,128)(2,1)S(1)} fusion(bf16[4,2,4,32,192]{4,3,2,1,0:T(8,128)(2,1)S(1)} %broadcast_select_fusion, f32[4,2,2,32,32]{4,3,2,1,0:T(8,128)S(1)} %div.78, f32[2,4,2,32,32]{4,3,2,1,0:T(8,128)S(1)} %reshape.824, f32[4]{0:T(128)S(1)} %convert_element_type.116, f32[4,2,2]{2,1,0:T(2,128)S(1)} %compare_select_fusion.6), kind=kOutput, calls=%fused_computation.13 | convolution fusion | flops 37896192 | bytes 987648 | tf_op jit(solution)/shard_map/qocij,qocid->qocjd/dot_general | solution.py:288
  44.6 0.4 convolution_convert_fusion.1
  45.1 0.4 fusion.6
  45.6 0.1 copy.95
  45.7 1.4 %convolution_bitcast_fusion = f32[5,192,96]{2,1,0:T(8,128)} fusion(bf16[1024,192,1]{1,0,2:T(8,128)(2,1)S(1)} %bitcast.88, bf16[5,96,1024]{2,1,0:T(8,128)(2,1)S(1)} %bitcast.86), kind=kOutput, calls=%fused_computation.11 | convolution fusion | flops 188743680 | bytes 1744896 | tf_op jit(solution)/shard_map/dot_general | solution.py:303
  (63 shorter events, 2.6 us)
Async XLA Ops:
  0.0 8.9 %copy-start = (f32[1,1,2,1024]{3,2,1,0:T(2,128)S(1)}, f32[1,1,2,1024]{3,2,1,0:T(2,128)}, u32[]{:S(2)}) copy-start(f32[1,1,2,1024]{3,2,1,0:T(2,128)} %param.11) | copy-start | bytes 24580
  0.0 8.9 %copy-start.1 = (s32[1,2]{1,0:T(1,128)S(1)}, s32[1,2]{1,0:T(1,128)}, u32[]{:S(2)}) copy-start(s32[1,2]{1,0:T(1,128)} %param.10) | copy-start | bytes 28
  0.8 8.4 %collective-permute-start = (bf16[4,768]{1,0:T(4,128)(2,1)S(1)}, bf16[4,768]{1,0:T(4,128)(2,1)S(1)}, u32[]{:S(2)}, u32[]{:S(2)}) collective-permute-start(bf16[4,768]{1,0:T(4,128)(2,1)S(1)} %pad_maximum_fusion.1), channel_id=1, source_target_pairs={{0,16},{16,0},{1,17},{17,1},{2,18},{18,2},{3,19},{19,3},{4,20},{20... | collective-permute-start | bytes 18440 | tf_op jit(solution)/shard_map/ppermute | solution.py:188
  10.0 1.4 %copy-start.2 = (bf16[5,192,768]{2,1,0:T(8,128)(2,1)S(1)}, bf16[5,192,768]{2,1,0:T(8,128)(2,1)}, u32[]{:S(2)}) copy-start(bf16[5,192,768]{2,1,0:T(8,128)(2,1)} %param.7) | copy-start | bytes 4423684
  13.8 14.4 %all-to-all-start = ((bf16[8,352,128]{2,1,0:T(8,128)(2,1)}), bf16[8,352,128]{2,1,0:T(8,128)(2,1)S(1)}, u32[]{:S(2)}, u32[]{:S(2)}) async-start(bf16[8,352,128]{2,1,0:T(8,128)(2,1)} %fusion.13), calls=%async_computation | async-start | bytes 1441792 | tf_op jit(solution)/shard_map/all_to_all | solution.py:244
  32.1 6.0 %collective-permute-start.1 = (f32[128,128]{1,0:T(8,128)S(1)}, f32[128,128]{1,0:T(8,128)S(1)}, u32[]{:S(2)}, u32[]{:S(2)}) collective-permute-start(f32[128,128]{1,0:T(8,128)S(1)} %reshape.823), channel_id=1, source_target_pairs={{0,4},{4,0},{8,12},{12,8},{1,5},{5,1},{9,13},{13,9},{2,6},{6,2},{1... | collective-permute-start | bytes 196616 | tf_op jit(solution)/shard_map/ppermute | solution.py:146
  38.1 5.8 %collective-permute-start.2 = (f32[128,128]{1,0:T(8,128)S(1)}, f32[128,128]{1,0:T(8,128)S(1)}, u32[]{:S(2)}, u32[]{:S(2)}) collective-permute-start(f32[128,128]{1,0:T(8,128)S(1)} %add.337), channel_id=1, source_target_pairs={{0,8},{4,12},{8,0},{12,4},{1,9},{5,13},{9,1},{13,5},{2,10},{6,14},... | collective-permute-start | bytes 196616 | tf_op jit(solution)/shard_map/ppermute | solution.py:146

commit v14 on v13

--- a/solution.py
+++ b/solution.py
@@ -140,12 +140,6 @@
 
 def axis_sum(value, axis):
     count = lax.axis_size(axis)
-    if count & (count - 1) == 0:
-        step = 1
-        while step < count:
-            value = value + lax.ppermute(value, axis, [(i, i ^ step) for i in range(count)])
-            step *= 2
-        return value
     total = value
     for shift in range(1, count):
         total = total + lax.ppermute(value, axis, [(i, (i + shift) % count) for i in range(count)])

time: 47.4 us -> 51.3 us (1.082)
  matrix products: 6.35 us -> 11.8 us
  waiting for transfers between devices: 13.7 us -> 10.7 us
  other arithmetic: 3.72 us -> 5.06 us
  local copies, waits for them, and re-layouts: 11.4 us -> 10.8 us
    dot_general x4, matrix products: 1.01 us -> 4.86 us  [sparse_path(): jnp.einsum('hti,oi->hto', act[:, offset:offset + TB], conv_weight[offset]...]
    ppermute x2 -> x3, waiting for transfers between devices: 2.98 us -> 0.01 us  [axis_sum(): lax.ppermute(value, axis, [(i, (i + shift) % count) for i in range(count)])]
    dot_general x1, matrix products: 0.24 us -> 1.21 us  [sparse_path(): jnp.einsum('hti,oi->hto', act[:, 0:TB], conv_weight[0], preferred_element...]
    div x1, other arithmetic: 0.01 us -> 0.86 us  [sparse_path(): predicted = summed / math.sqrt(width)]
    dot_general x1, matrix products: 0.5 us -> 1.16 us  [sparse_path(): jnp.einsum('qocij,qocid->qocjd', dpredicted, row_float, precision=lax.Pre...]
    unnamed x6, local copies, waits for them, and re-layouts: 0.58 us -> 0.01 us
    ppermute x2 -> x3, starting transfers between devices: 4.3 us -> 4.66 us  [axis_sum(): lax.ppermute(value, axis, [(i, (i + shift) % count) for i in range(count)])]
  transfers between devices with their start and end apart: 4 -> 5, of which waited for: 2 -> 1; matrix products, arithmetic and copies ran while one was open for 20% -> 21% of each run, Pallas kernels for 0% -> 0%
where the time goes in v14:
time: 51.3 us; the launch traced here: 50.7 us
  matrix products  11.8 us (23%)
  starting transfers between devices  11.2 us (22%)
  local copies, waits for them, and re-layouts  10.8 us (21%)
  waiting for transfers between devices  10.7 us (21%)
  other arithmetic  5.06 us (10%)
  between operations  1.13 us (2%)
    all_to_all x1, waiting for transfers between devices, sparse_path(): incoming = lax.all_to_all(outgoing, ('seq', 'dp'), 0, 0, tiled=True)  10.7 us
    dot_general x4, matrix products, sparse_path(): jnp.einsum('hti,oi->hto', act[:, offset:offset + TB], conv_weight[offset]...  4.86 us
    ppermute x3, starting transfers between devices, axis_sum(): lax.ppermute(value, axis, [(i, (i + shift) % count) for i in range(count)])  4.66 us
    all_to_all x1, starting transfers between devices, sparse_path(): incoming = lax.all_to_all(outgoing, ('seq', 'dp'), 0, 0, tiled=True)  3.54 us
    ppermute x1, starting transfers between devices, sparse_path(): lax.ppermute(jnp.concatenate([cells[length - halo:], cells[:halo]]), 'seq...  3 us
    concatenate x1, local copies, waits for them, and re-layouts, sparse_path(): jnp.concatenate([act_sides[:, :, offset:offset + TB] for offset in range(...  2.38 us
    dot_general x1, matrix products, sparse_path(): inside = jnp.dot(pick_inside, cells, preferred_element_type=jnp.float32)  1.85 us
    dot_general x1, matrix products, sparse_path(): jnp.dot(dconv.reshape(-1, narrow).T, shifted.reshape(-1, taps * cols), pr...  1.41 us
  transfers between devices with their start and end apart: 5, of which 1 were waited for; matrix products, arithmetic and copies ran while one was open for 21% of the time, Pallas kernels for 0%

profile of v14, /device:TPU:0, one launch (start us, length us, event | category | flops | bytes accessed | tf_op | source)
XLA Modules:
  0.0 50.7 jit_solution(9947008182911931946)
XLA Ops:
  0.0 0.8 %slice_bitcast_fusion.1 = (bf16[2,768]{1,0:T(2,128)(2,1)S(1)}, bf16[2,768]{1,0:T(2,128)(2,1)S(1)}) fusion(bf16[1,1024,768]{2,1,0:T(8,128)(2,1)} %param.6), kind=kLoop, calls=%fused_computation.134 | loop fusion | bytes 12288 | tf_op jit(solution)/shard_map/slice | solution.py:183
  0.8 3.0 %collective-permute-start = (bf16[4,768]{1,0:T(4,128)(2,1)S(1)}, bf16[4,768]{1,0:T(4,128)(2,1)S(1)}, u32[]{:S(2)}, u32[]{:S(2)}) collective-permute-start(bf16[4,768]{1,0:T(4,128)(2,1)S(1)} %pad_maximum_fusion.1), channel_id=1, source_target_pairs={{0,16},{16,0},{1,17},{17,1},{2,18},{18,2},{3,19},{19,3},{4,20},{20... | collective-permute-start | bytes 18440 | tf_op jit(solution)/shard_map/ppermute | solution.py:182
  3.8 0.8 %concatenate.139 = s32[8]{0:T(128)S(1)} reshape(s32[1,2,2,2]{3,2,1,0:T(2,128)} %param.9) | data formatting | bytes 64 | tf_op jit(solution)/shard_map/concatenate | solution.py:226
  4.6 1.0 %slice_reduce_fusion.1 = (s32[2,2]{1,0:T(2,128)S(1)}, s32[2,2]{1,0:T(2,128)S(1)}) fusion(s32[1,2,2,2]{3,2,1,0:T(2,128)} %param.9), kind=kLoop, calls=%fused_computation.155 | loop fusion | bytes 64 | tf_op jit(solution)/shard_map/slice | solution.py:166
  5.6 0.2 convert_reduce_fusion.1
  5.8 0.2 fusion.83
  6.4 1.8 %fusion = f32[144,768]{1,0:T(8,128)S(1)} fusion(bf16[1,1024,768]{2,1,0:T(8,128)(2,1)} %param.6, s32[144]{0:T(256)S(1)} %add.311), kind=kOutput, calls=%fused_computation.2 | convolution fusion | flops 226639872 | bytes 2015808 | tf_op jit(solution)/shard_map/dot_general | solution.py:193
  9.2 0.3 fusion.8
  9.5 0.3 reshape.828
  9.8 0.2 fusion.30
  10.0 0.2 fusion.43
  10.3 0.5 reshape.820
  10.7 1.2 %fusion.35 = f32[4,32,192]{2,1,0:T(8,128)S(1)} fusion(bf16[5,192,768]{2,1,0:T(8,128)(2,1)} %param.7, bf16[4,36,768]{2,1,0:T(8,128)(2,1)S(1)} %fusion.30), kind=kOutput, calls=%fused_computation.53 | convolution fusion | flops 37748736 | bytes 589824 | tf_op jit(solution)/shard_map/hti,oi->hto/dot_general | solution.py:204
  12.0 1.2 %convolution_add_fusion.4 = f32[4,32,192]{2,1,0:T(8,128)S(1)} fusion(f32[4,32,192]{2,1,0:T(8,128)S(1)} %fusion.35, bf16[5,192,768]{2,1,0:T(8,128)(2,1)} %param.7, bf16[4,36,768]{2,1,0:T(8,128)(2,1)S(1)} %fusion.30), kind=kOutput, calls=%fused_computation.22 | convolution fusion | flops 37773312 | bytes 720896 | tf_op jit(solution)/shard_map/hti,oi->hto/dot_general | solution.py:206
  13.2 1.2 %convolution_add_fusion.3 = f32[4,32,192]{2,1,0:T(8,128)S(1)} fusion(f32[4,32,192]{2,1,0:T(8,128)S(1)} %convolution_add_fusion.4, bf16[5,192,768]{2,1,0:T(8,128)(2,1)} %param.7, bf16[4,36,768]{2,1,0:T(8,128)(2,1)S(1)} %fusion.30), kind=kOutput, calls=%fused_computation.21 | convolution fusion | flops 37773312 | bytes 720896 | tf_op jit(solution)/shard_map/hti,oi->hto/dot_general | solution.py:206
  14.4 1.2 %convolution_add_fusion.2 = f32[4,32,192]{2,1,0:T(8,128)S(1)} fusion(f32[4,32,192]{2,1,0:T(8,128)S(1)} %convolution_add_fusion.3, bf16[5,192,768]{2,1,0:T(8,128)(2,1)} %param.7, bf16[4,36,768]{2,1,0:T(8,128)(2,1)S(1)} %fusion.30), kind=kOutput, calls=%fused_computation.20 | convolution fusion | flops 37773312 | bytes 720896 | tf_op jit(solution)/shard_map/hti,oi->hto/dot_general | solution.py:206
  15.6 1.2 %fusion.11 = bf16[4,32,192]{2,1,0:T(8,128)(2,1)S(1)} fusion(f32[4,32,192]{2,1,0:T(8,128)S(1)} %convolution_add_fusion.2, bf16[5,192,768]{2,1,0:T(8,128)(2,1)} %param.7, bf16[4,36,768]{2,1,0:T(8,128)(2,1)S(1)} %fusion.30, f32[4,32,768]{2,1,0:T(8,128)S(1)} %slice.158, s32[]{:T(128)S(6)} %select_n.143, f32[]{:T(128)} %bitcast.5), kind=kOutput, calls=%fused_computation.23 | convolution fusion | flops 37847040 | bytes 803332 | tf_op jit(solution)/shard_map/hti,oi->hto/dot_general | solution.py:206
  16.8 0.1 broadcast_in_dim.35
  17.1 0.9 %fusion.13 = bf16[8,352,128]{2,1,0:T(8,128)(2,1)} fusion(bf16[8,49,128]{2,1,0:T(8,128)(2,1)S(1)} %broadcast_in_dim.38, bf16[8,108,128]{2,1,0:T(8,128)(2,1)S(1)} %reshape.820, bf16[8,192,128]{2,1,0:T(8,128)(2,1)S(1)} %broadcast_in_dim.36), kind=kLoop, calls=%fused_computation.27 | loop fusion | flops 3604480 | bytes 1435648 | tf_op jit(solution)/shard_map/concatenate | solution.py:229
  18.0 3.5 %all-to-all-start = ((bf16[8,352,128]{2,1,0:T(8,128)(2,1)}), bf16[8,352,128]{2,1,0:T(8,128)(2,1)S(1)}, u32[]{:S(2)}, u32[]{:S(2)}) async-start(bf16[8,352,128]{2,1,0:T(8,128)(2,1)} %fusion.13), calls=%async_computation | async-start | bytes 1441792 | tf_op jit(solution)/shard_map/all_to_all | solution.py:238
  21.7 10.7 %all-to-all-done = bf16[8,352,128]{2,1,0:T(8,128)(2,1)S(1)} async-done(((bf16[8,352,128]{2,1,0:T(8,128)(2,1)}), bf16[8,352,128]{2,1,0:T(8,128)(2,1)S(1)}, u32[]{:S(2)}, u32[]{:S(2)}) %all-to-all-start) | async-done | bytes 720928 | tf_op jit(solution)/shard_map/all_to_all | solution.py:238
  32.6 0.2 fusion.93
  32.9 0.1 copy.89
  33.3 0.3 convert_reduce_fusion
  34.3 0.3 reshape_reshape.6
  34.6 0.6 %gather_fusion = bf16[32,32,192]{2,1,0:T(8,128)(2,1)S(1)} fusion(bf16[32,32,192]{2,1,0:T(8,128)(2,1)S(1)} %reshape_reshape.6, s32[1024]{0:T(1024)S(1)} %pad_clamp_fusion.1), kind=kCustom, calls=%fused_computation | custom fusion | bytes 786560 | tf_op jit(solution)/shard_map/jit(_take)/gather | solution.py:262
  35.2 0.1 broadcast_select_fusion
  35.3 0.2 fusion.48
  35.6 0.1 reshape.823
  35.7 3.6 %collective-permute-start.3 = (f32[128,128]{1,0:T(8,128)S(1)}, f32[128,128]{1,0:T(8,128)S(1)}, u32[]{:S(2)}, u32[]{:S(2)}) collective-permute-start(f32[128,128]{1,0:T(8,128)S(1)} %reshape.823), channel_id=1, source_target_pairs={{0,12},{4,0},{8,4},{12,8},{1,13},{5,1},{9,5},{13,9},{2,14},{6,2},{... | collective-permute-start | bytes 196616 | tf_op jit(solution)/shard_map/ppermute | solution.py:145
  39.3 1.0 %collective-permute-start.1 = (f32[128,128]{1,0:T(8,128)S(1)}, f32[128,128]{1,0:T(8,128)}, u32[]{:S(2)}, u32[]{:S(2)}) collective-permute-start(f32[128,128]{1,0:T(8,128)S(1)} %reshape.823), channel_id=1, source_target_pairs={{0,4},{4,8},{8,12},{12,0},{1,5},{5,9},{9,13},{13,1},{2,6},{6,10},{... | collective-permute-start | bytes 196616 | tf_op jit(solution)/shard_map/ppermute | solution.py:145
  40.4 0.5 reshape_reshape.7
  40.8 0.5 %convert_element_type.116 = f32[4]{0:T(128)} convert(s32[4]{0:T(128)S(1)} %get-tuple-element.26) | non-fusion elementwise | flops 4 | bytes 32 | tf_op jit(solution)/shard_map/convert_element_type | solution.py:271
  41.4 0.2 fusion.60
  41.8 0.1 reshape.824
  41.9 0.6 %gather_fusion.1 = bf16[32,36,96]{2,1,0:T(8,128)(2,1)S(1)} fusion(bf16[32,36,96]{2,1,0:T(8,128)(2,1)S(1)} %reshape_reshape.7, s32[1024]{0:T(1024)S(1)} %pad_clamp_fusion), kind=kCustom, calls=%fused_computation.1 | custom fusion | bytes 442496 | tf_op jit(solution)/shard_map/jit(_take)/gather | solution.py:295
  42.5 0.1 broadcast_select_fusion.1
  42.6 0.3 fusion.91
  42.9 2.4 %concatenate.149 = bf16[4,8,32,480]{3,2,1,0:T(8,128)(2,1)S(1)} concatenate(bf16[4,8,32,96]{3,2,1,0:T(8,128)(2,1)S(1)} %get-tuple-element.17, bf16[4,8,32,96]{3,2,1,0:T(8,128)(2,1)S(1)} %get-tuple-element.16, bf16[4,8,32,96]{3,2,1,0:T(8,128)(2,1)S(1)} %get-tuple-element.15, bf16[4,8,32,96]{3,2,1,0:T(8,128)(2,1)S(1)} %get-tuple-element.14, bf16[4,8,32,96]{3,2,1,0:T(8,128)(2,1)S(1)} %get-tuple-element.13), dimensions={3} | concatenate | bytes 1966080 | tf_op jit(solution)/shard_map/concatenate | solution.py:296
  45.3 0.5 %copy.96 = bf16[480,1024]{1,0:T(8,128)(2,1)S(1)} copy(bf16[480,1024]{0,1:T(8,128)(2,1)S(1)} %bitcast.85) | data formatting | bytes 1966080 | tf_op jit(solution)/shard_map/dot_general | solution.py:297
  45.9 0.2 multiply_reduce_fusion
  46.1 0.9 %add_multiply_fusion = f32[128,128]{1,0:T(8,128)S(1)} fusion(f32[128,128]{1,0:T(8,128)S(1)} %collective-permute-done.3, f32[128,128]{1,0:T(8,128)S(1)} %collective-permute-done.2, f32[128,128]{1,0:T(8,128)S(1)} %reshape.823, f32[128,128]{1,0:T(8,128)} %collective-permute-done.1), kind=kLoop, calls=%fused_computation.79 | loop fusion | flops 65536 | bytes 327680 | tf_op jit(solution)/shard_map/div | solution.py:268
  46.9 0.1 div.78
  47.1 1.2 %convolution_convert_fusion = bf16[4,2,2,32,192]{4,3,2,1,0:T(8,128)(2,1)S(1)} fusion(bf16[4,2,4,32,192]{4,3,2,1,0:T(8,128)(2,1)S(1)} %broadcast_select_fusion, f32[4,2,2,32,32]{4,3,2,1,0:T(8,128)S(1)} %div.78, f32[2,4,2,32,32]{4,3,2,1,0:T(8,128)S(1)} %reshape.824, f32[4]{0:T(128)} %convert_element_type.116, f32[4,2,2]{2,1,0:T(2,128)S(1)} %compare_select_fusion.6), kind=kOutput, calls=%fused_computation.13 | convolution fusion | flops 37896192 | bytes 987152 | tf_op jit(solution)/shard_map/qocij,qocid->qocjd/dot_general | solution.py:282
  48.2 0.4 convolution_convert_fusion.1
  48.8 0.4 fusion.6
  49.2 0.1 copy.95
  49.3 1.4 %convolution_bitcast_fusion = f32[5,192,96]{2,1,0:T(8,128)} fusion(bf16[1024,192,1]{1,0,2:T(8,128)(2,1)S(1)} %bitcast.88, bf16[5,96,1024]{2,1,0:T(8,128)(2,1)S(1)} %bitcast.86), kind=kOutput, calls=%fused_computation.11 | convolution fusion | flops 188743680 | bytes 1744896 | tf_op jit(solution)/shard_map/dot_general | solution.py:297
  (64 shorter events, 2.6 us)
Async XLA Ops:
  0.0 8.9 %copy-start = (f32[1,1,2,1024]{3,2,1,0:T(2,128)S(1)}, f32[1,1,2,1024]{3,2,1,0:T(2,128)}, u32[]{:S(2)}) copy-start(f32[1,1,2,1024]{3,2,1,0:T(2,128)} %param.11) | copy-start | bytes 24580
  0.0 8.9 %copy-start.1 = (s32[1,2]{1,0:T(1,128)S(1)}, s32[1,2]{1,0:T(1,128)}, u32[]{:S(2)}) copy-start(s32[1,2]{1,0:T(1,128)} %param.10) | copy-start | bytes 28
  0.8 8.4 %collective-permute-start = (bf16[4,768]{1,0:T(4,128)(2,1)S(1)}, bf16[4,768]{1,0:T(4,128)(2,1)S(1)}, u32[]{:S(2)}, u32[]{:S(2)}) collective-permute-start(bf16[4,768]{1,0:T(4,128)(2,1)S(1)} %pad_maximum_fusion.1), channel_id=1, source_target_pairs={{0,16},{16,0},{1,17},{17,1},{2,18},{18,2},{3,19},{19,3},{4,20},{20... | collective-permute-start | bytes 18440 | tf_op jit(solution)/shard_map/ppermute | solution.py:182
  18.0 14.4 %all-to-all-start = ((bf16[8,352,128]{2,1,0:T(8,128)(2,1)}), bf16[8,352,128]{2,1,0:T(8,128)(2,1)S(1)}, u32[]{:S(2)}, u32[]{:S(2)}) async-start(bf16[8,352,128]{2,1,0:T(8,128)(2,1)} %fusion.13), calls=%async_computation | async-start | bytes 1441792 | tf_op jit(solution)/shard_map/all_to_all | solution.py:238
  35.7 10.4 %collective-permute-start.3 = (f32[128,128]{1,0:T(8,128)S(1)}, f32[128,128]{1,0:T(8,128)S(1)}, u32[]{:S(2)}, u32[]{:S(2)}) collective-permute-start(f32[128,128]{1,0:T(8,128)S(1)} %reshape.823), channel_id=1, source_target_pairs={{0,12},{4,0},{8,4},{12,8},{1,13},{5,1},{9,5},{13,9},{2,14},{6,2},{... | collective-permute-start | bytes 196616 | tf_op jit(solution)/shard_map/ppermute | solution.py:145
  39.3 6.7 %collective-permute-start.2 = (f32[128,128]{1,0:T(8,128)S(1)}, f32[128,128]{1,0:T(8,128)S(1)}, u32[]{:S(2)}, u32[]{:S(2)}) collective-permute-start(f32[128,128]{1,0:T(8,128)S(1)} %reshape.823), channel_id=1, source_target_pairs={{0,8},{4,12},{8,0},{12,4},{1,9},{5,13},{9,1},{13,5},{2,10},{6,14},... | collective-permute-start | bytes 196616 | tf_op jit(solution)/shard_map/ppermute | solution.py:145
  39.3 6.7 %collective-permute-start.1 = (f32[128,128]{1,0:T(8,128)S(1)}, f32[128,128]{1,0:T(8,128)}, u32[]{:S(2)}, u32[]{:S(2)}) collective-permute-start(f32[128,128]{1,0:T(8,128)S(1)} %reshape.823), channel_id=1, source_target_pairs={{0,4},{4,8},{8,12},{12,0},{1,5},{5,9},{9,13},{13,1},{2,6},{6,10},{... | collective-permute-start | bytes 196616 | tf_op jit(solution)/shard_map/ppermute | solution.py:145
  45.9 2.4 %copy-start.2 = (f32[4]{0:T(128)S(1)}, f32[4]{0:T(128)}, u32[]{:S(2)}) copy-start(f32[4]{0:T(128)} %convert_element_type.116) | copy-start | bytes 52

commit v15 on v8

--- a/solution.py
+++ b/solution.py
@@ -187,13 +187,20 @@
     else:
         head = lax.ppermute(cells[length - halo :], "seq", [(i, i + 1) for i in range(ends)])
         tail = lax.ppermute(cells[:halo], "seq", [(i + 1, i) for i in range(ends)])
-    rows = picks[:, None] * TB - halo + jnp.arange(span)[None, :]
-    inside = jnp.take(cells, jnp.clip(rows, 0, length - 1), axis=0)
-    edge_rows = jnp.concatenate([head, tail], axis=0)
-    edge_index = jnp.where(rows < 0, rows + halo, rows - length + halo)
-    outside = jnp.take(edge_rows, jnp.clip(edge_index, 0, 2 * halo - 1), axis=0)
-    in_range = jnp.logical_and(rows >= 0, rows < length)
-    windows = jnp.where(in_range[..., None], inside, outside)
+    last = per_block - 1
+    stacked = cells.reshape(per_block, TB * width)
+    block_ids = jnp.arange(per_block)[None, :]
+
+    def select(offset, part):
+        choose = (picks[:, None] + offset == block_ids).astype(cells.dtype)
+        return jnp.dot(choose, part, preferred_element_type=jnp.float32)
+
+    middle = select(0, stacked).reshape(held, TB, width)
+    prev_tail = select(-1, stacked[:, (TB - halo) * width :]).reshape(held, halo, width)
+    next_head = select(1, stacked[:, : halo * width]).reshape(held, halo, width)
+    lower = jnp.where((picks == 0)[:, None, None], head[None].astype(jnp.float32), prev_tail)
+    upper = jnp.where((picks == last)[:, None, None], tail[None].astype(jnp.float32), next_head)
+    windows = jnp.concatenate([lower, middle, upper], axis=1).astype(cells.dtype)
     x_float = windows.astype(jnp.float32)
     act = jax.nn.gelu(x_float).astype(jnp.bfloat16)
     conv_out = jnp.einsum("hti,oi->hto", act[:, 0:TB], conv_weight[0], preferred_element_type=jnp.float32)
@@ -279,7 +286,9 @@
     grads = grads.reshape(groups, owners * n_sides, TB, narrow)
     flat_sides = sides.reshape(groups, owners * n_sides)
     same_block = flat_sides[:, :, None] == flat_sides[:, None, :]
-    total = jnp.sum(jnp.where(same_block[..., None, None], grads[:, None], 0.0), axis=2)
+    total = jnp.einsum(
+        "qab,qbtd->qatd", same_block.astype(jnp.float32), grads, precision=lax.Precision.HIGHEST
+    )
     earlier = jnp.arange(owners * n_sides)[None, :] < jnp.arange(owners * n_sides)[:, None]
     first = jnp.logical_not(jnp.any(jnp.logical_and(same_block, earlier[None]), axis=-1))
     scaling = 1.25 * keep_all.astype(jnp.float32)

time: 51.5 us -> 44.9 us (0.87)
  local copies, waits for them, and re-layouts: 12.8 us -> 9.45 us
  other arithmetic: 7.26 us -> 4.14 us
  waiting for transfers between devices: 14 us -> 11.9 us
  matrix products: 4.6 us -> 5.87 us
  starting transfers between devices: 11.2 us -> 12.1 us
    gather x6 -> x0, local copies, waits for them, and re-layouts: 4.31 us -> none  [the longest x3 3.02 us: sparse_path(): inside = jnp.take(cells, jnp.clip(rows, 0, length - 1), axis=0)]
    ppermute x3, waiting for transfers between devices: 3.28 us -> 1.21 us  [axis_sum(): lax.ppermute(value, axis, [(i, (i + shift) % count) for i in range(count)])]
    another operation x0 -> x2, local copies, waits for them, and re-layouts: none -> 1.98 us  [the longest x1 1.89 us: sparse_path(): stacked = cells.reshape(per_block, TB * width)]
    reduce_sum x1 -> x0, other arithmetic: 1.4 us -> none  [sparse_path(): jnp.sum(jnp.where(same_block[..., None, None], grads[:, None], 0.0), axis=2)]
    dot_general x0 -> x4, matrix products: none -> 1.23 us  [the longest x3 0.79 us: select(): return jnp.dot(choose, part, preferred_element_type=jnp.float32)]
    ppermute x3, starting transfers between devices: 4.66 us -> 5.56 us  [axis_sum(): lax.ppermute(value, axis, [(i, (i + shift) % count) for i in range(count)])]
    slice x1, local copies, waits for them, and re-layouts: 0.97 us -> 0.21 us  [sparse_path(): own_sides = jnp.concatenate([tiles[0, ..., 0], tiles[0, ..., 1]], axis=-1)]
    concatenate x1, local copies, waits for them, and re-layouts: 0.76 us -> 0.08 us  [sparse_path(): jnp.concatenate([tiles.reshape(-1), counts.reshape(-1), keep.reshape(-1)])]
  transfers between devices with their start and end apart: 5 -> 5, of which waited for: 2 -> 2; matrix products, arithmetic and copies ran while one was open for 18% -> 15% of each run, Pallas kernels for 0% -> 0%
where the time goes in v15:
time: 44.9 us; the launch traced here: 44.6 us
  starting transfers between devices  12.1 us (27%)
  waiting for transfers between devices  11.9 us (27%)
  local copies, waits for them, and re-layouts  9.45 us (21%)
  matrix products  5.87 us (13%)
  other arithmetic  4.14 us (9%)
  between operations  1.13 us (3%)
    all_to_all x1, waiting for transfers between devices, sparse_path(): incoming = lax.all_to_all(outgoing, ('seq', 'dp'), 0, 0, tiled=True)  10.7 us
    ppermute x3, starting transfers between devices, axis_sum(): lax.ppermute(value, axis, [(i, (i + shift) % count) for i in range(count)])  5.56 us
    all_to_all x1, starting transfers between devices, sparse_path(): incoming = lax.all_to_all(outgoing, ('seq', 'dp'), 0, 0, tiled=True)  3.54 us
    ppermute x1, starting transfers between devices, sparse_path(): lax.ppermute(jnp.concatenate([cells[length - halo:], cells[:halo]]), 'seq...  3 us
    dot_general x5, matrix products, sparse_path(): jnp.einsum('qato,qati->oi', dconv, act_sides[:, :, offset:offset + TB], p...  2.25 us
    another operation x1, local copies, waits for them, and re-layouts, sparse_path(): stacked = cells.reshape(per_block, TB * width)  1.89 us
    ppermute x3, waiting for transfers between devices, axis_sum(): lax.ppermute(value, axis, [(i, (i + shift) % count) for i in range(count)])  1.21 us
    unnamed x10, local copies, waits for them, and re-layouts  1.13 us
  transfers between devices with their start and end apart: 5, of which 2 were waited for; matrix products, arithmetic and copies ran while one was open for 15% of the time, Pallas kernels for 0%

profile of v15, /device:TPU:0, one launch (start us, length us, event | category | flops | bytes accessed | tf_op | source)
XLA Modules:
  0.0 44.6 jit_solution(404791762248108090)
XLA Ops:
  0.0 0.7 %slice_bitcast_fusion.1 = (bf16[2,768]{1,0:T(2,128)(2,1)S(1)}, bf16[2,768]{1,0:T(2,128)(2,1)S(1)}) fusion(bf16[1,1024,768]{2,1,0:T(8,128)(2,1)} %param.6), kind=kLoop, calls=%fused_computation.157 | loop fusion | bytes 12288 | tf_op jit(solution)/shard_map/slice | solution.py:183
  0.7 3.0 %collective-permute-start = (bf16[4,768]{1,0:T(4,128)(2,1)S(1)}, bf16[4,768]{1,0:T(4,128)(2,1)S(1)}, u32[]{:S(2)}, u32[]{:S(2)}) collective-permute-start(bf16[4,768]{1,0:T(4,128)(2,1)S(1)} %pad_maximum_fusion.1), channel_id=1, source_target_pairs={{0,16},{16,0},{1,17},{17,1},{2,18},{18,2},{3,19},{19,3},{4,20},{20... | collective-permute-start | bytes 18440 | tf_op jit(solution)/shard_map/ppermute | solution.py:182
  3.8 1.9 %reshape_squeeze.3 = bf16[32,24576]{1,0:T(8,128)(2,1)S(1)} reshape(bf16[1,1024,768]{2,1,0:T(8,128)(2,1)} %param.6) | data formatting | bytes 3145728 | tf_op jit(solution)/shard_map/reshape;squeeze | solution.py:191
  5.7 0.2 slice_reduce_fusion.1
  6.0 0.2 convert_reduce_fusion.1
  6.2 0.2 fusion.97
  6.7 0.2 fusion.68
  6.9 0.2 fusion.66
  7.1 0.4 fusion
  8.6 0.3 concatenate.140
  9.2 0.2 fusion.32
  9.6 0.3 copy-done.3
  10.0 0.2 fusion.38
  10.2 0.2 convolution_add_fusion.3
  10.5 0.2 convolution_add_fusion.2
  10.7 0.2 convolution_add_fusion.1
  11.0 0.3 fusion.10
  11.3 0.1 broadcast_in_dim.114
  11.5 0.3 fusion.33
  11.9 0.5 %reshape.813 = bf16[8,108,128]{2,1,0:T(8,128)(2,1)S(1)} reshape(bf16[8,4,36,96]{3,2,1,0:T(8,128)(2,1)S(1)} %fusion.33) | data formatting | bytes 442368 | tf_op jit(solution)/shard_map/reshape | solution.py:218
  12.5 0.9 %fusion.17 = bf16[8,352,128]{2,1,0:T(8,128)(2,1)} fusion(bf16[8,49,128]{2,1,0:T(8,128)(2,1)S(1)} %broadcast_in_dim.123, bf16[8,108,128]{2,1,0:T(8,128)(2,1)S(1)} %reshape.813, bf16[8,192,128]{2,1,0:T(8,128)(2,1)S(1)} %broadcast_in_dim.115), kind=kLoop, calls=%fused_computation.37 | loop fusion | flops 3604480 | bytes 1435648 | tf_op jit(solution)/shard_map/concatenate | solution.py:231
  13.4 3.5 %all-to-all-start = ((bf16[8,352,128]{2,1,0:T(8,128)(2,1)}), bf16[8,352,128]{2,1,0:T(8,128)(2,1)S(1)}, u32[]{:S(2)}, u32[]{:S(2)}) async-start(bf16[8,352,128]{2,1,0:T(8,128)(2,1)} %fusion.17), calls=%async_computation | async-start | bytes 1441792 | tf_op jit(solution)/shard_map/all_to_all | solution.py:240
  17.1 10.7 %all-to-all-done = bf16[8,352,128]{2,1,0:T(8,128)(2,1)S(1)} async-done(((bf16[8,352,128]{2,1,0:T(8,128)(2,1)}), bf16[8,352,128]{2,1,0:T(8,128)(2,1)S(1)}, u32[]{:S(2)}, u32[]{:S(2)}) %all-to-all-start) | async-done | bytes 720928 | tf_op jit(solution)/shard_map/all_to_all | solution.py:240
  28.3 0.3 convert_reduce_fusion
  29.4 0.3 reshape_reshape.6
  29.8 0.6 %gather_fusion = bf16[32,32,192]{2,1,0:T(8,128)(2,1)S(1)} fusion(bf16[32,32,192]{2,1,0:T(8,128)(2,1)S(1)} %reshape_reshape.6, s32[1024]{0:T(1024)S(1)} %pad_clamp_fusion.1), kind=kCustom, calls=%fused_computation | custom fusion | bytes 786560 | tf_op jit(solution)/shard_map/jit(_take)/gather | solution.py:264
  30.4 0.1 broadcast_select_fusion
  30.5 0.2 fusion.59
  30.9 1.6 %collective-permute-start.1 = (f32[128,128]{1,0:T(8,128)S(1)}, f32[128,128]{1,0:T(8,128)S(1)}, u32[]{:S(2)}, u32[]{:S(2)}) collective-permute-start(f32[128,128]{1,0:T(8,128)S(1)} %reshape.816), channel_id=1, source_target_pairs={{0,4},{4,8},{8,12},{12,0},{1,5},{5,9},{9,13},{13,1},{2,6},{6,10},{... | collective-permute-start | bytes 196616 | tf_op jit(solution)/shard_map/ppermute | solution.py:145
  32.5 2.6 %collective-permute-start.2 = (f32[128,128]{1,0:T(8,128)S(1)}, f32[128,128]{1,0:T(8,128)S(1)}, u32[]{:S(2)}, u32[]{:S(2)}) collective-permute-start(f32[128,128]{1,0:T(8,128)S(1)} %reshape.816), channel_id=1, source_target_pairs={{0,8},{4,12},{8,0},{12,4},{1,9},{5,13},{9,1},{13,5},{2,10},{6,14},... | collective-permute-start | bytes 196616 | tf_op jit(solution)/shard_map/ppermute | solution.py:145
  35.1 1.3 %collective-permute-start.3 = (f32[128,128]{1,0:T(8,128)S(1)}, f32[128,128]{1,0:T(8,128)S(1)}, u32[]{:S(2)}, u32[]{:S(2)}) collective-permute-start(f32[128,128]{1,0:T(8,128)S(1)} %reshape.816), channel_id=1, source_target_pairs={{0,12},{4,0},{8,4},{12,8},{1,13},{5,1},{9,5},{13,9},{2,14},{6,2},{... | collective-permute-start | bytes 196616 | tf_op jit(solution)/shard_map/ppermute | solution.py:145
  36.4 0.2 fusion.107
  36.9 0.5 %reshape_reshape.7 = bf16[32,36,96]{2,1,0:T(8,128)(2,1)S(1)} reshape(bf16[8,108,128]{2,1,0:T(8,128)(2,1)S(1)} %slice.184) | data formatting | bytes 442368 | tf_op jit(solution)/shard_map/reshape;reshape | solution.py:245
  37.3 0.1 reshape.817
  37.6 0.2 fusion.73
  37.8 0.6 %gather_fusion.1 = bf16[32,36,96]{2,1,0:T(8,128)(2,1)S(1)} fusion(bf16[32,36,96]{2,1,0:T(8,128)(2,1)S(1)} %reshape_reshape.7, s32[1024]{0:T(1024)S(1)} %pad_clamp_fusion), kind=kCustom, calls=%fused_computation.1 | custom fusion | bytes 442496 | tf_op jit(solution)/shard_map/jit(_take)/gather | solution.py:297
  38.5 0.2 multiply_reduce_fusion
  38.7 1.2 %collective-permute-done.2 = f32[128,128]{1,0:T(8,128)S(1)} collective-permute-done((f32[128,128]{1,0:T(8,128)S(1)}, f32[128,128]{1,0:T(8,128)S(1)}, u32[]{:S(2)}, u32[]{:S(2)}) %collective-permute-start.2) | collective-permute-done | bytes 65568 | tf_op jit(solution)/shard_map/ppermute | solution.py:145
  39.9 0.1 div.78
  40.1 0.4 convolution_convert_fusion.1
  40.5 0.5 %convolution_convert_fusion = bf16[4,2,2,32,192]{4,3,2,1,0:T(8,128)(2,1)S(1)} fusion(bf16[4,2,4,32,192]{4,3,2,1,0:T(8,128)(2,1)S(1)} %broadcast_select_fusion, f32[4,2,2,32,32]{4,3,2,1,0:T(8,128)S(1)} %div.78, f32[2,4,2,32,32]{4,3,2,1,0:T(8,128)S(1)} %reshape.817, f32[4]{0:T(128)S(1)} %convert_element_type.117, f32[4,2,2]{2,1,0:T(2,128)S(1)} %compare_select_fusion.6), kind=kOutput, calls=%fused_computation.12 | convolution fusion | flops 37896192 | bytes 987648 | tf_op jit(solution)/shard_map/qocij,qocid->qocjd/dot_general | solution.py:284
  41.1 0.4 fusion.7
  41.5 0.3 fusion.15
  41.9 0.3 fusion.14
  42.2 0.3 fusion.13
  42.5 0.3 fusion.12
  42.9 0.8 %copy-done.4 = f32[5,192,96]{2,1,0:T(8,128)} copy-done((f32[5,192,96]{2,1,0:T(8,128)}, f32[5,192,96]{2,1,0:T(8,128)S(1)}, u32[]{:S(2)}) %copy-start.4) | copy-done | bytes 368664
  43.6 1.0 %fusion.11 = f32[5,192,96]{2,1,0:T(8,128)} fusion(f32[5,192,96]{2,1,0:T(8,128)} %copy-done.4, bf16[4,8,32,192]{3,1,2,0:T(8,128)(2,1)S(1)} %fusion.7, bf16[4,8,36,96]{3,2,0,1:T(8,128)(2,1)S(1)} %copy_select_fusion), kind=kOutput, calls=%fused_computation.26 | convolution fusion | flops 37748736 | bytes 884736 | tf_op jit(solution)/shard_map/qato,qati->oi/dot_general | solution.py:300
  (80 shorter events, 3.6 us)
Async XLA Ops:
  0.7 8.2 %collective-permute-start = (bf16[4,768]{1,0:T(4,128)(2,1)S(1)}, bf16[4,768]{1,0:T(4,128)(2,1)S(1)}, u32[]{:S(2)}, u32[]{:S(2)}) collective-permute-start(bf16[4,768]{1,0:T(4,128)(2,1)S(1)} %pad_maximum_fusion.1), channel_id=1, source_target_pairs={{0,16},{16,0},{1,17},{17,1},{2,18},{18,2},{3,19},{19,3},{4,20},{20... | collective-permute-start | bytes 18440 | tf_op jit(solution)/shard_map/ppermute | solution.py:182
  3.8 1.9 %copy-start = (s32[1,2,2,2]{3,2,1,0:T(2,128)S(1)}, s32[1,2,2,2]{3,2,1,0:T(2,128)}, u32[]{:S(2)}) copy-start(s32[1,2,2,2]{3,2,1,0:T(2,128)} %param.9) | copy-start | bytes 100
  5.7 2.4 %copy-start.1 = (f32[1,1,2,1024]{3,2,1,0:T(2,128)S(1)}, f32[1,1,2,1024]{3,2,1,0:T(2,128)}, u32[]{:S(2)}) copy-start(f32[1,1,2,1024]{3,2,1,0:T(2,128)} %param.11) | copy-start | bytes 24580
  5.7 2.5 %copy-start.2 = (s32[1,2]{1,0:T(1,128)S(1)}, s32[1,2]{1,0:T(1,128)}, u32[]{:S(2)}) copy-start(s32[1,2]{1,0:T(1,128)} %param.10) | copy-start | bytes 28
  8.6 1.4 %copy-start.3 = (bf16[5,192,768]{2,1,0:T(8,128)(2,1)S(1)}, bf16[5,192,768]{2,1,0:T(8,128)(2,1)}, u32[]{:S(2)}) copy-start(bf16[5,192,768]{2,1,0:T(8,128)(2,1)} %param.7) | copy-start | bytes 4423684
  13.4 14.4 %all-to-all-start = ((bf16[8,352,128]{2,1,0:T(8,128)(2,1)}), bf16[8,352,128]{2,1,0:T(8,128)(2,1)S(1)}, u32[]{:S(2)}, u32[]{:S(2)}) async-start(bf16[8,352,128]{2,1,0:T(8,128)(2,1)} %fusion.17), calls=%async_computation | async-start | bytes 1441792 | tf_op jit(solution)/shard_map/all_to_all | solution.py:240
  30.9 7.9 %collective-permute-start.1 = (f32[128,128]{1,0:T(8,128)S(1)}, f32[128,128]{1,0:T(8,128)S(1)}, u32[]{:S(2)}, u32[]{:S(2)}) collective-permute-start(f32[128,128]{1,0:T(8,128)S(1)} %reshape.816), channel_id=1, source_target_pairs={{0,4},{4,8},{8,12},{12,0},{1,5},{5,9},{9,13},{13,1},{2,6},{6,10},{... | collective-permute-start | bytes 196616 | tf_op jit(solution)/shard_map/ppermute | solution.py:145
  32.5 7.4 %collective-permute-start.2 = (f32[128,128]{1,0:T(8,128)S(1)}, f32[128,128]{1,0:T(8,128)S(1)}, u32[]{:S(2)}, u32[]{:S(2)}) collective-permute-start(f32[128,128]{1,0:T(8,128)S(1)} %reshape.816), channel_id=1, source_target_pairs={{0,8},{4,12},{8,0},{12,4},{1,9},{5,13},{9,1},{13,5},{2,10},{6,14},... | collective-permute-start | bytes 196616 | tf_op jit(solution)/shard_map/ppermute | solution.py:145
  35.1 4.8 %collective-permute-start.3 = (f32[128,128]{1,0:T(8,128)S(1)}, f32[128,128]{1,0:T(8,128)S(1)}, u32[]{:S(2)}, u32[]{:S(2)}) collective-permute-start(f32[128,128]{1,0:T(8,128)S(1)} %reshape.816), channel_id=1, source_target_pairs={{0,12},{4,0},{8,4},{12,8},{1,13},{5,1},{9,5},{13,9},{2,14},{6,2},{... | collective-permute-start | bytes 196616 | tf_op jit(solution)/shard_map/ppermute | solution.py:145
  42.9 0.8 %copy-start.4 = (f32[5,192,96]{2,1,0:T(8,128)}, f32[5,192,96]{2,1,0:T(8,128)S(1)}, u32[]{:S(2)}) copy-start(f32[5,192,96]{2,1,0:T(8,128)S(1)} %fusion.12) | copy-start | bytes 1105924

commit v16 on v15

--- a/solution.py
+++ b/solution.py
@@ -188,16 +188,12 @@
         head = lax.ppermute(cells[length - halo :], "seq", [(i, i + 1) for i in range(ends)])
         tail = lax.ppermute(cells[:halo], "seq", [(i + 1, i) for i in range(ends)])
     last = per_block - 1
-    stacked = cells.reshape(per_block, TB * width)
-    block_ids = jnp.arange(per_block)[None, :]
-
-    def select(offset, part):
-        choose = (picks[:, None] + offset == block_ids).astype(cells.dtype)
-        return jnp.dot(choose, part, preferred_element_type=jnp.float32)
-
-    middle = select(0, stacked).reshape(held, TB, width)
-    prev_tail = select(-1, stacked[:, (TB - halo) * width :]).reshape(held, halo, width)
-    next_head = select(1, stacked[:, : halo * width]).reshape(held, halo, width)
+    stacked = cells.reshape(per_block, TB, width)
+    middle = jnp.take(stacked, picks, axis=0, mode="clip").astype(jnp.float32)
+    prev_tail = jnp.take(stacked[:, TB - halo :], jnp.maximum(picks - 1, 0), axis=0, mode="clip")
+    next_head = jnp.take(stacked[:, :halo], jnp.minimum(picks + 1, last), axis=0, mode="clip")
+    prev_tail = prev_tail.astype(jnp.float32)
+    next_head = next_head.astype(jnp.float32)
     lower = jnp.where((picks == 0)[:, None, None], head[None].astype(jnp.float32), prev_tail)
     upper = jnp.where((picks == last)[:, None, None], tail[None].astype(jnp.float32), next_head)
     windows = jnp.concatenate([lower, middle, upper], axis=1).astype(cells.dtype)

time: 44.9 us -> 51.4 us (1.14)
  local copies, waits for them, and re-layouts: 9.45 us -> 13.8 us
  waiting for transfers between devices: 11.9 us -> 14 us
  other arithmetic: 4.14 us -> 5.75 us
  starting transfers between devices: 12.1 us -> 11.2 us
  matrix products: 5.87 us -> 5.07 us
    gather x0 -> x3, local copies, waits for them, and re-layouts: none -> 3.14 us  [the longest x1 1.97 us: sparse_path(): middle = jnp.take(stacked, picks, axis=0, mode='clip').astype(jnp.float32)]
    ppermute x3, waiting for transfers between devices: 1.21 us -> 3.29 us  [axis_sum(): lax.ppermute(value, axis, [(i, (i + shift) % count) for i in range(count)])]
    another operation x1 -> x0, local copies, waits for them, and re-layouts: 1.89 us -> none  [sparse_path(): stacked = cells.reshape(per_block, TB * width)]
    slice x0 -> x1, local copies, waits for them, and re-layouts: none -> 1.28 us  [sparse_path(): stacked[:, TB - halo:]]
    ppermute x3, starting transfers between devices: 5.56 us -> 4.66 us  [axis_sum(): lax.ppermute(value, axis, [(i, (i + shift) % count) for i in range(count)])]
    another operation x4 -> x5, other arithmetic: 0.22 us -> 1.04 us
    dot_general x3 -> x0, matrix products: 0.79 us -> none  [select(): return jnp.dot(choose, part, preferred_element_type=jnp.float32)]
    concatenate x1, other arithmetic: 0.08 us -> 0.85 us  [sparse_path(): jnp.concatenate(pieces + [small]).astype(jnp.bfloat16).reshape(1, -1)]
  transfers between devices with their start and end apart: 5 -> 5, of which waited for: 2 -> 2; matrix products, arithmetic and copies ran while one was open for 15% -> 23% of each run, Pallas kernels for 0% -> 0%
where the time goes in v16:
time: 51.4 us; the launch traced here: 50.9 us
  waiting for transfers between devices  14 us (27%)
  local copies, waits for them, and re-layouts  13.8 us (27%)
  starting transfers between devices  11.2 us (22%)
  other arithmetic  5.75 us (11%)
  matrix products  5.07 us (10%)
  between operations  1.14 us (2%)
    all_to_all x1, waiting for transfers between devices, sparse_path(): incoming = lax.all_to_all(outgoing, ('seq', 'dp'), 0, 0, tiled=True)  10.7 us
    ppermute x3, starting transfers between devices, axis_sum(): lax.ppermute(value, axis, [(i, (i + shift) % count) for i in range(count)])  4.66 us
    all_to_all x1, starting transfers between devices, sparse_path(): incoming = lax.all_to_all(outgoing, ('seq', 'dp'), 0, 0, tiled=True)  3.54 us
    ppermute x3, waiting for transfers between devices, axis_sum(): lax.ppermute(value, axis, [(i, (i + shift) % count) for i in range(count)])  3.29 us
    ppermute x1, starting transfers between devices, sparse_path(): lax.ppermute(jnp.concatenate([cells[length - halo:], cells[:halo]]), 'seq...  3 us
    dot_general x5, matrix products, sparse_path(): jnp.einsum('qato,qati->oi', dconv, act_sides[:, :, offset:offset + TB], p...  2.25 us
    gather x1, local copies, waits for them, and re-layouts, sparse_path(): middle = jnp.take(stacked, picks, axis=0, mode='clip').astype(jnp.float32)  1.97 us
    slice x1, local copies, waits for them, and re-layouts, sparse_path(): stacked[:, TB - halo:]  1.28 us
  transfers between devices with their start and end apart: 5, of which 2 were waited for; matrix products, arithmetic and copies ran while one was open for 23% of the time, Pallas kernels for 0%

profile of v16, /device:TPU:0, one launch (start us, length us, event | category | flops | bytes accessed | tf_op | source)
XLA Modules:
  0.0 50.9 jit_solution(8910710414779831179)
XLA Ops:
  0.0 0.7 %slice_bitcast_fusion.1 = (bf16[2,768]{1,0:T(2,128)(2,1)S(1)}, bf16[2,768]{1,0:T(2,128)(2,1)S(1)}) fusion(bf16[1,1024,768]{2,1,0:T(8,128)(2,1)} %param.6), kind=kLoop, calls=%fused_computation.155 | loop fusion | bytes 12288 | tf_op jit(solution)/shard_map/slice | solution.py:183
  0.7 3.0 %collective-permute-start = (bf16[4,768]{1,0:T(4,128)(2,1)S(1)}, bf16[4,768]{1,0:T(4,128)(2,1)S(1)}, u32[]{:S(2)}, u32[]{:S(2)}) collective-permute-start(bf16[4,768]{1,0:T(4,128)(2,1)S(1)} %pad_maximum_fusion.1), channel_id=1, source_target_pairs={{0,16},{16,0},{1,17},{17,1},{2,18},{18,2},{3,19},{19,3},{4,20},{20... | collective-permute-start | bytes 18440 | tf_op jit(solution)/shard_map/ppermute | solution.py:182
  3.8 0.8 %concatenate.142 = s32[8]{0:T(128)S(1)} reshape(s32[1,2,2,2]{3,2,1,0:T(2,128)} %param.9) | data formatting | bytes 64 | tf_op jit(solution)/shard_map/concatenate | solution.py:224
  4.5 1.0 %slice_reduce_fusion.1 = (s32[2,2]{1,0:T(2,128)S(1)}, s32[2,2]{1,0:T(2,128)S(1)}) fusion(s32[1,2,2,2]{3,2,1,0:T(2,128)} %param.9), kind=kLoop, calls=%fused_computation.175 | loop fusion | bytes 64 | tf_op jit(solution)/shard_map/slice | solution.py:166
  5.6 0.2 convert_reduce_fusion.1
  5.8 0.2 fusion.88
  7.2 0.7 %reduce-precision_convert_fusion.1 = (bf16[2048]{0:T(1024)(128)(2,1)S(1)}, bf16[2048]{0:T(1024)(128)(2,1)S(1)}, bf16[2048]{0:T(1024)(128)(2,1)S(1)}) fusion(f32[1,8,2,128]{3,2,1,0:T(2,128)} %bitcast.123), kind=kLoop, calls=%fused_computation.116 | loop fusion | flops 16384 | bytes 20480 | tf_op jit(solution)/shard_map/convert.13
  8.0 1.3 %fusion.94 = (bf16[32,2,768]{2,1,0:T(2,128)(2,1)S(1)}, bf16[32,2,768]{2,1,0:T(2,128)(2,1)S(1)}) fusion(bf16[32,32,768]{2,1,0:T(8,128)(2,1)} %bitcast.116), kind=kLoop, calls=%fused_computation.202 | loop fusion | bytes 393216 | tf_op jit(solution)/shard_map/slice | solution.py:193
  9.2 0.8 %fusion.91 = bf16[1,11]{1,0:T(2,128)(2,1)S(1)} fusion(s32[1]{0:T(128)S(6)} %copy.164, s32[2]{0:T(128)} %bitcast.128, s32[8]{0:T(128)S(1)} %concatenate.142), kind=kLoop, calls=%fused_computation.194 | loop fusion | flops 44 | bytes 66 | tf_op jit(solution)/shard_map/concatenate | solution.py:225
  10.6 2.0 %gather_fusion.1 = bf16[4,32,768]{2,1,0:T(8,128)(2,1)S(1)} fusion(bf16[32,32,768]{2,1,0:T(8,128)(2,1)} %bitcast.117, s32[1024]{0:T(1024)S(1)} %pad_clamp_fusion.3), kind=kCustom, calls=%fused_computation.1 | custom fusion | bytes 393232 | tf_op jit(solution)/shard_map/jit(_take)/gather | solution.py:192
  12.6 0.6 %gather_fusion.2 = bf16[4,2,768]{2,1,0:T(2,128)(2,1)S(1)} fusion(bf16[32,2,768]{2,1,0:T(2,128)(2,1)S(1)} %get-tuple-element.12, s32[1024]{0:T(1024)S(1)} %pad_clamp_fusion.2), kind=kCustom, calls=%fused_computation.2 | custom fusion | bytes 24592 | tf_op jit(solution)/shard_map/jit(_take)/gather | solution.py:194
  13.2 0.6 %gather_fusion = bf16[4,2,768]{2,1,0:T(2,128)(2,1)S(1)} fusion(bf16[32,2,768]{2,1,0:T(2,128)(2,1)S(1)} %get-tuple-element.11, s32[1024]{0:T(1024)S(1)} %pad_clamp_fusion.4), kind=kCustom, calls=%fused_computation | custom fusion | bytes 24592 | tf_op jit(solution)/shard_map/jit(_take)/gather | solution.py:193
  13.9 0.3 convert_element_type.132
  14.7 0.2 fusion.29
  15.0 0.2 fusion.35
  15.3 0.2 convolution_add_fusion.3
  15.5 0.2 convolution_add_fusion.2
  15.8 0.2 convolution_add_fusion.1
  16.2 0.3 fusion.30
  16.6 0.5 reshape.819
  17.1 0.3 fusion.7
  17.4 0.1 broadcast_in_dim.118
  17.6 0.9 %fusion.14 = bf16[8,352,128]{2,1,0:T(8,128)(2,1)} fusion(bf16[8,49,128]{2,1,0:T(8,128)(2,1)S(1)} %broadcast_in_dim.127, bf16[8,108,128]{2,1,0:T(8,128)(2,1)S(1)} %reshape.819, bf16[8,192,128]{2,1,0:T(8,128)(2,1)S(1)} %broadcast_in_dim.119), kind=kLoop, calls=%fused_computation.37 | loop fusion | flops 3604480 | bytes 1435648 | tf_op jit(solution)/shard_map/concatenate | solution.py:227
  18.5 3.5 %all-to-all-start = ((bf16[8,352,128]{2,1,0:T(8,128)(2,1)}), bf16[8,352,128]{2,1,0:T(8,128)(2,1)S(1)}, u32[]{:S(2)}, u32[]{:S(2)}) async-start(bf16[8,352,128]{2,1,0:T(8,128)(2,1)} %fusion.14), calls=%async_computation | async-start | bytes 1441792 | tf_op jit(solution)/shard_map/all_to_all | solution.py:236
  22.3 10.7 %all-to-all-done = bf16[8,352,128]{2,1,0:T(8,128)(2,1)S(1)} async-done(((bf16[8,352,128]{2,1,0:T(8,128)(2,1)}), bf16[8,352,128]{2,1,0:T(8,128)(2,1)S(1)}, u32[]{:S(2)}, u32[]{:S(2)}) %all-to-all-start) | async-done | bytes 720928 | tf_op jit(solution)/shard_map/all_to_all | solution.py:236
  33.1 0.2 fusion.96
  33.8 0.3 convert_reduce_fusion
  34.9 0.3 reshape_reshape.6
  35.3 0.6 %gather_fusion.3 = bf16[32,32,192]{2,1,0:T(8,128)(2,1)S(1)} fusion(bf16[32,32,192]{2,1,0:T(8,128)(2,1)S(1)} %reshape_reshape.6, s32[1024]{0:T(1024)S(1)} %get-tuple-element.32), kind=kCustom, calls=%fused_computation.3 | custom fusion | bytes 786560 | tf_op jit(solution)/shard_map/jit(_take)/gather | solution.py:260
  35.8 0.1 broadcast_select_fusion
  36.0 0.2 fusion.56
  36.3 3.7 %collective-permute-start.3 = (f32[128,128]{1,0:T(8,128)S(1)}, f32[128,128]{1,0:T(8,128)S(1)}, u32[]{:S(2)}, u32[]{:S(2)}) collective-permute-start(f32[128,128]{1,0:T(8,128)S(1)} %reshape.822), channel_id=1, source_target_pairs={{0,12},{4,0},{8,4},{12,8},{1,13},{5,1},{9,5},{13,9},{2,14},{6,2},{... | collective-permute-start | bytes 196616 | tf_op jit(solution)/shard_map/ppermute | solution.py:145
  40.0 1.0 %collective-permute-start.1 = (f32[128,128]{1,0:T(8,128)S(1)}, f32[128,128]{1,0:T(8,128)S(1)}, u32[]{:S(2)}, u32[]{:S(2)}) collective-permute-start(f32[128,128]{1,0:T(8,128)S(1)} %reshape.822), channel_id=1, source_target_pairs={{0,4},{4,8},{8,12},{12,0},{1,5},{5,9},{9,13},{13,1},{2,6},{6,10},{... | collective-permute-start | bytes 196616 | tf_op jit(solution)/shard_map/ppermute | solution.py:145
  41.0 0.5 reshape_reshape.7
  41.5 0.2 fusion.66
  41.9 0.1 reshape.823
  42.0 0.6 %gather_fusion.4 = bf16[32,36,96]{2,1,0:T(8,128)(2,1)S(1)} fusion(bf16[32,36,96]{2,1,0:T(8,128)(2,1)S(1)} %reshape_reshape.7, s32[1024]{0:T(1024)S(1)} %get-tuple-element.31), kind=kCustom, calls=%fused_computation.4 | custom fusion | bytes 442496 | tf_op jit(solution)/shard_map/jit(_take)/gather | solution.py:293
  42.8 0.2 multiply_reduce_fusion
  42.9 3.3 %collective-permute-done.2 = f32[128,128]{1,0:T(8,128)S(1)} collective-permute-done((f32[128,128]{1,0:T(8,128)S(1)}, f32[128,128]{1,0:T(8,128)S(1)}, u32[]{:S(2)}, u32[]{:S(2)}) %collective-permute-start.2) | collective-permute-done | bytes 65568 | tf_op jit(solution)/shard_map/ppermute | solution.py:145
  46.4 0.5 convolution_convert_fusion
  46.9 0.4 convolution_convert_fusion.1
  47.4 0.4 fusion.4
  47.9 0.3 fusion.12
  48.2 0.3 fusion.11
  48.5 0.3 fusion.10
  48.8 0.3 fusion.9
  49.2 0.8 %copy-done.1 = f32[5,192,96]{2,1,0:T(8,128)} copy-done((f32[5,192,96]{2,1,0:T(8,128)}, f32[5,192,96]{2,1,0:T(8,128)S(1)}, u32[]{:S(2)}) %copy-start.1) | copy-done | bytes 368664
  49.9 1.0 %fusion.8 = f32[5,192,96]{2,1,0:T(8,128)} fusion(f32[5,192,96]{2,1,0:T(8,128)} %copy-done.1, bf16[4,8,32,192]{3,1,2,0:T(8,128)(2,1)S(1)} %fusion.4, bf16[4,8,36,96]{3,2,0,1:T(8,128)(2,1)S(1)} %copy_select_fusion), kind=kOutput, calls=%fused_computation.26 | convolution fusion | flops 37748736 | bytes 884736 | tf_op jit(solution)/shard_map/qato,qati->oi/dot_general | solution.py:296
  (82 shorter events, 4.4 us)
Async XLA Ops:
  0.7 13.5 %collective-permute-start = (bf16[4,768]{1,0:T(4,128)(2,1)S(1)}, bf16[4,768]{1,0:T(4,128)(2,1)S(1)}, u32[]{:S(2)}, u32[]{:S(2)}) collective-permute-start(bf16[4,768]{1,0:T(4,128)(2,1)S(1)} %pad_maximum_fusion.1), channel_id=1, source_target_pairs={{0,16},{16,0},{1,17},{17,1},{2,18},{18,2},{3,19},{19,3},{4,20},{20... | collective-permute-start | bytes 18440 | tf_op jit(solution)/shard_map/ppermute | solution.py:182
  9.2 5.8 %copy-start = (bf16[5,192,768]{2,1,0:T(8,128)(2,1)S(1)}, bf16[5,192,768]{2,1,0:T(8,128)(2,1)}, u32[]{:S(2)}) copy-start(bf16[5,192,768]{2,1,0:T(8,128)(2,1)} %param.7) | copy-start | bytes 4423684
  18.5 14.4 %all-to-all-start = ((bf16[8,352,128]{2,1,0:T(8,128)(2,1)}), bf16[8,352,128]{2,1,0:T(8,128)(2,1)S(1)}, u32[]{:S(2)}, u32[]{:S(2)}) async-start(bf16[8,352,128]{2,1,0:T(8,128)(2,1)} %fusion.14), calls=%async_computation | async-start | bytes 1441792 | tf_op jit(solution)/shard_map/all_to_all | solution.py:236
  36.3 6.6 %collective-permute-start.3 = (f32[128,128]{1,0:T(8,128)S(1)}, f32[128,128]{1,0:T(8,128)S(1)}, u32[]{:S(2)}, u32[]{:S(2)}) collective-permute-start(f32[128,128]{1,0:T(8,128)S(1)} %reshape.822), channel_id=1, source_target_pairs={{0,12},{4,0},{8,4},{12,8},{1,13},{5,1},{9,5},{13,9},{2,14},{6,2},{... | collective-permute-start | bytes 196616 | tf_op jit(solution)/shard_map/ppermute | solution.py:145
  40.0 6.3 %collective-permute-start.2 = (f32[128,128]{1,0:T(8,128)S(1)}, f32[128,128]{1,0:T(8,128)S(1)}, u32[]{:S(2)}, u32[]{:S(2)}) collective-permute-start(f32[128,128]{1,0:T(8,128)S(1)} %reshape.822), channel_id=1, source_target_pairs={{0,8},{4,12},{8,0},{12,4},{1,9},{5,13},{9,1},{13,5},{2,10},{6,14},... | collective-permute-start | bytes 196616 | tf_op jit(solution)/shard_map/ppermute | solution.py:145
  40.0 6.3 %collective-permute-start.1 = (f32[128,128]{1,0:T(8,128)S(1)}, f32[128,128]{1,0:T(8,128)S(1)}, u32[]{:S(2)}, u32[]{:S(2)}) collective-permute-start(f32[128,128]{1,0:T(8,128)S(1)} %reshape.822), channel_id=1, source_target_pairs={{0,4},{4,8},{8,12},{12,0},{1,5},{5,9},{9,13},{13,1},{2,6},{6,10},{... | collective-permute-start | bytes 196616 | tf_op jit(solution)/shard_map/ppermute | solution.py:145
  49.2 0.8 %copy-start.1 = (f32[5,192,96]{2,1,0:T(8,128)}, f32[5,192,96]{2,1,0:T(8,128)S(1)}, u32[]{:S(2)}) copy-start(f32[5,192,96]{2,1,0:T(8,128)S(1)} %fusion.9) | copy-start | bytes 1105924

commit v17 on v15

--- a/solution.py
+++ b/solution.py
@@ -203,11 +203,11 @@
     windows = jnp.concatenate([lower, middle, upper], axis=1).astype(cells.dtype)
     x_float = windows.astype(jnp.float32)
     act = jax.nn.gelu(x_float).astype(jnp.bfloat16)
-    conv_out = jnp.einsum("hti,oi->hto", act[:, 0:TB], conv_weight[0], preferred_element_type=jnp.float32)
-    for offset in range(1, taps):
-        conv_out = conv_out + jnp.einsum(
-            "hti,oi->hto", act[:, offset : offset + TB], conv_weight[offset], preferred_element_type=jnp.float32
-        )
+    unfolded = jnp.concatenate([act[:, offset : offset + TB] for offset in range(taps)], axis=-1)
+    flat_weight = conv_weight.transpose(0, 2, 1).reshape(taps * width, narrow)
+    conv_out = jnp.dot(
+        unfolded.reshape(held * TB, taps * width), flat_weight, preferred_element_type=jnp.float32
+    ).reshape(held, TB, narrow)
     my_scale = 1.25 * keep[0].astype(jnp.float32)
     x_part = lax.dynamic_slice_in_dim(x_float[:, halo : halo + TB], my_part * narrow, narrow, 2)
     mixed = (x_part + my_scale * conv_out).astype(jnp.bfloat16)

time: 44.9 us -> 46.6 us (1.038)
  local copies, waits for them, and re-layouts: 9.45 us -> 11.9 us
  matrix products: 5.87 us -> 5.04 us
    transpose x0 -> x1, local copies, waits for them, and re-layouts: none -> 2.56 us  [sparse_path(): flat_weight = conv_weight.transpose(0, 2, 1).reshape(taps * width, narrow)]
    dot_general x5 -> x1, matrix products: 1.25 us -> 0.43 us  [sparse_path(): jnp.dot(unfolded.reshape(held * TB, taps * width), flat_weight, preferred...]
    unnamed x10 -> x12, local copies, waits for them, and re-layouts: 1.13 us -> 0.96 us
  transfers between devices with their start and end apart: 5 -> 5, of which waited for: 2 -> 2; matrix products, arithmetic and copies ran while one was open for 15% -> 20% of each run, Pallas kernels for 0% -> 0%
where the time goes in v17:
time: 46.6 us; the launch traced here: 46.2 us
  starting transfers between devices  12.1 us (26%)
  local copies, waits for them, and re-layouts  11.9 us (26%)
  waiting for transfers between devices  11.9 us (26%)
  matrix products  5.04 us (11%)
  other arithmetic  4.13 us (9%)
  between operations  1.14 us (2%)
    all_to_all x1, waiting for transfers between devices, sparse_path(): incoming = lax.all_to_all(outgoing, ('seq', 'dp'), 0, 0, tiled=True)  10.7 us
    ppermute x3, starting transfers between devices, axis_sum(): lax.ppermute(value, axis, [(i, (i + shift) % count) for i in range(count)])  5.57 us
    all_to_all x1, starting transfers between devices, sparse_path(): incoming = lax.all_to_all(outgoing, ('seq', 'dp'), 0, 0, tiled=True)  3.54 us
    ppermute x1, starting transfers between devices, sparse_path(): lax.ppermute(jnp.concatenate([cells[length - halo:], cells[:halo]]), 'seq...  3 us
    transpose x1, local copies, waits for them, and re-layouts, sparse_path(): flat_weight = conv_weight.transpose(0, 2, 1).reshape(taps * width, narrow)  2.56 us
    dot_general x5, matrix products, sparse_path(): jnp.einsum('qato,qati->oi', dconv, act_sides[:, :, offset:offset + TB], p...  2.25 us
    another operation x1, local copies, waits for them, and re-layouts, sparse_path(): stacked = cells.reshape(per_block, TB * width)  1.89 us
    ppermute x3, waiting for transfers between devices, axis_sum(): lax.ppermute(value, axis, [(i, (i + shift) % count) for i in range(count)])  1.2 us
  transfers between devices with their start and end apart: 5, of which 2 were waited for; matrix products, arithmetic and copies ran while one was open for 20% of the time, Pallas kernels for 0%

profile of v17, /device:TPU:0, one launch (start us, length us, event | category | flops | bytes accessed | tf_op | source)
XLA Modules:
  0.0 46.2 jit_solution(5888420306792567314)
XLA Ops:
  0.0 0.7 %slice_bitcast_fusion.1 = (bf16[2,768]{1,0:T(2,128)(2,1)S(1)}, bf16[2,768]{1,0:T(2,128)(2,1)S(1)}) fusion(bf16[1,1024,768]{2,1,0:T(8,128)(2,1)} %param.6), kind=kLoop, calls=%fused_computation.142 | loop fusion | bytes 12288 | tf_op jit(solution)/shard_map/slice | solution.py:183
  0.7 3.0 %collective-permute-start = (bf16[4,768]{1,0:T(4,128)(2,1)S(1)}, bf16[4,768]{1,0:T(4,128)(2,1)S(1)}, u32[]{:S(2)}, u32[]{:S(2)}) collective-permute-start(bf16[4,768]{1,0:T(4,128)(2,1)S(1)} %pad_maximum_fusion.1), channel_id=1, source_target_pairs={{0,16},{16,0},{1,17},{17,1},{2,18},{18,2},{3,19},{19,3},{4,20},{20... | collective-permute-start | bytes 18440 | tf_op jit(solution)/shard_map/ppermute | solution.py:182
  3.8 1.9 %reshape_squeeze.3 = bf16[32,24576]{1,0:T(8,128)(2,1)S(1)} reshape(bf16[1,1024,768]{2,1,0:T(8,128)(2,1)} %param.6) | data formatting | bytes 3145728 | tf_op jit(solution)/shard_map/reshape;squeeze | solution.py:191
  5.7 0.2 slice_reduce_fusion.1
  6.0 0.2 convert_reduce_fusion.1
  6.2 0.2 fusion.80
  6.7 0.2 fusion.51
  6.9 0.2 fusion.49
  7.1 0.4 fusion
  8.6 2.6 %copy.135 = bf16[5,768,192]{2,1,0:T(8,128)(2,1)S(1)} copy(bf16[5,768,192]{1,2,0:T(8,128)(2,1)} %bitcast.108) | data formatting | bytes 2949120 | tf_op jit(solution)/shard_map/transpose | solution.py:207
  11.2 0.3 concatenate.144
  11.7 0.2 fusion.31
  12.5 0.4 fusion.9
  12.9 0.1 broadcast_in_dim.114
  13.1 0.1 fusion.53
  13.2 0.3 fusion.32
  13.5 0.5 %reshape.821 = bf16[8,108,128]{2,1,0:T(8,128)(2,1)S(1)} reshape(bf16[8,4,36,96]{3,2,1,0:T(8,128)(2,1)S(1)} %fusion.32) | data formatting | bytes 442368 | tf_op jit(solution)/shard_map/reshape | solution.py:218
  14.1 0.9 %fusion.16 = bf16[8,352,128]{2,1,0:T(8,128)(2,1)} fusion(bf16[8,49,128]{2,1,0:T(8,128)(2,1)S(1)} %broadcast_in_dim.123, bf16[8,108,128]{2,1,0:T(8,128)(2,1)S(1)} %reshape.821, bf16[8,192,128]{2,1,0:T(8,128)(2,1)S(1)} %broadcast_in_dim.115), kind=kLoop, calls=%fused_computation.33 | loop fusion | flops 3604480 | bytes 1435648 | tf_op jit(solution)/shard_map/concatenate | solution.py:231
  15.0 3.5 %all-to-all-start = ((bf16[8,352,128]{2,1,0:T(8,128)(2,1)}), bf16[8,352,128]{2,1,0:T(8,128)(2,1)S(1)}, u32[]{:S(2)}, u32[]{:S(2)}) async-start(bf16[8,352,128]{2,1,0:T(8,128)(2,1)} %fusion.16), calls=%async_computation | async-start | bytes 1441792 | tf_op jit(solution)/shard_map/all_to_all | solution.py:240
  18.8 10.7 %all-to-all-done = bf16[8,352,128]{2,1,0:T(8,128)(2,1)S(1)} async-done(((bf16[8,352,128]{2,1,0:T(8,128)(2,1)}), bf16[8,352,128]{2,1,0:T(8,128)(2,1)S(1)}, u32[]{:S(2)}, u32[]{:S(2)}) %all-to-all-start) | async-done | bytes 720928 | tf_op jit(solution)/shard_map/all_to_all | solution.py:240
  30.0 0.3 convert_reduce_fusion
  30.8 0.1 copy.146
  31.1 0.3 reshape_reshape.6
  31.4 0.6 %gather_fusion = bf16[32,32,192]{2,1,0:T(8,128)(2,1)S(1)} fusion(bf16[32,32,192]{2,1,0:T(8,128)(2,1)S(1)} %reshape_reshape.6, s32[1024]{0:T(1024)S(1)} %pad_clamp_fusion.1), kind=kCustom, calls=%fused_computation | custom fusion | bytes 786560 | tf_op jit(solution)/shard_map/jit(_take)/gather | solution.py:264
  32.0 0.1 broadcast_select_fusion
  32.1 0.2 fusion.47
  32.4 0.1 reshape.824
  32.5 1.6 %collective-permute-start.1 = (f32[128,128]{1,0:T(8,128)S(1)}, f32[128,128]{1,0:T(8,128)S(1)}, u32[]{:S(2)}, u32[]{:S(2)}) collective-permute-start(f32[128,128]{1,0:T(8,128)S(1)} %reshape.824), channel_id=1, source_target_pairs={{0,4},{4,8},{8,12},{12,0},{1,5},{5,9},{9,13},{13,1},{2,6},{6,10},{... | collective-permute-start | bytes 196616 | tf_op jit(solution)/shard_map/ppermute | solution.py:145
  34.1 2.6 %collective-permute-start.2 = (f32[128,128]{1,0:T(8,128)S(1)}, f32[128,128]{1,0:T(8,128)S(1)}, u32[]{:S(2)}, u32[]{:S(2)}) collective-permute-start(f32[128,128]{1,0:T(8,128)S(1)} %reshape.824), channel_id=1, source_target_pairs={{0,8},{4,12},{8,0},{12,4},{1,9},{5,13},{9,1},{13,5},{2,10},{6,14},... | collective-permute-start | bytes 196616 | tf_op jit(solution)/shard_map/ppermute | solution.py:145
  36.7 1.3 %collective-permute-start.3 = (f32[128,128]{1,0:T(8,128)S(1)}, f32[128,128]{1,0:T(8,128)S(1)}, u32[]{:S(2)}, u32[]{:S(2)}) collective-permute-start(f32[128,128]{1,0:T(8,128)S(1)} %reshape.824), channel_id=1, source_target_pairs={{0,12},{4,0},{8,4},{12,8},{1,13},{5,1},{9,5},{13,9},{2,14},{6,2},{... | collective-permute-start | bytes 196616 | tf_op jit(solution)/shard_map/ppermute | solution.py:145
  38.1 0.2 fusion.90
  38.5 0.5 reshape_reshape.7
  39.0 0.1 reshape.825
  39.2 0.2 fusion.56
  39.4 0.6 %gather_fusion.1 = bf16[32,36,96]{2,1,0:T(8,128)(2,1)S(1)} fusion(bf16[32,36,96]{2,1,0:T(8,128)(2,1)S(1)} %reshape_reshape.7, s32[1024]{0:T(1024)S(1)} %pad_clamp_fusion), kind=kCustom, calls=%fused_computation.1 | custom fusion | bytes 442496 | tf_op jit(solution)/shard_map/jit(_take)/gather | solution.py:297
  40.0 0.1 copy_select_fusion
  40.2 0.2 multiply_reduce_fusion
  40.3 1.2 %collective-permute-done.2 = f32[128,128]{1,0:T(8,128)S(1)} collective-permute-done((f32[128,128]{1,0:T(8,128)S(1)}, f32[128,128]{1,0:T(8,128)S(1)}, u32[]{:S(2)}, u32[]{:S(2)}) %collective-permute-start.2) | collective-permute-done | bytes 65568 | tf_op jit(solution)/shard_map/ppermute | solution.py:145
  41.6 0.1 div.78
  41.7 0.4 convolution_convert_fusion.1
  42.1 0.5 %convolution_convert_fusion = bf16[4,2,2,32,192]{4,3,2,1,0:T(8,128)(2,1)S(1)} fusion(bf16[4,2,4,32,192]{4,3,2,1,0:T(8,128)(2,1)S(1)} %broadcast_select_fusion, f32[4,2,2,32,32]{4,3,2,1,0:T(8,128)S(1)} %div.78, f32[2,4,2,32,32]{4,3,2,1,0:T(8,128)S(1)} %reshape.825, f32[4]{0:T(128)S(1)} %convert_element_type.117, f32[4,2,2]{2,1,0:T(2,128)S(1)} %compare_select_fusion.6), kind=kOutput, calls=%fused_computation.12 | convolution fusion | flops 37896192 | bytes 987648 | tf_op jit(solution)/shard_map/qocij,qocid->qocjd/dot_general | solution.py:284
  42.7 0.4 fusion.7
  43.2 0.3 fusion.14
  43.5 0.3 fusion.13
  43.8 0.3 fusion.12
  44.1 0.3 fusion.11
  44.5 0.8 %copy-done.3 = f32[5,192,96]{2,1,0:T(8,128)} copy-done((f32[5,192,96]{2,1,0:T(8,128)}, f32[5,192,96]{2,1,0:T(8,128)S(1)}, u32[]{:S(2)}) %copy-start.3) | copy-done | bytes 368664
  45.3 1.0 %fusion.10 = f32[5,192,96]{2,1,0:T(8,128)} fusion(f32[5,192,96]{2,1,0:T(8,128)} %copy-done.3, bf16[4,8,32,192]{3,1,2,0:T(8,128)(2,1)S(1)} %fusion.7, bf16[4,8,36,96]{3,2,0,1:T(8,128)(2,1)S(1)} %copy_select_fusion), kind=kOutput, calls=%fused_computation.22 | convolution fusion | flops 37748736 | bytes 884736 | tf_op jit(solution)/shard_map/qato,qati->oi/dot_general | solution.py:300
  (80 shorter events, 3.4 us)
Async XLA Ops:
  0.7 10.8 %collective-permute-start = (bf16[4,768]{1,0:T(4,128)(2,1)S(1)}, bf16[4,768]{1,0:T(4,128)(2,1)S(1)}, u32[]{:S(2)}, u32[]{:S(2)}) collective-permute-start(bf16[4,768]{1,0:T(4,128)(2,1)S(1)} %pad_maximum_fusion.1), channel_id=1, source_target_pairs={{0,16},{16,0},{1,17},{17,1},{2,18},{18,2},{3,19},{19,3},{4,20},{20... | collective-permute-start | bytes 18440 | tf_op jit(solution)/shard_map/ppermute | solution.py:182
  3.8 1.9 %copy-start = (s32[1,2,2,2]{3,2,1,0:T(2,128)S(1)}, s32[1,2,2,2]{3,2,1,0:T(2,128)}, u32[]{:S(2)}) copy-start(s32[1,2,2,2]{3,2,1,0:T(2,128)} %param.9) | copy-start | bytes 100
  5.7 2.4 %copy-start.1 = (f32[1,1,2,1024]{3,2,1,0:T(2,128)S(1)}, f32[1,1,2,1024]{3,2,1,0:T(2,128)}, u32[]{:S(2)}) copy-start(f32[1,1,2,1024]{3,2,1,0:T(2,128)} %param.11) | copy-start | bytes 24580
  5.7 2.5 %copy-start.2 = (s32[1,2]{1,0:T(1,128)S(1)}, s32[1,2]{1,0:T(1,128)}, u32[]{:S(2)}) copy-start(s32[1,2]{1,0:T(1,128)} %param.10) | copy-start | bytes 28
  15.0 14.4 %all-to-all-start = ((bf16[8,352,128]{2,1,0:T(8,128)(2,1)}), bf16[8,352,128]{2,1,0:T(8,128)(2,1)S(1)}, u32[]{:S(2)}, u32[]{:S(2)}) async-start(bf16[8,352,128]{2,1,0:T(8,128)(2,1)} %fusion.16), calls=%async_computation | async-start | bytes 1441792 | tf_op jit(solution)/shard_map/all_to_all | solution.py:240
  32.5 7.9 %collective-permute-start.1 = (f32[128,128]{1,0:T(8,128)S(1)}, f32[128,128]{1,0:T(8,128)S(1)}, u32[]{:S(2)}, u32[]{:S(2)}) collective-permute-start(f32[128,128]{1,0:T(8,128)S(1)} %reshape.824), channel_id=1, source_target_pairs={{0,4},{4,8},{8,12},{12,0},{1,5},{5,9},{9,13},{13,1},{2,6},{6,10},{... | collective-permute-start | bytes 196616 | tf_op jit(solution)/shard_map/ppermute | solution.py:145
  34.1 7.4 %collective-permute-start.2 = (f32[128,128]{1,0:T(8,128)S(1)}, f32[128,128]{1,0:T(8,128)S(1)}, u32[]{:S(2)}, u32[]{:S(2)}) collective-permute-start(f32[128,128]{1,0:T(8,128)S(1)} %reshape.824), channel_id=1, source_target_pairs={{0,8},{4,12},{8,0},{12,4},{1,9},{5,13},{9,1},{13,5},{2,10},{6,14},... | collective-permute-start | bytes 196616 | tf_op jit(solution)/shard_map/ppermute | solution.py:145
  36.7 4.8 %collective-permute-start.3 = (f32[128,128]{1,0:T(8,128)S(1)}, f32[128,128]{1,0:T(8,128)S(1)}, u32[]{:S(2)}, u32[]{:S(2)}) collective-permute-start(f32[128,128]{1,0:T(8,128)S(1)} %reshape.824), channel_id=1, source_target_pairs={{0,12},{4,0},{8,4},{12,8},{1,13},{5,1},{9,5},{13,9},{2,14},{6,2},{... | collective-permute-start | bytes 196616 | tf_op jit(solution)/shard_map/ppermute | solution.py:145
  44.5 0.8 %copy-start.3 = (f32[5,192,96]{2,1,0:T(8,128)}, f32[5,192,96]{2,1,0:T(8,128)S(1)}, u32[]{:S(2)}) copy-start(f32[5,192,96]{2,1,0:T(8,128)S(1)} %fusion.11) | copy-start | bytes 1105924

commit v18 on v15

--- a/solution.py
+++ b/solution.py
@@ -225,7 +225,10 @@
         piece = lax.reduce_precision(wide, exponent_bits=8, mantissa_bits=7)
         pieces.append(piece)
         wide = wide - piece
-    small = jnp.concatenate([tiles.reshape(-1), counts.reshape(-1), keep.reshape(-1)]).astype(jnp.float32)
+    own_slot = (own_source * groups + lax.axis_index("dp")) * held + jnp.arange(owners)[:, None] * PER + own_rank
+    small = jnp.concatenate(
+        [tiles.reshape(-1), counts.reshape(-1), keep.reshape(-1), own_slot.reshape(-1)]
+    ).astype(jnp.float32)
     meta_part = lanes(jnp.concatenate(pieces + [small]).astype(jnp.bfloat16).reshape(1, -1))
     rows_mixed, rows_act, rows_meta = mixed_part.shape[1], act_cut.shape[1], meta_part.shape[1]
     outgoing = jnp.concatenate(
@@ -253,13 +256,9 @@
     tiles_all = ints[:, :n_tiles].reshape(groups, owners, capacity, 2)
     counts_all = ints[:, n_tiles : n_tiles + owners]
     keep_all = ints[:, n_tiles + owners]
+    slot = ints[:, n_tiles + owners + 1 : n_tiles + owners + 1 + owners * n_sides].reshape(groups, owners, n_sides)
 
     sides = jnp.concatenate([tiles_all[..., 0], tiles_all[..., 1]], axis=-1)
-    source = sides // per_block
-    local = sides % per_block
-    same_source = source[..., :, None] == source[..., None, :]
-    rank = jnp.sum(jnp.logical_and(same_source, before), axis=-1)
-    slot = (source * groups + jnp.arange(groups)[:, None, None]) * held + jnp.arange(owners)[None, :, None] * PER + rank
 
     side_rows = jnp.take(mixed_in, slot, axis=0)
     row_side = side_rows[:, :, :capacity]

time: 44.9 us -> 44.2 us (0.984)
  transfers between devices with their start and end apart: 5 -> 5, of which waited for: 2 -> 2; matrix products, arithmetic and copies ran while one was open for 15% -> 16% of each run, Pallas kernels for 0% -> 0%
where the time goes in v18:
time: 44.2 us; the launch traced here: 43.9 us
  starting transfers between devices  12.1 us (27%)
  waiting for transfers between devices  11.9 us (27%)
  local copies, waits for them, and re-layouts  9.11 us (21%)
  matrix products  5.87 us (13%)
  other arithmetic  3.76 us (9%)
  between operations  1.12 us (3%)
    all_to_all x1, waiting for transfers between devices, sparse_path(): incoming = lax.all_to_all(outgoing, ('seq', 'dp'), 0, 0, tiled=True)  10.9 us
    ppermute x3, starting transfers between devices, axis_sum(): lax.ppermute(value, axis, [(i, (i + shift) % count) for i in range(count)])  5.56 us
    all_to_all x1, starting transfers between devices, sparse_path(): incoming = lax.all_to_all(outgoing, ('seq', 'dp'), 0, 0, tiled=True)  3.54 us
    ppermute x1, starting transfers between devices, sparse_path(): lax.ppermute(jnp.concatenate([cells[length - halo:], cells[:halo]]), 'seq...  3 us
    dot_general x5, matrix products, sparse_path(): jnp.einsum('qato,qati->oi', dconv, act_sides[:, :, offset:offset + TB], p...  2.25 us
    another operation x1, local copies, waits for them, and re-layouts, sparse_path(): stacked = cells.reshape(per_block, TB * width)  1.89 us
    unnamed x10, local copies, waits for them, and re-layouts  1.13 us
    ppermute x3, waiting for transfers between devices, axis_sum(): lax.ppermute(value, axis, [(i, (i + shift) % count) for i in range(count)])  1.06 us
  transfers between devices with their start and end apart: 5, of which 2 were waited for; matrix products, arithmetic and copies ran while one was open for 16% of the time, Pallas kernels for 0%

profile of v18, /device:TPU:0, one launch (start us, length us, event | category | flops | bytes accessed | tf_op | source)
XLA Modules:
  0.0 43.9 jit_solution(1076524410657746506)
XLA Ops:
  0.0 0.7 %slice_bitcast_fusion.1 = (bf16[2,768]{1,0:T(2,128)(2,1)S(1)}, bf16[2,768]{1,0:T(2,128)(2,1)S(1)}) fusion(bf16[1,1024,768]{2,1,0:T(8,128)(2,1)} %param.6), kind=kLoop, calls=%fused_computation.138 | loop fusion | bytes 12288 | tf_op jit(solution)/shard_map/slice | solution.py:183
  0.7 3.0 %collective-permute-start = (bf16[4,768]{1,0:T(4,128)(2,1)S(1)}, bf16[4,768]{1,0:T(4,128)(2,1)S(1)}, u32[]{:S(2)}, u32[]{:S(2)}) collective-permute-start(bf16[4,768]{1,0:T(4,128)(2,1)S(1)} %pad_maximum_fusion.1), channel_id=1, source_target_pairs={{0,16},{16,0},{1,17},{17,1},{2,18},{18,2},{3,19},{19,3},{4,20},{20... | collective-permute-start | bytes 18440 | tf_op jit(solution)/shard_map/ppermute | solution.py:182
  3.8 1.9 %reshape_squeeze.3 = bf16[32,24576]{1,0:T(8,128)(2,1)S(1)} reshape(bf16[1,1024,768]{2,1,0:T(8,128)(2,1)} %param.6) | data formatting | bytes 3145728 | tf_op jit(solution)/shard_map/reshape;squeeze | solution.py:191
  5.7 0.2 slice_reduce_fusion.1
  6.0 0.2 convert_reduce_fusion
  6.2 0.2 fusion.83
  6.8 0.2 fusion.68
  7.0 0.2 fusion.66
  7.2 0.4 fusion
  8.9 0.3 concatenate.89
  9.5 0.2 fusion.32
  10.0 0.3 copy-done.3
  10.3 0.2 fusion.38
  10.6 0.2 convolution_add_fusion.3
  10.8 0.2 convolution_add_fusion.2
  11.1 0.2 convolution_add_fusion.1
  11.3 0.3 fusion.10
  11.6 0.1 broadcast_in_dim.112
  11.9 0.3 fusion.33
  12.2 0.5 %reshape.430 = bf16[8,108,128]{2,1,0:T(8,128)(2,1)S(1)} reshape(bf16[8,4,36,96]{3,2,1,0:T(8,128)(2,1)S(1)} %fusion.33) | data formatting | bytes 442368 | tf_op jit(solution)/shard_map/reshape | solution.py:218
  12.8 0.9 %fusion.17 = bf16[8,352,128]{2,1,0:T(8,128)(2,1)} fusion(bf16[8,49,128]{2,1,0:T(8,128)(2,1)S(1)} %broadcast_in_dim.121, bf16[8,108,128]{2,1,0:T(8,128)(2,1)S(1)} %reshape.430, bf16[8,192,128]{2,1,0:T(8,128)(2,1)S(1)} %broadcast_in_dim.113), kind=kLoop, calls=%fused_computation.37 | loop fusion | flops 3604480 | bytes 1435648 | tf_op jit(solution)/shard_map/concatenate | solution.py:234
  13.7 3.5 %all-to-all-start = ((bf16[8,352,128]{2,1,0:T(8,128)(2,1)}), bf16[8,352,128]{2,1,0:T(8,128)(2,1)S(1)}, u32[]{:S(2)}, u32[]{:S(2)}) async-start(bf16[8,352,128]{2,1,0:T(8,128)(2,1)} %fusion.17), calls=%async_computation | async-start | bytes 1441792 | tf_op jit(solution)/shard_map/all_to_all | solution.py:243
  17.3 10.9 %all-to-all-done = bf16[8,352,128]{2,1,0:T(8,128)(2,1)S(1)} async-done(((bf16[8,352,128]{2,1,0:T(8,128)(2,1)}), bf16[8,352,128]{2,1,0:T(8,128)(2,1)S(1)}, u32[]{:S(2)}, u32[]{:S(2)}) %all-to-all-start) | async-done | bytes 720928 | tf_op jit(solution)/shard_map/all_to_all | solution.py:243
  28.6 0.3 reshape_reshape.6
  29.1 0.6 %gather_fusion = bf16[32,32,192]{2,1,0:T(8,128)(2,1)S(1)} fusion(bf16[32,32,192]{2,1,0:T(8,128)(2,1)S(1)} %reshape_reshape.6, s32[1024]{0:T(1024)S(1)} %pad_clamp_fusion.1), kind=kCustom, calls=%fused_computation | custom fusion | bytes 786560 | tf_op jit(solution)/shard_map/jit(_take)/gather | solution.py:263
  29.7 0.1 broadcast_select_fusion
  29.8 0.2 fusion.59
  30.0 0.1 reshape.435
  30.1 1.6 %collective-permute-start.1 = (f32[128,128]{1,0:T(8,128)S(1)}, f32[128,128]{1,0:T(8,128)S(1)}, u32[]{:S(2)}, u32[]{:S(2)}) collective-permute-start(f32[128,128]{1,0:T(8,128)S(1)} %reshape.435), channel_id=1, source_target_pairs={{0,4},{4,8},{8,12},{12,0},{1,5},{5,9},{9,13},{13,1},{2,6},{6,10},{... | collective-permute-start | bytes 196616 | tf_op jit(solution)/shard_map/ppermute | solution.py:145
  31.8 2.6 %collective-permute-start.2 = (f32[128,128]{1,0:T(8,128)S(1)}, f32[128,128]{1,0:T(8,128)S(1)}, u32[]{:S(2)}, u32[]{:S(2)}) collective-permute-start(f32[128,128]{1,0:T(8,128)S(1)} %reshape.435), channel_id=1, source_target_pairs={{0,8},{4,12},{8,0},{12,4},{1,9},{5,13},{9,1},{13,5},{2,10},{6,14},... | collective-permute-start | bytes 196616 | tf_op jit(solution)/shard_map/ppermute | solution.py:145
  34.4 1.3 %collective-permute-start.3 = (f32[128,128]{1,0:T(8,128)S(1)}, f32[128,128]{1,0:T(8,128)S(1)}, u32[]{:S(2)}, u32[]{:S(2)}) collective-permute-start(f32[128,128]{1,0:T(8,128)S(1)} %reshape.435), channel_id=1, source_target_pairs={{0,12},{4,0},{8,4},{12,8},{1,13},{5,1},{9,5},{13,9},{2,14},{6,2},{... | collective-permute-start | bytes 196616 | tf_op jit(solution)/shard_map/ppermute | solution.py:145
  35.7 0.2 fusion.93
  35.9 0.5 %reshape_reshape.7 = bf16[32,36,96]{2,1,0:T(8,128)(2,1)S(1)} reshape(bf16[8,108,128]{2,1,0:T(8,128)(2,1)S(1)} %slice.188) | data formatting | bytes 442368 | tf_op jit(solution)/shard_map/reshape;reshape | solution.py:248
  36.8 0.2 fusion.73
  37.0 0.1 reshape.436
  37.2 0.6 %gather_fusion.1 = bf16[32,36,96]{2,1,0:T(8,128)(2,1)S(1)} fusion(bf16[32,36,96]{2,1,0:T(8,128)(2,1)S(1)} %reshape_reshape.7, s32[1024]{0:T(1024)S(1)} %pad_clamp_fusion), kind=kCustom, calls=%fused_computation.1 | custom fusion | bytes 442496 | tf_op jit(solution)/shard_map/jit(_take)/gather | solution.py:296
  38.0 0.2 multiply_reduce_fusion
  38.1 1.1 %collective-permute-done.2 = f32[128,128]{1,0:T(8,128)S(1)} collective-permute-done((f32[128,128]{1,0:T(8,128)S(1)}, f32[128,128]{1,0:T(8,128)S(1)}, u32[]{:S(2)}, u32[]{:S(2)}) %collective-permute-start.2) | collective-permute-done | bytes 65568 | tf_op jit(solution)/shard_map/ppermute | solution.py:145
  39.2 0.1 div.46
  39.4 0.4 convolution_convert_fusion.1
  39.8 0.5 %convolution_convert_fusion = bf16[4,2,2,32,192]{4,3,2,1,0:T(8,128)(2,1)S(1)} fusion(bf16[4,2,4,32,192]{4,3,2,1,0:T(8,128)(2,1)S(1)} %broadcast_select_fusion, f32[4,2,2,32,32]{4,3,2,1,0:T(8,128)S(1)} %div.46, f32[2,4,2,32,32]{4,3,2,1,0:T(8,128)S(1)} %reshape.436, f32[4]{0:T(128)S(1)} %convert_element_type.113, f32[4,2,2]{2,1,0:T(2,128)S(1)} %compare_select_fusion.3), kind=kOutput, calls=%fused_computation.12 | convolution fusion | flops 37896192 | bytes 987648 | tf_op jit(solution)/shard_map/qocij,qocid->qocjd/dot_general | solution.py:283
  40.4 0.4 %fusion.7 = bf16[4,8,32,192]{3,1,2,0:T(8,128)(2,1)S(1)} fusion(bf16[4,8,32,192]{3,2,1,0:T(8,128)(2,1)S(1)} %bitcast.119, f32[4]{0:T(128)S(1)} %multiply_reduce_fusion, pred[4,8]{1,0:T(4,128)(4,1)S(1)} %not.7, s32[4,8]{1,0:T(4,128)S(1)} %copy.158), kind=kOutput, calls=%fused_computation.11 | convolution fusion | flops 3735808 | bytes 786608 | tf_op jit(solution)/shard_map/qab,qbtd->qatd/dot_general | solution.py:288
  40.8 0.3 fusion.15
  41.2 0.3 fusion.14
  41.5 0.3 fusion.13
  41.8 0.3 fusion.12
  42.2 0.8 %copy-done.4 = f32[5,192,96]{2,1,0:T(8,128)} copy-done((f32[5,192,96]{2,1,0:T(8,128)}, f32[5,192,96]{2,1,0:T(8,128)S(1)}, u32[]{:S(2)}) %copy-start.4) | copy-done | bytes 368664
  42.9 1.0 %fusion.11 = f32[5,192,96]{2,1,0:T(8,128)} fusion(f32[5,192,96]{2,1,0:T(8,128)} %copy-done.4, bf16[4,8,32,192]{3,1,2,0:T(8,128)(2,1)S(1)} %fusion.7, bf16[4,8,36,96]{3,2,0,1:T(8,128)(2,1)S(1)} %copy_select_fusion), kind=kOutput, calls=%fused_computation.26 | convolution fusion | flops 37748736 | bytes 884736 | tf_op jit(solution)/shard_map/qato,qati->oi/dot_general | solution.py:299
  (77 shorter events, 3.1 us)
Async XLA Ops:
  0.7 8.6 %collective-permute-start = (bf16[4,768]{1,0:T(4,128)(2,1)S(1)}, bf16[4,768]{1,0:T(4,128)(2,1)S(1)}, u32[]{:S(2)}, u32[]{:S(2)}) collective-permute-start(bf16[4,768]{1,0:T(4,128)(2,1)S(1)} %pad_maximum_fusion.1), channel_id=1, source_target_pairs={{0,16},{16,0},{1,17},{17,1},{2,18},{18,2},{3,19},{19,3},{4,20},{20... | collective-permute-start | bytes 18440 | tf_op jit(solution)/shard_map/ppermute | solution.py:182
  3.8 1.9 %copy-start = (s32[1,2,2,2]{3,2,1,0:T(2,128)S(1)}, s32[1,2,2,2]{3,2,1,0:T(2,128)}, u32[]{:S(2)}) copy-start(s32[1,2,2,2]{3,2,1,0:T(2,128)} %param.9) | copy-start | bytes 100
  5.7 2.8 %copy-start.1 = (f32[1,1,2,1024]{3,2,1,0:T(2,128)S(1)}, f32[1,1,2,1024]{3,2,1,0:T(2,128)}, u32[]{:S(2)}) copy-start(f32[1,1,2,1024]{3,2,1,0:T(2,128)} %param.11) | copy-start | bytes 24580
  5.7 2.8 %copy-start.2 = (s32[1,2]{1,0:T(1,128)S(1)}, s32[1,2]{1,0:T(1,128)}, u32[]{:S(2)}) copy-start(s32[1,2]{1,0:T(1,128)} %param.10) | copy-start | bytes 28
  8.9 1.4 %copy-start.3 = (bf16[5,192,768]{2,1,0:T(8,128)(2,1)S(1)}, bf16[5,192,768]{2,1,0:T(8,128)(2,1)}, u32[]{:S(2)}) copy-start(bf16[5,192,768]{2,1,0:T(8,128)(2,1)} %param.7) | copy-start | bytes 4423684
  13.7 14.4 %all-to-all-start = ((bf16[8,352,128]{2,1,0:T(8,128)(2,1)}), bf16[8,352,128]{2,1,0:T(8,128)(2,1)S(1)}, u32[]{:S(2)}, u32[]{:S(2)}) async-start(bf16[8,352,128]{2,1,0:T(8,128)(2,1)} %fusion.17), calls=%async_computation | async-start | bytes 1441792 | tf_op jit(solution)/shard_map/all_to_all | solution.py:243
  30.1 8.0 %collective-permute-start.1 = (f32[128,128]{1,0:T(8,128)S(1)}, f32[128,128]{1,0:T(8,128)S(1)}, u32[]{:S(2)}, u32[]{:S(2)}) collective-permute-start(f32[128,128]{1,0:T(8,128)S(1)} %reshape.435), channel_id=1, source_target_pairs={{0,4},{4,8},{8,12},{12,0},{1,5},{5,9},{9,13},{13,1},{2,6},{6,10},{... | collective-permute-start | bytes 196616 | tf_op jit(solution)/shard_map/ppermute | solution.py:145
  31.8 7.4 %collective-permute-start.2 = (f32[128,128]{1,0:T(8,128)S(1)}, f32[128,128]{1,0:T(8,128)S(1)}, u32[]{:S(2)}, u32[]{:S(2)}) collective-permute-start(f32[128,128]{1,0:T(8,128)S(1)} %reshape.435), channel_id=1, source_target_pairs={{0,8},{4,12},{8,0},{12,4},{1,9},{5,13},{9,1},{13,5},{2,10},{6,14},... | collective-permute-start | bytes 196616 | tf_op jit(solution)/shard_map/ppermute | solution.py:145
  34.4 4.8 %collective-permute-start.3 = (f32[128,128]{1,0:T(8,128)S(1)}, f32[128,128]{1,0:T(8,128)S(1)}, u32[]{:S(2)}, u32[]{:S(2)}) collective-permute-start(f32[128,128]{1,0:T(8,128)S(1)} %reshape.435), channel_id=1, source_target_pairs={{0,12},{4,0},{8,4},{12,8},{1,13},{5,1},{9,5},{13,9},{2,14},{6,2},{... | collective-permute-start | bytes 196616 | tf_op jit(solution)/shard_map/ppermute | solution.py:145
  42.1 0.8 %copy-start.4 = (f32[5,192,96]{2,1,0:T(8,128)}, f32[5,192,96]{2,1,0:T(8,128)S(1)}, u32[]{:S(2)}) copy-start(f32[5,192,96]{2,1,0:T(8,128)S(1)} %fusion.12) | copy-start | bytes 1105924

commit v19 on v18

--- a/solution.py
+++ b/solution.py
@@ -294,17 +294,15 @@
     dconv = (scaling[:, None, None, None] * total).astype(jnp.bfloat16)
     dconv = jnp.where(first[..., None, None], dconv, jnp.zeros_like(dconv))
     act_sides = jnp.take(act_in, slot.reshape(groups, owners * n_sides), axis=0)
-    return jnp.stack(
-        [
-            jnp.einsum(
-                "qato,qati->oi",
-                dconv,
-                act_sides[:, :, offset : offset + TB],
-                preferred_element_type=jnp.float32,
-            )
+    placed = jnp.stack(
+        [
+            jnp.pad(dconv, ((0, 0), (0, 0), (offset, span - TB - offset), (0, 0)))
             for offset in range(taps)
         ]
     )
+    lhs = placed.transpose(0, 4, 1, 2, 3).reshape(taps * narrow, -1)
+    product = jnp.dot(lhs, act_sides.reshape(-1, cols), preferred_element_type=jnp.float32)
+    return product.reshape(taps, narrow, cols)
 
 
 def per_device(features, conv_weight, keep, tiles, counts, targets):

time: 44.2 us -> 45.8 us (1.036)
  waiting for transfers between devices: 11.9 us -> 14.1 us
  starting transfers between devices: 12.1 us -> 11.2 us
  local copies, waits for them, and re-layouts: 9.11 us -> 9.82 us
    ppermute x3, waiting for transfers between devices: 1.06 us -> 3.24 us  [axis_sum(): lax.ppermute(value, axis, [(i, (i + shift) % count) for i in range(count)])]
    ppermute x3, starting transfers between devices: 5.56 us -> 4.66 us  [axis_sum(): lax.ppermute(value, axis, [(i, (i + shift) % count) for i in range(count)])]
    slice x1, local copies, waits for them, and re-layouts: 0.21 us -> 0.97 us  [sparse_path(): own_sides = jnp.concatenate([tiles[0, ..., 0], tiles[0, ..., 1]], axis=-1)]
    unnamed x10, local copies, waits for them, and re-layouts: 1.13 us -> 0.39 us
    concatenate x1, local copies, waits for them, and re-layouts: 0.08 us -> 0.76 us  [sparse_path(): jnp.concatenate([tiles.reshape(-1), counts.reshape(-1), keep.reshape(-1),...]
    dot_general x5 -> x1, matrix products: 2.25 us -> 1.88 us  [sparse_path(): jnp.dot(lhs, act_sides.reshape(-1, cols), preferred_element_type=jnp.floa...]
  transfers between devices with their start and end apart: 5 -> 5, of which waited for: 2 -> 2; matrix products, arithmetic and copies ran while one was open for 16% -> 18% of each run, Pallas kernels for 0% -> 0%
where the time goes in v19:
time: 45.8 us; the launch traced here: 45.4 us
  waiting for transfers between devices  14.1 us (31%)
  starting transfers between devices  11.2 us (24%)
  local copies, waits for them, and re-layouts  9.82 us (21%)
  matrix products  5.49 us (12%)
  other arithmetic  3.64 us (8%)
  between operations  1.14 us (2%)
    all_to_all x1, waiting for transfers between devices, sparse_path(): incoming = lax.all_to_all(outgoing, ('seq', 'dp'), 0, 0, tiled=True)  10.9 us
    ppermute x3, starting transfers between devices, axis_sum(): lax.ppermute(value, axis, [(i, (i + shift) % count) for i in range(count)])  4.66 us
    all_to_all x1, starting transfers between devices, sparse_path(): incoming = lax.all_to_all(outgoing, ('seq', 'dp'), 0, 0, tiled=True)  3.54 us
    ppermute x3, waiting for transfers between devices, axis_sum(): lax.ppermute(value, axis, [(i, (i + shift) % count) for i in range(count)])  3.24 us
    ppermute x1, starting transfers between devices, sparse_path(): lax.ppermute(jnp.concatenate([cells[length - halo:], cells[:halo]]), 'seq...  3 us
    another operation x1, local copies, waits for them, and re-layouts, sparse_path(): stacked = cells.reshape(per_block, TB * width)  1.89 us
    dot_general x1, matrix products, sparse_path(): jnp.dot(lhs, act_sides.reshape(-1, cols), preferred_element_type=jnp.floa...  1.88 us
    dot_general x4, matrix products, sparse_path(): jnp.einsum('hti,oi->hto', act[:, offset:offset + TB], conv_weight[offset]...  1.01 us
  transfers between devices with their start and end apart: 5, of which 2 were waited for; matrix products, arithmetic and copies ran while one was open for 18% of the time, Pallas kernels for 0%

profile of v19, /device:TPU:0, one launch (start us, length us, event | category | flops | bytes accessed | tf_op | source)
XLA Modules:
  0.0 45.4 jit_solution(586020709144545874)
XLA Ops:
  0.0 0.7 %slice_bitcast_fusion.1 = (bf16[2,768]{1,0:T(2,128)(2,1)S(1)}, bf16[2,768]{1,0:T(2,128)(2,1)S(1)}) fusion(bf16[1,1024,768]{2,1,0:T(8,128)(2,1)} %param.6), kind=kLoop, calls=%fused_computation.129 | loop fusion | bytes 12288 | tf_op jit(solution)/shard_map/slice | solution.py:183
  0.7 3.0 %collective-permute-start = (bf16[4,768]{1,0:T(4,128)(2,1)S(1)}, bf16[4,768]{1,0:T(4,128)(2,1)S(1)}, u32[]{:S(2)}, u32[]{:S(2)}) collective-permute-start(bf16[4,768]{1,0:T(4,128)(2,1)S(1)} %pad_maximum_fusion.1), channel_id=1, source_target_pairs={{0,16},{16,0},{1,17},{17,1},{2,18},{18,2},{3,19},{19,3},{4,20},{20... | collective-permute-start | bytes 18440 | tf_op jit(solution)/shard_map/ppermute | solution.py:182
  3.8 0.8 %concatenate.94 = s32[8]{0:T(128)S(1)} reshape(s32[1,2,2,2]{3,2,1,0:T(2,128)} %param.9) | data formatting | bytes 64 | tf_op jit(solution)/shard_map/concatenate | solution.py:229
  4.5 1.0 %slice_reduce_fusion.1 = (s32[2,2]{1,0:T(2,128)S(1)}, s32[2,2]{1,0:T(2,128)S(1)}) fusion(s32[1,2,2,2]{3,2,1,0:T(2,128)} %param.9), kind=kLoop, calls=%fused_computation.138 | loop fusion | bytes 64 | tf_op jit(solution)/shard_map/slice | solution.py:166
  5.7 0.2 convert_reduce_fusion
  6.0 0.2 fusion.77
  6.1 0.1 copy.106
  6.3 1.9 %reshape_squeeze.3 = bf16[32,24576]{1,0:T(8,128)(2,1)S(1)} reshape(bf16[1,1024,768]{2,1,0:T(8,128)(2,1)} %param.6) | data formatting | bytes 3145728 | tf_op jit(solution)/shard_map/reshape;squeeze | solution.py:191
  9.1 0.2 fusion.60
  9.3 0.2 fusion.62
  9.5 0.4 fusion.2
  10.1 0.1 reshape.441
  10.2 0.1 reshape.442
  10.4 0.3 concatenate.89
  11.0 0.2 fusion.32
  11.4 0.2 fusion.41
  11.6 0.2 convolution_add_fusion.3
  11.9 0.2 convolution_add_fusion.2
  12.1 0.2 convolution_add_fusion.1
  12.4 0.1 fusion.64
  12.5 0.3 fusion.33
  12.9 0.5 %reshape.443 = bf16[8,108,128]{2,1,0:T(8,128)(2,1)S(1)} reshape(bf16[8,4,36,96]{3,2,1,0:T(8,128)(2,1)S(1)} %fusion.33) | data formatting | bytes 442368 | tf_op jit(solution)/shard_map/reshape | solution.py:218
  13.4 0.3 fusion.15
  13.7 0.1 broadcast_in_dim.112
  13.9 0.9 %fusion.17 = bf16[8,352,128]{2,1,0:T(8,128)(2,1)} fusion(bf16[8,49,128]{2,1,0:T(8,128)(2,1)S(1)} %broadcast_in_dim.121, bf16[8,108,128]{2,1,0:T(8,128)(2,1)S(1)} %reshape.443, bf16[8,192,128]{2,1,0:T(8,128)(2,1)S(1)} %broadcast_in_dim.113), kind=kLoop, calls=%fused_computation.30 | loop fusion | flops 3604480 | bytes 1435648 | tf_op jit(solution)/shard_map/concatenate | solution.py:234
  14.8 3.5 %all-to-all-start = ((bf16[8,352,128]{2,1,0:T(8,128)(2,1)}), bf16[8,352,128]{2,1,0:T(8,128)(2,1)S(1)}, u32[]{:S(2)}, u32[]{:S(2)}) async-start(bf16[8,352,128]{2,1,0:T(8,128)(2,1)} %fusion.17), calls=%async_computation | async-start | bytes 1441792 | tf_op jit(solution)/shard_map/all_to_all | solution.py:243
  18.4 10.9 %all-to-all-done = bf16[8,352,128]{2,1,0:T(8,128)(2,1)S(1)} async-done(((bf16[8,352,128]{2,1,0:T(8,128)(2,1)}), bf16[8,352,128]{2,1,0:T(8,128)(2,1)S(1)}, u32[]{:S(2)}, u32[]{:S(2)}) %all-to-all-start) | async-done | bytes 720928 | tf_op jit(solution)/shard_map/all_to_all | solution.py:243
  29.5 0.2 fusion.88
  30.1 0.3 reshape_reshape.6
  30.4 0.6 %gather_fusion = bf16[32,32,192]{2,1,0:T(8,128)(2,1)S(1)} fusion(bf16[32,32,192]{2,1,0:T(8,128)(2,1)S(1)} %reshape_reshape.6, s32[1024]{0:T(1024)S(1)} %pad_clamp_fusion.1), kind=kCustom, calls=%fused_computation | custom fusion | bytes 786560 | tf_op jit(solution)/shard_map/jit(_take)/gather | solution.py:263
  31.0 0.1 broadcast_select_fusion
  31.1 0.2 fusion.52
  31.3 0.1 reshape.448
  31.5 3.6 %collective-permute-start.3 = (f32[128,128]{1,0:T(8,128)S(1)}, f32[128,128]{1,0:T(8,128)S(1)}, u32[]{:S(2)}, u32[]{:S(2)}) collective-permute-start(f32[128,128]{1,0:T(8,128)S(1)} %reshape.448), channel_id=1, source_target_pairs={{0,12},{4,0},{8,4},{12,8},{1,13},{5,1},{9,5},{13,9},{2,14},{6,2},{... | collective-permute-start | bytes 196616 | tf_op jit(solution)/shard_map/ppermute | solution.py:145
  35.1 1.0 %collective-permute-start.1 = (f32[128,128]{1,0:T(8,128)S(1)}, f32[128,128]{1,0:T(8,128)S(1)}, u32[]{:S(2)}, u32[]{:S(2)}) collective-permute-start(f32[128,128]{1,0:T(8,128)S(1)} %reshape.448), channel_id=1, source_target_pairs={{0,4},{4,8},{8,12},{12,0},{1,5},{5,9},{9,13},{13,1},{2,6},{6,10},{... | collective-permute-start | bytes 196616 | tf_op jit(solution)/shard_map/ppermute | solution.py:145
  36.1 0.5 %reshape_reshape.7 = bf16[32,36,96]{2,1,0:T(8,128)(2,1)S(1)} reshape(bf16[8,108,128]{2,1,0:T(8,128)(2,1)S(1)} %slice.168) | data formatting | bytes 442368 | tf_op jit(solution)/shard_map/reshape;reshape | solution.py:248
  37.0 0.2 fusion.67
  37.2 0.1 reshape.449
  37.3 0.6 %gather_fusion.1 = bf16[32,36,96]{2,1,0:T(8,128)(2,1)S(1)} fusion(bf16[32,36,96]{2,1,0:T(8,128)(2,1)S(1)} %reshape_reshape.7, s32[1024]{0:T(1024)S(1)} %pad_clamp_fusion), kind=kCustom, calls=%fused_computation.1 | custom fusion | bytes 442496 | tf_op jit(solution)/shard_map/jit(_take)/gather | solution.py:296
  38.0 0.2 multiply_reduce_fusion
  38.2 3.2 %collective-permute-done.2 = f32[128,128]{1,0:T(8,128)S(1)} collective-permute-done((f32[128,128]{1,0:T(8,128)S(1)}, f32[128,128]{1,0:T(8,128)S(1)}, u32[]{:S(2)}, u32[]{:S(2)}) %collective-permute-start.2) | collective-permute-done | bytes 65568 | tf_op jit(solution)/shard_map/ppermute | solution.py:145
  41.4 0.1 div.46
  41.5 0.5 %convolution_convert_fusion = bf16[4,2,2,32,192]{4,3,2,1,0:T(8,128)(2,1)S(1)} fusion(bf16[4,2,4,32,192]{4,3,2,1,0:T(8,128)(2,1)S(1)} %broadcast_select_fusion, f32[4,2,2,32,32]{4,3,2,1,0:T(8,128)S(1)} %div.46, f32[2,4,2,32,32]{4,3,2,1,0:T(8,128)S(1)} %reshape.449, f32[4]{0:T(128)S(1)} %convert_element_type.123, f32[4,2,2]{2,1,0:T(2,128)S(1)} %compare_select_fusion.3), kind=kOutput, calls=%fused_computation.15 | convolution fusion | flops 37896192 | bytes 987648 | tf_op jit(solution)/shard_map/qocij,qocid->qocjd/dot_general | solution.py:283
  42.0 0.4 convolution_convert_fusion.1
  42.6 0.4 fusion.9
  43.0 0.1 bitcast_dynamic-update-slice_fusion.4
  43.2 0.1 bitcast_dynamic-update-slice_fusion.2
  43.5 1.9 %fusion.10 = f32[5,192,96]{2,1,0:T(8,128)} fusion(bf16[5,192,4,8,36]{1,3,4,2,0:T(8,128)(2,1)S(1)} %bitcast.98, bf16[4,8,36,96]{3,2,1,0:T(8,128)(2,1)S(1)} %bitcast.97, pred[4,8]{1,0:T(4,128)(4,1)S(1)} %compare_and_fusion.2), kind=kOutput, calls=%fused_computation.14 | convolution fusion | flops 212447232 | bytes 2801696 | tf_op jit(solution)/shard_map/dot_general | solution.py:304
  (72 shorter events, 2.7 us)
Async XLA Ops:
  0.7 10.0 %collective-permute-start = (bf16[4,768]{1,0:T(4,128)(2,1)S(1)}, bf16[4,768]{1,0:T(4,128)(2,1)S(1)}, u32[]{:S(2)}, u32[]{:S(2)}) collective-permute-start(bf16[4,768]{1,0:T(4,128)(2,1)S(1)} %pad_maximum_fusion.1), channel_id=1, source_target_pairs={{0,16},{16,0},{1,17},{17,1},{2,18},{18,2},{3,19},{19,3},{4,20},{20... | collective-permute-start | bytes 18440 | tf_op jit(solution)/shard_map/ppermute | solution.py:182
  6.3 2.7 %copy-start = (f32[1,1,2,1024]{3,2,1,0:T(2,128)S(1)}, f32[1,1,2,1024]{3,2,1,0:T(2,128)}, u32[]{:S(2)}) copy-start(f32[1,1,2,1024]{3,2,1,0:T(2,128)} %param.11) | copy-start | bytes 24580
  8.2 1.7 %copy-start.1 = (s32[1,2]{1,0:T(1,128)S(1)}, s32[1,2]{1,0:T(1,128)}, u32[]{:S(2)}) copy-start(s32[1,2]{1,0:T(1,128)} %param.10) | copy-start | bytes 28
  9.9 1.5 %copy-start.2 = (bf16[5,192,768]{2,1,0:T(8,128)(2,1)S(1)}, bf16[5,192,768]{2,1,0:T(8,128)(2,1)}, u32[]{:S(2)}) copy-start(bf16[5,192,768]{2,1,0:T(8,128)(2,1)} %param.7) | copy-start | bytes 4423684
  14.8 14.4 %all-to-all-start = ((bf16[8,352,128]{2,1,0:T(8,128)(2,1)}), bf16[8,352,128]{2,1,0:T(8,128)(2,1)S(1)}, u32[]{:S(2)}, u32[]{:S(2)}) async-start(bf16[8,352,128]{2,1,0:T(8,128)(2,1)} %fusion.17), calls=%async_computation | async-start | bytes 1441792 | tf_op jit(solution)/shard_map/all_to_all | solution.py:243
  31.5 6.7 %collective-permute-start.3 = (f32[128,128]{1,0:T(8,128)S(1)}, f32[128,128]{1,0:T(8,128)S(1)}, u32[]{:S(2)}, u32[]{:S(2)}) collective-permute-start(f32[128,128]{1,0:T(8,128)S(1)} %reshape.448), channel_id=1, source_target_pairs={{0,12},{4,0},{8,4},{12,8},{1,13},{5,1},{9,5},{13,9},{2,14},{6,2},{... | collective-permute-start | bytes 196616 | tf_op jit(solution)/shard_map/ppermute | solution.py:145
  35.1 6.3 %collective-permute-start.2 = (f32[128,128]{1,0:T(8,128)S(1)}, f32[128,128]{1,0:T(8,128)S(1)}, u32[]{:S(2)}, u32[]{:S(2)}) collective-permute-start(f32[128,128]{1,0:T(8,128)S(1)} %reshape.448), channel_id=1, source_target_pairs={{0,8},{4,12},{8,0},{12,4},{1,9},{5,13},{9,1},{13,5},{2,10},{6,14},... | collective-permute-start | bytes 196616 | tf_op jit(solution)/shard_map/ppermute | solution.py:145
  35.1 6.3 %collective-permute-start.1 = (f32[128,128]{1,0:T(8,128)S(1)}, f32[128,128]{1,0:T(8,128)S(1)}, u32[]{:S(2)}, u32[]{:S(2)}) collective-permute-start(f32[128,128]{1,0:T(8,128)S(1)} %reshape.448), channel_id=1, source_target_pairs={{0,4},{4,8},{8,12},{12,0},{1,5},{5,9},{9,13},{13,1},{2,6},{6,10},{... | collective-permute-start | bytes 196616 | tf_op jit(solution)/shard_map/ppermute | solution.py:145

commit v20 on v18

--- a/solution.py
+++ b/solution.py
@@ -279,14 +279,17 @@
     )
     row_float = row_side.astype(jnp.float32)
     col_float = col_side.astype(jnp.float32)
-    drow = jnp.einsum("qocij,qocjd->qocid", dpredicted, col_float, precision=lax.Precision.HIGHEST)
-    dcol = jnp.einsum("qocij,qocid->qocjd", dpredicted, row_float, precision=lax.Precision.HIGHEST)
+    drow = jnp.einsum("qocij,qocjd->qocid", dpredicted, col_float, precision=lax.Precision.HIGH)
+    dcol = jnp.einsum("qocij,qocid->qocjd", dpredicted, row_float, precision=lax.Precision.HIGH)
     grads = jnp.concatenate([drow, dcol], axis=2).astype(jnp.bfloat16).astype(jnp.float32)
     grads = grads.reshape(groups, owners * n_sides, TB, narrow)
     flat_sides = sides.reshape(groups, owners * n_sides)
     same_block = flat_sides[:, :, None] == flat_sides[:, None, :]
     total = jnp.einsum(
-        "qab,qbtd->qatd", same_block.astype(jnp.float32), grads, precision=lax.Precision.HIGHEST
+        "qab,qbtd->qatd",
+        same_block.astype(jnp.bfloat16),
+        grads.astype(jnp.bfloat16),
+        preferred_element_type=jnp.float32,
     )
     earlier = jnp.arange(owners * n_sides)[None, :] < jnp.arange(owners * n_sides)[:, None]
     first = jnp.logical_not(jnp.any(jnp.logical_and(same_block, earlier[None]), axis=-1))

time: 44.2 us -> 44.1 us (level)
  no operation moved by 1% of the time
where the time goes in v20:
time: 44.1 us; the launch traced here: 43.8 us
  starting transfers between devices  12.1 us (27%)
  waiting for transfers between devices  11.9 us (27%)
  local copies, waits for them, and re-layouts  9.11 us (21%)
  matrix products  5.73 us (13%)
  other arithmetic  3.76 us (9%)
  between operations  1.11 us (3%)
    all_to_all x1, waiting for transfers between devices, sparse_path(): incoming = lax.all_to_all(outgoing, ('seq', 'dp'), 0, 0, tiled=True)  10.9 us
    ppermute x3, starting transfers between devices, axis_sum(): lax.ppermute(value, axis, [(i, (i + shift) % count) for i in range(count)])  5.56 us
    all_to_all x1, starting transfers between devices, sparse_path(): incoming = lax.all_to_all(outgoing, ('seq', 'dp'), 0, 0, tiled=True)  3.54 us
    ppermute x1, starting transfers between devices, sparse_path(): lax.ppermute(jnp.concatenate([cells[length - halo:], cells[:halo]]), 'seq...  3 us
    dot_general x5, matrix products, sparse_path(): jnp.einsum('qato,qati->oi', dconv, act_sides[:, :, offset:offset + TB], p...  2.25 us
    another operation x1, local copies, waits for them, and re-layouts, sparse_path(): stacked = cells.reshape(per_block, TB * width)  1.89 us
    unnamed x10, local copies, waits for them, and re-layouts  1.13 us
    ppermute x3, waiting for transfers between devices, axis_sum(): lax.ppermute(value, axis, [(i, (i + shift) % count) for i in range(count)])  1.06 us
  transfers between devices with their start and end apart: 5, of which 2 were waited for; matrix products, arithmetic and copies ran while one was open for 16% of the time, Pallas kernels for 0%

profile of v20, /device:TPU:0, one launch (start us, length us, event | category | flops | bytes accessed | tf_op | source)
XLA Modules:
  0.0 43.8 jit_solution(2758648023767690535)
XLA Ops:
  0.0 0.7 %slice_bitcast_fusion.1 = (bf16[2,768]{1,0:T(2,128)(2,1)S(1)}, bf16[2,768]{1,0:T(2,128)(2,1)S(1)}) fusion(bf16[1,1024,768]{2,1,0:T(8,128)(2,1)} %param.6), kind=kLoop, calls=%fused_computation.138 | loop fusion | bytes 12288 | tf_op jit(solution)/shard_map/slice | solution.py:183
  0.7 3.0 %collective-permute-start = (bf16[4,768]{1,0:T(4,128)(2,1)S(1)}, bf16[4,768]{1,0:T(4,128)(2,1)S(1)}, u32[]{:S(2)}, u32[]{:S(2)}) collective-permute-start(bf16[4,768]{1,0:T(4,128)(2,1)S(1)} %pad_maximum_fusion.1), channel_id=1, source_target_pairs={{0,16},{16,0},{1,17},{17,1},{2,18},{18,2},{3,19},{19,3},{4,20},{20... | collective-permute-start | bytes 18440 | tf_op jit(solution)/shard_map/ppermute | solution.py:182
  3.8 1.9 %reshape_squeeze.3 = bf16[32,24576]{1,0:T(8,128)(2,1)S(1)} reshape(bf16[1,1024,768]{2,1,0:T(8,128)(2,1)} %param.6) | data formatting | bytes 3145728 | tf_op jit(solution)/shard_map/reshape;squeeze | solution.py:191
  5.7 0.2 slice_reduce_fusion.1
  6.0 0.2 convert_reduce_fusion
  6.2 0.2 fusion.83
  6.8 0.2 fusion.68
  7.0 0.2 fusion.66
  7.2 0.4 fusion
  8.9 0.3 concatenate.89
  9.5 0.2 fusion.32
  10.0 0.3 copy-done.3
  10.3 0.2 fusion.38
  10.6 0.2 convolution_add_fusion.3
  10.8 0.2 convolution_add_fusion.2
  11.1 0.2 convolution_add_fusion.1
  11.3 0.3 fusion.10
  11.6 0.1 broadcast_in_dim.112
  11.9 0.3 fusion.33
  12.2 0.5 %reshape.430 = bf16[8,108,128]{2,1,0:T(8,128)(2,1)S(1)} reshape(bf16[8,4,36,96]{3,2,1,0:T(8,128)(2,1)S(1)} %fusion.33) | data formatting | bytes 442368 | tf_op jit(solution)/shard_map/reshape | solution.py:218
  12.8 0.9 %fusion.17 = bf16[8,352,128]{2,1,0:T(8,128)(2,1)} fusion(bf16[8,49,128]{2,1,0:T(8,128)(2,1)S(1)} %broadcast_in_dim.121, bf16[8,108,128]{2,1,0:T(8,128)(2,1)S(1)} %reshape.430, bf16[8,192,128]{2,1,0:T(8,128)(2,1)S(1)} %broadcast_in_dim.113), kind=kLoop, calls=%fused_computation.37 | loop fusion | flops 3604480 | bytes 1435648 | tf_op jit(solution)/shard_map/concatenate | solution.py:234
  13.7 3.5 %all-to-all-start = ((bf16[8,352,128]{2,1,0:T(8,128)(2,1)}), bf16[8,352,128]{2,1,0:T(8,128)(2,1)S(1)}, u32[]{:S(2)}, u32[]{:S(2)}) async-start(bf16[8,352,128]{2,1,0:T(8,128)(2,1)} %fusion.17), calls=%async_computation | async-start | bytes 1441792 | tf_op jit(solution)/shard_map/all_to_all | solution.py:243
  17.3 10.9 %all-to-all-done = bf16[8,352,128]{2,1,0:T(8,128)(2,1)S(1)} async-done(((bf16[8,352,128]{2,1,0:T(8,128)(2,1)}), bf16[8,352,128]{2,1,0:T(8,128)(2,1)S(1)}, u32[]{:S(2)}, u32[]{:S(2)}) %all-to-all-start) | async-done | bytes 720928 | tf_op jit(solution)/shard_map/all_to_all | solution.py:243
  28.6 0.3 reshape_reshape.6
  29.1 0.6 %gather_fusion = bf16[32,32,192]{2,1,0:T(8,128)(2,1)S(1)} fusion(bf16[32,32,192]{2,1,0:T(8,128)(2,1)S(1)} %reshape_reshape.6, s32[1024]{0:T(1024)S(1)} %pad_clamp_fusion.1), kind=kCustom, calls=%fused_computation | custom fusion | bytes 786560 | tf_op jit(solution)/shard_map/jit(_take)/gather | solution.py:263
  29.7 0.1 broadcast_select_fusion
  29.8 0.2 fusion.59
  30.0 0.1 reshape.435
  30.1 1.6 %collective-permute-start.1 = (f32[128,128]{1,0:T(8,128)S(1)}, f32[128,128]{1,0:T(8,128)S(1)}, u32[]{:S(2)}, u32[]{:S(2)}) collective-permute-start(f32[128,128]{1,0:T(8,128)S(1)} %reshape.435), channel_id=1, source_target_pairs={{0,4},{4,8},{8,12},{12,0},{1,5},{5,9},{9,13},{13,1},{2,6},{6,10},{... | collective-permute-start | bytes 196616 | tf_op jit(solution)/shard_map/ppermute | solution.py:145
  31.8 2.6 %collective-permute-start.2 = (f32[128,128]{1,0:T(8,128)S(1)}, f32[128,128]{1,0:T(8,128)S(1)}, u32[]{:S(2)}, u32[]{:S(2)}) collective-permute-start(f32[128,128]{1,0:T(8,128)S(1)} %reshape.435), channel_id=1, source_target_pairs={{0,8},{4,12},{8,0},{12,4},{1,9},{5,13},{9,1},{13,5},{2,10},{6,14},... | collective-permute-start | bytes 196616 | tf_op jit(solution)/shard_map/ppermute | solution.py:145
  34.4 1.3 %collective-permute-start.3 = (f32[128,128]{1,0:T(8,128)S(1)}, f32[128,128]{1,0:T(8,128)S(1)}, u32[]{:S(2)}, u32[]{:S(2)}) collective-permute-start(f32[128,128]{1,0:T(8,128)S(1)} %reshape.435), channel_id=1, source_target_pairs={{0,12},{4,0},{8,4},{12,8},{1,13},{5,1},{9,5},{13,9},{2,14},{6,2},{... | collective-permute-start | bytes 196616 | tf_op jit(solution)/shard_map/ppermute | solution.py:145
  35.7 0.2 fusion.93
  35.9 0.5 %reshape_reshape.7 = bf16[32,36,96]{2,1,0:T(8,128)(2,1)S(1)} reshape(bf16[8,108,128]{2,1,0:T(8,128)(2,1)S(1)} %slice.188) | data formatting | bytes 442368 | tf_op jit(solution)/shard_map/reshape;reshape | solution.py:248
  36.8 0.2 fusion.73
  37.0 0.1 reshape.436
  37.2 0.6 %gather_fusion.1 = bf16[32,36,96]{2,1,0:T(8,128)(2,1)S(1)} fusion(bf16[32,36,96]{2,1,0:T(8,128)(2,1)S(1)} %reshape_reshape.7, s32[1024]{0:T(1024)S(1)} %pad_clamp_fusion), kind=kCustom, calls=%fused_computation.1 | custom fusion | bytes 442496 | tf_op jit(solution)/shard_map/jit(_take)/gather | solution.py:299
  38.0 0.2 multiply_reduce_fusion
  38.1 1.1 %collective-permute-done.2 = f32[128,128]{1,0:T(8,128)S(1)} collective-permute-done((f32[128,128]{1,0:T(8,128)S(1)}, f32[128,128]{1,0:T(8,128)S(1)}, u32[]{:S(2)}, u32[]{:S(2)}) %collective-permute-start.2) | collective-permute-done | bytes 65568 | tf_op jit(solution)/shard_map/ppermute | solution.py:145
  39.2 0.1 div.46
  39.4 0.4 convolution_convert_fusion.1
  39.7 0.4 convolution_convert_fusion
  40.2 0.4 %fusion.7 = bf16[4,8,32,192]{3,1,2,0:T(8,128)(2,1)S(1)} fusion(bf16[4,8,32,192]{3,2,1,0:T(8,128)(2,1)S(1)} %bitcast.119, f32[4]{0:T(128)S(1)} %multiply_reduce_fusion, pred[4,8]{1,0:T(4,128)(4,1)S(1)} %not.7, s32[4,8]{1,0:T(4,128)S(1)} %copy.158), kind=kOutput, calls=%fused_computation.11 | convolution fusion | flops 3735808 | bytes 786608 | tf_op jit(solution)/shard_map/qab,qbtd->qatd/dot_general | solution.py:288
  40.7 0.3 fusion.15
  41.0 0.3 fusion.14
  41.4 0.3 fusion.13
  41.7 0.3 fusion.12
  42.0 0.8 %copy-done.4 = f32[5,192,96]{2,1,0:T(8,128)} copy-done((f32[5,192,96]{2,1,0:T(8,128)}, f32[5,192,96]{2,1,0:T(8,128)S(1)}, u32[]{:S(2)}) %copy-start.4) | copy-done | bytes 368664
  42.8 1.0 %fusion.11 = f32[5,192,96]{2,1,0:T(8,128)} fusion(f32[5,192,96]{2,1,0:T(8,128)} %copy-done.4, bf16[4,8,32,192]{3,1,2,0:T(8,128)(2,1)S(1)} %fusion.7, bf16[4,8,36,96]{3,2,0,1:T(8,128)(2,1)S(1)} %copy_select_fusion), kind=kOutput, calls=%fused_computation.26 | convolution fusion | flops 37748736 | bytes 884736 | tf_op jit(solution)/shard_map/qato,qati->oi/dot_general | solution.py:302
  (77 shorter events, 3.1 us)
Async XLA Ops:
  0.7 8.6 %collective-permute-start = (bf16[4,768]{1,0:T(4,128)(2,1)S(1)}, bf16[4,768]{1,0:T(4,128)(2,1)S(1)}, u32[]{:S(2)}, u32[]{:S(2)}) collective-permute-start(bf16[4,768]{1,0:T(4,128)(2,1)S(1)} %pad_maximum_fusion.1), channel_id=1, source_target_pairs={{0,16},{16,0},{1,17},{17,1},{2,18},{18,2},{3,19},{19,3},{4,20},{20... | collective-permute-start | bytes 18440 | tf_op jit(solution)/shard_map/ppermute | solution.py:182
  3.8 1.9 %copy-start = (s32[1,2,2,2]{3,2,1,0:T(2,128)S(1)}, s32[1,2,2,2]{3,2,1,0:T(2,128)}, u32[]{:S(2)}) copy-start(s32[1,2,2,2]{3,2,1,0:T(2,128)} %param.9) | copy-start | bytes 100
  5.7 2.8 %copy-start.1 = (f32[1,1,2,1024]{3,2,1,0:T(2,128)S(1)}, f32[1,1,2,1024]{3,2,1,0:T(2,128)}, u32[]{:S(2)}) copy-start(f32[1,1,2,1024]{3,2,1,0:T(2,128)} %param.11) | copy-start | bytes 24580
  5.7 2.8 %copy-start.2 = (s32[1,2]{1,0:T(1,128)S(1)}, s32[1,2]{1,0:T(1,128)}, u32[]{:S(2)}) copy-start(s32[1,2]{1,0:T(1,128)} %param.10) | copy-start | bytes 28
  8.9 1.4 %copy-start.3 = (bf16[5,192,768]{2,1,0:T(8,128)(2,1)S(1)}, bf16[5,192,768]{2,1,0:T(8,128)(2,1)}, u32[]{:S(2)}) copy-start(bf16[5,192,768]{2,1,0:T(8,128)(2,1)} %param.7) | copy-start | bytes 4423684
  13.7 14.4 %all-to-all-start = ((bf16[8,352,128]{2,1,0:T(8,128)(2,1)}), bf16[8,352,128]{2,1,0:T(8,128)(2,1)S(1)}, u32[]{:S(2)}, u32[]{:S(2)}) async-start(bf16[8,352,128]{2,1,0:T(8,128)(2,1)} %fusion.17), calls=%async_computation | async-start | bytes 1441792 | tf_op jit(solution)/shard_map/all_to_all | solution.py:243
  30.1 8.0 %collective-permute-start.1 = (f32[128,128]{1,0:T(8,128)S(1)}, f32[128,128]{1,0:T(8,128)S(1)}, u32[]{:S(2)}, u32[]{:S(2)}) collective-permute-start(f32[128,128]{1,0:T(8,128)S(1)} %reshape.435), channel_id=1, source_target_pairs={{0,4},{4,8},{8,12},{12,0},{1,5},{5,9},{9,13},{13,1},{2,6},{6,10},{... | collective-permute-start | bytes 196616 | tf_op jit(solution)/shard_map/ppermute | solution.py:145
  31.8 7.4 %collective-permute-start.2 = (f32[128,128]{1,0:T(8,128)S(1)}, f32[128,128]{1,0:T(8,128)S(1)}, u32[]{:S(2)}, u32[]{:S(2)}) collective-permute-start(f32[128,128]{1,0:T(8,128)S(1)} %reshape.435), channel_id=1, source_target_pairs={{0,8},{4,12},{8,0},{12,4},{1,9},{5,13},{9,1},{13,5},{2,10},{6,14},... | collective-permute-start | bytes 196616 | tf_op jit(solution)/shard_map/ppermute | solution.py:145
  34.4 4.8 %collective-permute-start.3 = (f32[128,128]{1,0:T(8,128)S(1)}, f32[128,128]{1,0:T(8,128)S(1)}, u32[]{:S(2)}, u32[]{:S(2)}) collective-permute-start(f32[128,128]{1,0:T(8,128)S(1)} %reshape.435), channel_id=1, source_target_pairs={{0,12},{4,0},{8,4},{12,8},{1,13},{5,1},{9,5},{13,9},{2,14},{6,2},{... | collective-permute-start | bytes 196616 | tf_op jit(solution)/shard_map/ppermute | solution.py:145
  42.0 0.8 %copy-start.4 = (f32[5,192,96]{2,1,0:T(8,128)}, f32[5,192,96]{2,1,0:T(8,128)S(1)}, u32[]{:S(2)}) copy-start(f32[5,192,96]{2,1,0:T(8,128)S(1)} %fusion.12) | copy-start | bytes 1105924

commit v21 on v18

--- a/solution.py
+++ b/solution.py
@@ -260,7 +260,10 @@
 
     sides = jnp.concatenate([tiles_all[..., 0], tiles_all[..., 1]], axis=-1)
 
-    side_rows = jnp.take(mixed_in, slot, axis=0)
+    pick_slot = (slot[..., None] == jnp.arange(peers * held)).astype(jnp.bfloat16)
+    side_rows = jnp.dot(
+        pick_slot.reshape(-1, peers * held), mixed_in.reshape(peers * held, -1), preferred_element_type=jnp.float32
+    ).astype(jnp.bfloat16).reshape(slot.shape + (TB, narrow))
     row_side = side_rows[:, :, :capacity]
     col_side = side_rows[:, :, capacity:]
     partial_tiles = jnp.einsum("qocid,qocjd->qocij", row_side, col_side, preferred_element_type=jnp.float32)

time: 44.2 us -> 44.1 us (level)
    gather x1 -> x0, local copies, waits for them, and re-layouts: 0.58 us -> none  [sparse_path(): side_rows = jnp.take(mixed_in, slot, axis=0)]
    reshape x2 -> x1, local copies, waits for them, and re-layouts: 0.16 us -> 0.61 us  [sparse_path(): side_rows = jnp.dot(pick_slot.reshape(-1, peers * held), mixed_in.reshape...]
where the time goes in v21:
time: 44.1 us; the launch traced here: 43.7 us
  starting transfers between devices  12.1 us (27%)
  waiting for transfers between devices  11.9 us (27%)
  local copies, waits for them, and re-layouts  8.8 us (20%)
  matrix products  6.18 us (14%)
  other arithmetic  3.62 us (8%)
  between operations  1.1 us (2%)
    all_to_all x1, waiting for transfers between devices, sparse_path(): incoming = lax.all_to_all(outgoing, ('seq', 'dp'), 0, 0, tiled=True)  10.9 us
    ppermute x3, starting transfers between devices, axis_sum(): lax.ppermute(value, axis, [(i, (i + shift) % count) for i in range(count)])  5.56 us
    all_to_all x1, starting transfers between devices, sparse_path(): incoming = lax.all_to_all(outgoing, ('seq', 'dp'), 0, 0, tiled=True)  3.54 us
    ppermute x1, starting transfers between devices, sparse_path(): lax.ppermute(jnp.concatenate([cells[length - halo:], cells[:halo]]), 'seq...  3 us
    dot_general x5, matrix products, sparse_path(): jnp.einsum('qato,qati->oi', dconv, act_sides[:, :, offset:offset + TB], p...  2.25 us
    another operation x1, local copies, waits for them, and re-layouts, sparse_path(): stacked = cells.reshape(per_block, TB * width)  1.89 us
    unnamed x10, local copies, waits for them, and re-layouts  1.13 us
    ppermute x3, waiting for transfers between devices, axis_sum(): lax.ppermute(value, axis, [(i, (i + shift) % count) for i in range(count)])  1.07 us
  transfers between devices with their start and end apart: 5, of which 2 were waited for; matrix products, arithmetic and copies ran while one was open for 16% of the time, Pallas kernels for 0%

profile of v21, /device:TPU:0, one launch (start us, length us, event | category | flops | bytes accessed | tf_op | source)
XLA Modules:
  0.0 43.7 jit_solution(13839593702720903324)
XLA Ops:
  0.0 0.7 %slice_bitcast_fusion.1 = (bf16[2,768]{1,0:T(2,128)(2,1)S(1)}, bf16[2,768]{1,0:T(2,128)(2,1)S(1)}) fusion(bf16[1,1024,768]{2,1,0:T(8,128)(2,1)} %param.6), kind=kLoop, calls=%fused_computation.135 | loop fusion | bytes 12288 | tf_op jit(solution)/shard_map/slice | solution.py:183
  0.7 3.0 %collective-permute-start = (bf16[4,768]{1,0:T(4,128)(2,1)S(1)}, bf16[4,768]{1,0:T(4,128)(2,1)S(1)}, u32[]{:S(2)}, u32[]{:S(2)}) collective-permute-start(bf16[4,768]{1,0:T(4,128)(2,1)S(1)} %pad_maximum_fusion.1), channel_id=1, source_target_pairs={{0,16},{16,0},{1,17},{17,1},{2,18},{18,2},{3,19},{19,3},{4,20},{20... | collective-permute-start | bytes 18440 | tf_op jit(solution)/shard_map/ppermute | solution.py:182
  3.8 1.9 %reshape_squeeze.3 = bf16[32,24576]{1,0:T(8,128)(2,1)S(1)} reshape(bf16[1,1024,768]{2,1,0:T(8,128)(2,1)} %param.6) | data formatting | bytes 3145728 | tf_op jit(solution)/shard_map/reshape;squeeze | solution.py:191
  5.7 0.2 slice_reduce_fusion.1
  6.0 0.2 convert_reduce_fusion
  6.2 0.2 fusion.84
  6.8 0.2 fusion.68
  7.0 0.2 fusion.66
  7.2 0.4 fusion
  8.9 0.3 concatenate.89
  9.5 0.2 fusion.32
  10.0 0.3 copy-done.3
  10.3 0.2 fusion.38
  10.6 0.2 convolution_add_fusion.3
  10.8 0.2 convolution_add_fusion.2
  11.1 0.2 convolution_add_fusion.1
  11.3 0.3 fusion.10
  11.6 0.1 broadcast_in_dim.103
  11.9 0.3 fusion.33
  12.2 0.5 %reshape.398 = bf16[8,108,128]{2,1,0:T(8,128)(2,1)S(1)} reshape(bf16[8,4,36,96]{3,2,1,0:T(8,128)(2,1)S(1)} %fusion.33) | data formatting | bytes 442368 | tf_op jit(solution)/shard_map/reshape | solution.py:218
  12.8 0.9 %fusion.17 = bf16[8,352,128]{2,1,0:T(8,128)(2,1)} fusion(bf16[8,49,128]{2,1,0:T(8,128)(2,1)S(1)} %broadcast_in_dim.112, bf16[8,108,128]{2,1,0:T(8,128)(2,1)S(1)} %reshape.398, bf16[8,192,128]{2,1,0:T(8,128)(2,1)S(1)} %broadcast_in_dim.104), kind=kLoop, calls=%fused_computation.37 | loop fusion | flops 3604480 | bytes 1435648 | tf_op jit(solution)/shard_map/concatenate | solution.py:234
  13.7 3.5 %all-to-all-start = ((bf16[8,352,128]{2,1,0:T(8,128)(2,1)}), bf16[8,352,128]{2,1,0:T(8,128)(2,1)S(1)}, u32[]{:S(2)}, u32[]{:S(2)}) async-start(bf16[8,352,128]{2,1,0:T(8,128)(2,1)} %fusion.17), calls=%async_computation | async-start | bytes 1441792 | tf_op jit(solution)/shard_map/all_to_all | solution.py:243
  17.3 10.9 %all-to-all-done = bf16[8,352,128]{2,1,0:T(8,128)(2,1)S(1)} async-done(((bf16[8,352,128]{2,1,0:T(8,128)(2,1)}), bf16[8,352,128]{2,1,0:T(8,128)(2,1)S(1)}, u32[]{:S(2)}, u32[]{:S(2)}) %all-to-all-start) | async-done | bytes 720928 | tf_op jit(solution)/shard_map/all_to_all | solution.py:243
  28.5 0.2 reshape_reshape_reshape.3
  28.7 0.3 convolution_convert_fusion
  29.0 0.6 %reshape.401 = bf16[4,2,4,32,192]{4,3,2,1,0:T(8,128)(2,1)S(1)} reshape(bf16[32,6144]{1,0:T(8,128)(2,1)S(1)} %convolution_convert_fusion) | data formatting | bytes 786432 | tf_op jit(solution)/shard_map/reshape | solution.py:266
  29.6 0.2 fusion.59
  29.9 0.1 reshape.402
  30.0 1.6 %collective-permute-start.1 = (f32[128,128]{1,0:T(8,128)S(1)}, f32[128,128]{1,0:T(8,128)S(1)}, u32[]{:S(2)}, u32[]{:S(2)}) collective-permute-start(f32[128,128]{1,0:T(8,128)S(1)} %reshape.402), channel_id=1, source_target_pairs={{0,4},{4,8},{8,12},{12,0},{1,5},{5,9},{9,13},{13,1},{2,6},{6,10},{... | collective-permute-start | bytes 196616 | tf_op jit(solution)/shard_map/ppermute | solution.py:145
  31.6 2.6 %collective-permute-start.2 = (f32[128,128]{1,0:T(8,128)S(1)}, f32[128,128]{1,0:T(8,128)S(1)}, u32[]{:S(2)}, u32[]{:S(2)}) collective-permute-start(f32[128,128]{1,0:T(8,128)S(1)} %reshape.402), channel_id=1, source_target_pairs={{0,8},{4,12},{8,0},{12,4},{1,9},{5,13},{9,1},{13,5},{2,10},{6,14},... | collective-permute-start | bytes 196616 | tf_op jit(solution)/shard_map/ppermute | solution.py:145
  34.2 1.3 %collective-permute-start.3 = (f32[128,128]{1,0:T(8,128)S(1)}, f32[128,128]{1,0:T(8,128)S(1)}, u32[]{:S(2)}, u32[]{:S(2)}) collective-permute-start(f32[128,128]{1,0:T(8,128)S(1)} %reshape.402), channel_id=1, source_target_pairs={{0,12},{4,0},{8,4},{12,8},{1,13},{5,1},{9,5},{13,9},{2,14},{6,2},{... | collective-permute-start | bytes 196616 | tf_op jit(solution)/shard_map/ppermute | solution.py:145
  35.6 0.2 fusion.94
  35.8 0.5 %reshape_reshape.3 = bf16[32,36,96]{2,1,0:T(8,128)(2,1)S(1)} reshape(bf16[8,108,128]{2,1,0:T(8,128)(2,1)S(1)} %slice.186) | data formatting | bytes 442368 | tf_op jit(solution)/shard_map/reshape;reshape | solution.py:248
  36.6 0.2 fusion.73
  36.8 0.1 reshape.403
  37.1 0.6 %gather_fusion = bf16[32,36,96]{2,1,0:T(8,128)(2,1)S(1)} fusion(bf16[32,36,96]{2,1,0:T(8,128)(2,1)S(1)} %reshape_reshape.3, s32[1024]{0:T(1024)S(1)} %pad_clamp_fusion), kind=kCustom, calls=%fused_computation | custom fusion | bytes 442496 | tf_op jit(solution)/shard_map/jit(_take)/gather | solution.py:299
  37.8 0.2 multiply_reduce_fusion
  38.0 1.1 %collective-permute-done.2 = f32[128,128]{1,0:T(8,128)S(1)} collective-permute-done((f32[128,128]{1,0:T(8,128)S(1)}, f32[128,128]{1,0:T(8,128)S(1)}, u32[]{:S(2)}, u32[]{:S(2)}) %collective-permute-start.2) | collective-permute-done | bytes 65568 | tf_op jit(solution)/shard_map/ppermute | solution.py:145
  39.1 0.1 div.46
  39.2 0.4 convolution_convert_fusion.2
  39.6 0.5 %convolution_convert_fusion.1 = bf16[4,2,2,32,192]{4,3,2,1,0:T(8,128)(2,1)S(1)} fusion(bf16[4,2,4,32,192]{4,3,2,1,0:T(8,128)(2,1)S(1)} %reshape.401, f32[4,2,2,32,32]{4,3,2,1,0:T(8,128)S(1)} %div.46, f32[2,4,2,32,32]{4,3,2,1,0:T(8,128)S(1)} %reshape.403, f32[4]{0:T(128)S(1)} %convert_element_type.118, f32[4,2,2]{2,1,0:T(2,128)S(1)} %compare_select_fusion.1), kind=kOutput, calls=%fused_computation.12 | convolution fusion | flops 37896192 | bytes 987648 | tf_op jit(solution)/shard_map/qocij,qocid->qocjd/dot_general | solution.py:286
  40.2 0.4 %fusion.7 = bf16[4,8,32,192]{3,1,2,0:T(8,128)(2,1)S(1)} fusion(bf16[4,8,32,192]{3,2,1,0:T(8,128)(2,1)S(1)} %bitcast.116, f32[4]{0:T(128)S(1)} %multiply_reduce_fusion, pred[4,8]{1,0:T(4,128)(4,1)S(1)} %not.7, s32[4,8]{1,0:T(4,128)S(1)} %copy.157), kind=kOutput, calls=%fused_computation.11 | convolution fusion | flops 3735808 | bytes 786608 | tf_op jit(solution)/shard_map/qab,qbtd->qatd/dot_general | solution.py:291
  40.7 0.3 fusion.15
  41.0 0.3 fusion.14
  41.3 0.3 fusion.13
  41.7 0.3 fusion.12
  42.0 0.8 %copy-done.4 = f32[5,192,96]{2,1,0:T(8,128)} copy-done((f32[5,192,96]{2,1,0:T(8,128)}, f32[5,192,96]{2,1,0:T(8,128)S(1)}, u32[]{:S(2)}) %copy-start.4) | copy-done | bytes 368664
  42.8 1.0 %fusion.11 = f32[5,192,96]{2,1,0:T(8,128)} fusion(f32[5,192,96]{2,1,0:T(8,128)} %copy-done.4, bf16[4,8,32,192]{3,1,2,0:T(8,128)(2,1)S(1)} %fusion.7, bf16[4,8,36,96]{3,2,0,1:T(8,128)(2,1)S(1)} %copy_select_fusion), kind=kOutput, calls=%fused_computation.26 | convolution fusion | flops 37748736 | bytes 884736 | tf_op jit(solution)/shard_map/qato,qati->oi/dot_general | solution.py:302
  (72 shorter events, 2.9 us)
Async XLA Ops:
  0.7 8.6 %collective-permute-start = (bf16[4,768]{1,0:T(4,128)(2,1)S(1)}, bf16[4,768]{1,0:T(4,128)(2,1)S(1)}, u32[]{:S(2)}, u32[]{:S(2)}) collective-permute-start(bf16[4,768]{1,0:T(4,128)(2,1)S(1)} %pad_maximum_fusion.1), channel_id=1, source_target_pairs={{0,16},{16,0},{1,17},{17,1},{2,18},{18,2},{3,19},{19,3},{4,20},{20... | collective-permute-start | bytes 18440 | tf_op jit(solution)/shard_map/ppermute | solution.py:182
  3.8 1.9 %copy-start = (s32[1,2,2,2]{3,2,1,0:T(2,128)S(1)}, s32[1,2,2,2]{3,2,1,0:T(2,128)}, u32[]{:S(2)}) copy-start(s32[1,2,2,2]{3,2,1,0:T(2,128)} %param.9) | copy-start | bytes 100
  5.7 2.8 %copy-start.1 = (f32[1,1,2,1024]{3,2,1,0:T(2,128)S(1)}, f32[1,1,2,1024]{3,2,1,0:T(2,128)}, u32[]{:S(2)}) copy-start(f32[1,1,2,1024]{3,2,1,0:T(2,128)} %param.11) | copy-start | bytes 24580
  5.7 2.8 %copy-start.2 = (s32[1,2]{1,0:T(1,128)S(1)}, s32[1,2]{1,0:T(1,128)}, u32[]{:S(2)}) copy-start(s32[1,2]{1,0:T(1,128)} %param.10) | copy-start | bytes 28
  8.9 1.4 %copy-start.3 = (bf16[5,192,768]{2,1,0:T(8,128)(2,1)S(1)}, bf16[5,192,768]{2,1,0:T(8,128)(2,1)}, u32[]{:S(2)}) copy-start(bf16[5,192,768]{2,1,0:T(8,128)(2,1)} %param.7) | copy-start | bytes 4423684
  13.7 14.4 %all-to-all-start = ((bf16[8,352,128]{2,1,0:T(8,128)(2,1)}), bf16[8,352,128]{2,1,0:T(8,128)(2,1)S(1)}, u32[]{:S(2)}, u32[]{:S(2)}) async-start(bf16[8,352,128]{2,1,0:T(8,128)(2,1)} %fusion.17), calls=%async_computation | async-start | bytes 1441792 | tf_op jit(solution)/shard_map/all_to_all | solution.py:243
  30.0 8.0 %collective-permute-start.1 = (f32[128,128]{1,0:T(8,128)S(1)}, f32[128,128]{1,0:T(8,128)S(1)}, u32[]{:S(2)}, u32[]{:S(2)}) collective-permute-start(f32[128,128]{1,0:T(8,128)S(1)} %reshape.402), channel_id=1, source_target_pairs={{0,4},{4,8},{8,12},{12,0},{1,5},{5,9},{9,13},{13,1},{2,6},{6,10},{... | collective-permute-start | bytes 196616 | tf_op jit(solution)/shard_map/ppermute | solution.py:145
  31.6 7.4 %collective-permute-start.2 = (f32[128,128]{1,0:T(8,128)S(1)}, f32[128,128]{1,0:T(8,128)S(1)}, u32[]{:S(2)}, u32[]{:S(2)}) collective-permute-start(f32[128,128]{1,0:T(8,128)S(1)} %reshape.402), channel_id=1, source_target_pairs={{0,8},{4,12},{8,0},{12,4},{1,9},{5,13},{9,1},{13,5},{2,10},{6,14},... | collective-permute-start | bytes 196616 | tf_op jit(solution)/shard_map/ppermute | solution.py:145
  34.2 4.9 %collective-permute-start.3 = (f32[128,128]{1,0:T(8,128)S(1)}, f32[128,128]{1,0:T(8,128)S(1)}, u32[]{:S(2)}, u32[]{:S(2)}) collective-permute-start(f32[128,128]{1,0:T(8,128)S(1)} %reshape.402), channel_id=1, source_target_pairs={{0,12},{4,0},{8,4},{12,8},{1,13},{5,1},{9,5},{13,9},{2,14},{6,2},{... | collective-permute-start | bytes 196616 | tf_op jit(solution)/shard_map/ppermute | solution.py:145
  42.0 0.8 %copy-start.4 = (f32[5,192,96]{2,1,0:T(8,128)}, f32[5,192,96]{2,1,0:T(8,128)S(1)}, u32[]{:S(2)}) copy-start(f32[5,192,96]{2,1,0:T(8,128)S(1)} %fusion.12) | copy-start | bytes 1105924

commit v22 on v21

--- a/solution.py
+++ b/solution.py
@@ -141,7 +141,8 @@
 def axis_sum(value, axis):
     count = lax.axis_size(axis)
     total = value
-    for shift in range(1, count):
+    middle = count // 2
+    for shift in [middle] + [k for k in range(1, count) if k != middle]:
         total = total + lax.ppermute(value, axis, [(i, (i + shift) % count) for i in range(count)])
     return total
 

time: 44.1 us -> 44.2 us (level)
  starting transfers between devices: 12.1 us -> 13 us
  waiting for transfers between devices: 11.9 us -> 11.1 us
    ppermute x3, starting transfers between devices: 5.56 us -> 6.47 us  [axis_sum(): lax.ppermute(value, axis, [(i, (i + shift) % count) for i in range(count)])]
    ppermute x3, waiting for transfers between devices: 1.07 us -> 0.28 us  [axis_sum(): lax.ppermute(value, axis, [(i, (i + shift) % count) for i in range(count)])]
where the time goes in v22:
time: 44.2 us; the launch traced here: 43.9 us
  starting transfers between devices  13 us (29%)
  waiting for transfers between devices  11.1 us (25%)
  local copies, waits for them, and re-layouts  8.8 us (20%)
  matrix products  6.18 us (14%)
  other arithmetic  3.62 us (8%)
  between operations  1.1 us (2%)
    all_to_all x1, waiting for transfers between devices, sparse_path(): incoming = lax.all_to_all(outgoing, ('seq', 'dp'), 0, 0, tiled=True)  10.9 us
    ppermute x3, starting transfers between devices, axis_sum(): lax.ppermute(value, axis, [(i, (i + shift) % count) for i in range(count)])  6.47 us
    all_to_all x1, starting transfers between devices, sparse_path(): incoming = lax.all_to_all(outgoing, ('seq', 'dp'), 0, 0, tiled=True)  3.54 us
    ppermute x1, starting transfers between devices, sparse_path(): lax.ppermute(jnp.concatenate([cells[length - halo:], cells[:halo]]), 'seq...  3 us
    dot_general x5, matrix products, sparse_path(): jnp.einsum('qato,qati->oi', dconv, act_sides[:, :, offset:offset + TB], p...  2.25 us
    another operation x1, local copies, waits for them, and re-layouts, sparse_path(): stacked = cells.reshape(per_block, TB * width)  1.89 us
    unnamed x10, local copies, waits for them, and re-layouts  1.13 us
    dot_general x4, matrix products, sparse_path(): jnp.einsum('hti,oi->hto', act[:, offset:offset + TB], conv_weight[offset]...  1.02 us
  transfers between devices with their start and end apart: 5, of which 2 were waited for; matrix products, arithmetic and copies ran while one was open for 16% of the time, Pallas kernels for 0%

profile of v22, /device:TPU:0, one launch (start us, length us, event | category | flops | bytes accessed | tf_op | source)
XLA Modules:
  0.0 43.9 jit_solution(13293488010732906292)
XLA Ops:
  0.0 0.7 %slice_bitcast_fusion.1 = (bf16[2,768]{1,0:T(2,128)(2,1)S(1)}, bf16[2,768]{1,0:T(2,128)(2,1)S(1)}) fusion(bf16[1,1024,768]{2,1,0:T(8,128)(2,1)} %param.6), kind=kLoop, calls=%fused_computation.135 | loop fusion | bytes 12288 | tf_op jit(solution)/shard_map/slice | solution.py:184
  0.7 3.0 %collective-permute-start = (bf16[4,768]{1,0:T(4,128)(2,1)S(1)}, bf16[4,768]{1,0:T(4,128)(2,1)S(1)}, u32[]{:S(2)}, u32[]{:S(2)}) collective-permute-start(bf16[4,768]{1,0:T(4,128)(2,1)S(1)} %pad_maximum_fusion.1), channel_id=1, source_target_pairs={{0,16},{16,0},{1,17},{17,1},{2,18},{18,2},{3,19},{19,3},{4,20},{20... | collective-permute-start | bytes 18440 | tf_op jit(solution)/shard_map/ppermute | solution.py:183
  3.8 1.9 %reshape_squeeze.3 = bf16[32,24576]{1,0:T(8,128)(2,1)S(1)} reshape(bf16[1,1024,768]{2,1,0:T(8,128)(2,1)} %param.6) | data formatting | bytes 3145728 | tf_op jit(solution)/shard_map/reshape;squeeze | solution.py:192
  5.7 0.2 slice_reduce_fusion.1
  6.0 0.2 convert_reduce_fusion
  6.2 0.2 fusion.84
  6.8 0.2 fusion.68
  7.0 0.2 fusion.66
  7.2 0.4 fusion
  8.9 0.3 concatenate.89
  9.5 0.2 fusion.32
  10.0 0.3 copy-done.3
  10.3 0.2 fusion.38
  10.6 0.2 convolution_add_fusion.3
  10.8 0.2 convolution_add_fusion.2
  11.1 0.2 convolution_add_fusion.1
  11.3 0.3 fusion.10
  11.6 0.1 broadcast_in_dim.103
  11.9 0.3 fusion.33
  12.2 0.5 %reshape.398 = bf16[8,108,128]{2,1,0:T(8,128)(2,1)S(1)} reshape(bf16[8,4,36,96]{3,2,1,0:T(8,128)(2,1)S(1)} %fusion.33) | data formatting | bytes 442368 | tf_op jit(solution)/shard_map/reshape | solution.py:219
  12.8 0.9 %fusion.17 = bf16[8,352,128]{2,1,0:T(8,128)(2,1)} fusion(bf16[8,49,128]{2,1,0:T(8,128)(2,1)S(1)} %broadcast_in_dim.112, bf16[8,108,128]{2,1,0:T(8,128)(2,1)S(1)} %reshape.398, bf16[8,192,128]{2,1,0:T(8,128)(2,1)S(1)} %broadcast_in_dim.104), kind=kLoop, calls=%fused_computation.37 | loop fusion | flops 3604480 | bytes 1435648 | tf_op jit(solution)/shard_map/concatenate | solution.py:235
  13.7 3.5 %all-to-all-start = ((bf16[8,352,128]{2,1,0:T(8,128)(2,1)}), bf16[8,352,128]{2,1,0:T(8,128)(2,1)S(1)}, u32[]{:S(2)}, u32[]{:S(2)}) async-start(bf16[8,352,128]{2,1,0:T(8,128)(2,1)} %fusion.17), calls=%async_computation | async-start | bytes 1441792 | tf_op jit(solution)/shard_map/all_to_all | solution.py:244
  17.3 10.9 %all-to-all-done = bf16[8,352,128]{2,1,0:T(8,128)(2,1)S(1)} async-done(((bf16[8,352,128]{2,1,0:T(8,128)(2,1)}), bf16[8,352,128]{2,1,0:T(8,128)(2,1)S(1)}, u32[]{:S(2)}, u32[]{:S(2)}) %all-to-all-start) | async-done | bytes 720928 | tf_op jit(solution)/shard_map/all_to_all | solution.py:244
  28.5 0.2 reshape_reshape_reshape.3
  28.7 0.3 convolution_convert_fusion
  29.0 0.6 %reshape.401 = bf16[4,2,4,32,192]{4,3,2,1,0:T(8,128)(2,1)S(1)} reshape(bf16[32,6144]{1,0:T(8,128)(2,1)S(1)} %convolution_convert_fusion) | data formatting | bytes 786432 | tf_op jit(solution)/shard_map/reshape | solution.py:267
  29.6 0.2 fusion.59
  29.9 0.1 reshape.402
  30.0 2.6 %collective-permute-start.1 = (f32[128,128]{1,0:T(8,128)S(1)}, f32[128,128]{1,0:T(8,128)S(1)}, u32[]{:S(2)}, u32[]{:S(2)}) collective-permute-start(f32[128,128]{1,0:T(8,128)S(1)} %reshape.402), channel_id=1, source_target_pairs={{0,8},{4,12},{8,0},{12,4},{1,9},{5,13},{9,1},{13,5},{2,10},{6,14},... | collective-permute-start | bytes 196616 | tf_op jit(solution)/shard_map/ppermute | solution.py:146
  32.6 1.6 %collective-permute-start.2 = (f32[128,128]{1,0:T(8,128)S(1)}, f32[128,128]{1,0:T(8,128)S(1)}, u32[]{:S(2)}, u32[]{:S(2)}) collective-permute-start(f32[128,128]{1,0:T(8,128)S(1)} %reshape.402), channel_id=1, source_target_pairs={{0,4},{4,8},{8,12},{12,0},{1,5},{5,9},{9,13},{13,1},{2,6},{6,10},{... | collective-permute-start | bytes 196616 | tf_op jit(solution)/shard_map/ppermute | solution.py:146
  34.2 2.2 %collective-permute-start.3 = (f32[128,128]{1,0:T(8,128)S(1)}, f32[128,128]{1,0:T(8,128)S(1)}, u32[]{:S(2)}, u32[]{:S(2)}) collective-permute-start(f32[128,128]{1,0:T(8,128)S(1)} %reshape.402), channel_id=1, source_target_pairs={{0,12},{4,0},{8,4},{12,8},{1,13},{5,1},{9,5},{13,9},{2,14},{6,2},{... | collective-permute-start | bytes 196616 | tf_op jit(solution)/shard_map/ppermute | solution.py:146
  36.5 0.2 fusion.94
  36.7 0.5 %reshape_reshape.3 = bf16[32,36,96]{2,1,0:T(8,128)(2,1)S(1)} reshape(bf16[8,108,128]{2,1,0:T(8,128)(2,1)S(1)} %slice.186) | data formatting | bytes 442368 | tf_op jit(solution)/shard_map/reshape;reshape | solution.py:249
  37.5 0.2 fusion.73
  37.8 0.1 reshape.403
  38.0 0.6 %gather_fusion = bf16[32,36,96]{2,1,0:T(8,128)(2,1)S(1)} fusion(bf16[32,36,96]{2,1,0:T(8,128)(2,1)S(1)} %reshape_reshape.3, s32[1024]{0:T(1024)S(1)} %pad_clamp_fusion), kind=kCustom, calls=%fused_computation | custom fusion | bytes 442496 | tf_op jit(solution)/shard_map/jit(_take)/gather | solution.py:300
  38.7 0.2 multiply_reduce_fusion
  38.9 0.3 collective-permute-done.3
  39.2 0.1 div.46
  39.3 0.4 convolution_convert_fusion.2
  39.7 0.5 %convolution_convert_fusion.1 = bf16[4,2,2,32,192]{4,3,2,1,0:T(8,128)(2,1)S(1)} fusion(bf16[4,2,4,32,192]{4,3,2,1,0:T(8,128)(2,1)S(1)} %reshape.401, f32[4,2,2,32,32]{4,3,2,1,0:T(8,128)S(1)} %div.46, f32[2,4,2,32,32]{4,3,2,1,0:T(8,128)S(1)} %reshape.403, f32[4]{0:T(128)S(1)} %convert_element_type.118, f32[4,2,2]{2,1,0:T(2,128)S(1)} %compare_select_fusion.1), kind=kOutput, calls=%fused_computation.12 | convolution fusion | flops 37896192 | bytes 987648 | tf_op jit(solution)/shard_map/qocij,qocid->qocjd/dot_general | solution.py:287
  40.3 0.4 %fusion.7 = bf16[4,8,32,192]{3,1,2,0:T(8,128)(2,1)S(1)} fusion(bf16[4,8,32,192]{3,2,1,0:T(8,128)(2,1)S(1)} %bitcast.116, f32[4]{0:T(128)S(1)} %multiply_reduce_fusion, pred[4,8]{1,0:T(4,128)(4,1)S(1)} %not.7, s32[4,8]{1,0:T(4,128)S(1)} %copy.157), kind=kOutput, calls=%fused_computation.11 | convolution fusion | flops 3735808 | bytes 786608 | tf_op jit(solution)/shard_map/qab,qbtd->qatd/dot_general | solution.py:292
  40.8 0.3 fusion.15
  41.1 0.3 fusion.14
  41.5 0.3 fusion.13
  41.8 0.3 fusion.12
  42.1 0.8 %copy-done.4 = f32[5,192,96]{2,1,0:T(8,128)} copy-done((f32[5,192,96]{2,1,0:T(8,128)}, f32[5,192,96]{2,1,0:T(8,128)S(1)}, u32[]{:S(2)}) %copy-start.4) | copy-done | bytes 368664
  42.9 1.0 %fusion.11 = f32[5,192,96]{2,1,0:T(8,128)} fusion(f32[5,192,96]{2,1,0:T(8,128)} %copy-done.4, bf16[4,8,32,192]{3,1,2,0:T(8,128)(2,1)S(1)} %fusion.7, bf16[4,8,36,96]{3,2,0,1:T(8,128)(2,1)S(1)} %copy_select_fusion), kind=kOutput, calls=%fused_computation.26 | convolution fusion | flops 37748736 | bytes 884736 | tf_op jit(solution)/shard_map/qato,qati->oi/dot_general | solution.py:303
  (72 shorter events, 2.9 us)
Async XLA Ops:
  0.7 8.6 %collective-permute-start = (bf16[4,768]{1,0:T(4,128)(2,1)S(1)}, bf16[4,768]{1,0:T(4,128)(2,1)S(1)}, u32[]{:S(2)}, u32[]{:S(2)}) collective-permute-start(bf16[4,768]{1,0:T(4,128)(2,1)S(1)} %pad_maximum_fusion.1), channel_id=1, source_target_pairs={{0,16},{16,0},{1,17},{17,1},{2,18},{18,2},{3,19},{19,3},{4,20},{20... | collective-permute-start | bytes 18440 | tf_op jit(solution)/shard_map/ppermute | solution.py:183
  3.8 1.9 %copy-start = (s32[1,2,2,2]{3,2,1,0:T(2,128)S(1)}, s32[1,2,2,2]{3,2,1,0:T(2,128)}, u32[]{:S(2)}) copy-start(s32[1,2,2,2]{3,2,1,0:T(2,128)} %param.9) | copy-start | bytes 100
  5.7 2.8 %copy-start.1 = (f32[1,1,2,1024]{3,2,1,0:T(2,128)S(1)}, f32[1,1,2,1024]{3,2,1,0:T(2,128)}, u32[]{:S(2)}) copy-start(f32[1,1,2,1024]{3,2,1,0:T(2,128)} %param.11) | copy-start | bytes 24580
  5.7 2.8 %copy-start.2 = (s32[1,2]{1,0:T(1,128)S(1)}, s32[1,2]{1,0:T(1,128)}, u32[]{:S(2)}) copy-start(s32[1,2]{1,0:T(1,128)} %param.10) | copy-start | bytes 28
  8.9 1.4 %copy-start.3 = (bf16[5,192,768]{2,1,0:T(8,128)(2,1)S(1)}, bf16[5,192,768]{2,1,0:T(8,128)(2,1)}, u32[]{:S(2)}) copy-start(bf16[5,192,768]{2,1,0:T(8,128)(2,1)} %param.7) | copy-start | bytes 4423684
  13.7 14.4 %all-to-all-start = ((bf16[8,352,128]{2,1,0:T(8,128)(2,1)}), bf16[8,352,128]{2,1,0:T(8,128)(2,1)S(1)}, u32[]{:S(2)}, u32[]{:S(2)}) async-start(bf16[8,352,128]{2,1,0:T(8,128)(2,1)} %fusion.17), calls=%async_computation | async-start | bytes 1441792 | tf_op jit(solution)/shard_map/all_to_all | solution.py:244
  30.0 8.9 %collective-permute-start.1 = (f32[128,128]{1,0:T(8,128)S(1)}, f32[128,128]{1,0:T(8,128)S(1)}, u32[]{:S(2)}, u32[]{:S(2)}) collective-permute-start(f32[128,128]{1,0:T(8,128)S(1)} %reshape.402), channel_id=1, source_target_pairs={{0,8},{4,12},{8,0},{12,4},{1,9},{5,13},{9,1},{13,5},{2,10},{6,14},... | collective-permute-start | bytes 196616 | tf_op jit(solution)/shard_map/ppermute | solution.py:146
  32.6 6.3 %collective-permute-start.2 = (f32[128,128]{1,0:T(8,128)S(1)}, f32[128,128]{1,0:T(8,128)S(1)}, u32[]{:S(2)}, u32[]{:S(2)}) collective-permute-start(f32[128,128]{1,0:T(8,128)S(1)} %reshape.402), channel_id=1, source_target_pairs={{0,4},{4,8},{8,12},{12,0},{1,5},{5,9},{9,13},{13,1},{2,6},{6,10},{... | collective-permute-start | bytes 196616 | tf_op jit(solution)/shard_map/ppermute | solution.py:146
  34.2 5.0 %collective-permute-start.3 = (f32[128,128]{1,0:T(8,128)S(1)}, f32[128,128]{1,0:T(8,128)S(1)}, u32[]{:S(2)}, u32[]{:S(2)}) collective-permute-start(f32[128,128]{1,0:T(8,128)S(1)} %reshape.402), channel_id=1, source_target_pairs={{0,12},{4,0},{8,4},{12,8},{1,13},{5,1},{9,5},{13,9},{2,14},{6,2},{... | collective-permute-start | bytes 196616 | tf_op jit(solution)/shard_map/ppermute | solution.py:146
  42.1 0.8 %copy-start.4 = (f32[5,192,96]{2,1,0:T(8,128)}, f32[5,192,96]{2,1,0:T(8,128)S(1)}, u32[]{:S(2)}) copy-start(f32[5,192,96]{2,1,0:T(8,128)S(1)} %fusion.12) | copy-start | bytes 1105924

commit v23 on v21

--- a/solution.py
+++ b/solution.py
@@ -233,13 +233,16 @@
     rows_mixed, rows_act, rows_meta = mixed_part.shape[1], act_cut.shape[1], meta_part.shape[1]
     outgoing = jnp.concatenate(
         [
-            jnp.broadcast_to(mixed_part, (peers, rows_mixed, 128)),
+            jnp.zeros((peers, rows_mixed, 128), jnp.bfloat16),
             act_cut,
             jnp.broadcast_to(meta_part, (peers, rows_meta, 128)),
         ],
         axis=1,
     )
     outgoing = jnp.pad(outgoing, ((0, 0), (0, -outgoing.shape[1] % 16), (0, 0)))
+    outgoing = lax.dynamic_update_slice_in_dim(
+        outgoing, jnp.broadcast_to(mixed_part, (peers, rows_mixed, 128)), 0, axis=1
+    )
     incoming = lax.all_to_all(outgoing, ("seq", "dp"), 0, 0, tiled=True)
     n_mixed = held * TB * narrow
     n_act = held * span * cols

time: 44.1 us -> 45 us (1.020)
  local copies, waits for them, and re-layouts: 8.8 us -> 10.4 us
  other arithmetic: 3.62 us -> 2.86 us
    pad x0 -> x1, local copies, waits for them, and re-layouts: none -> 0.91 us  [sparse_path(): outgoing = jnp.pad(outgoing, ((0, 0), (0, -outgoing.shape[1] % 16), (0, 0)))]
    dynamic_update_slice x0 -> x1, local copies, waits for them, and re-layouts: none -> 0.81 us  [sparse_path(): lax.dynamic_update_slice_in_dim(outgoing, jnp.broadcast_to(mixed_part, (p...]
    concatenate x1, other arithmetic: 0.94 us -> 0.18 us  [sparse_path(): jnp.concatenate([jnp.zeros((peers, rows_mixed, 128), jnp.bfloat16), act_c...]
where the time goes in v23:
time: 45 us; the launch traced here: 44.6 us
  starting transfers between devices  12.1 us (27%)
  waiting for transfers between devices  11.9 us (26%)
  local copies, waits for them, and re-layouts  10.4 us (23%)
  matrix products  6.18 us (14%)
  other arithmetic  2.86 us (6%)
  between operations  1.12 us (2%)
    all_to_all x1, waiting for transfers between devices, sparse_path(): incoming = lax.all_to_all(outgoing, ('seq', 'dp'), 0, 0, tiled=True)  10.9 us
    ppermute x3, starting transfers between devices, axis_sum(): lax.ppermute(value, axis, [(i, (i + shift) % count) for i in range(count)])  5.57 us
    all_to_all x1, starting transfers between devices, sparse_path(): incoming = lax.all_to_all(outgoing, ('seq', 'dp'), 0, 0, tiled=True)  3.54 us
    ppermute x1, starting transfers between devices, sparse_path(): lax.ppermute(jnp.concatenate([cells[length - halo:], cells[:halo]]), 'seq...  3 us
    dot_general x5, matrix products, sparse_path(): jnp.einsum('qato,qati->oi', dconv, act_sides[:, :, offset:offset + TB], p...  2.25 us
    another operation x1, local copies, waits for them, and re-layouts, sparse_path(): stacked = cells.reshape(per_block, TB * width)  1.89 us
    unnamed x10, local copies, waits for them, and re-layouts  1.1 us
    ppermute x3, waiting for transfers between devices, axis_sum(): lax.ppermute(value, axis, [(i, (i + shift) % count) for i in range(count)])  1.06 us
  transfers between devices with their start and end apart: 5, of which 2 were waited for; matrix products, arithmetic and copies ran while one was open for 16% of the time, Pallas kernels for 0%

profile of v23, /device:TPU:0, one launch (start us, length us, event | category | flops | bytes accessed | tf_op | source)
XLA Modules:
  0.0 44.6 jit_solution(2713165371388221278)
XLA Ops:
  0.0 0.7 %slice_bitcast_fusion.1 = (bf16[2,768]{1,0:T(2,128)(2,1)S(1)}, bf16[2,768]{1,0:T(2,128)(2,1)S(1)}) fusion(bf16[1,1024,768]{2,1,0:T(8,128)(2,1)} %param.6), kind=kLoop, calls=%fused_computation.131 | loop fusion | bytes 12288 | tf_op jit(solution)/shard_map/slice | solution.py:183
  0.7 3.0 %collective-permute-start = (bf16[4,768]{1,0:T(4,128)(2,1)S(1)}, bf16[4,768]{1,0:T(4,128)(2,1)S(1)}, u32[]{:S(2)}, u32[]{:S(2)}) collective-permute-start(bf16[4,768]{1,0:T(4,128)(2,1)S(1)} %pad_maximum_fusion.2), channel_id=1, source_target_pairs={{0,16},{16,0},{1,17},{17,1},{2,18},{18,2},{3,19},{19,3},{4,20},{20... | collective-permute-start | bytes 18440 | tf_op jit(solution)/shard_map/ppermute | solution.py:182
  3.8 1.9 %reshape_squeeze.3 = bf16[32,24576]{1,0:T(8,128)(2,1)S(1)} reshape(bf16[1,1024,768]{2,1,0:T(8,128)(2,1)} %param.6) | data formatting | bytes 3145728 | tf_op jit(solution)/shard_map/reshape;squeeze | solution.py:191
  5.7 0.2 slice_reduce_fusion.1
  6.0 0.2 convert_reduce_fusion
  6.2 0.2 fusion.79
  6.8 0.2 fusion.63
  7.0 0.2 fusion.61
  7.2 0.4 fusion
  8.9 0.3 concatenate.88
  9.5 0.2 fusion.27
  10.0 0.3 copy-done.3
  10.3 0.2 fusion.33
  10.6 0.2 convolution_add_fusion.3
  10.8 0.2 convolution_add_fusion.2
  11.1 0.2 convolution_add_fusion.1
  11.3 0.3 fusion.7
  11.6 0.1 broadcast_in_dim.115
  11.9 0.3 fusion.28
  12.2 0.5 %reshape.396 = bf16[8,108,128]{2,1,0:T(8,128)(2,1)S(1)} reshape(bf16[8,4,36,96]{3,2,1,0:T(8,128)(2,1)S(1)} %fusion.28) | data formatting | bytes 442368 | tf_op jit(solution)/shard_map/reshape | solution.py:218
  12.7 0.2 pad_maximum_fusion
  12.9 0.9 %pad.9 = bf16[8,352,128]{2,1,0:T(8,128)(2,1)} pad(bf16[8,349,128]{2,1,0:T(8,128)(2,1)S(1)} %pad_maximum_fusion, bf16[]{:T(256)} %constant.39.clone.1), padding=0_0x0_3x0_0 | pad | bytes 1435650 | tf_op jit(solution)/shard_map/jit(_pad)/pad | solution.py:242
  13.8 0.8 %broadcast_dynamic-update-slice_fusion = bf16[8,352,128]{2,1,0:T(8,128)(2,1)} fusion(bf16[8,352,128]{2,1,0:T(8,128)(2,1)} %pad.9, bf16[192,128]{1,0:T(8,128)(2,1)S(1)} %broadcast_in_dim.115), kind=kLoop, calls=%fused_computation.86 | loop fusion | bytes 442368 | tf_op jit(solution)/shard_map/dynamic_update_slice | solution.py:243
  14.6 3.5 %all-to-all-start = ((bf16[8,352,128]{2,1,0:T(8,128)(2,1)}), bf16[8,352,128]{2,1,0:T(8,128)(2,1)S(1)}, u32[]{:S(2)}, u32[]{:S(2)}) async-start(bf16[8,352,128]{2,1,0:T(8,128)(2,1)} %broadcast_dynamic-update-slice_fusion), calls=%async_computation | async-start | bytes 1441792 | tf_op jit(solution)/shard_map/all_to_all | solution.py:246
  18.2 10.9 %all-to-all-done = bf16[8,352,128]{2,1,0:T(8,128)(2,1)S(1)} async-done(((bf16[8,352,128]{2,1,0:T(8,128)(2,1)}), bf16[8,352,128]{2,1,0:T(8,128)(2,1)S(1)}, u32[]{:S(2)}, u32[]{:S(2)}) %all-to-all-start) | async-done | bytes 720928 | tf_op jit(solution)/shard_map/all_to_all | solution.py:246
  29.4 0.2 reshape_reshape_reshape.3
  29.6 0.3 convolution_convert_fusion
  29.9 0.6 %reshape.401 = bf16[4,2,4,32,192]{4,3,2,1,0:T(8,128)(2,1)S(1)} reshape(bf16[32,6144]{1,0:T(8,128)(2,1)S(1)} %convolution_convert_fusion) | data formatting | bytes 786432 | tf_op jit(solution)/shard_map/reshape | solution.py:269
  30.6 0.2 fusion.54
  30.9 1.6 %collective-permute-start.1 = (f32[128,128]{1,0:T(8,128)S(1)}, f32[128,128]{1,0:T(8,128)S(1)}, u32[]{:S(2)}, u32[]{:S(2)}) collective-permute-start(f32[128,128]{1,0:T(8,128)S(1)} %reshape.402), channel_id=1, source_target_pairs={{0,4},{4,8},{8,12},{12,0},{1,5},{5,9},{9,13},{13,1},{2,6},{6,10},{... | collective-permute-start | bytes 196616 | tf_op jit(solution)/shard_map/ppermute | solution.py:145
  32.5 2.6 %collective-permute-start.2 = (f32[128,128]{1,0:T(8,128)S(1)}, f32[128,128]{1,0:T(8,128)S(1)}, u32[]{:S(2)}, u32[]{:S(2)}) collective-permute-start(f32[128,128]{1,0:T(8,128)S(1)} %reshape.402), channel_id=1, source_target_pairs={{0,8},{4,12},{8,0},{12,4},{1,9},{5,13},{9,1},{13,5},{2,10},{6,14},... | collective-permute-start | bytes 196616 | tf_op jit(solution)/shard_map/ppermute | solution.py:145
  35.1 1.4 %collective-permute-start.3 = (f32[128,128]{1,0:T(8,128)S(1)}, f32[128,128]{1,0:T(8,128)S(1)}, u32[]{:S(2)}, u32[]{:S(2)}) collective-permute-start(f32[128,128]{1,0:T(8,128)S(1)} %reshape.402), channel_id=1, source_target_pairs={{0,12},{4,0},{8,4},{12,8},{1,13},{5,1},{9,5},{13,9},{2,14},{6,2},{... | collective-permute-start | bytes 196616 | tf_op jit(solution)/shard_map/ppermute | solution.py:145
  36.5 0.2 fusion.89
  36.7 0.5 %reshape_reshape.3 = bf16[32,36,96]{2,1,0:T(8,128)(2,1)S(1)} reshape(bf16[8,108,128]{2,1,0:T(8,128)(2,1)S(1)} %slice.186) | data formatting | bytes 442368 | tf_op jit(solution)/shard_map/reshape;reshape | solution.py:251
  37.5 0.2 fusion.68
  37.8 0.1 reshape.403
  38.0 0.6 %gather_fusion = bf16[32,36,96]{2,1,0:T(8,128)(2,1)S(1)} fusion(bf16[32,36,96]{2,1,0:T(8,128)(2,1)S(1)} %reshape_reshape.3, s32[1024]{0:T(1024)S(1)} %pad_clamp_fusion), kind=kCustom, calls=%fused_computation | custom fusion | bytes 442496 | tf_op jit(solution)/shard_map/jit(_take)/gather | solution.py:302
  38.7 0.2 multiply_reduce_fusion
  38.9 1.1 %collective-permute-done.2 = f32[128,128]{1,0:T(8,128)S(1)} collective-permute-done((f32[128,128]{1,0:T(8,128)S(1)}, f32[128,128]{1,0:T(8,128)S(1)}, u32[]{:S(2)}, u32[]{:S(2)}) %collective-permute-start.2) | collective-permute-done | bytes 65568 | tf_op jit(solution)/shard_map/ppermute | solution.py:145
  40.1 0.4 convolution_convert_fusion.2
  40.5 0.5 %convolution_convert_fusion.1 = bf16[4,2,2,32,192]{4,3,2,1,0:T(8,128)(2,1)S(1)} fusion(bf16[4,2,4,32,192]{4,3,2,1,0:T(8,128)(2,1)S(1)} %reshape.401, f32[4,2,2,32,32]{4,3,2,1,0:T(8,128)S(1)} %div.46, f32[2,4,2,32,32]{4,3,2,1,0:T(8,128)S(1)} %reshape.403, f32[4]{0:T(128)S(1)} %convert_element_type.118, f32[4,2,2]{2,1,0:T(2,128)S(1)} %compare_select_fusion.1), kind=kOutput, calls=%fused_computation.8 | convolution fusion | flops 37896192 | bytes 987648 | tf_op jit(solution)/shard_map/qocij,qocid->qocjd/dot_general | solution.py:289
  41.1 0.4 fusion.4
  41.6 0.3 fusion.12
  41.9 0.3 fusion.11
  42.2 0.3 fusion.10
  42.6 0.3 fusion.9
  42.9 0.8 %copy-done.4 = f32[5,192,96]{2,1,0:T(8,128)} copy-done((f32[5,192,96]{2,1,0:T(8,128)}, f32[5,192,96]{2,1,0:T(8,128)S(1)}, u32[]{:S(2)}) %copy-start.4) | copy-done | bytes 368664
  43.7 1.0 %fusion.8 = f32[5,192,96]{2,1,0:T(8,128)} fusion(f32[5,192,96]{2,1,0:T(8,128)} %copy-done.4, bf16[4,8,32,192]{3,1,2,0:T(8,128)(2,1)S(1)} %fusion.4, bf16[4,8,36,96]{3,2,0,1:T(8,128)(2,1)S(1)} %copy_select_fusion), kind=kOutput, calls=%fused_computation.22 | convolution fusion | flops 37748736 | bytes 884736 | tf_op jit(solution)/shard_map/qato,qati->oi/dot_general | solution.py:305
  (75 shorter events, 3.1 us)
Async XLA Ops:
  0.7 8.6 %collective-permute-start = (bf16[4,768]{1,0:T(4,128)(2,1)S(1)}, bf16[4,768]{1,0:T(4,128)(2,1)S(1)}, u32[]{:S(2)}, u32[]{:S(2)}) collective-permute-start(bf16[4,768]{1,0:T(4,128)(2,1)S(1)} %pad_maximum_fusion.2), channel_id=1, source_target_pairs={{0,16},{16,0},{1,17},{17,1},{2,18},{18,2},{3,19},{19,3},{4,20},{20... | collective-permute-start | bytes 18440 | tf_op jit(solution)/shard_map/ppermute | solution.py:182
  3.8 1.9 %copy-start = (s32[1,2,2,2]{3,2,1,0:T(2,128)S(1)}, s32[1,2,2,2]{3,2,1,0:T(2,128)}, u32[]{:S(2)}) copy-start(s32[1,2,2,2]{3,2,1,0:T(2,128)} %param.9) | copy-start | bytes 100
  5.7 2.8 %copy-start.1 = (f32[1,1,2,1024]{3,2,1,0:T(2,128)S(1)}, f32[1,1,2,1024]{3,2,1,0:T(2,128)}, u32[]{:S(2)}) copy-start(f32[1,1,2,1024]{3,2,1,0:T(2,128)} %param.11) | copy-start | bytes 24580
  5.7 2.8 %copy-start.2 = (s32[1,2]{1,0:T(1,128)S(1)}, s32[1,2]{1,0:T(1,128)}, u32[]{:S(2)}) copy-start(s32[1,2]{1,0:T(1,128)} %param.10) | copy-start | bytes 28
  8.9 1.4 %copy-start.3 = (bf16[5,192,768]{2,1,0:T(8,128)(2,1)S(1)}, bf16[5,192,768]{2,1,0:T(8,128)(2,1)}, u32[]{:S(2)}) copy-start(bf16[5,192,768]{2,1,0:T(8,128)(2,1)} %param.7) | copy-start | bytes 4423684
  14.6 14.4 %all-to-all-start = ((bf16[8,352,128]{2,1,0:T(8,128)(2,1)}), bf16[8,352,128]{2,1,0:T(8,128)(2,1)S(1)}, u32[]{:S(2)}, u32[]{:S(2)}) async-start(bf16[8,352,128]{2,1,0:T(8,128)(2,1)} %broadcast_dynamic-update-slice_fusion), calls=%async_computation | async-start | bytes 1441792 | tf_op jit(solution)/shard_map/all_to_all | solution.py:246
  30.9 8.0 %collective-permute-start.1 = (f32[128,128]{1,0:T(8,128)S(1)}, f32[128,128]{1,0:T(8,128)S(1)}, u32[]{:S(2)}, u32[]{:S(2)}) collective-permute-start(f32[128,128]{1,0:T(8,128)S(1)} %reshape.402), channel_id=1, source_target_pairs={{0,4},{4,8},{8,12},{12,0},{1,5},{5,9},{9,13},{13,1},{2,6},{6,10},{... | collective-permute-start | bytes 196616 | tf_op jit(solution)/shard_map/ppermute | solution.py:145
  32.5 7.4 %collective-permute-start.2 = (f32[128,128]{1,0:T(8,128)S(1)}, f32[128,128]{1,0:T(8,128)S(1)}, u32[]{:S(2)}, u32[]{:S(2)}) collective-permute-start(f32[128,128]{1,0:T(8,128)S(1)} %reshape.402), channel_id=1, source_target_pairs={{0,8},{4,12},{8,0},{12,4},{1,9},{5,13},{9,1},{13,5},{2,10},{6,14},... | collective-permute-start | bytes 196616 | tf_op jit(solution)/shard_map/ppermute | solution.py:145
  35.1 4.8 %collective-permute-start.3 = (f32[128,128]{1,0:T(8,128)S(1)}, f32[128,128]{1,0:T(8,128)S(1)}, u32[]{:S(2)}, u32[]{:S(2)}) collective-permute-start(f32[128,128]{1,0:T(8,128)S(1)} %reshape.402), channel_id=1, source_target_pairs={{0,12},{4,0},{8,4},{12,8},{1,13},{5,1},{9,5},{13,9},{2,14},{6,2},{... | collective-permute-start | bytes 196616 | tf_op jit(solution)/shard_map/ppermute | solution.py:145
  42.9 0.8 %copy-start.4 = (f32[5,192,96]{2,1,0:T(8,128)}, f32[5,192,96]{2,1,0:T(8,128)S(1)}, u32[]{:S(2)}) copy-start(f32[5,192,96]{2,1,0:T(8,128)S(1)} %fusion.9) | copy-start | bytes 1105924

commit v24 on v21

--- a/solution.py
+++ b/solution.py
@@ -289,7 +289,10 @@
     flat_sides = sides.reshape(groups, owners * n_sides)
     same_block = flat_sides[:, :, None] == flat_sides[:, None, :]
     total = jnp.einsum(
-        "qab,qbtd->qatd", same_block.astype(jnp.float32), grads, precision=lax.Precision.HIGHEST
+        "qab,qbtd->qatd",
+        same_block.astype(jnp.bfloat16),
+        grads.astype(jnp.bfloat16),
+        preferred_element_type=jnp.float32,
     )
     earlier = jnp.arange(owners * n_sides)[None, :] < jnp.arange(owners * n_sides)[:, None]
     first = jnp.logical_not(jnp.any(jnp.logical_and(same_block, earlier[None]), axis=-1))

time: 44.1 us -> 44.1 us (level)
  no operation moved by 1% of the time
where the time goes in v24:
time: 44.1 us; the launch traced here: 43.7 us
  starting transfers between devices  12.1 us (27%)
  waiting for transfers between devices  11.9 us (27%)
  local copies, waits for them, and re-layouts  8.8 us (20%)
  matrix products  6.18 us (14%)
  other arithmetic  3.62 us (8%)
  between operations  1.1 us (2%)
    all_to_all x1, waiting for transfers between devices, sparse_path(): incoming = lax.all_to_all(outgoing, ('seq', 'dp'), 0, 0, tiled=True)  10.9 us
    ppermute x3, starting transfers between devices, axis_sum(): lax.ppermute(value, axis, [(i, (i + shift) % count) for i in range(count)])  5.56 us
    all_to_all x1, starting transfers between devices, sparse_path(): incoming = lax.all_to_all(outgoing, ('seq', 'dp'), 0, 0, tiled=True)  3.54 us
    ppermute x1, starting transfers between devices, sparse_path(): lax.ppermute(jnp.concatenate([cells[length - halo:], cells[:halo]]), 'seq...  3 us
    dot_general x5, matrix products, sparse_path(): jnp.einsum('qato,qati->oi', dconv, act_sides[:, :, offset:offset + TB], p...  2.25 us
    another operation x1, local copies, waits for them, and re-layouts, sparse_path(): stacked = cells.reshape(per_block, TB * width)  1.89 us
    unnamed x10, local copies, waits for them, and re-layouts  1.13 us
    ppermute x3, waiting for transfers between devices, axis_sum(): lax.ppermute(value, axis, [(i, (i + shift) % count) for i in range(count)])  1.07 us
  transfers between devices with their start and end apart: 5, of which 2 were waited for; matrix products, arithmetic and copies ran while one was open for 16% of the time, Pallas kernels for 0%

profile of v24, /device:TPU:0, one launch (start us, length us, event | category | flops | bytes accessed | tf_op | source)
XLA Modules:
  0.0 43.7 jit_solution(13839593702720903324)
XLA Ops:
  0.0 0.7 %slice_bitcast_fusion.1 = (bf16[2,768]{1,0:T(2,128)(2,1)S(1)}, bf16[2,768]{1,0:T(2,128)(2,1)S(1)}) fusion(bf16[1,1024,768]{2,1,0:T(8,128)(2,1)} %param.6), kind=kLoop, calls=%fused_computation.135 | loop fusion | bytes 12288 | tf_op jit(solution)/shard_map/slice | solution.py:183
  0.7 3.0 %collective-permute-start = (bf16[4,768]{1,0:T(4,128)(2,1)S(1)}, bf16[4,768]{1,0:T(4,128)(2,1)S(1)}, u32[]{:S(2)}, u32[]{:S(2)}) collective-permute-start(bf16[4,768]{1,0:T(4,128)(2,1)S(1)} %pad_maximum_fusion.1), channel_id=1, source_target_pairs={{0,16},{16,0},{1,17},{17,1},{2,18},{18,2},{3,19},{19,3},{4,20},{20... | collective-permute-start | bytes 18440 | tf_op jit(solution)/shard_map/ppermute | solution.py:182
  3.8 1.9 %reshape_squeeze.3 = bf16[32,24576]{1,0:T(8,128)(2,1)S(1)} reshape(bf16[1,1024,768]{2,1,0:T(8,128)(2,1)} %param.6) | data formatting | bytes 3145728 | tf_op jit(solution)/shard_map/reshape;squeeze | solution.py:191
  5.7 0.2 slice_reduce_fusion.1
  6.0 0.2 convert_reduce_fusion
  6.2 0.2 fusion.84
  6.8 0.2 fusion.68
  7.0 0.2 fusion.66
  7.2 0.4 fusion
  8.9 0.3 concatenate.89
  9.5 0.2 fusion.32
  10.0 0.3 copy-done.3
  10.3 0.2 fusion.38
  10.6 0.2 convolution_add_fusion.3
  10.8 0.2 convolution_add_fusion.2
  11.1 0.2 convolution_add_fusion.1
  11.3 0.3 fusion.10
  11.6 0.1 broadcast_in_dim.103
  11.9 0.3 fusion.33
  12.2 0.5 %reshape.398 = bf16[8,108,128]{2,1,0:T(8,128)(2,1)S(1)} reshape(bf16[8,4,36,96]{3,2,1,0:T(8,128)(2,1)S(1)} %fusion.33) | data formatting | bytes 442368 | tf_op jit(solution)/shard_map/reshape | solution.py:218
  12.8 0.9 %fusion.17 = bf16[8,352,128]{2,1,0:T(8,128)(2,1)} fusion(bf16[8,49,128]{2,1,0:T(8,128)(2,1)S(1)} %broadcast_in_dim.112, bf16[8,108,128]{2,1,0:T(8,128)(2,1)S(1)} %reshape.398, bf16[8,192,128]{2,1,0:T(8,128)(2,1)S(1)} %broadcast_in_dim.104), kind=kLoop, calls=%fused_computation.37 | loop fusion | flops 3604480 | bytes 1435648 | tf_op jit(solution)/shard_map/concatenate | solution.py:234
  13.7 3.5 %all-to-all-start = ((bf16[8,352,128]{2,1,0:T(8,128)(2,1)}), bf16[8,352,128]{2,1,0:T(8,128)(2,1)S(1)}, u32[]{:S(2)}, u32[]{:S(2)}) async-start(bf16[8,352,128]{2,1,0:T(8,128)(2,1)} %fusion.17), calls=%async_computation | async-start | bytes 1441792 | tf_op jit(solution)/shard_map/all_to_all | solution.py:243
  17.3 10.9 %all-to-all-done = bf16[8,352,128]{2,1,0:T(8,128)(2,1)S(1)} async-done(((bf16[8,352,128]{2,1,0:T(8,128)(2,1)}), bf16[8,352,128]{2,1,0:T(8,128)(2,1)S(1)}, u32[]{:S(2)}, u32[]{:S(2)}) %all-to-all-start) | async-done | bytes 720928 | tf_op jit(solution)/shard_map/all_to_all | solution.py:243
  28.5 0.2 reshape_reshape_reshape.3
  28.7 0.3 convolution_convert_fusion
  29.0 0.6 %reshape.401 = bf16[4,2,4,32,192]{4,3,2,1,0:T(8,128)(2,1)S(1)} reshape(bf16[32,6144]{1,0:T(8,128)(2,1)S(1)} %convolution_convert_fusion) | data formatting | bytes 786432 | tf_op jit(solution)/shard_map/reshape | solution.py:266
  29.6 0.2 fusion.59
  29.9 0.1 reshape.402
  30.0 1.6 %collective-permute-start.1 = (f32[128,128]{1,0:T(8,128)S(1)}, f32[128,128]{1,0:T(8,128)S(1)}, u32[]{:S(2)}, u32[]{:S(2)}) collective-permute-start(f32[128,128]{1,0:T(8,128)S(1)} %reshape.402), channel_id=1, source_target_pairs={{0,4},{4,8},{8,12},{12,0},{1,5},{5,9},{9,13},{13,1},{2,6},{6,10},{... | collective-permute-start | bytes 196616 | tf_op jit(solution)/shard_map/ppermute | solution.py:145
  31.6 2.6 %collective-permute-start.2 = (f32[128,128]{1,0:T(8,128)S(1)}, f32[128,128]{1,0:T(8,128)S(1)}, u32[]{:S(2)}, u32[]{:S(2)}) collective-permute-start(f32[128,128]{1,0:T(8,128)S(1)} %reshape.402), channel_id=1, source_target_pairs={{0,8},{4,12},{8,0},{12,4},{1,9},{5,13},{9,1},{13,5},{2,10},{6,14},... | collective-permute-start | bytes 196616 | tf_op jit(solution)/shard_map/ppermute | solution.py:145
  34.2 1.3 %collective-permute-start.3 = (f32[128,128]{1,0:T(8,128)S(1)}, f32[128,128]{1,0:T(8,128)S(1)}, u32[]{:S(2)}, u32[]{:S(2)}) collective-permute-start(f32[128,128]{1,0:T(8,128)S(1)} %reshape.402), channel_id=1, source_target_pairs={{0,12},{4,0},{8,4},{12,8},{1,13},{5,1},{9,5},{13,9},{2,14},{6,2},{... | collective-permute-start | bytes 196616 | tf_op jit(solution)/shard_map/ppermute | solution.py:145
  35.6 0.2 fusion.94
  35.8 0.5 %reshape_reshape.3 = bf16[32,36,96]{2,1,0:T(8,128)(2,1)S(1)} reshape(bf16[8,108,128]{2,1,0:T(8,128)(2,1)S(1)} %slice.186) | data formatting | bytes 442368 | tf_op jit(solution)/shard_map/reshape;reshape | solution.py:248
  36.6 0.2 fusion.73
  36.8 0.1 reshape.403
  37.1 0.6 %gather_fusion = bf16[32,36,96]{2,1,0:T(8,128)(2,1)S(1)} fusion(bf16[32,36,96]{2,1,0:T(8,128)(2,1)S(1)} %reshape_reshape.3, s32[1024]{0:T(1024)S(1)} %pad_clamp_fusion), kind=kCustom, calls=%fused_computation | custom fusion | bytes 442496 | tf_op jit(solution)/shard_map/jit(_take)/gather | solution.py:302
  37.8 0.2 multiply_reduce_fusion
  38.0 1.1 %collective-permute-done.2 = f32[128,128]{1,0:T(8,128)S(1)} collective-permute-done((f32[128,128]{1,0:T(8,128)S(1)}, f32[128,128]{1,0:T(8,128)S(1)}, u32[]{:S(2)}, u32[]{:S(2)}) %collective-permute-start.2) | collective-permute-done | bytes 65568 | tf_op jit(solution)/shard_map/ppermute | solution.py:145
  39.1 0.1 div.46
  39.2 0.4 convolution_convert_fusion.2
  39.6 0.5 %convolution_convert_fusion.1 = bf16[4,2,2,32,192]{4,3,2,1,0:T(8,128)(2,1)S(1)} fusion(bf16[4,2,4,32,192]{4,3,2,1,0:T(8,128)(2,1)S(1)} %reshape.401, f32[4,2,2,32,32]{4,3,2,1,0:T(8,128)S(1)} %div.46, f32[2,4,2,32,32]{4,3,2,1,0:T(8,128)S(1)} %reshape.403, f32[4]{0:T(128)S(1)} %convert_element_type.120, f32[4,2,2]{2,1,0:T(2,128)S(1)} %compare_select_fusion.1), kind=kOutput, calls=%fused_computation.12 | convolution fusion | flops 37896192 | bytes 987648 | tf_op jit(solution)/shard_map/qocij,qocid->qocjd/dot_general | solution.py:286
  40.2 0.4 %fusion.7 = bf16[4,8,32,192]{3,1,2,0:T(8,128)(2,1)S(1)} fusion(bf16[4,8,32,192]{3,2,1,0:T(8,128)(2,1)S(1)} %bitcast.116, f32[4]{0:T(128)S(1)} %multiply_reduce_fusion, pred[4,8]{1,0:T(4,128)(4,1)S(1)} %not.7, s32[4,8]{1,0:T(4,128)S(1)} %copy.157), kind=kOutput, calls=%fused_computation.11 | convolution fusion | flops 3735808 | bytes 786608 | tf_op jit(solution)/shard_map/qab,qbtd->qatd/dot_general | solution.py:291
  40.7 0.3 fusion.15
  41.0 0.3 fusion.14
  41.3 0.3 fusion.13
  41.7 0.3 fusion.12
  42.0 0.8 %copy-done.4 = f32[5,192,96]{2,1,0:T(8,128)} copy-done((f32[5,192,96]{2,1,0:T(8,128)}, f32[5,192,96]{2,1,0:T(8,128)S(1)}, u32[]{:S(2)}) %copy-start.4) | copy-done | bytes 368664
  42.8 1.0 %fusion.11 = f32[5,192,96]{2,1,0:T(8,128)} fusion(f32[5,192,96]{2,1,0:T(8,128)} %copy-done.4, bf16[4,8,32,192]{3,1,2,0:T(8,128)(2,1)S(1)} %fusion.7, bf16[4,8,36,96]{3,2,0,1:T(8,128)(2,1)S(1)} %copy_select_fusion), kind=kOutput, calls=%fused_computation.26 | convolution fusion | flops 37748736 | bytes 884736 | tf_op jit(solution)/shard_map/qato,qati->oi/dot_general | solution.py:305
  (72 shorter events, 2.9 us)
Async XLA Ops:
  0.7 8.6 %collective-permute-start = (bf16[4,768]{1,0:T(4,128)(2,1)S(1)}, bf16[4,768]{1,0:T(4,128)(2,1)S(1)}, u32[]{:S(2)}, u32[]{:S(2)}) collective-permute-start(bf16[4,768]{1,0:T(4,128)(2,1)S(1)} %pad_maximum_fusion.1), channel_id=1, source_target_pairs={{0,16},{16,0},{1,17},{17,1},{2,18},{18,2},{3,19},{19,3},{4,20},{20... | collective-permute-start | bytes 18440 | tf_op jit(solution)/shard_map/ppermute | solution.py:182
  3.8 1.9 %copy-start = (s32[1,2,2,2]{3,2,1,0:T(2,128)S(1)}, s32[1,2,2,2]{3,2,1,0:T(2,128)}, u32[]{:S(2)}) copy-start(s32[1,2,2,2]{3,2,1,0:T(2,128)} %param.9) | copy-start | bytes 100
  5.7 2.8 %copy-start.1 = (f32[1,1,2,1024]{3,2,1,0:T(2,128)S(1)}, f32[1,1,2,1024]{3,2,1,0:T(2,128)}, u32[]{:S(2)}) copy-start(f32[1,1,2,1024]{3,2,1,0:T(2,128)} %param.11) | copy-start | bytes 24580
  5.7 2.8 %copy-start.2 = (s32[1,2]{1,0:T(1,128)S(1)}, s32[1,2]{1,0:T(1,128)}, u32[]{:S(2)}) copy-start(s32[1,2]{1,0:T(1,128)} %param.10) | copy-start | bytes 28
  8.9 1.4 %copy-start.3 = (bf16[5,192,768]{2,1,0:T(8,128)(2,1)S(1)}, bf16[5,192,768]{2,1,0:T(8,128)(2,1)}, u32[]{:S(2)}) copy-start(bf16[5,192,768]{2,1,0:T(8,128)(2,1)} %param.7) | copy-start | bytes 4423684
  13.7 14.4 %all-to-all-start = ((bf16[8,352,128]{2,1,0:T(8,128)(2,1)}), bf16[8,352,128]{2,1,0:T(8,128)(2,1)S(1)}, u32[]{:S(2)}, u32[]{:S(2)}) async-start(bf16[8,352,128]{2,1,0:T(8,128)(2,1)} %fusion.17), calls=%async_computation | async-start | bytes 1441792 | tf_op jit(solution)/shard_map/all_to_all | solution.py:243
  30.0 8.0 %collective-permute-start.1 = (f32[128,128]{1,0:T(8,128)S(1)}, f32[128,128]{1,0:T(8,128)S(1)}, u32[]{:S(2)}, u32[]{:S(2)}) collective-permute-start(f32[128,128]{1,0:T(8,128)S(1)} %reshape.402), channel_id=1, source_target_pairs={{0,4},{4,8},{8,12},{12,0},{1,5},{5,9},{9,13},{13,1},{2,6},{6,10},{... | collective-permute-start | bytes 196616 | tf_op jit(solution)/shard_map/ppermute | solution.py:145
  31.6 7.4 %collective-permute-start.2 = (f32[128,128]{1,0:T(8,128)S(1)}, f32[128,128]{1,0:T(8,128)S(1)}, u32[]{:S(2)}, u32[]{:S(2)}) collective-permute-start(f32[128,128]{1,0:T(8,128)S(1)} %reshape.402), channel_id=1, source_target_pairs={{0,8},{4,12},{8,0},{12,4},{1,9},{5,13},{9,1},{13,5},{2,10},{6,14},... | collective-permute-start | bytes 196616 | tf_op jit(solution)/shard_map/ppermute | solution.py:145
  34.2 4.9 %collective-permute-start.3 = (f32[128,128]{1,0:T(8,128)S(1)}, f32[128,128]{1,0:T(8,128)S(1)}, u32[]{:S(2)}, u32[]{:S(2)}) collective-permute-start(f32[128,128]{1,0:T(8,128)S(1)} %reshape.402), channel_id=1, source_target_pairs={{0,12},{4,0},{8,4},{12,8},{1,13},{5,1},{9,5},{13,9},{2,14},{6,2},{... | collective-permute-start | bytes 196616 | tf_op jit(solution)/shard_map/ppermute | solution.py:145
  42.0 0.8 %copy-start.4 = (f32[5,192,96]{2,1,0:T(8,128)}, f32[5,192,96]{2,1,0:T(8,128)S(1)}, u32[]{:S(2)}) copy-start(f32[5,192,96]{2,1,0:T(8,128)S(1)} %fusion.12) | copy-start | bytes 1105924

commit v25 on v24

--- a/solution.py
+++ b/solution.py
@@ -282,8 +282,8 @@
     )
     row_float = row_side.astype(jnp.float32)
     col_float = col_side.astype(jnp.float32)
-    drow = jnp.einsum("qocij,qocjd->qocid", dpredicted, col_float, precision=lax.Precision.HIGHEST)
-    dcol = jnp.einsum("qocij,qocid->qocjd", dpredicted, row_float, precision=lax.Precision.HIGHEST)
+    drow = jnp.einsum("qocij,qocjd->qocid", dpredicted, col_float, precision=lax.Precision.HIGH)
+    dcol = jnp.einsum("qocij,qocid->qocjd", dpredicted, row_float, precision=lax.Precision.HIGH)
     grads = jnp.concatenate([drow, dcol], axis=2).astype(jnp.bfloat16).astype(jnp.float32)
     grads = grads.reshape(groups, owners * n_sides, TB, narrow)
     flat_sides = sides.reshape(groups, owners * n_sides)

time: 44.1 us -> 43.9 us (level)
  no operation moved by 1% of the time
where the time goes in v25:
time: 43.9 us; the launch traced here: 43.6 us
  starting transfers between devices  12.1 us (28%)
  waiting for transfers between devices  11.9 us (27%)
  local copies, waits for them, and re-layouts  8.8 us (20%)
  matrix products  6.04 us (14%)
  other arithmetic  3.62 us (8%)
  between operations  1.1 us (3%)
    all_to_all x1, waiting for transfers between devices, sparse_path(): incoming = lax.all_to_all(outgoing, ('seq', 'dp'), 0, 0, tiled=True)  10.9 us
    ppermute x3, starting transfers between devices, axis_sum(): lax.ppermute(value, axis, [(i, (i + shift) % count) for i in range(count)])  5.56 us
    all_to_all x1, starting transfers between devices, sparse_path(): incoming = lax.all_to_all(outgoing, ('seq', 'dp'), 0, 0, tiled=True)  3.54 us
    ppermute x1, starting transfers between devices, sparse_path(): lax.ppermute(jnp.concatenate([cells[length - halo:], cells[:halo]]), 'seq...  3 us
    dot_general x5, matrix products, sparse_path(): jnp.einsum('qato,qati->oi', dconv, act_sides[:, :, offset:offset + TB], p...  2.25 us
    another operation x1, local copies, waits for them, and re-layouts, sparse_path(): stacked = cells.reshape(per_block, TB * width)  1.89 us
    unnamed x10, local copies, waits for them, and re-layouts  1.13 us
    ppermute x3, waiting for transfers between devices, axis_sum(): lax.ppermute(value, axis, [(i, (i + shift) % count) for i in range(count)])  1.07 us
  transfers between devices with their start and end apart: 5, of which 2 were waited for; matrix products, arithmetic and copies ran while one was open for 16% of the time, Pallas kernels for 0%

profile of v25, /device:TPU:0, one launch (start us, length us, event | category | flops | bytes accessed | tf_op | source)
XLA Modules:
  0.0 43.6 jit_solution(15718937802317430097)
XLA Ops:
  0.0 0.7 %slice_bitcast_fusion.1 = (bf16[2,768]{1,0:T(2,128)(2,1)S(1)}, bf16[2,768]{1,0:T(2,128)(2,1)S(1)}) fusion(bf16[1,1024,768]{2,1,0:T(8,128)(2,1)} %param.6), kind=kLoop, calls=%fused_computation.135 | loop fusion | bytes 12288 | tf_op jit(solution)/shard_map/slice | solution.py:183
  0.7 3.0 %collective-permute-start = (bf16[4,768]{1,0:T(4,128)(2,1)S(1)}, bf16[4,768]{1,0:T(4,128)(2,1)S(1)}, u32[]{:S(2)}, u32[]{:S(2)}) collective-permute-start(bf16[4,768]{1,0:T(4,128)(2,1)S(1)} %pad_maximum_fusion.1), channel_id=1, source_target_pairs={{0,16},{16,0},{1,17},{17,1},{2,18},{18,2},{3,19},{19,3},{4,20},{20... | collective-permute-start | bytes 18440 | tf_op jit(solution)/shard_map/ppermute | solution.py:182
  3.8 1.9 %reshape_squeeze.3 = bf16[32,24576]{1,0:T(8,128)(2,1)S(1)} reshape(bf16[1,1024,768]{2,1,0:T(8,128)(2,1)} %param.6) | data formatting | bytes 3145728 | tf_op jit(solution)/shard_map/reshape;squeeze | solution.py:191
  5.7 0.2 slice_reduce_fusion.1
  6.0 0.2 convert_reduce_fusion
  6.2 0.2 fusion.84
  6.8 0.2 fusion.68
  7.0 0.2 fusion.66
  7.2 0.4 fusion
  8.9 0.3 concatenate.89
  9.5 0.2 fusion.32
  10.0 0.3 copy-done.3
  10.3 0.2 fusion.38
  10.6 0.2 convolution_add_fusion.3
  10.8 0.2 convolution_add_fusion.2
  11.1 0.2 convolution_add_fusion.1
  11.3 0.3 fusion.10
  11.6 0.1 broadcast_in_dim.103
  11.9 0.3 fusion.33
  12.2 0.5 %reshape.398 = bf16[8,108,128]{2,1,0:T(8,128)(2,1)S(1)} reshape(bf16[8,4,36,96]{3,2,1,0:T(8,128)(2,1)S(1)} %fusion.33) | data formatting | bytes 442368 | tf_op jit(solution)/shard_map/reshape | solution.py:218
  12.8 0.9 %fusion.17 = bf16[8,352,128]{2,1,0:T(8,128)(2,1)} fusion(bf16[8,49,128]{2,1,0:T(8,128)(2,1)S(1)} %broadcast_in_dim.112, bf16[8,108,128]{2,1,0:T(8,128)(2,1)S(1)} %reshape.398, bf16[8,192,128]{2,1,0:T(8,128)(2,1)S(1)} %broadcast_in_dim.104), kind=kLoop, calls=%fused_computation.37 | loop fusion | flops 3604480 | bytes 1435648 | tf_op jit(solution)/shard_map/concatenate | solution.py:234
  13.7 3.5 %all-to-all-start = ((bf16[8,352,128]{2,1,0:T(8,128)(2,1)}), bf16[8,352,128]{2,1,0:T(8,128)(2,1)S(1)}, u32[]{:S(2)}, u32[]{:S(2)}) async-start(bf16[8,352,128]{2,1,0:T(8,128)(2,1)} %fusion.17), calls=%async_computation | async-start | bytes 1441792 | tf_op jit(solution)/shard_map/all_to_all | solution.py:243
  17.3 10.9 %all-to-all-done = bf16[8,352,128]{2,1,0:T(8,128)(2,1)S(1)} async-done(((bf16[8,352,128]{2,1,0:T(8,128)(2,1)}), bf16[8,352,128]{2,1,0:T(8,128)(2,1)S(1)}, u32[]{:S(2)}, u32[]{:S(2)}) %all-to-all-start) | async-done | bytes 720928 | tf_op jit(solution)/shard_map/all_to_all | solution.py:243
  28.5 0.2 reshape_reshape_reshape.3
  28.7 0.3 convolution_convert_fusion
  29.0 0.6 %reshape.401 = bf16[4,2,4,32,192]{4,3,2,1,0:T(8,128)(2,1)S(1)} reshape(bf16[32,6144]{1,0:T(8,128)(2,1)S(1)} %convolution_convert_fusion) | data formatting | bytes 786432 | tf_op jit(solution)/shard_map/reshape | solution.py:266
  29.6 0.2 fusion.59
  29.9 0.1 reshape.402
  30.0 1.6 %collective-permute-start.1 = (f32[128,128]{1,0:T(8,128)S(1)}, f32[128,128]{1,0:T(8,128)S(1)}, u32[]{:S(2)}, u32[]{:S(2)}) collective-permute-start(f32[128,128]{1,0:T(8,128)S(1)} %reshape.402), channel_id=1, source_target_pairs={{0,4},{4,8},{8,12},{12,0},{1,5},{5,9},{9,13},{13,1},{2,6},{6,10},{... | collective-permute-start | bytes 196616 | tf_op jit(solution)/shard_map/ppermute | solution.py:145
  31.6 2.6 %collective-permute-start.2 = (f32[128,128]{1,0:T(8,128)S(1)}, f32[128,128]{1,0:T(8,128)S(1)}, u32[]{:S(2)}, u32[]{:S(2)}) collective-permute-start(f32[128,128]{1,0:T(8,128)S(1)} %reshape.402), channel_id=1, source_target_pairs={{0,8},{4,12},{8,0},{12,4},{1,9},{5,13},{9,1},{13,5},{2,10},{6,14},... | collective-permute-start | bytes 196616 | tf_op jit(solution)/shard_map/ppermute | solution.py:145
  34.2 1.3 %collective-permute-start.3 = (f32[128,128]{1,0:T(8,128)S(1)}, f32[128,128]{1,0:T(8,128)S(1)}, u32[]{:S(2)}, u32[]{:S(2)}) collective-permute-start(f32[128,128]{1,0:T(8,128)S(1)} %reshape.402), channel_id=1, source_target_pairs={{0,12},{4,0},{8,4},{12,8},{1,13},{5,1},{9,5},{13,9},{2,14},{6,2},{... | collective-permute-start | bytes 196616 | tf_op jit(solution)/shard_map/ppermute | solution.py:145
  35.6 0.2 fusion.94
  35.8 0.5 %reshape_reshape.3 = bf16[32,36,96]{2,1,0:T(8,128)(2,1)S(1)} reshape(bf16[8,108,128]{2,1,0:T(8,128)(2,1)S(1)} %slice.186) | data formatting | bytes 442368 | tf_op jit(solution)/shard_map/reshape;reshape | solution.py:248
  36.6 0.2 fusion.73
  36.8 0.1 reshape.403
  37.1 0.6 %gather_fusion = bf16[32,36,96]{2,1,0:T(8,128)(2,1)S(1)} fusion(bf16[32,36,96]{2,1,0:T(8,128)(2,1)S(1)} %reshape_reshape.3, s32[1024]{0:T(1024)S(1)} %pad_clamp_fusion), kind=kCustom, calls=%fused_computation | custom fusion | bytes 442496 | tf_op jit(solution)/shard_map/jit(_take)/gather | solution.py:302
  37.8 0.2 multiply_reduce_fusion
  38.0 1.1 %collective-permute-done.2 = f32[128,128]{1,0:T(8,128)S(1)} collective-permute-done((f32[128,128]{1,0:T(8,128)S(1)}, f32[128,128]{1,0:T(8,128)S(1)}, u32[]{:S(2)}, u32[]{:S(2)}) %collective-permute-start.2) | collective-permute-done | bytes 65568 | tf_op jit(solution)/shard_map/ppermute | solution.py:145
  39.1 0.1 div.46
  39.2 0.4 convolution_convert_fusion.2
  39.6 0.4 convolution_convert_fusion.1
  40.1 0.4 %fusion.7 = bf16[4,8,32,192]{3,1,2,0:T(8,128)(2,1)S(1)} fusion(bf16[4,8,32,192]{3,2,1,0:T(8,128)(2,1)S(1)} %bitcast.116, f32[4]{0:T(128)S(1)} %multiply_reduce_fusion, pred[4,8]{1,0:T(4,128)(4,1)S(1)} %not.7, s32[4,8]{1,0:T(4,128)S(1)} %copy.157), kind=kOutput, calls=%fused_computation.11 | convolution fusion | flops 3735808 | bytes 786608 | tf_op jit(solution)/shard_map/qab,qbtd->qatd/dot_general | solution.py:291
  40.5 0.3 fusion.15
  40.9 0.3 fusion.14
  41.2 0.3 fusion.13
  41.5 0.3 fusion.12
  41.9 0.8 %copy-done.4 = f32[5,192,96]{2,1,0:T(8,128)} copy-done((f32[5,192,96]{2,1,0:T(8,128)}, f32[5,192,96]{2,1,0:T(8,128)S(1)}, u32[]{:S(2)}) %copy-start.4) | copy-done | bytes 368664
  42.6 1.0 %fusion.11 = f32[5,192,96]{2,1,0:T(8,128)} fusion(f32[5,192,96]{2,1,0:T(8,128)} %copy-done.4, bf16[4,8,32,192]{3,1,2,0:T(8,128)(2,1)S(1)} %fusion.7, bf16[4,8,36,96]{3,2,0,1:T(8,128)(2,1)S(1)} %copy_select_fusion), kind=kOutput, calls=%fused_computation.26 | convolution fusion | flops 37748736 | bytes 884736 | tf_op jit(solution)/shard_map/qato,qati->oi/dot_general | solution.py:305
  (72 shorter events, 2.9 us)
Async XLA Ops:
  0.7 8.6 %collective-permute-start = (bf16[4,768]{1,0:T(4,128)(2,1)S(1)}, bf16[4,768]{1,0:T(4,128)(2,1)S(1)}, u32[]{:S(2)}, u32[]{:S(2)}) collective-permute-start(bf16[4,768]{1,0:T(4,128)(2,1)S(1)} %pad_maximum_fusion.1), channel_id=1, source_target_pairs={{0,16},{16,0},{1,17},{17,1},{2,18},{18,2},{3,19},{19,3},{4,20},{20... | collective-permute-start | bytes 18440 | tf_op jit(solution)/shard_map/ppermute | solution.py:182
  3.8 1.9 %copy-start = (s32[1,2,2,2]{3,2,1,0:T(2,128)S(1)}, s32[1,2,2,2]{3,2,1,0:T(2,128)}, u32[]{:S(2)}) copy-start(s32[1,2,2,2]{3,2,1,0:T(2,128)} %param.9) | copy-start | bytes 100
  5.7 2.8 %copy-start.1 = (f32[1,1,2,1024]{3,2,1,0:T(2,128)S(1)}, f32[1,1,2,1024]{3,2,1,0:T(2,128)}, u32[]{:S(2)}) copy-start(f32[1,1,2,1024]{3,2,1,0:T(2,128)} %param.11) | copy-start | bytes 24580
  5.7 2.8 %copy-start.2 = (s32[1,2]{1,0:T(1,128)S(1)}, s32[1,2]{1,0:T(1,128)}, u32[]{:S(2)}) copy-start(s32[1,2]{1,0:T(1,128)} %param.10) | copy-start | bytes 28
  8.9 1.4 %copy-start.3 = (bf16[5,192,768]{2,1,0:T(8,128)(2,1)S(1)}, bf16[5,192,768]{2,1,0:T(8,128)(2,1)}, u32[]{:S(2)}) copy-start(bf16[5,192,768]{2,1,0:T(8,128)(2,1)} %param.7) | copy-start | bytes 4423684
  13.7 14.4 %all-to-all-start = ((bf16[8,352,128]{2,1,0:T(8,128)(2,1)}), bf16[8,352,128]{2,1,0:T(8,128)(2,1)S(1)}, u32[]{:S(2)}, u32[]{:S(2)}) async-start(bf16[8,352,128]{2,1,0:T(8,128)(2,1)} %fusion.17), calls=%async_computation | async-start | bytes 1441792 | tf_op jit(solution)/shard_map/all_to_all | solution.py:243
  30.0 8.0 %collective-permute-start.1 = (f32[128,128]{1,0:T(8,128)S(1)}, f32[128,128]{1,0:T(8,128)S(1)}, u32[]{:S(2)}, u32[]{:S(2)}) collective-permute-start(f32[128,128]{1,0:T(8,128)S(1)} %reshape.402), channel_id=1, source_target_pairs={{0,4},{4,8},{8,12},{12,0},{1,5},{5,9},{9,13},{13,1},{2,6},{6,10},{... | collective-permute-start | bytes 196616 | tf_op jit(solution)/shard_map/ppermute | solution.py:145
  31.6 7.4 %collective-permute-start.2 = (f32[128,128]{1,0:T(8,128)S(1)}, f32[128,128]{1,0:T(8,128)S(1)}, u32[]{:S(2)}, u32[]{:S(2)}) collective-permute-start(f32[128,128]{1,0:T(8,128)S(1)} %reshape.402), channel_id=1, source_target_pairs={{0,8},{4,12},{8,0},{12,4},{1,9},{5,13},{9,1},{13,5},{2,10},{6,14},... | collective-permute-start | bytes 196616 | tf_op jit(solution)/shard_map/ppermute | solution.py:145
  34.2 4.9 %collective-permute-start.3 = (f32[128,128]{1,0:T(8,128)S(1)}, f32[128,128]{1,0:T(8,128)S(1)}, u32[]{:S(2)}, u32[]{:S(2)}) collective-permute-start(f32[128,128]{1,0:T(8,128)S(1)} %reshape.402), channel_id=1, source_target_pairs={{0,12},{4,0},{8,4},{12,8},{1,13},{5,1},{9,5},{13,9},{2,14},{6,2},{... | collective-permute-start | bytes 196616 | tf_op jit(solution)/shard_map/ppermute | solution.py:145
  41.9 0.8 %copy-start.4 = (f32[5,192,96]{2,1,0:T(8,128)}, f32[5,192,96]{2,1,0:T(8,128)S(1)}, u32[]{:S(2)}) copy-start(f32[5,192,96]{2,1,0:T(8,128)S(1)} %fusion.12) | copy-start | bytes 1105924

commit v26 on v24

--- a/solution.py
+++ b/solution.py
@@ -299,7 +299,10 @@
     scaling = 1.25 * keep_all.astype(jnp.float32)
     dconv = (scaling[:, None, None, None] * total).astype(jnp.bfloat16)
     dconv = jnp.where(first[..., None, None], dconv, jnp.zeros_like(dconv))
-    act_sides = jnp.take(act_in, slot.reshape(groups, owners * n_sides), axis=0)
+    pick_act = (slot.reshape(groups, owners * n_sides)[..., None] == jnp.arange(peers * held)).astype(jnp.bfloat16)
+    act_sides = jnp.dot(
+        pick_act.reshape(-1, peers * held), act_in.reshape(peers * held, -1), preferred_element_type=jnp.float32
+    ).astype(jnp.bfloat16).reshape(groups, owners * n_sides, span, cols)
     return jnp.stack(
         [
             jnp.einsum(

time: 44.1 us -> 46.2 us (1.048)
  waiting for transfers between devices: 11.9 us -> 14 us
  local copies, waits for them, and re-layouts: 8.8 us -> 9.72 us
  starting transfers between devices: 12.1 us -> 11.2 us
    ppermute x3, waiting for transfers between devices: 1.07 us -> 3.13 us  [axis_sum(): lax.ppermute(value, axis, [(i, (i + shift) % count) for i in range(count)])]
    ppermute x3, starting transfers between devices: 5.56 us -> 4.65 us  [axis_sum(): lax.ppermute(value, axis, [(i, (i + shift) % count) for i in range(count)])]
    slice x1, local copies, waits for them, and re-layouts: 0.21 us -> 0.97 us  [sparse_path(): own_sides = jnp.concatenate([tiles[0, ..., 0], tiles[0, ..., 1]], axis=-1)]
    concatenate x1, local copies, waits for them, and re-layouts: 0.08 us -> 0.76 us  [sparse_path(): jnp.concatenate([tiles.reshape(-1), counts.reshape(-1), keep.reshape(-1),...]
    gather x1 -> x0, local copies, waits for them, and re-layouts: 0.62 us -> none  [sparse_path(): act_sides = jnp.take(act_in, slot.reshape(groups, owners * n_sides), axis=0)]
    unnamed x10 -> x8, local copies, waits for them, and re-layouts: 1.13 us -> 0.79 us
  transfers between devices with their start and end apart: 5 -> 5, of which waited for: 2 -> 2; matrix products, arithmetic and copies ran while one was open for 16% -> 18% of each run, Pallas kernels for 0% -> 0%
where the time goes in v26:
time: 46.2 us; the launch traced here: 45.8 us
  waiting for transfers between devices  14 us (30%)
  starting transfers between devices  11.2 us (24%)
  local copies, waits for them, and re-layouts  9.72 us (21%)
  matrix products  6.43 us (14%)
  other arithmetic  3.34 us (7%)
  between operations  1.13 us (2%)
    all_to_all x1, waiting for transfers between devices, sparse_path(): incoming = lax.all_to_all(outgoing, ('seq', 'dp'), 0, 0, tiled=True)  10.9 us
    ppermute x3, starting transfers between devices, axis_sum(): lax.ppermute(value, axis, [(i, (i + shift) % count) for i in range(count)])  4.65 us
    all_to_all x1, starting transfers between devices, sparse_path(): incoming = lax.all_to_all(outgoing, ('seq', 'dp'), 0, 0, tiled=True)  3.54 us
    ppermute x3, waiting for transfers between devices, axis_sum(): lax.ppermute(value, axis, [(i, (i + shift) % count) for i in range(count)])  3.13 us
    ppermute x1, starting transfers between devices, sparse_path(): lax.ppermute(jnp.concatenate([cells[length - halo:], cells[:halo]]), 'seq...  3 us
    dot_general x5, matrix products, sparse_path(): jnp.einsum('qato,qati->oi', dconv, act_sides[:, :, offset:offset + TB], p...  2.25 us
    another operation x1, local copies, waits for them, and re-layouts, sparse_path(): stacked = cells.reshape(per_block, TB * width)  1.89 us
    dot_general x4, matrix products, sparse_path(): jnp.einsum('hti,oi->hto', act[:, offset:offset + TB], conv_weight[offset]...  1.01 us
  transfers between devices with their start and end apart: 5, of which 2 were waited for; matrix products, arithmetic and copies ran while one was open for 18% of the time, Pallas kernels for 0%

profile of v26, /device:TPU:0, one launch (start us, length us, event | category | flops | bytes accessed | tf_op | source)
XLA Modules:
  0.0 45.8 jit_solution(3851256785713283378)
XLA Ops:
  0.0 0.7 %slice_bitcast_fusion.1 = (bf16[2,768]{1,0:T(2,128)(2,1)S(1)}, bf16[2,768]{1,0:T(2,128)(2,1)S(1)}) fusion(bf16[1,1024,768]{2,1,0:T(8,128)(2,1)} %param.6), kind=kLoop, calls=%fused_computation.133 | loop fusion | bytes 12288 | tf_op jit(solution)/shard_map/slice | solution.py:183
  0.7 3.0 %collective-permute-start = (bf16[4,768]{1,0:T(4,128)(2,1)S(1)}, bf16[4,768]{1,0:T(4,128)(2,1)S(1)}, u32[]{:S(2)}, u32[]{:S(2)}) collective-permute-start(bf16[4,768]{1,0:T(4,128)(2,1)S(1)} %pad_maximum_fusion.1), channel_id=1, source_target_pairs={{0,16},{16,0},{1,17},{17,1},{2,18},{18,2},{3,19},{19,3},{4,20},{20... | collective-permute-start | bytes 18440 | tf_op jit(solution)/shard_map/ppermute | solution.py:182
  3.8 0.8 %concatenate.94 = s32[8]{0:T(128)S(1)} reshape(s32[1,2,2,2]{3,2,1,0:T(2,128)} %param.9) | data formatting | bytes 64 | tf_op jit(solution)/shard_map/concatenate | solution.py:229
  4.5 1.0 %slice_reduce_fusion.1 = (s32[2,2]{1,0:T(2,128)S(1)}, s32[2,2]{1,0:T(2,128)S(1)}) fusion(s32[1,2,2,2]{3,2,1,0:T(2,128)} %param.9), kind=kLoop, calls=%fused_computation.142 | loop fusion | bytes 64 | tf_op jit(solution)/shard_map/slice | solution.py:166
  5.7 0.2 convert_reduce_fusion
  6.0 0.2 fusion.85
  6.3 1.9 %reshape_squeeze.3 = bf16[32,24576]{1,0:T(8,128)(2,1)S(1)} reshape(bf16[1,1024,768]{2,1,0:T(8,128)(2,1)} %param.6) | data formatting | bytes 3145728 | tf_op jit(solution)/shard_map/reshape;squeeze | solution.py:191
  9.1 0.2 fusion.66
  9.3 0.2 fusion.68
  9.5 0.4 fusion
  10.4 0.3 concatenate.89
  11.0 0.2 fusion.32
  11.4 0.2 fusion.38
  11.6 0.2 convolution_add_fusion.3
  11.9 0.2 convolution_add_fusion.2
  12.1 0.2 convolution_add_fusion.1
  12.5 0.3 fusion.33
  12.9 0.5 %reshape.400 = bf16[8,108,128]{2,1,0:T(8,128)(2,1)S(1)} reshape(bf16[8,4,36,96]{3,2,1,0:T(8,128)(2,1)S(1)} %fusion.33) | data formatting | bytes 442368 | tf_op jit(solution)/shard_map/reshape | solution.py:218
  13.4 0.3 fusion.10
  13.7 0.1 broadcast_in_dim.92
  13.9 0.9 %fusion.17 = bf16[8,352,128]{2,1,0:T(8,128)(2,1)} fusion(bf16[8,49,128]{2,1,0:T(8,128)(2,1)S(1)} %broadcast_in_dim.101, bf16[8,108,128]{2,1,0:T(8,128)(2,1)S(1)} %reshape.400, bf16[8,192,128]{2,1,0:T(8,128)(2,1)S(1)} %broadcast_in_dim.93), kind=kLoop, calls=%fused_computation.37 | loop fusion | flops 3604480 | bytes 1435648 | tf_op jit(solution)/shard_map/concatenate | solution.py:234
  14.8 3.5 %all-to-all-start = ((bf16[8,352,128]{2,1,0:T(8,128)(2,1)}), bf16[8,352,128]{2,1,0:T(8,128)(2,1)S(1)}, u32[]{:S(2)}, u32[]{:S(2)}) async-start(bf16[8,352,128]{2,1,0:T(8,128)(2,1)} %fusion.17), calls=%async_computation | async-start | bytes 1441792 | tf_op jit(solution)/shard_map/all_to_all | solution.py:243
  18.4 10.9 %all-to-all-done = bf16[8,352,128]{2,1,0:T(8,128)(2,1)S(1)} async-done(((bf16[8,352,128]{2,1,0:T(8,128)(2,1)}), bf16[8,352,128]{2,1,0:T(8,128)(2,1)S(1)}, u32[]{:S(2)}, u32[]{:S(2)}) %all-to-all-start) | async-done | bytes 720928 | tf_op jit(solution)/shard_map/all_to_all | solution.py:243
  29.4 0.2 fusion.97
  29.7 0.2 reshape_reshape_reshape.6
  30.0 0.3 convolution_convert_fusion
  30.3 0.6 %reshape.403 = bf16[4,2,4,32,192]{4,3,2,1,0:T(8,128)(2,1)S(1)} reshape(bf16[32,6144]{1,0:T(8,128)(2,1)S(1)} %convolution_convert_fusion) | data formatting | bytes 786432 | tf_op jit(solution)/shard_map/reshape | solution.py:266
  30.9 0.2 fusion.59
  31.1 0.1 reshape.404
  31.2 3.6 %collective-permute-start.3 = (f32[128,128]{1,0:T(8,128)S(1)}, f32[128,128]{1,0:T(8,128)S(1)}, u32[]{:S(2)}, u32[]{:S(2)}) collective-permute-start(f32[128,128]{1,0:T(8,128)S(1)} %reshape.404), channel_id=1, source_target_pairs={{0,12},{4,0},{8,4},{12,8},{1,13},{5,1},{9,5},{13,9},{2,14},{6,2},{... | collective-permute-start | bytes 196616 | tf_op jit(solution)/shard_map/ppermute | solution.py:145
  34.9 1.0 %collective-permute-start.1 = (f32[128,128]{1,0:T(8,128)S(1)}, f32[128,128]{1,0:T(8,128)S(1)}, u32[]{:S(2)}, u32[]{:S(2)}) collective-permute-start(f32[128,128]{1,0:T(8,128)S(1)} %reshape.404), channel_id=1, source_target_pairs={{0,4},{4,8},{8,12},{12,0},{1,5},{5,9},{9,13},{13,1},{2,6},{6,10},{... | collective-permute-start | bytes 196616 | tf_op jit(solution)/shard_map/ppermute | solution.py:145
  35.9 0.3 reshape_reshape_reshape.7
  36.3 0.3 convolution_convert_fusion.1
  36.7 0.2 fusion.73
  36.9 0.5 %reshape.406 = bf16[4,8,36,96]{3,2,1,0:T(8,128)(2,1)S(1)} reshape(bf16[32,3456]{1,0:T(8,128)(2,1)S(1)} %convolution_convert_fusion.1) | data formatting | bytes 442368 | tf_op jit(solution)/shard_map/reshape | solution.py:305
  37.4 0.1 reshape.405
  37.5 0.3 fusion.94
  37.8 0.2 multiply_reduce_fusion
  38.0 3.1 %collective-permute-done.2 = f32[128,128]{1,0:T(8,128)S(1)} collective-permute-done((f32[128,128]{1,0:T(8,128)S(1)}, f32[128,128]{1,0:T(8,128)S(1)}, u32[]{:S(2)}, u32[]{:S(2)}) %collective-permute-start.2) | collective-permute-done | bytes 65568 | tf_op jit(solution)/shard_map/ppermute | solution.py:145
  41.3 0.5 %convolution_convert_fusion.2 = bf16[4,2,2,32,192]{4,3,2,1,0:T(8,128)(2,1)S(1)} fusion(bf16[4,2,4,32,192]{4,3,2,1,0:T(8,128)(2,1)S(1)} %reshape.403, f32[4,2,2,32,32]{4,3,2,1,0:T(8,128)S(1)} %div.46, f32[2,4,2,32,32]{4,3,2,1,0:T(8,128)S(1)} %reshape.405, f32[4]{0:T(128)S(1)} %convert_element_type.124, f32[4,2,2]{2,1,0:T(2,128)S(1)} %compare_select_fusion.1), kind=kOutput, calls=%fused_computation.12 | convolution fusion | flops 37896192 | bytes 987648 | tf_op jit(solution)/shard_map/qocij,qocid->qocjd/dot_general | solution.py:286
  41.8 0.4 convolution_convert_fusion.3
  42.3 0.4 fusion.7
  42.8 0.3 fusion.15
  43.1 0.3 fusion.14
  43.4 0.3 fusion.13
  43.8 0.3 fusion.12
  44.1 0.8 %copy-done.3 = f32[5,192,96]{2,1,0:T(8,128)} copy-done((f32[5,192,96]{2,1,0:T(8,128)}, f32[5,192,96]{2,1,0:T(8,128)S(1)}, u32[]{:S(2)}) %copy-start.3) | copy-done | bytes 368664
  44.9 1.0 %fusion.11 = f32[5,192,96]{2,1,0:T(8,128)} fusion(f32[5,192,96]{2,1,0:T(8,128)} %copy-done.3, bf16[4,8,32,192]{3,1,2,0:T(8,128)(2,1)S(1)} %fusion.7, bf16[4,8,32,96]{3,2,1,0:T(8,128)(2,1)S(1)} %get-tuple-element.13), kind=kOutput, calls=%fused_computation.26 | convolution fusion | flops 37748736 | bytes 688128 | tf_op jit(solution)/shard_map/qato,qati->oi/dot_general | solution.py:308
  (67 shorter events, 2.5 us)
Async XLA Ops:
  0.7 10.0 %collective-permute-start = (bf16[4,768]{1,0:T(4,128)(2,1)S(1)}, bf16[4,768]{1,0:T(4,128)(2,1)S(1)}, u32[]{:S(2)}, u32[]{:S(2)}) collective-permute-start(bf16[4,768]{1,0:T(4,128)(2,1)S(1)} %pad_maximum_fusion.1), channel_id=1, source_target_pairs={{0,16},{16,0},{1,17},{17,1},{2,18},{18,2},{3,19},{19,3},{4,20},{20... | collective-permute-start | bytes 18440 | tf_op jit(solution)/shard_map/ppermute | solution.py:182
  6.3 2.7 %copy-start = (f32[1,1,2,1024]{3,2,1,0:T(2,128)S(1)}, f32[1,1,2,1024]{3,2,1,0:T(2,128)}, u32[]{:S(2)}) copy-start(f32[1,1,2,1024]{3,2,1,0:T(2,128)} %param.11) | copy-start | bytes 24580
  8.2 1.7 %copy-start.1 = (s32[1,2]{1,0:T(1,128)S(1)}, s32[1,2]{1,0:T(1,128)}, u32[]{:S(2)}) copy-start(s32[1,2]{1,0:T(1,128)} %param.10) | copy-start | bytes 28
  9.9 1.5 %copy-start.2 = (bf16[5,192,768]{2,1,0:T(8,128)(2,1)S(1)}, bf16[5,192,768]{2,1,0:T(8,128)(2,1)}, u32[]{:S(2)}) copy-start(bf16[5,192,768]{2,1,0:T(8,128)(2,1)} %param.7) | copy-start | bytes 4423684
  14.8 14.4 %all-to-all-start = ((bf16[8,352,128]{2,1,0:T(8,128)(2,1)}), bf16[8,352,128]{2,1,0:T(8,128)(2,1)S(1)}, u32[]{:S(2)}, u32[]{:S(2)}) async-start(bf16[8,352,128]{2,1,0:T(8,128)(2,1)} %fusion.17), calls=%async_computation | async-start | bytes 1441792 | tf_op jit(solution)/shard_map/all_to_all | solution.py:243
  31.2 6.8 %collective-permute-start.3 = (f32[128,128]{1,0:T(8,128)S(1)}, f32[128,128]{1,0:T(8,128)S(1)}, u32[]{:S(2)}, u32[]{:S(2)}) collective-permute-start(f32[128,128]{1,0:T(8,128)S(1)} %reshape.404), channel_id=1, source_target_pairs={{0,12},{4,0},{8,4},{12,8},{1,13},{5,1},{9,5},{13,9},{2,14},{6,2},{... | collective-permute-start | bytes 196616 | tf_op jit(solution)/shard_map/ppermute | solution.py:145
  34.9 6.3 %collective-permute-start.2 = (f32[128,128]{1,0:T(8,128)S(1)}, f32[128,128]{1,0:T(8,128)S(1)}, u32[]{:S(2)}, u32[]{:S(2)}) collective-permute-start(f32[128,128]{1,0:T(8,128)S(1)} %reshape.404), channel_id=1, source_target_pairs={{0,8},{4,12},{8,0},{12,4},{1,9},{5,13},{9,1},{13,5},{2,10},{6,14},... | collective-permute-start | bytes 196616 | tf_op jit(solution)/shard_map/ppermute | solution.py:145
  34.9 6.3 %collective-permute-start.1 = (f32[128,128]{1,0:T(8,128)S(1)}, f32[128,128]{1,0:T(8,128)S(1)}, u32[]{:S(2)}, u32[]{:S(2)}) collective-permute-start(f32[128,128]{1,0:T(8,128)S(1)} %reshape.404), channel_id=1, source_target_pairs={{0,4},{4,8},{8,12},{12,0},{1,5},{5,9},{9,13},{13,1},{2,6},{6,10},{... | collective-permute-start | bytes 196616 | tf_op jit(solution)/shard_map/ppermute | solution.py:145
  44.1 0.8 %copy-start.3 = (f32[5,192,96]{2,1,0:T(8,128)}, f32[5,192,96]{2,1,0:T(8,128)S(1)}, u32[]{:S(2)}) copy-start(f32[5,192,96]{2,1,0:T(8,128)S(1)} %fusion.12) | copy-start | bytes 1105924
